TPU v7x, 32 devices: a whole 2x2x4 slice. The times are simulated.
32 devices in a mesh: tm: 2 (over x), gx: 4 (over y, core), gy: 4 (over z).
Axes of the slice: x: 2, y: 2, z: 4, core: 2. Of those that a mesh axis runs over, the one named last changes fastest.
Arguments:
- potential: float32 [64, 4, 128, 512], P('tm', None, 'gx', 'gy'), may hold values from -6 to 6
- source: float32 [64, 4, 128, 512], P('tm', None, 'gx', 'gy'), may hold values from -6 to 6
- region: int32 [128, 512], P('gx', 'gy'), may hold values from 0 to 7
- level_index: int32 [64], P('tm'), may hold values from 0 to 15
- reluctivity: float32 [16, 8], replicated, may hold values from 0.2 to 1
- saturation: float32 [8], replicated, may hold values from 0.05 to 0.4
- inverse: float32 [64, 128, 32], P('tm', 'gx'), may hold values from -1 to 1
- transmit: float32 [64, 4], P('tm', 'gx'), may hold values from 0.05 to 1.1
Outputs:
- correction: float32 [64, 4, 128, 512], P('tm', None, 'gx', 'gy')
All inputs are finite; a program needn't handle non-finite values.
Results may differ from a plain program's by a relative error of at most 0.00012.
Values sent between devices are 32-bit elements; how exact they have to be, the bound alone decides.
No kernel may reach another device: no remote copies, remote signals or barrier semaphores. Data moves between devices by JAX's collectives and lax.ppermute only.
A program may use at most 64 MiB of HBM per device.

v0:
```python
import math

import jax
import jax.numpy as jnp
from jax import lax
from jax.sharding import PartitionSpec as P

axial_coupling = 0.5


def with_halo(block, sides, width):
    for axis, dim in sides:
        count = lax.axis_size(axis)
        forward = [(i, i + 1) for i in range(count - 1)]
        backward = [(target, source) for source, target in forward]
        low = lax.ppermute(
            lax.slice_in_dim(block, block.shape[dim] - width, None, axis=dim), axis, forward
        )
        high = lax.ppermute(lax.slice_in_dim(block, 0, width, axis=dim), axis, backward)
        block = jnp.concatenate([low, block, high], axis=dim)
    return block


def shifted(block, axis, distance):
    devices = range(lax.axis_size(axis))
    route = [(i - distance, i) for i in devices if i - distance in devices]
    return lax.ppermute(block, axis, route)


def fourier_rows(row_count, sample_ids, sample_count):
    row_ids = lax.iota(jnp.int32, row_count)
    half_count = sample_count // 2
    harmonic = jnp.where(row_ids <= half_count, row_ids, row_ids - half_count)
    phase_index = harmonic[:, None] * sample_ids[None, :] % sample_count
    angle_value = phase_index.astype(jnp.float32) * (2.0 * math.pi / sample_count)
    dft_table = jnp.where(
        (row_ids <= half_count)[:, None], jnp.cos(angle_value), jnp.sin(angle_value)
    )
    return dft_table * math.sqrt(2.0 / sample_count)


def local(potential, source, region, level_index, reluctivity, saturation, inverse, transmit):
    samples_dev, planes, cells_x, cells_y = potential.shape
    sample_count = samples_dev * lax.axis_size("tm")
    level_count = reluctivity.shape[0]
    kind_count = reluctivity.shape[1]
    stacked = jnp.concatenate(
        [
            potential.reshape(samples_dev * planes, cells_x, cells_y),
            region.astype(jnp.float32)[None],
        ],
        axis=0,
    )
    padded = with_halo(stacked, (("gx", 1), ("gy", 2)), 1)
    field_all = padded[:-1].reshape(samples_dev, planes, cells_x + 2, cells_y + 2)
    material = padded[-1, :-1, :-1]
    pick_level = (level_index[:, None] == lax.iota(jnp.int32, level_count)[None, :]).astype(
        jnp.float32
    )
    base_rows = jnp.sum(pick_level[:, :, None] * reluctivity[None], axis=1)
    kind_ids = lax.iota(jnp.int32, kind_count).astype(jnp.float32)
    pick_kind = (material[None] == kind_ids[:, None, None]).astype(jnp.float32)
    base_cell = jnp.sum(base_rows[:, :, None, None] * pick_kind[None], axis=1)
    slope_cell = jnp.sum(saturation[:, None, None] * pick_kind, axis=0)
    corner = field_all[:, :, :-1, :-1]
    step_x = field_all[:, :, 1:, :-1] - corner
    step_y = field_all[:, :, :-1, 1:] - corner
    reluct = base_cell[:, None] * (1.0 + slope_cell * (step_x * step_x + step_y * step_y))
    flux_x = reluct * step_x
    flux_y = reluct * step_y
    curl_part = (
        flux_x[:, :, :-1, 1:] - flux_x[:, :, 1:, 1:] + flux_y[:, :, 1:, :-1] - flux_y[:, :, 1:, 1:]
    )
    zero_plane = jnp.zeros_like(potential[:, :1])
    plane_below = jnp.concatenate([zero_plane, potential[:, :-1]], axis=1)
    plane_above = jnp.concatenate([potential[:, 1:], zero_plane], axis=1)
    residual_time = (
        curl_part + axial_coupling * (2.0 * potential - plane_below - plane_above) - source
    )
    sample_ids = lax.axis_index("tm") * samples_dev + lax.iota(jnp.int32, samples_dev)
    flat_resid = residual_time.reshape(samples_dev, planes * cells_x * cells_y)
    dft_table = fourier_rows(samples_dev * lax.axis_size("tm"), sample_ids, sample_count)
    spectra = lax.psum_scatter(
        jnp.dot(
            dft_table,
            flat_resid,
            precision=lax.Precision.HIGHEST,
            preferred_element_type=jnp.float32,
        ),
        "tm",
        scatter_dimension=0,
        tiled=True,
    )
    spectra = spectra.reshape(samples_dev, planes, cells_x, cells_y)
    solved = jnp.einsum("qab,qpbj->qpaj", inverse, spectra, precision=lax.Precision.HIGHEST)
    line_tail = solved[:, :, cells_x - 1, :]
    gain_here = transmit[:, 0] * inverse[:, cells_x - 1, 0]
    factor = gain_here[:, None, None]

    def advance(turn_index, carried):
        return shifted(line_tail + factor * carried, "gx", 1)

    incoming = lax.fori_loop(0, lax.axis_size("gx") - 1, advance, jnp.zeros_like(line_tail))
    injected = transmit[:, 0][:, None, None] * incoming
    correction = solved + injected[:, :, None, :] * inverse[:, :, 0][:, None, :, None]
    return correction


def solution(mesh):
    in_specs = (
        P("tm", None, "gx", "gy"),
        P("tm", None, "gx", "gy"),
        P("gx", "gy"),
        P("tm"),
        P(),
        P(),
        P("tm", "gx", None),
        P("tm", "gx"),
    )
    out_specs = P("tm", None, "gx", "gy")
    return jax.shard_map(local, mesh=mesh, in_specs=in_specs, out_specs=out_specs, check_vma=False)
```

profile of v0, /device:TPU:12, one launch (start us, length us, event | category | flops | bytes accessed | tf_op | source)
XLA Modules:
  0.0 181.5 jit_solution(13811950934091916016)
XLA Ops:
  7.4 1.3 pad_maximum_fusion.7
  8.7 1.9 %collective-permute-start.1 = (f32[129,1,128]{2,1,0:T(1,128)S(1)}, f32[129,1,128]{2,1,0:T(1,128)S(1)}, u32[]{:S(2)}, u32[]{:S(2)}) collective-permute-start(f32[129,1,128]{2,1,0:T(1,128)S(1)} %get-tuple-element.43), channel_id=1, source_target_pairs={{0,4},{4,8},{8,12},{1,5},{5,9},{9,13},{2,6},{6,10},{10,14},{3,7},{... | collective-permute-start | bytes 198152 | tf_op jit(solution)/shard_map/ppermute | solution.py:16
  10.6 3.6 %collective-permute-start.2 = (f32[129,1,128]{2,1,0:T(1,128)S(1)}, f32[129,1,128]{2,1,0:T(1,128)S(1)}, u32[]{:S(2)}, u32[]{:S(2)}) collective-permute-start(f32[129,1,128]{2,1,0:T(1,128)S(1)} %get-tuple-element.44), channel_id=1, source_target_pairs={{4,0},{8,4},{12,8},{5,1},{9,5},{13,9},{6,2},{10,6},{14,10},{7,3},{... | collective-permute-start | bytes 198152 | tf_op jit(solution)/shard_map/ppermute | solution.py:19
  14.3 2.1 %fusion.37 = (f32[32,3,32,128]{3,2,1,0:T(8,128)}, f32[32,3,32,128]{3,2,1,0:T(8,128)}) fusion(f32[32,4,32,128]{3,2,1,0:T(8,128)S(1)} %copy-done), kind=kLoop, calls=%fused_computation.74 | loop fusion | bytes 6291456 | tf_op jit(solution)/shard_map/slice | solution.py:75
  17.1 3.1 %fusion.36 = (f32[129,34,1]{2,1,0:T(8,128)}, f32[129,34,1]{2,1,0:T(8,128)}) fusion(f32[129,34,128]{2,1,0:T(8,128)S(1)} %pad_maximum_fusion.5), kind=kLoop, calls=%fused_computation.73 | loop fusion | bytes 70176 | tf_op jit(solution)/shard_map/slice | solution.py:19
  20.2 3.1 %copy.50 = f32[129,34,1]{0,2,1:T(1,128)S(1)} copy(f32[129,34,1]{2,1,0:T(8,128)} %get-tuple-element.42) | data formatting | bytes 35088 | tf_op jit(solution)/shard_map/slice | solution.py:17
  23.3 3.5 %collective-permute-start.3 = (f32[129,34,1]{0,2,1:T(1,128)S(1)}, f32[129,34,1]{0,2,1:T(1,128)S(1)}, u32[]{:S(2)}, u32[]{:S(2)}) collective-permute-start(f32[129,34,1]{0,2,1:T(1,128)S(1)} %copy.50), channel_id=1, source_target_pairs={{0,1},{1,2},{2,3},{4,5},{5,6},{6,7},{8,9},{9,10},{10,11},{12,13},{... | collective-permute-start | bytes 52640 | tf_op jit(solution)/shard_map/ppermute | solution.py:16
  26.8 3.1 %copy.53 = f32[129,34,1]{0,2,1:T(1,128)S(1)} copy(f32[129,34,1]{2,1,0:T(8,128)} %get-tuple-element.41) | data formatting | bytes 35088 | tf_op jit(solution)/shard_map/slice | solution.py:19
  29.9 2.4 %collective-permute-start.4 = (f32[129,34,1]{0,2,1:T(1,128)S(1)}, f32[129,34,1]{0,2,1:T(1,128)S(1)}, u32[]{:S(2)}, u32[]{:S(2)}) collective-permute-start(f32[129,34,1]{0,2,1:T(1,128)S(1)} %copy.53), channel_id=1, source_target_pairs={{1,0},{2,1},{3,2},{5,4},{6,5},{7,6},{9,8},{10,9},{11,10},{13,12},{... | collective-permute-start | bytes 52640 | tf_op jit(solution)/shard_map/ppermute | solution.py:19
  32.3 4.0 %copy.100 = f32[32,3,32,128]{3,1,0,2:T(4,128)} copy(f32[32,3,32,128]{3,2,1,0:T(8,128)} %get-tuple-element.45) | data formatting | bytes 3145728
  36.3 2.4 %copy.99 = f32[32,3,32,128]{3,1,0,2:T(4,128)} copy(f32[32,3,32,128]{3,2,1,0:T(8,128)S(1)} %copy-done.4) | data formatting | bytes 3145728
  38.7 3.0 %copy.51 = f32[129,34,1]{2,1,0:T(8,128)} copy(f32[129,34,1]{0,2,1:T(1,128)S(1)} %collective-permute-done.3) | data formatting | bytes 35088 | tf_op jit(solution)/shard_map/ppermute | solution.py:16
  41.8 3.0 %copy.55 = f32[129,34,1]{2,1,0:T(8,128)} copy(f32[129,34,1]{0,2,1:T(1,128)S(1)} %collective-permute-done.4) | data formatting | bytes 35088 | tf_op jit(solution)/shard_map/ppermute | solution.py:19
  44.8 10.0 %pad_maximum_fusion = f32[128,34,130]{2,1,0:T(8,128)} fusion(f32[129,34,1]{2,1,0:T(8,128)} %copy.55, f32[129,34,1]{2,1,0:T(8,128)} %copy.51, f32[129,1,128]{2,1,0:T(1,128)S(1)} %collective-permute-done.2, f32[129,1,128]{2,1,0:T(1,128)S(1)} %collective-permute-done.1, f32[1,32,128]{2,1,0:T(8,128)S(1)} %convert_bitcast_fusion, f32[128,32,128]{2,1,0:T(8,128)S(1)} %bitcast.33), kind=kLoop, calls=%fused_computation.2 | loop fusion | flops 2828800 | bytes 4543760 | tf_op jit(solution)/shard_map/concatenate | solution.py:20
  54.7 13.1 %fusion.35 = (f32[32,4,33,129]{3,2,1,0:T(8,128)}, f32[32,4,33,129]{3,2,1,0:T(8,128)}, f32[32,4,33,129]{3,2,1,0:T(8,128)}) fusion(f32[32,4,34,130]{3,2,1,0:T(8,128)} %bitcast.35), kind=kLoop, calls=%fused_computation.72 | loop fusion | bytes 13077504 | tf_op jit(solution)/shard_map/slice | solution.py:67
  68.9 3.1 %multiply_reduce_fusion = f32[32,33,129]{2,1,0:T(8,128)S(1)} fusion(f32[8,33,129]{2,0,1:T(8,128)S(1)} %compare_convert_fusion, f32[32,8]{1,0:T(8,128)S(1)} %copy.49), kind=kLoop, calls=%fused_computation.1 | loop fusion | flops 2043360 | bytes 682144 | tf_op jit(solution)/shard_map/reduce_sum | solution.py:63
  72.5 8.9 %fusion.1 = (f32[32,4,33,129]{3,1,0,2:T(4,128)S(1)}, f32[32,4,33,129]{3,1,0,2:T(4,128)S(1)}) fusion(f32[33,129]{1,0:T(8,128)S(1)} %fusion.8, f32[32,33,129]{2,0,1:T(8,128)S(1)} %copy.52, f32[32,4,33,129]{3,2,1,0:T(8,128)} %get-tuple-element.39, f32[32,4,33,129]{3,2,1,0:T(8,128)} %get-tuple-element.40, f32[32,4,33,129]{3,2,1,0:T(8,128)S(1)} %copy-done.1), kind=kLoop, calls=%fused_computation.11 | loop fusion | flops 5448960 | bytes 11459844 | tf_op jit(solution)/shard_map/mul | solution.py:69
  81.5 6.2 %fusion.6 = f32[32,4,32,128]{3,1,0,2:T(4,128)S(1)} fusion(f32[32,4,33,129]{3,1,0,2:T(4,128)S(1)} %get-tuple-element.37, f32[32,4,33,129]{3,1,0,2:T(4,128)S(1)} %get-tuple-element.36, f32[32,4,32,128]{3,2,1,0:T(8,128)} %param.11, f32[32,3,32,128]{3,1,0,2:T(4,128)S(1)} %copy-done.3, f32[32,3,32,128]{3,1,0,2:T(4,128)S(1)} %copy-done.2, ...), kind=kLoop, calls=%fused_computation.18 | loop fusion | flops 4718592 | bytes 17825792 | tf_op jit(solution)/shard_map/sub | solution.py:78
  87.7 1.2 copy.61
  88.9 7.1 %fusion.2 = f32[64,16384]{1,0:T(8,128)} fusion(f32[4,8,128,128]{3,2,1,0:T(8,128)S(1)} %bitcast.36, s32[32]{0:T(128)S(1)} %iota_add_fusion, s32[64]{0:T(128)S(1)} %add_select_fusion.1, pred[64]{0:T(512)(128)(4,1)S(1)} %iota_compare_fusion.1), kind=kOutput, calls=%fused_computation.13 | convolution fusion | flops 402685952 | bytes 6291904 | tf_op jit(solution)/shard_map/dot_general | solution.py:84
  96.1 1.0 copy-done.5
  97.5 54.2 %reduce-scatter.2.cloned.1.call-done = f32[32,16384]{1,0:T(8,128)} async-done(((f32[64,16384]{1,0:T(8,128)}), f32[32,16384]{1,0:T(8,128)}) %reduce-scatter.2.cloned.1.call-update) | async-done | bytes 2097168 | tf_op jit(solution)/shard_map/reduce_scatter | solution.py:83
  151.7 2.0 %copy.72 = f32[4,8,128,128]{3,2,1,0:T(8,128)S(1)} copy(f32[4,8,128,128]{3,1,2,0:T(8,128)} %bitcast.40) | data formatting | bytes 4194304
  153.6 2.0 %convolution_bitcast_fusion = f32[32,4,32,128]{3,2,1,0:T(8,128)S(1)} fusion(f32[32,4,32,128]{3,2,1,0:T(8,128)S(1)} %bitcast.37, f32[32,32,32]{2,1,0:T(8,128)S(1)} %copy-done.5), kind=kOutput, calls=%fused_computation.22 | convolution fusion | flops 201326592 | bytes 4325376 | tf_op jit(solution)/shard_map/qab,qpbj->qpaj/dot_general | solution.py:95
  155.7 17.1 %while.10 = (s32[]{:T(128)}, f32[32,4,128]{2,1,0:T(4,128)S(1)}, f32[32,1,1]{0,2,1:T(1,128)S(1)}, f32[32,4,128]{2,1,0:T(4,128)S(1)}, s32[]{:T(128)}) while((s32[]{:T(128)}, f32[32,4,128]{2,1,0:T(4,128)S(1)}, f32[32,1,1]{0,2,1:T(1,128)S(1)}, f32[32,4,128]{2,1,0:T(4,128)S(1)}, s32[]{:T(128)}) %tuple.29), condition=%wide.region_5.6_spmd, body=%wide.region_4.5_spmd.sunk | while | flops 32770 | bytes 458981 | solution.py:103
  155.8 1.9 %collective-permute-start = (f32[32,4,128]{2,1,0:T(4,128)S(1)}, f32[32,4,128]{2,1,0:T(4,128)S(1)}, u32[]{:S(2)}, u32[]{:S(2)}) collective-permute-start(f32[32,4,128]{2,1,0:T(4,128)S(1)} %multiply_add_fusion.3), channel_id=1, source_target_pairs={{0,4},{4,8},{8,12},{1,5},{5,9},{9,13},{2,6},{6,10},{10,14},{3,7},{... | collective-permute-start | bytes 196616 | tf_op jit(solution)/shard_map/while/body/eval_jaxpr/ppermute | solution.py:27
  157.7 3.7 %collective-permute-done = f32[32,4,128]{2,1,0:T(4,128)S(1)} collective-permute-done((f32[32,4,128]{2,1,0:T(4,128)S(1)}, f32[32,4,128]{2,1,0:T(4,128)S(1)}, u32[]{:S(2)}, u32[]{:S(2)}) %collective-permute-start) | collective-permute-done | bytes 65568 | tf_op jit(solution)/shard_map/while/body/eval_jaxpr/ppermute | solution.py:27
  161.5 1.9 %collective-permute-start = (f32[32,4,128]{2,1,0:T(4,128)S(1)}, f32[32,4,128]{2,1,0:T(4,128)S(1)}, u32[]{:S(2)}, u32[]{:S(2)}) collective-permute-start(f32[32,4,128]{2,1,0:T(4,128)S(1)} %multiply_add_fusion.3), channel_id=1, source_target_pairs={{0,4},{4,8},{8,12},{1,5},{5,9},{9,13},{2,6},{6,10},{10,14},{3,7},{... | collective-permute-start | bytes 196616 | tf_op jit(solution)/shard_map/while/body/eval_jaxpr/ppermute | solution.py:27
  163.4 3.7 %collective-permute-done = f32[32,4,128]{2,1,0:T(4,128)S(1)} collective-permute-done((f32[32,4,128]{2,1,0:T(4,128)S(1)}, f32[32,4,128]{2,1,0:T(4,128)S(1)}, u32[]{:S(2)}, u32[]{:S(2)}) %collective-permute-start) | collective-permute-done | bytes 65568 | tf_op jit(solution)/shard_map/while/body/eval_jaxpr/ppermute | solution.py:27
  167.2 1.9 %collective-permute-start = (f32[32,4,128]{2,1,0:T(4,128)S(1)}, f32[32,4,128]{2,1,0:T(4,128)S(1)}, u32[]{:S(2)}, u32[]{:S(2)}) collective-permute-start(f32[32,4,128]{2,1,0:T(4,128)S(1)} %multiply_add_fusion.3), channel_id=1, source_target_pairs={{0,4},{4,8},{8,12},{1,5},{5,9},{9,13},{2,6},{6,10},{10,14},{3,7},{... | collective-permute-start | bytes 196616 | tf_op jit(solution)/shard_map/while/body/eval_jaxpr/ppermute | solution.py:27
  169.1 3.7 %collective-permute-done = f32[32,4,128]{2,1,0:T(4,128)S(1)} collective-permute-done((f32[32,4,128]{2,1,0:T(4,128)S(1)}, f32[32,4,128]{2,1,0:T(4,128)S(1)}, u32[]{:S(2)}, u32[]{:S(2)}) %collective-permute-start) | collective-permute-done | bytes 65568 | tf_op jit(solution)/shard_map/while/body/eval_jaxpr/ppermute | solution.py:27
  172.9 1.8 multiply_add_fusion.1
  (49 shorter events, 4.0 us)
Async XLA Ops:
  6.5 7.8 %copy-start = (f32[32,4,32,128]{3,2,1,0:T(8,128)S(1)}, f32[32,4,32,128]{3,2,1,0:T(8,128)}, u32[]{:S(2)}) copy-start(f32[32,4,32,128]{3,2,1,0:T(8,128)} %param.10) | copy-start | bytes 6291460
  6.5 145.1 %reduce-scatter.2.cloned.1.call-start = ((), (), s32[]{:S(2)}) async-start(), calls=%async_computation.1 | async-start | bytes 6291456 | tf_op jit(solution)/shard_map/reduce_scatter | solution.py:83
  8.7 8.0 %collective-permute-start.1 = (f32[129,1,128]{2,1,0:T(1,128)S(1)}, f32[129,1,128]{2,1,0:T(1,128)S(1)}, u32[]{:S(2)}, u32[]{:S(2)}) collective-permute-start(f32[129,1,128]{2,1,0:T(1,128)S(1)} %get-tuple-element.43), channel_id=1, source_target_pairs={{0,4},{4,8},{8,12},{1,5},{5,9},{9,13},{2,6},{6,10},{10,14},{3,7},{... | collective-permute-start | bytes 198152 | tf_op jit(solution)/shard_map/ppermute | solution.py:16
  10.6 6.0 %collective-permute-start.2 = (f32[129,1,128]{2,1,0:T(1,128)S(1)}, f32[129,1,128]{2,1,0:T(1,128)S(1)}, u32[]{:S(2)}, u32[]{:S(2)}) collective-permute-start(f32[129,1,128]{2,1,0:T(1,128)S(1)} %get-tuple-element.44), channel_id=1, source_target_pairs={{4,0},{8,4},{12,8},{5,1},{9,5},{13,9},{6,2},{10,6},{14,10},{7,3},{... | collective-permute-start | bytes 198152 | tf_op jit(solution)/shard_map/ppermute | solution.py:19
  14.3 2.2 %copy-start.6 = (f32[16,8]{0,1:T(8,128)S(1)}, f32[16,8]{0,1:T(8,128)}, u32[]{:S(2)}) copy-start(f32[16,8]{0,1:T(8,128)} %param.14) | copy-start | bytes 1540
  14.3 2.2 %copy-start.8 = (s32[32]{0:T(128)S(1)}, s32[32]{0:T(128)}, u32[]{:S(2)}) copy-start(s32[32]{0:T(128)} %param.13) | copy-start | bytes 388
  23.3 15.4 %collective-permute-start.3 = (f32[129,34,1]{0,2,1:T(1,128)S(1)}, f32[129,34,1]{0,2,1:T(1,128)S(1)}, u32[]{:S(2)}, u32[]{:S(2)}) collective-permute-start(f32[129,34,1]{0,2,1:T(1,128)S(1)} %copy.50), channel_id=1, source_target_pairs={{0,1},{1,2},{2,3},{4,5},{5,6},{6,7},{8,9},{9,10},{10,11},{12,13},{... | collective-permute-start | bytes 52640 | tf_op jit(solution)/shard_map/ppermute | solution.py:16
  29.9 11.9 %collective-permute-start.4 = (f32[129,34,1]{0,2,1:T(1,128)S(1)}, f32[129,34,1]{0,2,1:T(1,128)S(1)}, u32[]{:S(2)}, u32[]{:S(2)}) collective-permute-start(f32[129,34,1]{0,2,1:T(1,128)S(1)} %copy.53), channel_id=1, source_target_pairs={{1,0},{2,1},{3,2},{5,4},{6,5},{7,6},{9,8},{10,9},{11,10},{13,12},{... | collective-permute-start | bytes 52640 | tf_op jit(solution)/shard_map/ppermute | solution.py:19
  32.3 4.0 %copy-start.4 = (f32[32,3,32,128]{3,2,1,0:T(8,128)S(1)}, f32[32,3,32,128]{3,2,1,0:T(8,128)}, u32[]{:S(2)}) copy-start(f32[32,3,32,128]{3,2,1,0:T(8,128)} %get-tuple-element.46) | copy-start | bytes 4718596
  67.8 4.7 %copy-start.1 = (f32[32,4,33,129]{3,2,1,0:T(8,128)S(1)}, f32[32,4,33,129]{3,2,1,0:T(8,128)}, u32[]{:S(2)}) copy-start(f32[32,4,33,129]{3,2,1,0:T(8,128)} %get-tuple-element.38) | copy-start | bytes 6538756
  68.8 3.6 %copy-start.9 = (f32[8]{0:T(128)S(1)}, f32[8]{0:T(128)}, u32[]{:S(2)}) copy-start(f32[8]{0:T(128)} %param.15) | copy-start | bytes 100
  72.5 8.9 %copy-start.2 = (f32[32,3,32,128]{3,1,0,2:T(4,128)S(1)}, f32[32,3,32,128]{3,1,0,2:T(4,128)}, u32[]{:S(2)}) copy-start(f32[32,3,32,128]{3,1,0,2:T(4,128)} %copy.100) | copy-start | bytes 4718596
  72.5 8.9 %copy-start.3 = (f32[32,3,32,128]{3,1,0,2:T(4,128)S(1)}, f32[32,3,32,128]{3,1,0,2:T(4,128)}, u32[]{:S(2)}) copy-start(f32[32,3,32,128]{3,1,0,2:T(4,128)} %copy.99) | copy-start | bytes 4718596
  96.1 1.0 copy-start.5
  96.1 1.4 copy-start.7
  155.8 5.6 %collective-permute-start = (f32[32,4,128]{2,1,0:T(4,128)S(1)}, f32[32,4,128]{2,1,0:T(4,128)S(1)}, u32[]{:S(2)}, u32[]{:S(2)}) collective-permute-start(f32[32,4,128]{2,1,0:T(4,128)S(1)} %multiply_add_fusion.3), channel_id=1, source_target_pairs={{0,4},{4,8},{8,12},{1,5},{5,9},{9,13},{2,6},{6,10},{10,14},{3,7},{... | collective-permute-start | bytes 196616 | tf_op jit(solution)/shard_map/while/body/eval_jaxpr/ppermute | solution.py:27
  161.5 5.6 %collective-permute-start = (f32[32,4,128]{2,1,0:T(4,128)S(1)}, f32[32,4,128]{2,1,0:T(4,128)S(1)}, u32[]{:S(2)}, u32[]{:S(2)}) collective-permute-start(f32[32,4,128]{2,1,0:T(4,128)S(1)} %multiply_add_fusion.3), channel_id=1, source_target_pairs={{0,4},{4,8},{8,12},{1,5},{5,9},{9,13},{2,6},{6,10},{10,14},{3,7},{... | collective-permute-start | bytes 196616 | tf_op jit(solution)/shard_map/while/body/eval_jaxpr/ppermute | solution.py:27
  167.2 5.6 %collective-permute-start = (f32[32,4,128]{2,1,0:T(4,128)S(1)}, f32[32,4,128]{2,1,0:T(4,128)S(1)}, u32[]{:S(2)}, u32[]{:S(2)}) collective-permute-start(f32[32,4,128]{2,1,0:T(4,128)S(1)} %multiply_add_fusion.3), channel_id=1, source_target_pairs={{0,4},{4,8},{8,12},{1,5},{5,9},{9,13},{2,6},{6,10},{10,14},{3,7},{... | collective-permute-start | bytes 196616 | tf_op jit(solution)/shard_map/while/body/eval_jaxpr/ppermute | solution.py:27
Sparse Core Ops, SparseCore 0:
  96.2 55.4 reduce-scatter.1
where the time goes:
time: 182 us; the launch traced here: 181 us
  waiting for transfers between devices  65.2 us (36%)
  local copies, waits for them, and re-layouts  42.1 us (23%)
  other arithmetic  34.2 us (19%)
  starting transfers between devices  17.2 us (9%)
  between operations  13.7 us (8%)
  matrix products  9.08 us (5%)
    reduce_scatter x1, waiting for transfers between devices, local(): lax.psum_scatter(jnp.dot(dft_table, flat_resid, precision=lax.Precision.H...  54.2 us
    slice x1, local copies, waits for them, and re-layouts, local(): step_y = field_all[:, :, :-1, 1:] - corner  13.1 us
    ppermute x3, waiting for transfers between devices, shifted(): return lax.ppermute(block, axis, route)  11 us
    concatenate x2, other arithmetic, with_halo(): block = jnp.concatenate([low, block, high], axis=dim)  10.4 us
    unnamed x26, local copies, waits for them, and re-layouts  9.82 us
    mul x1, other arithmetic, local(): flux_x = reluct * step_x  8.89 us
    dot_general x1, matrix products, local(): jnp.dot(dft_table, flat_resid, precision=lax.Precision.HIGHEST, preferred...  7.13 us
    sub x1, other arithmetic, local(): curl_part + axial_coupling * (2.0 * potential - plane_below - plane_above)  6.24 us
  transfers between devices with their start and end apart: 8, of which 4 were waited for; matrix products, arithmetic and copies ran while one was open for 8% of the time, Pallas kernels for 0%

commit v1 on v0

v1 whole, which is shorter than its diff:
```python
import math

import jax
import jax.numpy as jnp
from jax import lax
from jax.sharding import PartitionSpec as P

axial_coupling = 0.5


def shifted(block, axes, sizes, delta):
    coords = [(i, j) for i in range(sizes[0]) for j in range(sizes[1])]
    route = []
    for i, j in coords:
        si, sj = i - delta[0], j - delta[1]
        if 0 <= si < sizes[0] and 0 <= sj < sizes[1]:
            route.append((si * sizes[1] + sj, i * sizes[1] + j))
    return lax.ppermute(block, axes, route)


def fourier_rows(row_ids, sample_ids, sample_count):
    half_count = sample_count // 2
    harmonic = jnp.where(row_ids <= half_count, row_ids, row_ids - half_count)
    phase_index = harmonic[:, None] * sample_ids[None, :] % sample_count
    angle_value = phase_index.astype(jnp.float32) * (2.0 * math.pi / sample_count)
    dft_table = jnp.where(
        (row_ids <= half_count)[:, None], jnp.cos(angle_value), jnp.sin(angle_value)
    )
    return dft_table * math.sqrt(2.0 / sample_count)


def local(potential, source, region, level_index, reluctivity, saturation, inverse, transmit):
    samples_dev, planes, cells_x, cells_y = potential.shape
    n_tm = lax.axis_size("tm")
    n_gx = lax.axis_size("gx")
    n_gy = lax.axis_size("gy")
    me_tm = lax.axis_index("tm")
    me_gx = lax.axis_index("gx")
    sample_count = samples_dev * n_tm
    grid = ("gx", "gy")
    sizes = (n_gx, n_gy)
    a = potential
    regf = region.astype(jnp.float32)

    msg_xlo = jnp.concatenate(
        [a[:, :, cells_x - 1, :].reshape(samples_dev * planes, cells_y), regf[cells_x - 1][None]], axis=0
    )
    msg_ylo = jnp.concatenate(
        [a[:, :, :, cells_y - 1].reshape(samples_dev * planes, cells_x), regf[:, cells_y - 1][None]], axis=0
    )
    got_xlo = shifted(msg_xlo, grid, sizes, (1, 0))
    got_ylo = shifted(msg_ylo, grid, sizes, (0, 1))
    got_xhi = shifted(a[:, :, 0, :], grid, sizes, (-1, 0))
    got_yhi = shifted(a[:, :, :, 0], grid, sizes, (0, -1))
    got_c1 = shifted(a[:, :, cells_x - 1, 0], grid, sizes, (1, -1))
    got_c2 = shifted(a[:, :, 0, cells_y - 1], grid, sizes, (-1, 1))

    xlo = got_xlo[:-1].reshape(samples_dev, planes, cells_y)
    reg_xlo = got_xlo[-1]
    ylo = got_ylo[:-1].reshape(samples_dev, planes, cells_x)
    reg_ylo = got_ylo[-1]
    xhi, yhi = got_xhi, got_yhi

    onehot = (level_index[:, None] == lax.iota(jnp.int32, reluctivity.shape[0])[None, :]).astype(jnp.float32)
    base_rows = jnp.sum(onehot[:, :, None] * reluctivity[None], axis=1)

    reg_xm = jnp.concatenate([reg_xlo[None, :].astype(jnp.int32), region[:-1]], axis=0)
    reg_ym = jnp.concatenate([reg_ylo[:, None].astype(jnp.int32), region[:, :-1]], axis=1)

    def reluct_of(kind, s_rows):
        out = s_rows[:, 0][:, None, None, None] + jnp.zeros(kind.shape, jnp.float32)[None, None]
        for k in range(1, s_rows.shape[-1]):
            out = jnp.where((kind == k)[None, None], s_rows[:, k][:, None, None, None], out)
        sl = jnp.full(kind.shape, saturation[0], jnp.float32)
        for k in range(1, saturation.shape[0]):
            sl = jnp.where(kind == k, saturation[k], sl)
        return out, sl[None, None]

    a_xp = jnp.concatenate([a[:, :, 1:, :], xhi[:, :, None, :]], axis=2)
    a_yp = jnp.concatenate([a[:, :, :, 1:], yhi[:, :, :, None]], axis=3)
    a_xm = jnp.concatenate([xlo[:, :, None, :], a[:, :, :-1, :]], axis=2)
    a_ym = jnp.concatenate([ylo[:, :, :, None], a[:, :, :, :-1]], axis=3)
    top = jnp.concatenate([xlo[:, :, 1:], got_c1[:, :, None]], axis=2)
    inner = jnp.concatenate([a[:, :, :-1, 1:], yhi[:, :, :-1, None]], axis=3)
    a_xm_yp = jnp.concatenate([top[:, :, None, :], inner], axis=2)
    bottom = jnp.concatenate([got_c2[:, :, None], xhi[:, :, :-1]], axis=2)
    inner2 = jnp.concatenate([ylo[:, :, 1:, None], a[:, :, 1:, :-1]], axis=3)
    a_xp_ym = jnp.concatenate([inner2, bottom[:, :, None, :]], axis=2)

    b0, s0 = reluct_of(region, base_rows)
    b1, s1 = reluct_of(reg_xm, base_rows)
    b2, s2 = reluct_of(reg_ym, base_rows)

    sx0 = a_xp - a
    sy0 = a_yp - a
    r0 = b0 * (1.0 + s0 * (sx0 * sx0 + sy0 * sy0))
    fx0 = r0 * sx0
    fy0 = r0 * sy0
    sx1 = a - a_xm
    sy1 = a_xm_yp - a_xm
    fx1 = b1 * (1.0 + s1 * (sx1 * sx1 + sy1 * sy1)) * sx1
    sx2 = a_xp_ym - a_ym
    sy2 = a - a_ym
    fy2 = b2 * (1.0 + s2 * (sx2 * sx2 + sy2 * sy2)) * sy2
    curl_part = fx1 - fx0 + fy2 - fy0
    zero_plane = jnp.zeros_like(a[:, :1])
    plane_below = jnp.concatenate([zero_plane, a[:, :-1]], axis=1)
    plane_above = jnp.concatenate([a[:, 1:], zero_plane], axis=1)
    residual_time = curl_part + axial_coupling * (2.0 * a - plane_below - plane_above) - source

    sample_ids = me_tm * samples_dev + lax.iota(jnp.int32, samples_dev)
    q_dev = samples_dev

    spectra_planes = []
    pending = []
    for p in range(planes):
        flat = residual_time[:, p].reshape(samples_dev, cells_x * cells_y)
        own_tab = fourier_rows(me_tm * q_dev + lax.iota(jnp.int32, q_dev), sample_ids, sample_count)
        acc = jnp.dot(own_tab, flat, precision=lax.Precision.HIGHEST, preferred_element_type=jnp.float32)
        for d in range(1, n_tm):
            owner = (me_tm + d) % n_tm
            tab = fourier_rows(owner * q_dev + lax.iota(jnp.int32, q_dev), sample_ids, sample_count)
            part = jnp.dot(tab, flat, precision=lax.Precision.HIGHEST, preferred_element_type=jnp.float32)
            route = [(i, (i + d) % n_tm) for i in range(n_tm)]
            acc = acc + lax.ppermute(part, "tm", route)
        spectra_planes.append(acc.reshape(q_dev, cells_x, cells_y))
    spectra = jnp.stack(spectra_planes, axis=1)

    solved = jnp.einsum("qab,qpbj->qpaj", inverse, spectra, precision=lax.Precision.HIGHEST)
    line_tail = solved[:, :, cells_x - 1, :]
    gain_here = transmit[:, 0] * inverse[:, cells_x - 1, 0]

    tails = []
    gains = []
    for d in range(n_gx - 1, 0, -1):
        route = [(i, i + d) for i in range(n_gx - d)]
        tails.append(lax.ppermute(line_tail, "gx", route))
        gains.append(lax.ppermute(gain_here, "gx", route))
    carried = jnp.zeros_like(line_tail)
    for idx, d in enumerate(range(n_gx - 1, 0, -1)):
        stepped = tails[idx] + gains[idx][:, None, None] * carried
        carried = jnp.where(me_gx >= d, stepped, carried)
    injected = transmit[:, 0][:, None, None] * carried
    correction = solved + injected[:, :, None, :] * inverse[:, :, 0][:, None, :, None]
    return correction


def solution(mesh):
    in_specs = (
        P("tm", None, "gx", "gy"),
        P("tm", None, "gx", "gy"),
        P("gx", "gy"),
        P("tm"),
        P(),
        P(),
        P("tm", "gx", None),
        P("tm", "gx"),
    )
    out_specs = P("tm", None, "gx", "gy")
    return jax.shard_map(local, mesh=mesh, in_specs=in_specs, out_specs=out_specs, check_vma=False)
```

time: 182 us -> 148 us (0.81)
  waiting for transfers between devices: 65.2 us -> 37.4 us
  between operations: 13.7 us -> 0.79 us
  starting transfers between devices: 17.2 us -> 30.1 us
  local copies, waits for them, and re-layouts: 42.1 us -> 33 us
    reduce_scatter x1 -> x0, waiting for transfers between devices: 54.2 us -> none  [local(): lax.psum_scatter(jnp.dot(dft_table, flat_resid, precision=lax.Precision.H...]
    ppermute x7 -> x16, waiting for transfers between devices: 11 us -> 37.4 us  [the longest x4 33.8 us: local(): acc = acc + lax.ppermute(part, 'tm', route)]
    select_n x0 -> x6, other arithmetic: none -> 17.6 us  [the longest x3 15.1 us: reluct_of(): sl = jnp.where(kind == k, saturation[k], sl)]
    ppermute x7 -> x16, starting transfers between devices: 17.2 us -> 30.1 us  [the longest x6 17.3 us: shifted(): return lax.ppermute(block, axes, route)]
    concatenate x2 -> x4, other arithmetic: 10.4 us -> 1.47 us  [the longest x1 0.64 us: local(): jnp.concatenate([a[:, :, :, cells_y - 1].reshape(samples_dev * planes, ce...]
    mul x2, other arithmetic: 8.99 us -> 0.83 us  [the longest x1 0.63 us: local(): stepped = tails[idx] + gains[idx][:, None, None] * carried]
    broadcast_in_dim x1 -> x7, local copies, waits for them, and re-layouts: 0.01 us -> 7.52 us  [the longest x2 2.25 us: local(): inner = jnp.concatenate([a[:, :, :-1, 1:], yhi[:, :, :-1, None]], axis=3)]
    unnamed x26 -> x72, local copies, waits for them, and re-layouts: 9.82 us -> 3.24 us
  transfers between devices with their start and end apart: 8 -> 16, of which waited for: 4 -> 6; matrix products, arithmetic and copies ran while one was open for 8% -> 48% of each run, Pallas kernels for 0% -> 0%
where the time goes in v1:
time: 148 us; the launch traced here: 146 us
  waiting for transfers between devices  37.4 us (25%)
  other arithmetic  34.8 us (24%)
  local copies, waits for them, and re-layouts  33 us (22%)
  starting transfers between devices  30.1 us (20%)
  matrix products  9.93 us (7%)
    ppermute x4, waiting for transfers between devices, local(): acc = acc + lax.ppermute(part, 'tm', route)  33.8 us
    ppermute x6, starting transfers between devices, shifted(): return lax.ppermute(block, axes, route)  17.3 us
    select_n x3, other arithmetic, reluct_of(): sl = jnp.where(kind == k, saturation[k], sl)  15.1 us
    sub x1, other arithmetic, local(): curl_part + axial_coupling * (2.0 * a - plane_below - plane_above) - source  11.2 us
    slice x1, local copies, waits for them, and re-layouts, local(): a[:, :, :, cells_y - 1].reshape(samples_dev * planes, cells_x)  5.08 us
    ppermute x3, starting transfers between devices, local(): gains.append(lax.ppermute(gain_here, 'gx', route))  4.6 us
    ppermute x4, starting transfers between devices, local(): acc = acc + lax.ppermute(part, 'tm', route)  4.33 us
    dot_general x4, matrix products, local(): jnp.dot(own_tab, flat, precision=lax.Precision.HIGHEST, preferred_element...  3.99 us
  transfers between devices with their start and end apart: 16, of which 6 were waited for; matrix products, arithmetic and copies ran while one was open for 48% of the time, Pallas kernels for 0%

profile of v1, /device:TPU:12, one launch (start us, length us, event | category | flops | bytes accessed | tf_op | source)
XLA Modules:
  0.0 146.0 jit_solution(13808794256978564638)
XLA Ops:
  0.0 5.1 %slice_reduce_fusion = (f32[32,4,32]{2,1,0:T(4,128)S(1)}, f32[32,4,32,1]{3,2,1,0:T(8,128)}) fusion(f32[32,4,32,128]{3,2,1,0:T(8,128)} %param.8), kind=kLoop, calls=%fused_computation.36 | loop fusion | bytes 65536 | tf_op jit(solution)/shard_map/slice | solution.py:49
  5.9 3.5 %collective-permute-start.4 = (f32[129,32]{1,0:T(8,128)}, f32[129,32]{1,0:T(8,128)}, u32[]{:S(2)}, u32[]{:S(2)}) collective-permute-start(f32[129,32]{1,0:T(8,128)} %pad_maximum_fusion.3), channel_id=1, source_target_pairs={{0,1},{1,2},{2,3},{4,5},{5,6},{6,7},{8,9},{9,10},{10,11},{12,13},{... | collective-permute-start | bytes 49544 | tf_op jit(solution)/shard_map/ppermute | solution.py:18
  10.8 1.9 %collective-permute-start = (f32[129,128]{1,0:T(8,128)}, f32[129,128]{1,0:T(8,128)}, u32[]{:S(2)}, u32[]{:S(2)}) collective-permute-start(f32[129,128]{1,0:T(8,128)} %pad_maximum_fusion.2), channel_id=1, source_target_pairs={{0,4},{1,5},{2,6},{3,7},{4,8},{5,9},{6,10},{7,11},{8,12},{9,13},{1... | collective-permute-start | bytes 198152 | tf_op jit(solution)/shard_map/ppermute | solution.py:18
  13.0 1.9 %collective-permute-start.1 = (f32[32,4]{0,1:T(4,128)S(1)}, f32[32,4]{0,1:T(4,128)S(1)}, u32[]{:S(2)}, u32[]{:S(2)}) collective-permute-start(f32[32,4]{0,1:T(4,128)S(1)} %bitcast.161), channel_id=1, source_target_pairs={{1,4},{2,5},{3,6},{5,8},{6,9},{7,10},{9,12},{10,13},{11,14},{17,20... | collective-permute-start | bytes 1544 | tf_op jit(solution)/shard_map/ppermute | solution.py:18
  15.0 4.7 %collective-permute-start.5 = (f32[32,4]{0,1:T(4,128)S(1)}, f32[32,4]{0,1:T(4,128)S(1)}, u32[]{:S(2)}, u32[]{:S(2)}) collective-permute-start(f32[32,4]{0,1:T(4,128)S(1)} %bitcast.160), channel_id=1, source_target_pairs={{4,1},{5,2},{6,3},{8,5},{9,6},{10,7},{12,9},{13,10},{14,11},{20,17... | collective-permute-start | bytes 1544 | tf_op jit(solution)/shard_map/ppermute | solution.py:18
  19.7 2.4 %copy.108 = f32[32,4,32,1]{2,0,1,3:T(8,128)S(1)} copy(f32[32,4,32,1]{3,2,1,0:T(8,128)} %get-tuple-element.40) | data formatting | bytes 32768
  22.1 2.9 %collective-permute-start.2 = (f32[32,4,32]{2,0,1:T(8,128)S(1)}, f32[32,4,32]{2,0,1:T(8,128)S(1)}, u32[]{:S(2)}, u32[]{:S(2)}) collective-permute-start(f32[32,4,32]{2,0,1:T(8,128)S(1)} %bitcast.153), channel_id=1, source_target_pairs={{1,0},{2,1},{3,2},{5,4},{6,5},{7,6},{9,8},{10,9},{11,10},{13,12},{... | collective-permute-start | bytes 49160 | tf_op jit(solution)/shard_map/ppermute | solution.py:18
  24.9 2.7 %fusion.104 = (f32[32,4,31,128]{3,2,1,0:T(8,128)}, f32[32,4,31,128]{3,2,1,0:T(8,128)}) fusion(f32[32,4,32,128]{3,2,1,0:T(8,128)S(1)} %copy-done), kind=kLoop, calls=%fused_computation.183 | loop fusion | bytes 8126464 | tf_op jit(solution)/shard_map/slice | solution.py:81
  27.6 2.8 %fusion.105 = (f32[32,4,32,127]{3,2,1,0:T(8,128)}, f32[32,4,32,127]{3,2,1,0:T(8,128)}) fusion(f32[32,4,32,128]{3,2,1,0:T(8,128)S(1)} %copy-done), kind=kLoop, calls=%fused_computation.184 | loop fusion | bytes 8323072 | tf_op jit(solution)/shard_map/slice | solution.py:80
  30.4 2.8 %fusion.107 = (f32[32,4,31,127]{3,2,1,0:T(8,128)}, f32[32,4,31,127]{3,2,1,0:T(8,128)}) fusion(f32[32,4,32,128]{3,2,1,0:T(8,128)S(1)} %copy-done), kind=kLoop, calls=%fused_computation.186 | loop fusion | bytes 8062976 | tf_op jit(solution)/shard_map/slice | solution.py:87
  33.2 2.2 %fusion.106 = (f32[32,3,32,128]{3,2,1,0:T(8,128)}, f32[32,3,32,128]{3,2,1,0:T(8,128)}) fusion(f32[32,4,32,128]{3,2,1,0:T(8,128)S(1)} %copy-done), kind=kLoop, calls=%fused_computation.185 | loop fusion | bytes 6291456 | tf_op jit(solution)/shard_map/slice | solution.py:107
  37.3 5.0 %select_select_fusion.4 = (f32[32,128]{1,0:T(8,128)S(1)}, pred[32,128]{1,0:T(8,128)(4,1)S(1)}, pred[32,128]{1,0:T(8,128)(4,1)S(1)}, pred[32,128]{1,0:T(8,128)(4,...) fusion(f32[]{:T(128)} %bitcast.16, f32[]{:T(128)} %bitcast.15, ...), kind=kLoop, calls=%fused_computation.96 | loop fusion | flops 57344 | bytes 61472 | tf_op jit(solution)/shard_map/jit(_where)/select_n | solution.py:76
  43.0 2.5 %collective-permute-start.3 = (f32[32,4,128]{2,1,0:T(4,128)}, f32[32,4,128]{2,1,0:T(4,128)S(1)}, u32[]{:S(2)}, u32[]{:S(2)}) collective-permute-start(f32[32,4,128]{2,1,0:T(4,128)} %bitcast.25), channel_id=1, source_target_pairs={{4,0},{5,1},{6,2},{7,3},{8,4},{9,5},{10,6},{11,7},{12,8},{13,9},{1... | collective-permute-start | bytes 196616 | tf_op jit(solution)/shard_map/ppermute | solution.py:18
  47.6 2.2 %copy.92 = f32[32,4,31,1]{3,2,1,0:T(8,128)} copy(f32[32,4,31,1]{2,0,1,3:T(8,128)S(1)} %slice_bitcast_fusion) | data formatting | bytes 31744 | tf_op jit(solution)/shard_map/broadcast_in_dim | solution.py:84
  49.9 2.1 %copy.95 = f32[32,4,32,1]{3,2,1,0:T(8,128)} copy(f32[32,4,32,1]{2,0,3,1:T(8,128)S(1)} %bitcast.147) | data formatting | bytes 32768 | tf_op jit(solution)/shard_map/broadcast_in_dim | solution.py:80
  52.8 5.1 %select_select_fusion.3 = (f32[32,128]{1,0:T(8,128)S(1)}, pred[32,128]{1,0:T(8,128)(4,1)S(1)}, pred[32,128]{1,0:T(8,128)(4,1)S(1)}, pred[32,128]{1,0:T(8,128)(4,...) fusion(f32[]{:T(128)} %bitcast.16, f32[]{:T(128)} %bitcast.15, ...), kind=kLoop, calls=%fused_computation.95 | loop fusion | flops 61440 | bytes 61472 | tf_op jit(solution)/shard_map/jit(_where)/select_n | solution.py:76
  58.0 1.8 %select_select_fusion = f32[32,32,128]{2,1,0:T(8,128)} fusion(f32[32]{0:T(128)S(1)} %copy-done.7, f32[32]{0:T(128)S(1)} %copy-done.10, f32[32]{0:T(128)S(1)} %copy-done.13, f32[32]{0:T(128)S(1)} %copy-done.16, f32[32]{0:T(128)S(1)} %copy-done.19, f32[32]{0:T(128)S(1)} %copy-done.22, f32[32]{0:T(128)S(1)} %copy-done.25, f32[32]{0:T(128)} %copy-done.4, ...), kind=kLoop, calls=%fused_computation.55 | loop fusion | flops 917504 | bytes 553984 | tf_op jit(solution)/shard_map/jit(_where)/select_n | solution.py:73
  60.8 2.2 %copy.98 = f32[32,4,31,1]{3,2,1,0:T(8,128)} copy(f32[32,4,31,1]{2,0,1,3:T(8,128)S(1)} %bitcast.148) | data formatting | bytes 31744 | tf_op jit(solution)/shard_map/broadcast_in_dim | solution.py:87
  63.0 2.2 %copy.101 = f32[32,4,32,1]{3,2,1,0:T(8,128)} copy(f32[32,4,32,1]{2,1,0,3:T(4,128)S(1)} %bitcast.141) | data formatting | bytes 32768 | tf_op jit(solution)/shard_map/broadcast_in_dim;reshape | solution.py:82
  67.0 5.0 %select_select_fusion.5 = (f32[32,128]{1,0:T(8,128)S(1)}, pred[32,128]{1,0:T(8,128)(4,1)S(1)}, pred[32,128]{1,0:T(8,128)(4,1)S(1)}, pred[32,128]{1,0:T(8,128)(4,...) fusion(f32[]{:T(128)} %bitcast.16, f32[]{:T(128)} %bitcast.15, ...), kind=kLoop, calls=%fused_computation.97 | loop fusion | flops 61440 | bytes 61472 | tf_op jit(solution)/shard_map/jit(_where)/select_n | solution.py:76
  72.5 11.2 %fusion.10 = f32[32,4,32,128]{3,2,1,0:T(8,128)S(1)} fusion(f32[32,4,32,128]{3,2,1,0:T(8,128)} %param.9, f32[32,4,31,1]{3,2,1,0:T(8,128)} %copy.92, f32[32,4,31,127]{3,2,1,0:T(8,128)} %get-tuple-element.42, f32[32,4,1,128]{3,2,1,0:T(1,128)S(1)} %bitcast.145, f32[32,4,1,128]{3,2,1,0:T(1,128)S(1)} %bitcast.144, f32[32,4,31,127]{3,2,1,0:T(8,128)} %get-tuple-element.41, ...), kind=kLoop, calls=%fused_computation.16 | loop fusion | flops 23592960 | bytes 23642112 | tf_op jit(solution)/shard_map/sub | solution.py:109
  84.9 1.6 %collective-permute-start.6 = (f32[32,4096]{1,0:T(8,128)S(1)}, f32[32,4096]{1,0:T(8,128)S(1)}, u32[]{:S(2)}, u32[]{:S(2)}) collective-permute-start(f32[32,4096]{1,0:T(8,128)S(1)} %fusion.41), channel_id=1, source_target_pairs={{0,16},{16,0},{1,17},{17,1},{2,18},{18,2},{3,19},{19,3},{4,20},{20... | collective-permute-start | bytes 1572872 | tf_op jit(solution)/shard_map/ppermute | solution.py:125
  89.0 1.6 %collective-permute-start.8 = (f32[32,4096]{1,0:T(8,128)S(1)}, f32[32,4096]{1,0:T(8,128)S(1)}, u32[]{:S(2)}, u32[]{:S(2)}) collective-permute-start(f32[32,4096]{1,0:T(8,128)S(1)} %fusion.35), channel_id=1, source_target_pairs={{0,16},{16,0},{1,17},{17,1},{2,18},{18,2},{3,19},{19,3},{4,20},{20... | collective-permute-start | bytes 1572872 | tf_op jit(solution)/shard_map/ppermute | solution.py:125
  92.2 7.5 %collective-permute-done.6 = f32[32,4096]{1,0:T(8,128)S(1)} collective-permute-done((f32[32,4096]{1,0:T(8,128)S(1)}, f32[32,4096]{1,0:T(8,128)S(1)}, u32[]{:S(2)}, u32[]{:S(2)}) %collective-permute-start.6) | collective-permute-done | bytes 524320 | tf_op jit(solution)/shard_map/ppermute | solution.py:125
  99.7 1.9 %collective-permute-start.11 = (f32[32]{0:T(128)}, f32[32]{0:T(128)S(1)}, u32[]{:S(2)}, u32[]{:S(2)}) collective-permute-start(f32[32]{0:T(128)} %bitcast_multiply_fusion), channel_id=1, source_target_pairs={{0,4},{4,8},{8,12},{1,5},{5,9},{9,13},{2,6},{6,10},{10,14},{3,7},{... | collective-permute-start | bytes 392 | tf_op jit(solution)/shard_map/ppermute | solution.py:138
  102.7 8.2 %collective-permute-done.7 = f32[32,4096]{1,0:T(8,128)S(1)} collective-permute-done((f32[32,4096]{1,0:T(8,128)S(1)}, f32[32,4096]{1,0:T(8,128)S(1)}, u32[]{:S(2)}, u32[]{:S(2)}) %collective-permute-start.7) | collective-permute-done | bytes 524320 | tf_op jit(solution)/shard_map/ppermute | solution.py:125
  113.6 8.6 %collective-permute-done.8 = f32[32,4096]{1,0:T(8,128)S(1)} collective-permute-done((f32[32,4096]{1,0:T(8,128)S(1)}, f32[32,4096]{1,0:T(8,128)S(1)}, u32[]{:S(2)}, u32[]{:S(2)}) %collective-permute-start.8) | collective-permute-done | bytes 524320 | tf_op jit(solution)/shard_map/ppermute | solution.py:125
  123.3 9.5 %collective-permute-done.9 = f32[32,4096]{1,0:T(8,128)S(1)} collective-permute-done((f32[32,4096]{1,0:T(8,128)S(1)}, f32[32,4096]{1,0:T(8,128)S(1)}, u32[]{:S(2)}, u32[]{:S(2)}) %collective-permute-start.9) | collective-permute-done | bytes 524320 | tf_op jit(solution)/shard_map/ppermute | solution.py:125
  133.9 2.0 %fusion.25 = f32[32,4,32,128]{3,2,1,0:T(8,128)S(1)} fusion(f32[32,1,32,128]{3,2,1,0:T(8,128)S(1)} %bitcast.137, f32[32,1,32,128]{3,2,1,0:T(8,128)S(1)} %bitcast.136, f32[32,1,32,128]{3,2,1,0:T(8,128)S(1)} %bitcast.135, f32[32,1,32,128]{3,2,1,0:T(8,128)S(1)} %bitcast.134, f32[32,32,32]{2,1,0:T(8,128)S(1)} %copy-done.1), kind=kOutput, calls=%fused_computation.37 | convolution fusion | flops 202899456 | bytes 4325376 | tf_op jit(solution)/shard_map/qab,qpbj->qpaj/dot_general | solution.py:129
  136.0 1.9 %collective-permute-start.10 = (f32[32,4,128]{2,1,0:T(4,128)S(1)}, f32[32,4,128]{2,1,0:T(4,128)S(1)}, u32[]{:S(2)}, u32[]{:S(2)}) collective-permute-start(f32[32,4,128]{2,1,0:T(4,128)S(1)} %bitcast.154), channel_id=1, source_target_pairs={{0,4},{4,8},{8,12},{1,5},{5,9},{9,13},{2,6},{6,10},{10,14},{3,7},{... | collective-permute-start | bytes 196616 | tf_op jit(solution)/shard_map/ppermute | solution.py:137
  141.5 2.5 %collective-permute-done.12 = f32[32,4,128]{2,1,0:T(4,128)S(1)} collective-permute-done((f32[32,4,128]{2,1,0:T(4,128)S(1)}, f32[32,4,128]{2,1,0:T(4,128)S(1)}, u32[]{:S(2)}, u32[]{:S(2)}) %collective-permute-start.12) | collective-permute-done | bytes 65568 | tf_op jit(solution)/shard_map/ppermute | solution.py:137
  144.3 1.7 %multiply_add_fusion = f32[32,4,32,128]{3,2,1,0:T(8,128)} fusion(f32[32,4,32,128]{3,2,1,0:T(8,128)S(1)} %fusion.25, f32[32,32]{1,0:T(8,128)S(1)} %bitcast.152, f32[32,4,128]{2,1,0:T(4,128)S(1)} %select_multiply_fusion), kind=kLoop, calls=%fused_computation.35 | loop fusion | flops 1048576 | bytes 4263936 | tf_op jit(solution)/shard_map/add | solution.py:144
  (133 shorter events, 26.2 us)
Async XLA Ops:
  0.0 9.4 %copy-start = (f32[32,4,32,128]{3,2,1,0:T(8,128)S(1)}, f32[32,4,32,128]{3,2,1,0:T(8,128)}, u32[]{:S(2)}) copy-start(f32[32,4,32,128]{3,2,1,0:T(8,128)} %param.8) | copy-start | bytes 6291460
  5.9 46.1 %collective-permute-start.4 = (f32[129,32]{1,0:T(8,128)}, f32[129,32]{1,0:T(8,128)}, u32[]{:S(2)}, u32[]{:S(2)}) collective-permute-start(f32[129,32]{1,0:T(8,128)} %pad_maximum_fusion.3), channel_id=1, source_target_pairs={{0,1},{1,2},{2,3},{4,5},{5,6},{6,7},{8,9},{9,10},{10,11},{12,13},{... | collective-permute-start | bytes 49544 | tf_op jit(solution)/shard_map/ppermute | solution.py:18
  10.8 54.5 %collective-permute-start = (f32[129,128]{1,0:T(8,128)}, f32[129,128]{1,0:T(8,128)}, u32[]{:S(2)}, u32[]{:S(2)}) collective-permute-start(f32[129,128]{1,0:T(8,128)} %pad_maximum_fusion.2), channel_id=1, source_target_pairs={{0,4},{1,5},{2,6},{3,7},{4,8},{5,9},{6,10},{7,11},{8,12},{9,13},{1... | collective-permute-start | bytes 198152 | tf_op jit(solution)/shard_map/ppermute | solution.py:18
  13.0 29.9 %collective-permute-start.1 = (f32[32,4]{0,1:T(4,128)S(1)}, f32[32,4]{0,1:T(4,128)S(1)}, u32[]{:S(2)}, u32[]{:S(2)}) collective-permute-start(f32[32,4]{0,1:T(4,128)S(1)} %bitcast.161), channel_id=1, source_target_pairs={{1,4},{2,5},{3,6},{5,8},{6,9},{7,10},{9,12},{10,13},{11,14},{17,20... | collective-permute-start | bytes 1544 | tf_op jit(solution)/shard_map/ppermute | solution.py:18
  15.0 30.6 %collective-permute-start.5 = (f32[32,4]{0,1:T(4,128)S(1)}, f32[32,4]{0,1:T(4,128)S(1)}, u32[]{:S(2)}, u32[]{:S(2)}) collective-permute-start(f32[32,4]{0,1:T(4,128)S(1)} %bitcast.160), channel_id=1, source_target_pairs={{4,1},{5,2},{6,3},{8,5},{9,6},{10,7},{12,9},{13,10},{14,11},{20,17... | collective-permute-start | bytes 1544 | tf_op jit(solution)/shard_map/ppermute | solution.py:18
  22.1 25.5 %collective-permute-start.2 = (f32[32,4,32]{2,0,1:T(8,128)S(1)}, f32[32,4,32]{2,0,1:T(8,128)S(1)}, u32[]{:S(2)}, u32[]{:S(2)}) collective-permute-start(f32[32,4,32]{2,0,1:T(8,128)S(1)} %bitcast.153), channel_id=1, source_target_pairs={{1,0},{2,1},{3,2},{5,4},{6,5},{7,6},{9,8},{10,9},{11,10},{13,12},{... | collective-permute-start | bytes 49160 | tf_op jit(solution)/shard_map/ppermute | solution.py:18
  36.3 15.7 %copy-start.4 = (f32[32]{0:T(128)}, f32[32]{0:T(128)S(1)}, u32[]{:S(2)}) copy-start(f32[32]{0:T(128)S(1)} %get-tuple-element.47) | copy-start | bytes 388
  43.0 22.2 %collective-permute-start.3 = (f32[32,4,128]{2,1,0:T(4,128)}, f32[32,4,128]{2,1,0:T(4,128)S(1)}, u32[]{:S(2)}, u32[]{:S(2)}) collective-permute-start(f32[32,4,128]{2,1,0:T(4,128)} %bitcast.25), channel_id=1, source_target_pairs={{4,0},{5,1},{6,2},{7,3},{8,4},{9,5},{10,6},{11,7},{12,8},{13,9},{1... | collective-permute-start | bytes 196616 | tf_op jit(solution)/shard_map/ppermute | solution.py:18
  45.6 93.6 %collective-permute-start.15 = (f32[32]{0:T(128)}, f32[32]{0:T(128)}, u32[]{:S(2)}, u32[]{:S(2)}) collective-permute-start(f32[32]{0:T(128)} %bitcast_multiply_fusion), channel_id=1, source_target_pairs={{0,12},{1,13},{2,14},{3,15},{16,28},{17,29},{18,30},{19,31}} | collective-permute-start | bytes 392 | tf_op jit(solution)/shard_map/ppermute | solution.py:138
  49.9 8.0 %copy-start.13 = (f32[32]{0:T(128)S(1)}, f32[32]{0:T(128)}, u32[]{:S(2)}) copy-start(f32[32]{0:T(128)} %copy-done.12) | copy-start | bytes 388
  49.9 8.0 %copy-start.16 = (f32[32]{0:T(128)S(1)}, f32[32]{0:T(128)}, u32[]{:S(2)}) copy-start(f32[32]{0:T(128)} %copy-done.15) | copy-start | bytes 388
  49.9 8.0 %copy-start.19 = (f32[32]{0:T(128)S(1)}, f32[32]{0:T(128)}, u32[]{:S(2)}) copy-start(f32[32]{0:T(128)} %copy-done.18) | copy-start | bytes 388
  49.9 8.0 %copy-start.22 = (f32[32]{0:T(128)S(1)}, f32[32]{0:T(128)}, u32[]{:S(2)}) copy-start(f32[32]{0:T(128)} %copy-done.21) | copy-start | bytes 388
  49.9 8.0 %copy-start.25 = (f32[32]{0:T(128)S(1)}, f32[32]{0:T(128)}, u32[]{:S(2)}) copy-start(f32[32]{0:T(128)} %copy-done.24) | copy-start | bytes 388
  63.0 9.1 %copy-start.5 = (f32[32]{0:T(128)S(1)}, f32[32]{0:T(128)}, u32[]{:S(2)}) copy-start(f32[32]{0:T(128)} %copy-done.4) | copy-start | bytes 388
  63.0 9.1 %copy-start.8 = (f32[32]{0:T(128)S(1)}, f32[32]{0:T(128)}, u32[]{:S(2)}) copy-start(f32[32]{0:T(128)} %copy-done.6) | copy-start | bytes 388
  63.0 9.1 %copy-start.11 = (f32[32]{0:T(128)S(1)}, f32[32]{0:T(128)}, u32[]{:S(2)}) copy-start(f32[32]{0:T(128)} %copy-done.9) | copy-start | bytes 388
  63.0 9.1 %copy-start.14 = (f32[32]{0:T(128)S(1)}, f32[32]{0:T(128)}, u32[]{:S(2)}) copy-start(f32[32]{0:T(128)} %copy-done.12) | copy-start | bytes 388
  63.0 9.1 %copy-start.17 = (f32[32]{0:T(128)S(1)}, f32[32]{0:T(128)}, u32[]{:S(2)}) copy-start(f32[32]{0:T(128)} %copy-done.15) | copy-start | bytes 388
  63.0 9.1 %copy-start.20 = (f32[32]{0:T(128)S(1)}, f32[32]{0:T(128)}, u32[]{:S(2)}) copy-start(f32[32]{0:T(128)} %copy-done.18) | copy-start | bytes 388
  63.0 9.1 %copy-start.23 = (f32[32]{0:T(128)S(1)}, f32[32]{0:T(128)}, u32[]{:S(2)}) copy-start(f32[32]{0:T(128)} %copy-done.21) | copy-start | bytes 388
  63.0 9.1 %copy-start.26 = (f32[32]{0:T(128)S(1)}, f32[32]{0:T(128)}, u32[]{:S(2)}) copy-start(f32[32]{0:T(128)} %copy-done.24) | copy-start | bytes 388
  84.9 14.8 %collective-permute-start.6 = (f32[32,4096]{1,0:T(8,128)S(1)}, f32[32,4096]{1,0:T(8,128)S(1)}, u32[]{:S(2)}, u32[]{:S(2)}) collective-permute-start(f32[32,4096]{1,0:T(8,128)S(1)} %fusion.41), channel_id=1, source_target_pairs={{0,16},{16,0},{1,17},{17,1},{2,18},{18,2},{3,19},{19,3},{4,20},{20... | collective-permute-start | bytes 1572872 | tf_op jit(solution)/shard_map/ppermute | solution.py:125
  87.4 23.5 %collective-permute-start.7 = (f32[32,4096]{1,0:T(8,128)S(1)}, f32[32,4096]{1,0:T(8,128)S(1)}, u32[]{:S(2)}, u32[]{:S(2)}) collective-permute-start(f32[32,4096]{1,0:T(8,128)S(1)} %fusion.38), channel_id=1, source_target_pairs={{0,16},{16,0},{1,17},{17,1},{2,18},{18,2},{3,19},{19,3},{4,20},{20... | collective-permute-start | bytes 1572872 | tf_op jit(solution)/shard_map/ppermute | solution.py:125
  89.0 33.1 %collective-permute-start.8 = (f32[32,4096]{1,0:T(8,128)S(1)}, f32[32,4096]{1,0:T(8,128)S(1)}, u32[]{:S(2)}, u32[]{:S(2)}) collective-permute-start(f32[32,4096]{1,0:T(8,128)S(1)} %fusion.35), channel_id=1, source_target_pairs={{0,16},{16,0},{1,17},{17,1},{2,18},{18,2},{3,19},{19,3},{4,20},{20... | collective-permute-start | bytes 1572872 | tf_op jit(solution)/shard_map/ppermute | solution.py:125
  91.6 41.1 %collective-permute-start.9 = (f32[32,4096]{1,0:T(8,128)S(1)}, f32[32,4096]{1,0:T(8,128)S(1)}, u32[]{:S(2)}, u32[]{:S(2)}) collective-permute-start(f32[32,4096]{1,0:T(8,128)S(1)} %fusion.32), channel_id=1, source_target_pairs={{0,16},{16,0},{1,17},{17,1},{2,18},{18,2},{3,19},{19,3},{4,20},{20... | collective-permute-start | bytes 1572872 | tf_op jit(solution)/shard_map/ppermute | solution.py:125
  99.7 40.8 %collective-permute-start.11 = (f32[32]{0:T(128)}, f32[32]{0:T(128)S(1)}, u32[]{:S(2)}, u32[]{:S(2)}) collective-permute-start(f32[32]{0:T(128)} %bitcast_multiply_fusion), channel_id=1, source_target_pairs={{0,4},{4,8},{8,12},{1,5},{5,9},{9,13},{2,6},{6,10},{10,14},{3,7},{... | collective-permute-start | bytes 392 | tf_op jit(solution)/shard_map/ppermute | solution.py:138
  110.9 29.6 %collective-permute-start.13 = (f32[32]{0:T(128)}, f32[32]{0:T(128)S(1)}, u32[]{:S(2)}, u32[]{:S(2)}) collective-permute-start(f32[32]{0:T(128)} %bitcast_multiply_fusion), channel_id=1, source_target_pairs={{0,8},{4,12},{1,9},{5,13},{2,10},{6,14},{3,11},{7,15},{16,24},{20,... | collective-permute-start | bytes 392 | tf_op jit(solution)/shard_map/ppermute | solution.py:138
  133.9 10.2 %copy-start.30 = (f32[32,1]{0,1:T(1,128)S(1)}, f32[32,1]{0,1:T(1,128)}, u32[]{:S(2)}) copy-start(f32[32,1]{0,1:T(1,128)} %param.15) | copy-start | bytes 388
  136.0 5.6 %collective-permute-start.10 = (f32[32,4,128]{2,1,0:T(4,128)S(1)}, f32[32,4,128]{2,1,0:T(4,128)S(1)}, u32[]{:S(2)}, u32[]{:S(2)}) collective-permute-start(f32[32,4,128]{2,1,0:T(4,128)S(1)} %bitcast.154), channel_id=1, source_target_pairs={{0,4},{4,8},{8,12},{1,5},{5,9},{9,13},{2,6},{6,10},{10,14},{3,7},{... | collective-permute-start | bytes 196616 | tf_op jit(solution)/shard_map/ppermute | solution.py:137
  137.9 6.2 %collective-permute-start.12 = (f32[32,4,128]{2,1,0:T(4,128)S(1)}, f32[32,4,128]{2,1,0:T(4,128)S(1)}, u32[]{:S(2)}, u32[]{:S(2)}) collective-permute-start(f32[32,4,128]{2,1,0:T(4,128)S(1)} %bitcast.155), channel_id=1, source_target_pairs={{0,8},{4,12},{1,9},{5,13},{2,10},{6,14},{3,11},{7,15},{16,24},{20,... | collective-permute-start | bytes 196616 | tf_op jit(solution)/shard_map/ppermute | solution.py:137
  139.2 4.9 %collective-permute-start.14 = (f32[32,4,128]{2,1,0:T(4,128)S(1)}, f32[32,4,128]{2,1,0:T(4,128)S(1)}, u32[]{:S(2)}, u32[]{:S(2)}) collective-permute-start(f32[32,4,128]{2,1,0:T(4,128)S(1)} %bitcast.156), channel_id=1, source_target_pairs={{0,12},{1,13},{2,14},{3,15},{16,28},{17,29},{18,30},{19,31}} | collective-permute-start | bytes 196616 | tf_op jit(solution)/shard_map/ppermute | solution.py:137
  (16 other events, 83.3 us)

commit v2 on v1

v2 whole, which is shorter than its diff:
```python
import functools
import math

import jax
import jax.numpy as jnp
from jax import lax
from jax.experimental import pallas as pl
from jax.experimental.pallas import tpu as pltpu
from jax.sharding import PartitionSpec as P

axial_coupling = 0.5
SAMPLE_BLOCK = 8


def shifted(block, axes, sizes, delta):
    route = []
    for i in range(sizes[0]):
        for j in range(sizes[1]):
            si, sj = i - delta[0], j - delta[1]
            if 0 <= si < sizes[0] and 0 <= sj < sizes[1]:
                route.append((si * sizes[1] + sj, i * sizes[1] + j))
    return lax.ppermute(block, axes, route)


def fourier_rows(row_ids, sample_ids, sample_count):
    half_count = sample_count // 2
    harmonic = jnp.where(row_ids <= half_count, row_ids, row_ids - half_count)
    phase_index = harmonic[:, None] * sample_ids[None, :] % sample_count
    angle_value = phase_index.astype(jnp.float32) * (2.0 * math.pi / sample_count)
    dft_table = jnp.where(
        (row_ids <= half_count)[:, None], jnp.cos(angle_value), jnp.sin(angle_value)
    )
    return dft_table * math.sqrt(2.0 / sample_count)


def residual_kernel(has_lo, has_hi, kinds, *refs):
    it = iter(refs)
    a_ref = next(it)
    lo_ref = next(it) if has_lo else None
    hi_ref = next(it) if has_hi else None
    src_ref, xlo_ref, xhi_ref, ylo_ref, yhi_ref, c1_ref, c2_ref, base_ref = [next(it) for _ in range(8)]
    reg_ref, reg_xlo_ref, reg_ylo_ref, sat_ref, sat_xlo_ref, sat_ylo_ref, out_ref = [next(it) for _ in range(7)]
    blk = pl.program_id(0)
    n_s, nx, ny = a_ref.shape
    ix = lax.broadcasted_iota(jnp.int32, (nx, ny), 0)
    iy = lax.broadcasted_iota(jnp.int32, (nx, ny), 1)
    ix_col = lax.broadcasted_iota(jnp.int32, (nx, 1), 0)
    iy_row = lax.broadcasted_iota(jnp.int32, (1, ny), 1)
    reg = reg_ref[...]
    reg_xlo = reg_xlo_ref[...]
    reg_ylo = reg_ylo_ref[...]
    sat = sat_ref[...]
    sat_xlo = sat_xlo_ref[...]
    sat_ylo = sat_ylo_ref[...]

    def lookup(kind, s_glob):
        out = jnp.full(kind.shape, base_ref[s_glob, 0], jnp.float32)
        for k in range(1, kinds):
            out = jnp.where(kind == k, base_ref[s_glob, k], out)
        return out

    def body(s, carry):
        s_glob = blk * n_s + s
        a = a_ref[s]
        row_hi = xhi_ref[pl.ds(s, 1), :]
        row_lo = xlo_ref[pl.ds(s, 1), :]
        col_hi = yhi_ref[s]
        col_lo = ylo_ref[s]
        c1 = c1_ref[0, s_glob]
        c2 = c2_ref[0, s_glob]
        base = lookup(reg, s_glob)
        base_xlo = lookup(reg_xlo, s_glob)
        base_ylo = lookup(reg_ylo, s_glob)
        a_xp = jnp.where(ix == nx - 1, row_hi, pltpu.roll(a, nx - 1, 0))
        a_yp = jnp.where(iy == ny - 1, col_hi, pltpu.roll(a, ny - 1, 1))
        sx = a_xp - a
        sy = a_yp - a
        rel = base * (1.0 + sat * (sx * sx + sy * sy))
        fx = rel * sx
        fy = rel * sy
        lo_yp = jnp.where(iy_row == ny - 1, c1, pltpu.roll(row_lo, ny - 1, 1))
        sx_l = a[0:1, :] - row_lo
        sy_l = lo_yp - row_lo
        fx_l = base_xlo * (1.0 + sat_xlo * (sx_l * sx_l + sy_l * sy_l)) * sx_l
        lo_xp = jnp.where(ix_col == nx - 1, c2, pltpu.roll(col_lo, nx - 1, 0))
        sx_c = lo_xp - col_lo
        sy_c = a[:, 0:1] - col_lo
        fy_c = base_ylo * (1.0 + sat_ylo * (sx_c * sx_c + sy_c * sy_c)) * sy_c
        fx_down = jnp.where(ix == 0, fx_l, pltpu.roll(fx, 1, 0))
        fy_left = jnp.where(iy == 0, fy_c, pltpu.roll(fy, 1, 1))
        curl = fx_down - fx + fy_left - fy
        axial = 2.0 * a
        if has_lo:
            axial = axial - lo_ref[s]
        if has_hi:
            axial = axial - hi_ref[s]
        out_ref[s] = curl + axial_coupling * axial - src_ref[s]
        return carry

    lax.fori_loop(0, n_s, body, 0)


def residual_plane(p, a, src, xlo, xhi, ylo_c, yhi_c, c1, c2, base_rows, reg, reg_xlo, reg_ylo, sat, sat_xlo, sat_ylo):
    n_s, planes, nx, ny = a.shape
    kinds = base_rows.shape[1]
    sb = min(SAMPLE_BLOCK, n_s)
    has_lo = p > 0
    has_hi = p < planes - 1
    tile = lambda q: pl.BlockSpec((sb, None, nx, ny), lambda i: (i, q, 0, 0))
    vmem_whole = pl.BlockSpec(memory_space=pltpu.VMEM)
    smem_whole = pl.BlockSpec(memory_space=pltpu.SMEM)
    in_specs = [tile(p)]
    args = [a]
    if has_lo:
        in_specs.append(tile(p - 1))
        args.append(a)
    if has_hi:
        in_specs.append(tile(p + 1))
        args.append(a)
    in_specs += [
        tile(p),
        pl.BlockSpec((None, sb, ny), lambda i: (p, i, 0)),
        pl.BlockSpec((None, sb, ny), lambda i: (p, i, 0)),
        pl.BlockSpec((None, sb, nx, 1), lambda i: (p, i, 0, 0)),
        pl.BlockSpec((None, sb, nx, 1), lambda i: (p, i, 0, 0)),
        smem_whole,
        smem_whole,
        smem_whole,
    ] + [vmem_whole] * 6
    args += [src, xlo, xhi, ylo_c, yhi_c, c1[p:p + 1], c2[p:p + 1], base_rows, reg, reg_xlo, reg_ylo, sat, sat_xlo, sat_ylo]
    return pl.pallas_call(
        functools.partial(residual_kernel, has_lo, has_hi, kinds),
        grid=(n_s // sb,),
        in_specs=in_specs,
        out_specs=pl.BlockSpec((sb, nx, ny), lambda i: (i, 0, 0)),
        out_shape=jax.ShapeDtypeStruct((n_s, nx, ny), jnp.float32),
        name="residual_plane",
    )(*args)


def local(potential, source, region, level_index, reluctivity, saturation, inverse, transmit):
    samples_dev, planes, cells_x, cells_y = potential.shape
    n_tm = lax.axis_size("tm")
    n_gx = lax.axis_size("gx")
    n_gy = lax.axis_size("gy")
    me_tm = lax.axis_index("tm")
    me_gx = lax.axis_index("gx")
    sample_count = samples_dev * n_tm
    grid = ("gx", "gy")
    sizes = (n_gx, n_gy)
    a = potential
    regf = region.astype(jnp.float32)
    kinds = reluctivity.shape[1]

    msg_xlo = jnp.concatenate(
        [a[:, :, cells_x - 1, :].reshape(samples_dev * planes, cells_y), regf[cells_x - 1][None]], axis=0
    )
    msg_ylo = jnp.concatenate(
        [a[:, :, :, cells_y - 1].reshape(samples_dev * planes, cells_x), regf[:, cells_y - 1][None]], axis=0
    )
    got_xlo = shifted(msg_xlo, grid, sizes, (1, 0))
    got_ylo = shifted(msg_ylo, grid, sizes, (0, 1))
    xhi = shifted(a[:, :, 0, :], grid, sizes, (-1, 0))
    yhi = shifted(a[:, :, :, 0], grid, sizes, (0, -1))
    c1 = shifted(a[:, :, cells_x - 1, 0], grid, sizes, (1, -1))
    c2 = shifted(a[:, :, 0, cells_y - 1], grid, sizes, (-1, 1))

    xlo = got_xlo[:-1].reshape(samples_dev, planes, cells_y)
    reg_xlo = got_xlo[-1].astype(jnp.int32)[None, :]
    ylo = got_ylo[:-1].reshape(samples_dev, planes, cells_x)
    reg_ylo = got_ylo[-1].astype(jnp.int32)[:, None]
    xlo = jnp.transpose(xlo, (1, 0, 2))
    xhi = jnp.transpose(xhi, (1, 0, 2))
    ylo_c = jnp.transpose(ylo, (1, 0, 2))[..., None]
    yhi_c = jnp.transpose(yhi, (1, 0, 2))[..., None]
    c1 = c1.T
    c2 = c2.T

    onehot = (level_index[:, None] == lax.iota(jnp.int32, reluctivity.shape[0])[None, :]).astype(jnp.float32)
    base_rows = jnp.sum(onehot[:, :, None] * reluctivity[None], axis=1)

    def sat_of(kind):
        out = jnp.full(kind.shape, saturation[0], jnp.float32)
        for k in range(1, kinds):
            out = jnp.where(kind == k, saturation[k], out)
        return out

    sat = sat_of(region)
    sat_xlo = sat_of(reg_xlo)
    sat_ylo = sat_of(reg_ylo)

    sample_ids = me_tm * samples_dev + lax.iota(jnp.int32, samples_dev)
    q_dev = samples_dev

    spectra_planes = []
    for p in range(planes):
        resid = residual_plane(
            p, a, source, xlo, xhi, ylo_c, yhi_c, c1, c2, base_rows,
            region, reg_xlo, reg_ylo, sat, sat_xlo, sat_ylo,
        )
        flat = resid.reshape(samples_dev, cells_x * cells_y)
        parts = []
        for d in range(1, n_tm):
            owner = (me_tm + d) % n_tm
            tab = fourier_rows(owner * q_dev + lax.iota(jnp.int32, q_dev), sample_ids, sample_count)
            part = jnp.dot(tab, flat, precision=lax.Precision.HIGHEST, preferred_element_type=jnp.float32)
            route = [(i, (i + d) % n_tm) for i in range(n_tm)]
            parts.append(lax.ppermute(part, "tm", route))
        own_tab = fourier_rows(me_tm * q_dev + lax.iota(jnp.int32, q_dev), sample_ids, sample_count)
        acc = jnp.dot(own_tab, flat, precision=lax.Precision.HIGHEST, preferred_element_type=jnp.float32)
        for got in parts:
            acc = acc + got
        spectra_planes.append(acc.reshape(q_dev, cells_x, cells_y))
    spectra = jnp.stack(spectra_planes, axis=1)

    solved = jnp.einsum("qab,qpbj->qpaj", inverse, spectra, precision=lax.Precision.HIGHEST)
    line_tail = solved[:, :, cells_x - 1, :]
    gain_here = transmit[:, 0] * inverse[:, cells_x - 1, 0]

    tails = []
    gains = []
    for d in range(n_gx - 1, 0, -1):
        route = [(i, i + d) for i in range(n_gx - d)]
        tails.append(lax.ppermute(line_tail, "gx", route))
        gains.append(lax.ppermute(gain_here, "gx", route))
    carried = jnp.zeros_like(line_tail)
    for idx, d in enumerate(range(n_gx - 1, 0, -1)):
        stepped = tails[idx] + gains[idx][:, None, None] * carried
        carried = jnp.where(me_gx >= d, stepped, carried)
    injected = transmit[:, 0][:, None, None] * carried
    correction = solved + injected[:, :, None, :] * inverse[:, :, 0][:, None, :, None]
    return correction


def solution(mesh):
    in_specs = (
        P("tm", None, "gx", "gy"),
        P("tm", None, "gx", "gy"),
        P("gx", "gy"),
        P("tm"),
        P(),
        P(),
        P("tm", "gx", None),
        P("tm", "gx"),
    )
    out_specs = P("tm", None, "gx", "gy")
    return jax.shard_map(local, mesh=mesh, in_specs=in_specs, out_specs=out_specs, check_vma=False)
```

time: 148 us -> 131 us (0.89)
  Pallas kernels: 0 us -> 28.4 us
  waiting for transfers between devices: 37.4 us -> 19 us
  local copies, waits for them, and re-layouts: 33 us -> 17.8 us
  other arithmetic: 34.8 us -> 20.2 us
  matrix products: 9.93 us -> 14.7 us
    pallas_call x0 -> x4, Pallas kernels: none -> 28.4 us  [residual_plane(): pl.pallas_call(functools.partial(residual_kernel, has_lo, has_hi, kinds),...]
    ppermute x4, waiting for transfers between devices: 33.8 us -> 15.4 us  [local(): parts.append(lax.ppermute(part, 'tm', route))]
    sub x1 -> x0, other arithmetic: 11.2 us -> none  [local(): curl_part + axial_coupling * (2.0 * a - plane_below - plane_above) - source]
    slice x13 -> x8, local copies, waits for them, and re-layouts: 17.7 us -> 8.36 us  [the longest x1 3.62 us: local(): yhi = shifted(a[:, :, :, 0], grid, sizes, (0, -1))]
    dot_general x4, matrix products: 3.95 us -> 8.69 us  [local(): jnp.dot(tab, flat, precision=lax.Precision.HIGHEST, preferred_element_typ...]
    broadcast_in_dim x7 -> x2, local copies, waits for them, and re-layouts: 7.52 us -> 4.31 us  [the longest x1 2.17 us: local(): yhi_c = jnp.transpose(yhi, (1, 0, 2))[..., None]]
    another operation x1 -> x0, local copies, waits for them, and re-layouts: 2.17 us -> none  [local(): a_ym = jnp.concatenate([ylo[:, :, :, None], a[:, :, :, :-1]], axis=3)]
    unnamed x72 -> x32, local copies, waits for them, and re-layouts: 3.24 us -> 2.21 us
  transfers between devices with their start and end apart: 16 -> 16, of which waited for: 6 -> 5; matrix products, arithmetic and copies ran while one was open for 48% -> 37% of each run, Pallas kernels for 0% -> 22%
where the time goes in v2:
time: 131 us; the launch traced here: 130 us
  starting transfers between devices  29.4 us (22%)
  Pallas kernels  28.4 us (22%)
  other arithmetic  20.2 us (15%)
  waiting for transfers between devices  19 us (15%)
  local copies, waits for them, and re-layouts  17.8 us (14%)
  matrix products  14.7 us (11%)
    pallas_call x4, Pallas kernels, residual_plane(): pl.pallas_call(functools.partial(residual_kernel, has_lo, has_hi, kinds),...  28.4 us
    ppermute x6, starting transfers between devices, shifted(): return lax.ppermute(block, axes, route)  17.3 us
    select_n x3, other arithmetic, sat_of(): out = jnp.where(kind == k, saturation[k], out)  16.8 us
    ppermute x4, waiting for transfers between devices, local(): parts.append(lax.ppermute(part, 'tm', route))  15.4 us
    dot_general x4, matrix products, local(): jnp.dot(tab, flat, precision=lax.Precision.HIGHEST, preferred_element_typ...  8.69 us
    ppermute x4, starting transfers between devices, local(): parts.append(lax.ppermute(part, 'tm', route))  4.19 us
    ppermute x3, starting transfers between devices, local(): gains.append(lax.ppermute(gain_here, 'gx', route))  4.02 us
    dot_general x4, matrix products, local(): jnp.dot(own_tab, flat, precision=lax.Precision.HIGHEST, preferred_element...  3.99 us
  transfers between devices with their start and end apart: 16, of which 5 were waited for; matrix products, arithmetic and copies ran while one was open for 37% of the time, Pallas kernels for 22%

profile of v2, /device:TPU:12, one launch (start us, length us, event | category | flops | bytes accessed | tf_op | source)
XLA Modules:
  0.0 130.0 jit_solution(3275459502928348472)
XLA Ops:
  2.5 1.3 %fusion.88 = (f32[32,4,1,128]{3,2,1,0:T(1,128)S(1)}, f32[32,4,1,128]{3,2,1,0:T(1,128)S(1)}) fusion(f32[32,4,32,128]{3,2,1,0:T(8,128)} %refs_1_.7), kind=kLoop, calls=%fused_computation.132 | loop fusion | bytes 262144 | tf_op jit(solution)/shard_map/slice | solution.py:163
  3.9 1.9 %collective-permute-start.1 = (f32[32,4,128]{2,0,1:T(8,128)S(1)}, f32[32,4,128]{2,0,1:T(8,128)S(1)}, u32[]{:S(2)}, u32[]{:S(2)}) collective-permute-start(f32[32,4,128]{2,0,1:T(8,128)S(1)} %bitcast.128), channel_id=1, source_target_pairs={{4,0},{5,1},{6,2},{7,3},{8,4},{9,5},{10,6},{11,7},{12,8},{13,9},{1... | collective-permute-start | bytes 196616 | tf_op jit(solution)/shard_map/ppermute | solution.py:22
  6.5 2.4 %collective-permute-start = (f32[129,128]{1,0:T(8,128)S(1)}, f32[129,128]{1,0:T(8,128)S(1)}, u32[]{:S(2)}, u32[]{:S(2)}) collective-permute-start(f32[129,128]{1,0:T(8,128)S(1)} %pad_maximum_fusion), channel_id=1, source_target_pairs={{0,4},{1,5},{2,6},{3,7},{4,8},{5,9},{6,10},{7,11},{8,12},{9,13},{1... | collective-permute-start | bytes 198152 | tf_op jit(solution)/shard_map/ppermute | solution.py:22
  9.0 1.4 %fusion.86 = (f32[32,4,1,1]{3,2,1,0:T(1,128)S(1)}, f32[32,4,1,1]{3,2,1,0:T(1,128)S(1)}) fusion(f32[32,4,32,128]{3,2,1,0:T(8,128)} %refs_1_.7), kind=kLoop, calls=%fused_computation.130 | loop fusion | bytes 2048 | tf_op jit(solution)/shard_map/slice | solution.py:166
  10.5 1.9 %collective-permute-start.4 = (f32[32,4]{0,1:T(4,128)S(1)}, f32[32,4]{0,1:T(4,128)S(1)}, u32[]{:S(2)}, u32[]{:S(2)}) collective-permute-start(f32[32,4]{0,1:T(4,128)S(1)} %bitcast.134), channel_id=1, source_target_pairs={{1,4},{2,5},{3,6},{5,8},{6,9},{7,10},{9,12},{10,13},{11,14},{17,20... | collective-permute-start | bytes 1544 | tf_op jit(solution)/shard_map/ppermute | solution.py:22
  12.5 5.2 %collective-permute-start.5 = (f32[32,4]{0,1:T(4,128)S(1)}, f32[32,4]{0,1:T(4,128)S(1)}, u32[]{:S(2)}, u32[]{:S(2)}) collective-permute-start(f32[32,4]{0,1:T(4,128)S(1)} %bitcast.133), channel_id=1, source_target_pairs={{4,1},{5,2},{6,3},{8,5},{9,6},{10,7},{12,9},{13,10},{14,11},{20,17... | collective-permute-start | bytes 1544 | tf_op jit(solution)/shard_map/ppermute | solution.py:22
  18.0 3.6 %fusion.87 = (f32[32,4,32,1]{3,2,1,0:T(8,128)S(1)}, f32[32,4,32]{2,1,0:T(4,128)S(1)}) fusion(f32[32,4,32,128]{3,2,1,0:T(8,128)} %refs_1_.7), kind=kLoop, calls=%fused_computation.131 | loop fusion | bytes 65536 | tf_op jit(solution)/shard_map/slice | solution.py:164
  22.6 5.6 %select_select_fusion.1.refs_13_.refs_14_ = f32[32,128]{1,0:T(8,128)} fusion(s32[32,128]{1,0:T(8,128)S(1)} %copy-done.6, f32[]{:T(128)} %bitcast.23, f32[]{:T(128)} %bitcast.22, f32[]{:T(128)} %bitcast.21, f32[]{:T(128)} %bitcast.20, f32[]{:T(128)} %bitcast.19, f32[]{:T(128)} %bitcast.18, f32[]{:T(128)} %bitcast.17, f32[]{:T(128)} %bitcast.16), kind=kLoop, calls=%fused_computation.67 | loop fusion | flops 57344 | bytes 32800 | tf_op jit(solution)/shard_map/jit(_where)/select_n | solution.py:185
  29.9 2.4 %collective-permute-start.3 = (f32[32,4,32]{2,0,1:T(8,128)S(1)}, f32[32,4,32]{2,0,1:T(8,128)S(1)}, u32[]{:S(2)}, u32[]{:S(2)}) collective-permute-start(f32[32,4,32]{2,0,1:T(8,128)S(1)} %bitcast.126), channel_id=1, source_target_pairs={{1,0},{2,1},{3,2},{5,4},{6,5},{7,6},{9,8},{10,9},{11,10},{13,12},{... | collective-permute-start | bytes 49160 | tf_op jit(solution)/shard_map/ppermute | solution.py:22
  32.9 3.5 %collective-permute-start.2 = (f32[129,32]{1,0:T(8,128)S(1)}, f32[129,32]{1,0:T(8,128)S(1)}, u32[]{:S(2)}, u32[]{:S(2)}) collective-permute-start(f32[129,32]{1,0:T(8,128)S(1)} %pad_maximum_fusion.1), channel_id=1, source_target_pairs={{0,1},{1,2},{2,3},{4,5},{5,6},{6,7},{8,9},{9,10},{10,11},{12,13},{... | collective-permute-start | bytes 49544 | tf_op jit(solution)/shard_map/ppermute | solution.py:22
  36.9 2.2 %copy.110.refs_6_.refs_7_ = f32[4,32,32,1]{3,2,1,0:T(8,128)} copy(f32[4,32,32,1]{2,1,0,3:T(8,128)S(1)} %bitcast.127) | data formatting | bytes 32768 | tf_op jit(solution)/shard_map/broadcast_in_dim | solution.py:175
  39.2 5.6 %select_select_fusion.refs_15_.refs_16_ = f32[32,1]{1,0:T(8,128)} fusion(s32[32,1]{1,0:T(8,128)S(1)} %copy.112.refs_12_.refs_13_, f32[]{:T(128)} %bitcast.23, f32[]{:T(128)} %bitcast.22, f32[]{:T(128)} %bitcast.21, f32[]{:T(128)} %bitcast.20, f32[]{:T(128)} %bitcast.19, f32[]{:T(128)} %bitcast.18, f32[]{:T(128)} %bitcast.17, f32[]{:T(128)} %bitcast.16), kind=kLoop, calls=%fused_computation.66 | loop fusion | flops 448 | bytes 288 | tf_op jit(solution)/shard_map/jit(_where)/select_n | solution.py:185
  44.8 2.1 %copy.109.refs_5_.refs_6_ = f32[4,32,32,1]{3,2,1,0:T(8,128)} copy(f32[4,32,32,1]{2,1,0,3:T(8,128)S(1)} %bitcast.121) | data formatting | bytes 32768 | tf_op jit(solution)/shard_map/broadcast_in_dim | solution.py:174
  47.0 5.6 %compare_select_fusion.6 = (f32[1,128]{1,0:T(1,128)}, s32[1,128]{1,0:T(1,128)}) fusion(f32[]{:T(128)} %bitcast.23, f32[]{:T(128)} %bitcast.22, f32[]{:T(128)} %bitcast.21, f32[]{:T(128)} %bitcast.20, f32[]{:T(128)} %bitcast.19, f32[]{:T(128)} %bitcast.18, f32[]{:T(128)} %bitcast.17, f32[]{:T(128)} %bitcast.16, f32[129,128]{1,0:T(8,128)S(1)} %collective-permute-done), kind=kLoop, calls=%fused_computation.77 | loop fusion | flops 1920 | bytes 1568 | tf_op jit(solution)/shard_map/jit(_where)/select_n | solution.py:185
  53.8 7.1 %residual_plane.7 = f32[32,32,128]{2,1,0:T(8,128)} custom-call(f32[32,4,32,128]{3,2,1,0:T(8,128)} %refs_1_.7, f32[32,4,32,128]{3,2,1,0:T(8,128)} %refs_1_.7, f32[32,4,32,128]{3,2,1,0:T(8,128)} %refs_2_.7, f32[4,32,128]{2,1,0:T(8,128)} %bitcast.112, f32[4,32,128]{2,1,0:T(8,128)} %bitcast.116, f32[4,32,32,1]{3,2,1,0:T(8,128)} %copy.109.refs_5_.refs_6_, ...), custom_call_target="tpu_custom_call" | custom-call | tf_op jit(solution)/shard_map/residual_plane/pallas_call | solution.py:131
  60.9 7.1 %residual_plane.6 = f32[32,32,128]{2,1,0:T(8,128)} custom-call(f32[32,4,32,128]{3,2,1,0:T(8,128)} %refs_1_.7, f32[32,4,32,128]{3,2,1,0:T(8,128)} %refs_1_.7, f32[32,4,32,128]{3,2,1,0:T(8,128)} %refs_1_.7, f32[32,4,32,128]{3,2,1,0:T(8,128)} %refs_2_.7, f32[4,32,128]{2,1,0:T(8,128)} %bitcast.113, f32[4,32,128]{2,1,0:T(8,128)} %bitcast.117, ...), custom_call_target="tpu_custom_call" | custom-call | tf_op jit(solution)/shard_map/residual_plane/pallas_call | solution.py:131
  68.1 2.8 %fusion.18 = f32[32,4096]{1,0:T(8,128)} fusion(f32[4,8,32,128]{3,2,1,0:T(8,128)} %bitcast.99, s32[32]{0:T(128)S(1)} %get-tuple-element.29, s32[32]{0:T(128)S(1)} %get-tuple-element.30, pred[32]{0:T(512)(128)(4,1)S(1)} %fusion.44), kind=kOutput, calls=%fused_computation.22 | convolution fusion | flops 50348032 | bytes 1048864 | tf_op jit(solution)/shard_map/dot_general | solution.py:206
  71.9 1.6 %collective-permute-start.9 = (f32[32,4096]{1,0:T(8,128)S(1)}, f32[32,4096]{1,0:T(8,128)S(1)}, u32[]{:S(2)}, u32[]{:S(2)}) collective-permute-start(f32[32,4096]{1,0:T(8,128)S(1)} %fusion.15), channel_id=1, source_target_pairs={{0,16},{16,0},{1,17},{17,1},{2,18},{18,2},{3,19},{19,3},{4,20},{20... | collective-permute-start | bytes 1572872 | tf_op jit(solution)/shard_map/ppermute | solution.py:208
  74.0 7.1 %residual_plane.4 = f32[32,32,128]{2,1,0:T(8,128)} custom-call(f32[32,4,32,128]{3,2,1,0:T(8,128)} %refs_1_.7, f32[32,4,32,128]{3,2,1,0:T(8,128)} %refs_1_.7, f32[32,4,32,128]{3,2,1,0:T(8,128)} %refs_2_.7, f32[4,32,128]{2,1,0:T(8,128)} %bitcast.114, f32[4,32,128]{2,1,0:T(8,128)} %bitcast.118, f32[4,32,32,1]{3,2,1,0:T(8,128)} %copy.109.refs_5_.refs_6_, ...), custom_call_target="tpu_custom_call" | custom-call | tf_op jit(solution)/shard_map/residual_plane/pallas_call | solution.py:131
  81.0 2.8 %fusion.24 = f32[32,4096]{1,0:T(8,128)} fusion(f32[4,8,32,128]{3,2,1,0:T(8,128)} %bitcast.103, s32[32]{0:T(128)S(1)} %get-tuple-element.29, s32[32]{0:T(128)S(1)} %get-tuple-element.30, pred[32]{0:T(512)(128)(4,1)S(1)} %fusion.44), kind=kOutput, calls=%fused_computation.28 | convolution fusion | flops 50348032 | bytes 1048864 | tf_op jit(solution)/shard_map/dot_general | solution.py:206
  83.8 1.5 %collective-permute-start.6 = (f32[32,4096]{1,0:T(8,128)}, f32[32,4096]{1,0:T(8,128)S(1)}, u32[]{:S(2)}, u32[]{:S(2)}) collective-permute-start(f32[32,4096]{1,0:T(8,128)} %fusion.24), channel_id=1, source_target_pairs={{0,16},{16,0},{1,17},{17,1},{2,18},{18,2},{3,19},{19,3},{4,20},{20... | collective-permute-start | bytes 1572872 | tf_op jit(solution)/shard_map/ppermute | solution.py:208
  85.3 7.1 %residual_plane.5 = f32[32,32,128]{2,1,0:T(8,128)} custom-call(f32[32,4,32,128]{3,2,1,0:T(8,128)} %refs_1_.7, f32[32,4,32,128]{3,2,1,0:T(8,128)} %refs_1_.7, f32[32,4,32,128]{3,2,1,0:T(8,128)} %refs_1_.7, f32[32,4,32,128]{3,2,1,0:T(8,128)} %refs_2_.7, f32[4,32,128]{2,1,0:T(8,128)} %bitcast.115, f32[4,32,128]{2,1,0:T(8,128)} %bitcast.119, ...), custom_call_target="tpu_custom_call" | custom-call | tf_op jit(solution)/shard_map/residual_plane/pallas_call | solution.py:131
  92.5 2.1 %fusion.21 = f32[32,4096]{1,0:T(8,128)S(1)} fusion(f32[4,8,32,128]{3,2,1,0:T(8,128)} %bitcast.101, s32[32]{0:T(128)S(1)} %get-tuple-element.29, s32[32]{0:T(128)S(1)} %get-tuple-element.30, pred[32]{0:T(512)(128)(4,1)S(1)} %fusion.44), kind=kOutput, calls=%fused_computation.25 | convolution fusion | flops 50348032 | bytes 1048864 | tf_op jit(solution)/shard_map/dot_general | solution.py:206
  95.2 1.3 collective-permute-start.13
  98.0 2.1 %collective-permute-start.11 = (f32[32]{0:T(128)S(1)}, f32[32]{0:T(128)S(1)}, u32[]{:S(2)}, u32[]{:S(2)}) collective-permute-start(f32[32]{0:T(128)S(1)} %bitcast_multiply_fusion), channel_id=1, source_target_pairs={{0,4},{4,8},{8,12},{1,5},{5,9},{9,13},{2,6},{6,10},{10,14},{3,7},{... | collective-permute-start | bytes 392 | tf_op jit(solution)/shard_map/ppermute | solution.py:225
  101.3 8.0 %collective-permute-done.6 = f32[32,4096]{1,0:T(8,128)S(1)} collective-permute-done((f32[32,4096]{1,0:T(8,128)}, f32[32,4096]{1,0:T(8,128)S(1)}, u32[]{:S(2)}, u32[]{:S(2)}) %collective-permute-start.6) | collective-permute-done | bytes 524320 | tf_op jit(solution)/shard_map/ppermute | solution.py:208
  110.4 6.9 %collective-permute-done.7 = f32[32,4096]{1,0:T(8,128)S(1)} collective-permute-done((f32[32,4096]{1,0:T(8,128)S(1)}, f32[32,4096]{1,0:T(8,128)S(1)}, u32[]{:S(2)}, u32[]{:S(2)}) %collective-permute-start.7) | collective-permute-done | bytes 524320 | tf_op jit(solution)/shard_map/ppermute | solution.py:208
  118.4 2.0 %fusion.8 = f32[32,4,32,128]{3,2,1,0:T(8,128)S(1)} fusion(f32[32,1,32,128]{3,2,1,0:T(8,128)S(1)} %bitcast.108, f32[32,1,32,128]{3,2,1,0:T(8,128)S(1)} %bitcast.109, f32[32,1,32,128]{3,2,1,0:T(8,128)S(1)} %bitcast.111, f32[32,1,32,128]{3,2,1,0:T(8,128)S(1)} %bitcast.110, f32[32,32,32]{2,1,0:T(8,128)S(1)} %copy-done.4), kind=kOutput, calls=%fused_computation.14 | convolution fusion | flops 202899456 | bytes 4325376 | tf_op jit(solution)/shard_map/qab,qpbj->qpaj/dot_general | solution.py:216
  121.2 1.3 collective-permute-start.12
  122.5 1.9 %collective-permute-start.10 = (f32[32,4,128]{2,1,0:T(4,128)S(1)}, f32[32,4,128]{2,1,0:T(4,128)S(1)}, u32[]{:S(2)}, u32[]{:S(2)}) collective-permute-start(f32[32,4,128]{2,1,0:T(4,128)S(1)} %bitcast.131), channel_id=1, source_target_pairs={{0,4},{4,8},{8,12},{1,5},{5,9},{9,13},{2,6},{6,10},{10,14},{3,7},{... | collective-permute-start | bytes 196616 | tf_op jit(solution)/shard_map/ppermute | solution.py:224
  124.4 2.9 %collective-permute-done.12 = f32[32,4,128]{2,1,0:T(4,128)S(1)} collective-permute-done((f32[32,4,128]{2,1,0:T(4,128)S(1)}, f32[32,4,128]{2,1,0:T(4,128)S(1)}, u32[]{:S(2)}, u32[]{:S(2)}) %collective-permute-start.12) | collective-permute-done | bytes 65568 | tf_op jit(solution)/shard_map/ppermute | solution.py:224
  128.3 1.7 %multiply_add_fusion = f32[32,4,32,128]{3,2,1,0:T(8,128)} fusion(f32[32,4,32,128]{3,2,1,0:T(8,128)S(1)} %fusion.8, f32[32,32]{1,0:T(8,128)S(1)} %bitcast.125, f32[32,4,128]{2,1,0:T(4,128)S(1)} %select_multiply_fusion), kind=kLoop, calls=%fused_computation.12 | loop fusion | flops 1048576 | bytes 4263936 | tf_op jit(solution)/shard_map/add | solution.py:231
  (82 shorter events, 17.5 us)
Async XLA Ops:
  1.9 120.6 %collective-permute-start.15 = (f32[32]{0:T(128)S(1)}, f32[32]{0:T(128)S(1)}, u32[]{:S(2)}, u32[]{:S(2)}) collective-permute-start(f32[32]{0:T(128)S(1)} %bitcast_multiply_fusion), channel_id=1, source_target_pairs={{0,12},{1,13},{2,14},{3,15},{16,28},{17,29},{18,30},{19,31}} | collective-permute-start | bytes 392 | tf_op jit(solution)/shard_map/ppermute | solution.py:225
  3.9 49.3 %collective-permute-start.1 = (f32[32,4,128]{2,0,1:T(8,128)S(1)}, f32[32,4,128]{2,0,1:T(8,128)S(1)}, u32[]{:S(2)}, u32[]{:S(2)}) collective-permute-start(f32[32,4,128]{2,0,1:T(8,128)S(1)} %bitcast.128), channel_id=1, source_target_pairs={{4,0},{5,1},{6,2},{7,3},{8,4},{9,5},{10,6},{11,7},{12,8},{13,9},{1... | collective-permute-start | bytes 196616 | tf_op jit(solution)/shard_map/ppermute | solution.py:22
  6.5 40.4 %collective-permute-start = (f32[129,128]{1,0:T(8,128)S(1)}, f32[129,128]{1,0:T(8,128)S(1)}, u32[]{:S(2)}, u32[]{:S(2)}) collective-permute-start(f32[129,128]{1,0:T(8,128)S(1)} %pad_maximum_fusion), channel_id=1, source_target_pairs={{0,4},{1,5},{2,6},{3,7},{4,8},{5,9},{6,10},{7,11},{8,12},{9,13},{1... | collective-permute-start | bytes 198152 | tf_op jit(solution)/shard_map/ppermute | solution.py:22
  10.5 19.5 %collective-permute-start.4 = (f32[32,4]{0,1:T(4,128)S(1)}, f32[32,4]{0,1:T(4,128)S(1)}, u32[]{:S(2)}, u32[]{:S(2)}) collective-permute-start(f32[32,4]{0,1:T(4,128)S(1)} %bitcast.134), channel_id=1, source_target_pairs={{1,4},{2,5},{3,6},{5,8},{6,9},{7,10},{9,12},{10,13},{11,14},{17,20... | collective-permute-start | bytes 1544 | tf_op jit(solution)/shard_map/ppermute | solution.py:22
  12.5 20.4 %collective-permute-start.5 = (f32[32,4]{0,1:T(4,128)S(1)}, f32[32,4]{0,1:T(4,128)S(1)}, u32[]{:S(2)}, u32[]{:S(2)}) collective-permute-start(f32[32,4]{0,1:T(4,128)S(1)} %bitcast.133), channel_id=1, source_target_pairs={{4,1},{5,2},{6,3},{8,5},{9,6},{10,7},{12,9},{13,10},{14,11},{20,17... | collective-permute-start | bytes 1544 | tf_op jit(solution)/shard_map/ppermute | solution.py:22
  18.0 3.7 %copy-start.8 = (f32[8]{0:T(128)S(1)}, f32[8]{0:T(128)}, u32[]{:S(2)}) copy-start(f32[8]{0:T(128)} %param.13) | copy-start | bytes 100
  18.0 4.4 %copy-start.11 = (s32[32]{0:T(128)S(1)}, s32[32]{0:T(128)}, u32[]{:S(2)}) copy-start(s32[32]{0:T(128)} %param.11) | copy-start | bytes 388
  18.0 4.4 %copy-start.9 = (f32[16,8]{0,1:T(8,128)S(1)}, f32[16,8]{0,1:T(8,128)}, u32[]{:S(2)}) copy-start(f32[16,8]{0,1:T(8,128)} %param.12) | copy-start | bytes 1540
  18.0 4.5 %copy-start.6 = (s32[32,128]{1,0:T(8,128)S(1)}, s32[32,128]{1,0:T(8,128)}, u32[]{:S(2)}) copy-start(s32[32,128]{1,0:T(8,128)} %refs_10_.3) | copy-start | bytes 49156
  18.0 10.8 %copy-start.4 = (f32[32,32,32]{2,1,0:T(8,128)S(1)}, f32[32,32,32]{2,1,0:T(8,128)}, u32[]{:S(2)}) copy-start(f32[32,32,32]{2,1,0:T(8,128)} %param.14) | copy-start | bytes 393220
  29.9 7.0 %collective-permute-start.3 = (f32[32,4,32]{2,0,1:T(8,128)S(1)}, f32[32,4,32]{2,0,1:T(8,128)S(1)}, u32[]{:S(2)}, u32[]{:S(2)}) collective-permute-start(f32[32,4,32]{2,0,1:T(8,128)S(1)} %bitcast.126), channel_id=1, source_target_pairs={{1,0},{2,1},{3,2},{5,4},{6,5},{7,6},{9,8},{10,9},{11,10},{13,12},{... | collective-permute-start | bytes 49160 | tf_op jit(solution)/shard_map/ppermute | solution.py:22
  32.9 6.2 %collective-permute-start.2 = (f32[129,32]{1,0:T(8,128)S(1)}, f32[129,32]{1,0:T(8,128)S(1)}, u32[]{:S(2)}, u32[]{:S(2)}) collective-permute-start(f32[129,32]{1,0:T(8,128)S(1)} %pad_maximum_fusion.1), channel_id=1, source_target_pairs={{0,1},{1,2},{2,3},{4,5},{5,6},{6,7},{8,9},{9,10},{10,11},{12,13},{... | collective-permute-start | bytes 49544 | tf_op jit(solution)/shard_map/ppermute | solution.py:22
  39.2 14.0 %copy-start.7 = (s32[32,1]{1,0:T(8,128)}, s32[32,1]{1,0:T(8,128)S(1)}, u32[]{:S(2)}) copy-start(s32[32,1]{1,0:T(8,128)S(1)} %copy.112.refs_12_.refs_13_) | copy-start | bytes 388
  53.2 0.6 copy-start.5
  60.9 10.0 %copy-start.3 = (f32[32,32,128]{2,1,0:T(8,128)S(1)}, f32[32,32,128]{2,1,0:T(8,128)}, u32[]{:S(2)}) copy-start(f32[32,32,128]{2,1,0:T(8,128)} %residual_plane.7) | copy-start | bytes 1572868
  71.9 23.3 %collective-permute-start.9 = (f32[32,4096]{1,0:T(8,128)S(1)}, f32[32,4096]{1,0:T(8,128)S(1)}, u32[]{:S(2)}, u32[]{:S(2)}) collective-permute-start(f32[32,4096]{1,0:T(8,128)S(1)} %fusion.15), channel_id=1, source_target_pairs={{0,16},{16,0},{1,17},{17,1},{2,18},{18,2},{3,19},{19,3},{4,20},{20... | collective-permute-start | bytes 1572872 | tf_op jit(solution)/shard_map/ppermute | solution.py:208
  73.4 24.6 %collective-permute-start.8 = (f32[32,4096]{1,0:T(8,128)}, f32[32,4096]{1,0:T(8,128)S(1)}, u32[]{:S(2)}, u32[]{:S(2)}) collective-permute-start(f32[32,4096]{1,0:T(8,128)} %fusion.18), channel_id=1, source_target_pairs={{0,16},{16,0},{1,17},{17,1},{2,18},{18,2},{3,19},{19,3},{4,20},{20... | collective-permute-start | bytes 1572872 | tf_op jit(solution)/shard_map/ppermute | solution.py:208
  83.8 25.4 %collective-permute-start.6 = (f32[32,4096]{1,0:T(8,128)}, f32[32,4096]{1,0:T(8,128)S(1)}, u32[]{:S(2)}, u32[]{:S(2)}) collective-permute-start(f32[32,4096]{1,0:T(8,128)} %fusion.24), channel_id=1, source_target_pairs={{0,16},{16,0},{1,17},{17,1},{2,18},{18,2},{3,19},{19,3},{4,20},{20... | collective-permute-start | bytes 1572872 | tf_op jit(solution)/shard_map/ppermute | solution.py:208
  92.4 7.7 %copy-start = (f32[32,32,128]{2,1,0:T(8,128)S(1)}, f32[32,32,128]{2,1,0:T(8,128)}, u32[]{:S(2)}) copy-start(f32[32,32,128]{2,1,0:T(8,128)} %residual_plane.6) | copy-start | bytes 1572868
  94.5 22.7 %collective-permute-start.7 = (f32[32,4096]{1,0:T(8,128)S(1)}, f32[32,4096]{1,0:T(8,128)S(1)}, u32[]{:S(2)}, u32[]{:S(2)}) collective-permute-start(f32[32,4096]{1,0:T(8,128)S(1)} %fusion.21), channel_id=1, source_target_pairs={{0,16},{16,0},{1,17},{17,1},{2,18},{18,2},{3,19},{19,3},{4,20},{20... | collective-permute-start | bytes 1572872 | tf_op jit(solution)/shard_map/ppermute | solution.py:208
  95.2 29.3 %collective-permute-start.13 = (f32[32]{0:T(128)S(1)}, f32[32]{0:T(128)S(1)}, u32[]{:S(2)}, u32[]{:S(2)}) collective-permute-start(f32[32]{0:T(128)S(1)} %bitcast_multiply_fusion), channel_id=1, source_target_pairs={{0,8},{4,12},{1,9},{5,13},{2,10},{6,14},{3,11},{7,15},{16,24},{20,... | collective-permute-start | bytes 392 | tf_op jit(solution)/shard_map/ppermute | solution.py:225
  97.4 11.8 %copy-start.2 = (f32[32,32,128]{2,1,0:T(8,128)S(1)}, f32[32,32,128]{2,1,0:T(8,128)}, u32[]{:S(2)}) copy-start(f32[32,32,128]{2,1,0:T(8,128)} %residual_plane.4) | copy-start | bytes 1572868
  98.0 26.4 %collective-permute-start.11 = (f32[32]{0:T(128)S(1)}, f32[32]{0:T(128)S(1)}, u32[]{:S(2)}, u32[]{:S(2)}) collective-permute-start(f32[32]{0:T(128)S(1)} %bitcast_multiply_fusion), channel_id=1, source_target_pairs={{0,4},{4,8},{8,12},{1,5},{5,9},{9,13},{2,6},{6,10},{10,14},{3,7},{... | collective-permute-start | bytes 392 | tf_op jit(solution)/shard_map/ppermute | solution.py:225
  101.2 16.1 %copy-start.1 = (f32[32,32,128]{2,1,0:T(8,128)S(1)}, f32[32,32,128]{2,1,0:T(8,128)}, u32[]{:S(2)}) copy-start(f32[32,32,128]{2,1,0:T(8,128)} %residual_plane.5) | copy-start | bytes 1572868
  118.4 9.7 %copy-start.10 = (f32[32,1]{0,1:T(1,128)S(1)}, f32[32,1]{0,1:T(1,128)}, u32[]{:S(2)}) copy-start(f32[32,1]{0,1:T(1,128)} %param.15) | copy-start | bytes 388
  120.5 3.9 %collective-permute-start.14 = (f32[32,4,128]{2,1,0:T(4,128)S(1)}, f32[32,4,128]{2,1,0:T(4,128)S(1)}, u32[]{:S(2)}, u32[]{:S(2)}) collective-permute-start(f32[32,4,128]{2,1,0:T(4,128)S(1)} %bitcast.129), channel_id=1, source_target_pairs={{0,12},{1,13},{2,14},{3,15},{16,28},{17,29},{18,30},{19,31}} | collective-permute-start | bytes 196616 | tf_op jit(solution)/shard_map/ppermute | solution.py:224
  121.2 6.2 %collective-permute-start.12 = (f32[32,4,128]{2,1,0:T(4,128)S(1)}, f32[32,4,128]{2,1,0:T(4,128)S(1)}, u32[]{:S(2)}, u32[]{:S(2)}) collective-permute-start(f32[32,4,128]{2,1,0:T(4,128)S(1)} %bitcast.130), channel_id=1, source_target_pairs={{0,8},{4,12},{1,9},{5,13},{2,10},{6,14},{3,11},{7,15},{16,24},{20,... | collective-permute-start | bytes 196616 | tf_op jit(solution)/shard_map/ppermute | solution.py:224
  122.5 5.6 %collective-permute-start.10 = (f32[32,4,128]{2,1,0:T(4,128)S(1)}, f32[32,4,128]{2,1,0:T(4,128)S(1)}, u32[]{:S(2)}, u32[]{:S(2)}) collective-permute-start(f32[32,4,128]{2,1,0:T(4,128)S(1)} %bitcast.131), channel_id=1, source_target_pairs={{0,4},{4,8},{8,12},{1,5},{5,9},{9,13},{2,6},{6,10},{10,14},{3,7},{... | collective-permute-start | bytes 196616 | tf_op jit(solution)/shard_map/ppermute | solution.py:224

commit v3 on v1

v3 whole, which is shorter than its diff:
```python
import functools
import math

import jax
import jax.numpy as jnp
from jax import lax
from jax.experimental import pallas as pl
from jax.experimental.pallas import tpu as pltpu
from jax.sharding import PartitionSpec as P

axial_coupling = 0.5
SAMPLE_BLOCK = 8


def shifted(block, axes, sizes, delta):
    route = []
    for i in range(sizes[0]):
        for j in range(sizes[1]):
            si, sj = i - delta[0], j - delta[1]
            if 0 <= si < sizes[0] and 0 <= sj < sizes[1]:
                route.append((si * sizes[1] + sj, i * sizes[1] + j))
    return lax.ppermute(block, axes, route)


def fourier_rows(row_ids, sample_ids, sample_count):
    half_count = sample_count // 2
    harmonic = jnp.where(row_ids <= half_count, row_ids, row_ids - half_count)
    phase_index = harmonic[:, None] * sample_ids[None, :] % sample_count
    angle_value = phase_index.astype(jnp.float32) * (2.0 * math.pi / sample_count)
    dft_table = jnp.where(
        (row_ids <= half_count)[:, None], jnp.cos(angle_value), jnp.sin(angle_value)
    )
    return dft_table * math.sqrt(2.0 / sample_count)


def row_to_col(row, ix, iy):
    full = jnp.broadcast_to(row, ix.shape)
    return jnp.sum(jnp.where(ix == iy, full, 0.0), axis=1, keepdims=True)


def col_to_row(col, ix, iy):
    full = jnp.broadcast_to(col, ix.shape)
    return jnp.sum(jnp.where(ix == iy, full, 0.0), axis=0, keepdims=True)


def edges_kernel(a_ref, x31_ref, x0_ref, y127_ref, y0_ref):
    n_s, planes, nx, ny = a_ref.shape
    ix = lax.broadcasted_iota(jnp.int32, (nx, ny), 0)
    iy = lax.broadcasted_iota(jnp.int32, (nx, ny), 1)

    def body(s, carry):
        for p in range(planes):
            a = a_ref[s, p]
            x31_ref[p, pl.ds(s, 1), :] = a[nx - 1:nx, :]
            x0_ref[p, pl.ds(s, 1), :] = a[0:1, :]
            y127_ref[p, pl.ds(s, 1), :] = col_to_row(a[:, ny - 1:ny], ix, iy)
            y0_ref[p, pl.ds(s, 1), :] = col_to_row(a[:, 0:1], ix, iy)
        return carry

    lax.fori_loop(0, n_s, body, 0)


def edges(a):
    n_s, planes, nx, ny = a.shape
    sb = min(SAMPLE_BLOCK, n_s)
    out = jax.ShapeDtypeStruct((planes, n_s, ny), jnp.float32)
    spec = pl.BlockSpec((planes, sb, ny), lambda i: (0, i, 0))
    return pl.pallas_call(
        edges_kernel,
        grid=(n_s // sb,),
        in_specs=[pl.BlockSpec((sb, planes, nx, ny), lambda i: (i, 0, 0, 0))],
        out_specs=[spec] * 4,
        out_shape=[out] * 4,
        name="halo_edges",
    )(a)


def residual_kernel(kinds, a_ref, src_ref, xlo_ref, xhi_ref, ylo_ref, yhi_ref, c1_ref, c2_ref, base_ref, sat_ref,
                    reg_ref, reg_xlo_ref, reg_ylo_ref, out_ref):
    blk = pl.program_id(0)
    n_s, planes, nx, ny = a_ref.shape
    ix = lax.broadcasted_iota(jnp.int32, (nx, ny), 0)
    iy = lax.broadcasted_iota(jnp.int32, (nx, ny), 1)
    ix_col = lax.broadcasted_iota(jnp.int32, (nx, 1), 0)
    iy_row = lax.broadcasted_iota(jnp.int32, (1, ny), 1)
    reg = reg_ref[...]
    reg_xlo = reg_xlo_ref[...]
    reg_ylo = row_to_col(reg_ylo_ref[...].astype(jnp.float32), ix, iy).astype(jnp.int32)

    def lookup(kind, table, row):
        out = jnp.full(kind.shape, table[row, 0] if row is not None else table[0], jnp.float32)
        for k in range(1, kinds):
            out = jnp.where(kind == k, table[row, k] if row is not None else table[k], out)
        return out

    sat = lookup(reg, sat_ref, None)
    sat_xlo = lookup(reg_xlo, sat_ref, None)
    sat_ylo = lookup(reg_ylo, sat_ref, None)

    def body(s, carry):
        s_glob = blk * n_s + s
        base = lookup(reg, base_ref, s_glob)
        base_xlo = lookup(reg_xlo, base_ref, s_glob)
        base_ylo = lookup(reg_ylo, base_ref, s_glob)
        tiles = [a_ref[s, p] for p in range(planes)]
        for p in range(planes):
            a = tiles[p]
            row_hi = xhi_ref[p, pl.ds(s, 1), :]
            row_lo = xlo_ref[p, pl.ds(s, 1), :]
            col_hi = row_to_col(yhi_ref[p, pl.ds(s, 1), :], ix, iy)
            col_lo = row_to_col(ylo_ref[p, pl.ds(s, 1), :], ix, iy)
            c1 = c1_ref[p, s_glob]
            c2 = c2_ref[p, s_glob]
            a_xp = jnp.where(ix == nx - 1, row_hi, pltpu.roll(a, nx - 1, 0))
            a_yp = jnp.where(iy == ny - 1, col_hi, pltpu.roll(a, ny - 1, 1))
            sx = a_xp - a
            sy = a_yp - a
            rel = base * (1.0 + sat * (sx * sx + sy * sy))
            fx = rel * sx
            fy = rel * sy
            lo_yp = jnp.where(iy_row == ny - 1, c1, pltpu.roll(row_lo, ny - 1, 1))
            sx_l = a[0:1, :] - row_lo
            sy_l = lo_yp - row_lo
            fx_l = base_xlo * (1.0 + sat_xlo * (sx_l * sx_l + sy_l * sy_l)) * sx_l
            lo_xp = jnp.where(ix_col == nx - 1, c2, pltpu.roll(col_lo, nx - 1, 0))
            sx_c = lo_xp - col_lo
            sy_c = a[:, 0:1] - col_lo
            fy_c = base_ylo * (1.0 + sat_ylo * (sx_c * sx_c + sy_c * sy_c)) * sy_c
            fx_down = jnp.where(ix == 0, fx_l, pltpu.roll(fx, 1, 0))
            fy_left = jnp.where(iy == 0, fy_c, pltpu.roll(fy, 1, 1))
            curl = fx_down - fx + fy_left - fy
            axial = 2.0 * a
            if p > 0:
                axial = axial - tiles[p - 1]
            if p < planes - 1:
                axial = axial - tiles[p + 1]
            out_ref[p, s] = curl + axial_coupling * axial - src_ref[s, p]
        return carry

    lax.fori_loop(0, n_s, body, 0)


def residual(a, src, xlo, xhi, ylo, yhi, c1, c2, base_rows, saturation, reg, reg_xlo, reg_ylo):
    n_s, planes, nx, ny = a.shape
    kinds = base_rows.shape[1]
    sb = min(SAMPLE_BLOCK, n_s)
    tile = pl.BlockSpec((sb, planes, nx, ny), lambda i: (i, 0, 0, 0))
    edge = pl.BlockSpec((planes, sb, ny), lambda i: (0, i, 0))
    vmem_whole = pl.BlockSpec(memory_space=pltpu.VMEM)
    smem_whole = pl.BlockSpec(memory_space=pltpu.SMEM)
    return pl.pallas_call(
        functools.partial(residual_kernel, kinds),
        grid=(n_s // sb,),
        in_specs=[tile, tile, edge, edge, edge, edge] + [smem_whole] * 4 + [vmem_whole] * 3,
        out_specs=pl.BlockSpec((planes, sb, nx, ny), lambda i: (0, i, 0, 0)),
        out_shape=jax.ShapeDtypeStruct((planes, n_s, nx, ny), jnp.float32),
        name="residual",
    )(a, src, xlo, xhi, ylo, yhi, c1, c2, base_rows, saturation, reg, reg_xlo, reg_ylo)


def local(potential, source, region, level_index, reluctivity, saturation, inverse, transmit):
    samples_dev, planes, cells_x, cells_y = potential.shape
    n_tm = lax.axis_size("tm")
    n_gx = lax.axis_size("gx")
    n_gy = lax.axis_size("gy")
    me_tm = lax.axis_index("tm")
    me_gx = lax.axis_index("gx")
    sample_count = samples_dev * n_tm
    grid = ("gx", "gy")
    sizes = (n_gx, n_gy)
    rows = planes * samples_dev

    e_x31, e_x0, e_y127, e_y0 = edges(potential)
    regf = region.astype(jnp.float32)
    pad = jnp.zeros((7, cells_y), jnp.float32)
    reg_col = jnp.pad(regf[:, cells_y - 1], (0, cells_y - cells_x))
    msg_xlo = jnp.concatenate([e_x31.reshape(rows, cells_y), regf[cells_x - 1][None], pad], axis=0)
    msg_ylo = jnp.concatenate([e_y127.reshape(rows, cells_y), reg_col[None], pad], axis=0)
    got_xlo = shifted(msg_xlo, grid, sizes, (1, 0))
    got_ylo = shifted(msg_ylo, grid, sizes, (0, 1))
    xhi = shifted(e_x0, grid, sizes, (-1, 0))
    yhi = shifted(e_y0, grid, sizes, (0, -1))
    c1 = shifted(e_x31[:, :, 0], grid, sizes, (1, -1))
    c2 = shifted(e_x0[:, :, cells_y - 1], grid, sizes, (-1, 1))

    xlo = got_xlo[:rows].reshape(planes, samples_dev, cells_y)
    reg_xlo = got_xlo[rows:rows + 1].astype(jnp.int32)
    ylo = got_ylo[:rows].reshape(planes, samples_dev, cells_y)
    reg_ylo = got_ylo[rows:rows + 1].astype(jnp.int32)

    onehot = (level_index[:, None] == lax.iota(jnp.int32, reluctivity.shape[0])[None, :]).astype(jnp.float32)
    base_rows = jnp.sum(onehot[:, :, None] * reluctivity[None], axis=1)

    resid = residual(potential, source, xlo, xhi, ylo, yhi, c1, c2, base_rows, saturation,
                     region, reg_xlo, reg_ylo)

    sample_ids = me_tm * samples_dev + lax.iota(jnp.int32, samples_dev)
    q_dev = samples_dev

    spectra_planes = []
    for p in range(planes):
        plane = resid[p]
        parts = []
        for d in range(1, n_tm):
            owner = (me_tm + d) % n_tm
            tab = fourier_rows(owner * q_dev + lax.iota(jnp.int32, q_dev), sample_ids, sample_count)
            part = jnp.einsum("qs,sxy->qxy", tab, plane, precision=lax.Precision.HIGHEST)
            route = [(i, (i + d) % n_tm) for i in range(n_tm)]
            parts.append(lax.ppermute(part, "tm", route))
        own_tab = fourier_rows(me_tm * q_dev + lax.iota(jnp.int32, q_dev), sample_ids, sample_count)
        acc = jnp.einsum("qs,sxy->qxy", own_tab, plane, precision=lax.Precision.HIGHEST)
        for got in parts:
            acc = acc + got
        spectra_planes.append(acc)
    spectra = jnp.stack(spectra_planes, axis=1)

    solved = jnp.einsum("qab,qpbj->qpaj", inverse, spectra, precision=lax.Precision.HIGHEST)
    line_tail = solved[:, :, cells_x - 1, :]
    gain_here = transmit[:, 0] * inverse[:, cells_x - 1, 0]
    msg_tail = jnp.concatenate([line_tail, jnp.broadcast_to(gain_here[:, None, None], (q_dev, 1, cells_y))], axis=1)

    carried = jnp.zeros_like(line_tail)
    for d in range(n_gx - 1, 0, -1):
        route = [(i, i + d) for i in range(n_gx - d)]
        got = lax.ppermute(msg_tail, "gx", route)
        stepped = got[:, :planes] + got[:, planes:planes + 1] * carried
        carried = jnp.where(me_gx >= d, stepped, carried)
    injected = transmit[:, 0][:, None, None] * carried
    correction = solved + injected[:, :, None, :] * inverse[:, :, 0][:, None, :, None]
    return correction


def solution(mesh):
    in_specs = (
        P("tm", None, "gx", "gy"),
        P("tm", None, "gx", "gy"),
        P("gx", "gy"),
        P("tm"),
        P(),
        P(),
        P("tm", "gx", None),
        P("tm", "gx"),
    )
    out_specs = P("tm", None, "gx", "gy")
    return jax.shard_map(local, mesh=mesh, in_specs=in_specs, out_specs=out_specs, check_vma=False)
```

time: 148 us -> 114 us (0.77)
  other arithmetic: 34.8 us -> 5.02 us
  local copies, waits for them, and re-layouts: 33 us -> 7.12 us
  Pallas kernels: 0 us -> 20.3 us
  waiting for transfers between devices: 37.4 us -> 42.1 us
  starting transfers between devices: 30.1 us -> 26.1 us
  matrix products: 9.93 us -> 11.6 us
    pallas_call x0 -> x2, Pallas kernels: none -> 20.3 us  [the longest x1 14.7 us: residual(): pl.pallas_call(functools.partial(residual_kernel, kinds), grid=(n_s // sb...]
    select_n x6 -> x0, other arithmetic: 17.6 us -> none  [the longest x3 15.1 us: reluct_of(): sl = jnp.where(kind == k, saturation[k], sl)]
    slice x16 -> x7, local copies, waits for them, and re-layouts: 19.5 us -> 3.41 us  [the longest x1 1 us: local(): c2 = shifted(e_x0[:, :, cells_y - 1], grid, sizes, (-1, 1))]
    sub x1 -> x0, other arithmetic: 11.2 us -> none  [local(): curl_part + axial_coupling * (2.0 * a - plane_below - plane_above) - source]
    broadcast_in_dim x7 -> x3, local copies, waits for them, and re-layouts: 7.52 us -> 0.09 us  [the longest x1 0.09 us: local(): jnp.broadcast_to(gain_here[:, None, None], (q_dev, 1, cells_y))]
    ppermute x10 -> x7, waiting for transfers between devices: 37.3 us -> 42.1 us  [the longest x4 36.3 us: local(): parts.append(lax.ppermute(part, 'tm', route))]
    ppermute x10 -> x7, starting transfers between devices: 12.8 us -> 8.21 us  [the longest x4 4.33 us: local(): parts.append(lax.ppermute(part, 'tm', route))]
    unnamed x72 -> x19, local copies, waits for them, and re-layouts: 3.24 us -> 1.04 us
  transfers between devices with their start and end apart: 16 -> 13, of which waited for: 6 -> 5; matrix products, arithmetic and copies ran while one was open for 48% -> 10% of each run, Pallas kernels for 0% -> 0%
where the time goes in v3:
time: 114 us; the launch traced here: 113 us
  waiting for transfers between devices  42.1 us (37%)
  starting transfers between devices  26.1 us (23%)
  Pallas kernels  20.3 us (18%)
  matrix products  11.6 us (10%)
  local copies, waits for them, and re-layouts  7.12 us (6%)
  other arithmetic  5.02 us (4%)
    ppermute x4, waiting for transfers between devices, local(): parts.append(lax.ppermute(part, 'tm', route))  36.3 us
    ppermute x6, starting transfers between devices, shifted(): return lax.ppermute(block, axes, route)  17.9 us
    pallas_call x1, Pallas kernels, residual(): pl.pallas_call(functools.partial(residual_kernel, kinds), grid=(n_s // sb...  14.7 us
    ppermute x3, waiting for transfers between devices, local(): got = lax.ppermute(msg_tail, 'gx', route)  5.83 us
    pallas_call x1, Pallas kernels, edges(): pl.pallas_call(edges_kernel, grid=(n_s // sb,), in_specs=[pl.BlockSpec((s...  5.63 us
    ppermute x4, starting transfers between devices, local(): parts.append(lax.ppermute(part, 'tm', route))  4.33 us
    dot_general x4, matrix products, local(): jnp.einsum('qs,sxy->qxy', own_tab, plane, precision=lax.Precision.HIGHEST)  4.03 us
    dot_general x4, matrix products, local(): jnp.einsum('qs,sxy->qxy', tab, plane, precision=lax.Precision.HIGHEST)  3.95 us
  transfers between devices with their start and end apart: 13, of which 5 were waited for; matrix products, arithmetic and copies ran while one was open for 10% of the time, Pallas kernels for 0%

profile of v3, /device:TPU:12, one launch (start us, length us, event | category | flops | bytes accessed | tf_op | source)
XLA Modules:
  0.0 112.7 jit_solution(14102059478888131000)
XLA Ops:
  0.0 0.8 convert_element_type.31
  1.0 5.6 %halo_edges.1 = (f32[4,32,128]{2,1,0:T(8,128)}, f32[4,32,128]{2,1,0:T(8,128)}, f32[4,32,128]{2,1,0:T(8,128)}, f32[4,32,128]{2,1,0:T(8,128)}) custom-call(f32[32,4,32,128]{3,2,1,0:T(8,128)} %a_ref.3), custom_call_target="tpu_custom_call" | custom-call | tf_op jit(solution)/shard_map/halo_edges/pallas_call | solution.py:68
  6.7 1.0 maximum_maximum_fusion.1
  7.7 1.9 %collective-permute-start = (f32[136,128]{1,0:T(8,128)S(1)}, f32[136,128]{1,0:T(8,128)S(1)}, u32[]{:S(2)}, u32[]{:S(2)}) collective-permute-start(f32[136,128]{1,0:T(8,128)S(1)} %get-tuple-element.18), channel_id=1, source_target_pairs={{0,4},{1,5},{2,6},{3,7},{4,8},{5,9},{6,10},{7,11},{8,12},{9,13},{1... | collective-permute-start | bytes 208904 | tf_op jit(solution)/shard_map/ppermute | solution.py:22
  9.6 3.6 %collective-permute-start.1 = (f32[4,32,128]{2,1,0:T(8,128)}, f32[4,32,128]{2,1,0:T(8,128)S(1)}, u32[]{:S(2)}, u32[]{:S(2)}) collective-permute-start(f32[4,32,128]{2,1,0:T(8,128)} %get-tuple-element.10), channel_id=1, source_target_pairs={{4,0},{5,1},{6,2},{7,3},{8,4},{9,5},{10,6},{11,7},{12,8},{13,9},{1... | collective-permute-start | bytes 196616 | tf_op jit(solution)/shard_map/ppermute | solution.py:22
  13.2 3.5 %collective-permute-start.2 = (f32[136,128]{1,0:T(8,128)S(1)}, f32[136,128]{1,0:T(8,128)S(1)}, u32[]{:S(2)}, u32[]{:S(2)}) collective-permute-start(f32[136,128]{1,0:T(8,128)S(1)} %get-tuple-element.17), channel_id=1, source_target_pairs={{0,1},{1,2},{2,3},{4,5},{5,6},{6,7},{8,9},{9,10},{10,11},{12,13},{... | collective-permute-start | bytes 208904 | tf_op jit(solution)/shard_map/ppermute | solution.py:22
  16.7 2.4 %collective-permute-start.3 = (f32[4,32,128]{2,1,0:T(8,128)}, f32[4,32,128]{2,1,0:T(8,128)S(1)}, u32[]{:S(2)}, u32[]{:S(2)}) collective-permute-start(f32[4,32,128]{2,1,0:T(8,128)} %get-tuple-element.12), channel_id=1, source_target_pairs={{1,0},{2,1},{3,2},{5,4},{6,5},{7,6},{9,8},{10,9},{11,10},{13,12},{... | collective-permute-start | bytes 196616 | tf_op jit(solution)/shard_map/ppermute | solution.py:22
  19.1 0.9 slice_reduce_fusion.1
  20.0 1.9 %collective-permute-start.4 = (f32[4,32]{1,0:T(4,128)S(1)}, f32[4,32]{1,0:T(4,128)S(1)}, u32[]{:S(2)}, u32[]{:S(2)}) collective-permute-start(f32[4,32]{1,0:T(4,128)S(1)} %slice_reduce_fusion.1), channel_id=1, source_target_pairs={{1,4},{2,5},{3,6},{5,8},{6,9},{7,10},{9,12},{10,13},{11,14},{17,20... | collective-permute-start | bytes 1544 | tf_op jit(solution)/shard_map/ppermute | solution.py:22
  22.0 1.0 slice_reduce_fusion
  24.0 4.5 %collective-permute-start.5 = (f32[4,32]{1,0:T(4,128)S(1)}, f32[4,32]{1,0:T(4,128)S(1)}, u32[]{:S(2)}, u32[]{:S(2)}) collective-permute-start(f32[4,32]{1,0:T(4,128)S(1)} %slice_reduce_fusion), channel_id=1, source_target_pairs={{4,1},{5,2},{6,3},{8,5},{9,6},{10,7},{12,9},{13,10},{14,11},{20,17... | collective-permute-start | bytes 1544 | tf_op jit(solution)/shard_map/ppermute | solution.py:22
  31.6 14.7 %residual.1 = f32[4,32,32,128]{3,2,1,0:T(8,128)} custom-call(f32[32,4,32,128]{3,2,1,0:T(8,128)} %a_ref.3, f32[32,4,32,128]{3,2,1,0:T(8,128)} %src_ref.1, f32[4,32,128]{2,1,0:T(8,128)} %bitcast.61, f32[4,32,128]{2,1,0:T(8,128)} %copy-done.1, f32[4,32,128]{2,1,0:T(8,128)} %bitcast.62, f32[4,32,128]{2,1,0:T(8,128)} %copy-done.2, f32[4,32]{1,0:T(4,128)} %copy-done.4, ...), custom_call_target="tpu_custom_call" | custom-call | tf_op jit(solution)/shard_map/residual/pallas_call | solution.py:151
  46.2 1.7 %slice_bitcast_fusion.3 = (f32[32,32,128]{2,1,0:T(8,128)S(1)}, f32[32,32,128]{2,1,0:T(8,128)S(1)}, f32[32,32,128]{2,1,0:T(8,128)S(1)}, f32[32,32,128]{2,1,0:T(8,128)S(1)}) fusion(f32[4,32,32,128]{3,2,1,0:T(8,128)} %residual.1), kind=kLoop, calls=%fused_computation.16 | loop fusion | bytes 4194304 | tf_op jit(solution)/shard_map/squeeze | solution.py:202
  48.0 1.0 fusion.10
  49.0 1.6 %collective-permute-start.9 = (f32[32,32,128]{2,0,1:T(8,128)S(1)}, f32[32,32,128]{2,0,1:T(8,128)S(1)}, u32[]{:S(2)}, u32[]{:S(2)}) collective-permute-start(f32[32,32,128]{2,0,1:T(8,128)S(1)} %fusion.10), channel_id=1, source_target_pairs={{0,16},{16,0},{1,17},{17,1},{2,18},{18,2},{3,19},{19,3},{4,20},{20... | collective-permute-start | bytes 1572872 | tf_op jit(solution)/shard_map/ppermute | solution.py:209
  50.6 1.0 fusion.13
  52.1 1.0 fusion.16
  53.1 1.6 %collective-permute-start.7 = (f32[32,32,128]{2,0,1:T(8,128)S(1)}, f32[32,32,128]{2,0,1:T(8,128)S(1)}, u32[]{:S(2)}, u32[]{:S(2)}) collective-permute-start(f32[32,32,128]{2,0,1:T(8,128)S(1)} %fusion.16), channel_id=1, source_target_pairs={{0,16},{16,0},{1,17},{17,1},{2,18},{18,2},{3,19},{19,3},{4,20},{20... | collective-permute-start | bytes 1572872 | tf_op jit(solution)/shard_map/ppermute | solution.py:209
  54.7 1.0 fusion.19
  56.3 7.6 %collective-permute-done.9 = f32[32,32,128]{2,0,1:T(8,128)S(1)} collective-permute-done((f32[32,32,128]{2,0,1:T(8,128)S(1)}, f32[32,32,128]{2,0,1:T(8,128)S(1)}, u32[]{:S(2)}, u32[]{:S(2)}) %collective-permute-start.9) | collective-permute-done | bytes 524320 | tf_op jit(solution)/shard_map/ppermute | solution.py:209
  63.9 1.0 fusion.5
  64.9 10.2 %collective-permute-done.8 = f32[32,32,128]{2,0,1:T(8,128)S(1)} collective-permute-done((f32[32,32,128]{2,0,1:T(8,128)S(1)}, f32[32,32,128]{2,0,1:T(8,128)S(1)}, u32[]{:S(2)}, u32[]{:S(2)}) %collective-permute-start.8) | collective-permute-done | bytes 524320 | tf_op jit(solution)/shard_map/ppermute | solution.py:209
  75.1 1.0 fusion.6
  76.2 10.2 %collective-permute-done.7 = f32[32,32,128]{2,0,1:T(8,128)S(1)} collective-permute-done((f32[32,32,128]{2,0,1:T(8,128)S(1)}, f32[32,32,128]{2,0,1:T(8,128)S(1)}, u32[]{:S(2)}, u32[]{:S(2)}) %collective-permute-start.7) | collective-permute-done | bytes 524320 | tf_op jit(solution)/shard_map/ppermute | solution.py:209
  86.4 1.0 fusion.7
  87.4 8.2 %collective-permute-done.6 = f32[32,32,128]{2,0,1:T(8,128)S(1)} collective-permute-done((f32[32,32,128]{2,0,1:T(8,128)S(1)}, f32[32,32,128]{2,0,1:T(8,128)S(1)}, u32[]{:S(2)}, u32[]{:S(2)}) %collective-permute-start.6) | collective-permute-done | bytes 524320 | tf_op jit(solution)/shard_map/ppermute | solution.py:209
  95.6 1.0 fusion.8
  96.8 3.6 %fusion.2 = f32[32,4,32,128]{3,2,1,0:T(8,128)S(1)} fusion(f32[32,4,32,128]{3,0,2,1:T(8,128)S(1)} %pad_maximum_fusion, f32[32,32,32]{2,1,0:T(8,128)S(1)} %copy-done), kind=kOutput, calls=%fused_computation.4 | convolution fusion | flops 201326592 | bytes 4325376 | tf_op jit(solution)/shard_map/qab,qpbj->qpaj/dot_general | solution.py:217
  101.6 1.9 %collective-permute-start.10 = (f32[32,5,128]{2,1,0:T(8,128)S(1)}, f32[32,5,128]{2,1,0:T(8,128)S(1)}, u32[]{:S(2)}, u32[]{:S(2)}) collective-permute-start(f32[32,5,128]{2,1,0:T(8,128)S(1)} %pad_maximum_fusion.1), channel_id=1, source_target_pairs={{0,4},{4,8},{8,12},{1,5},{5,9},{9,13},{2,6},{6,10},{10,14},{3,7},{... | collective-permute-start | bytes 245768 | tf_op jit(solution)/shard_map/ppermute | solution.py:225
  103.6 1.3 %collective-permute-start.11 = (f32[32,5,128]{2,1,0:T(8,128)S(1)}, f32[32,5,128]{2,1,0:T(8,128)S(1)}, u32[]{:S(2)}, u32[]{:S(2)}) collective-permute-start(f32[32,5,128]{2,1,0:T(8,128)S(1)} %pad_maximum_fusion.1), channel_id=1, source_target_pairs={{0,8},{4,12},{1,9},{5,13},{2,10},{6,14},{3,11},{7,15},{16,24},{20,... | collective-permute-start | bytes 245768 | tf_op jit(solution)/shard_map/ppermute | solution.py:225
  104.9 5.8 %collective-permute-done.11 = f32[32,5,128]{2,1,0:T(8,128)S(1)} collective-permute-done((f32[32,5,128]{2,1,0:T(8,128)S(1)}, f32[32,5,128]{2,1,0:T(8,128)S(1)}, u32[]{:S(2)}, u32[]{:S(2)}) %collective-permute-start.11) | collective-permute-done | bytes 81952 | tf_op jit(solution)/shard_map/ppermute | solution.py:225
  110.9 1.8 %multiply_add_fusion = f32[32,4,32,128]{3,2,1,0:T(8,128)} fusion(f32[32,4,32,128]{3,2,1,0:T(8,128)S(1)} %fusion.2, f32[32,32]{1,0:T(8,128)S(1)} %bitcast.65, f32[32,4,128]{2,1,0:T(4,128)S(1)} %fusion.25), kind=kLoop, calls=%fused_computation.3 | loop fusion | flops 1048576 | bytes 4263936 | tf_op jit(solution)/shard_map/add | solution.py:229
  (56 shorter events, 6.9 us)
Async XLA Ops:
  0.0 23.0 %copy-start.3 = (f32[16,8]{0,1:T(8,128)S(1)}, f32[16,8]{0,1:T(8,128)}, u32[]{:S(2)}) copy-start(f32[16,8]{0,1:T(8,128)} %param.12) | copy-start | bytes 1540
  0.0 23.1 %copy-start.7 = (s32[32]{0:T(128)S(1)}, s32[32]{0:T(128)}, u32[]{:S(2)}) copy-start(s32[32]{0:T(128)} %param.11) | copy-start | bytes 388
  0.0 23.8 %copy-start = (f32[32,32,32]{2,1,0:T(8,128)S(1)}, f32[32,32,32]{2,1,0:T(8,128)}, u32[]{:S(2)}) copy-start(f32[32,32,32]{2,1,0:T(8,128)} %param.14) | copy-start | bytes 393220
  0.0 24.0 %copy-start.6 = (f32[32,1]{0,1:T(1,128)S(1)}, f32[32,1]{0,1:T(1,128)}, u32[]{:S(2)}) copy-start(f32[32,1]{0,1:T(1,128)} %param.15) | copy-start | bytes 388
  7.7 16.3 %collective-permute-start = (f32[136,128]{1,0:T(8,128)S(1)}, f32[136,128]{1,0:T(8,128)S(1)}, u32[]{:S(2)}, u32[]{:S(2)}) collective-permute-start(f32[136,128]{1,0:T(8,128)S(1)} %get-tuple-element.18), channel_id=1, source_target_pairs={{0,4},{1,5},{2,6},{3,7},{4,8},{5,9},{6,10},{7,11},{8,12},{9,13},{1... | collective-permute-start | bytes 208904 | tf_op jit(solution)/shard_map/ppermute | solution.py:22
  9.6 21.3 %collective-permute-start.1 = (f32[4,32,128]{2,1,0:T(8,128)}, f32[4,32,128]{2,1,0:T(8,128)S(1)}, u32[]{:S(2)}, u32[]{:S(2)}) collective-permute-start(f32[4,32,128]{2,1,0:T(8,128)} %get-tuple-element.10), channel_id=1, source_target_pairs={{4,0},{5,1},{6,2},{7,3},{8,4},{9,5},{10,6},{11,7},{12,8},{13,9},{1... | collective-permute-start | bytes 196616 | tf_op jit(solution)/shard_map/ppermute | solution.py:22
  13.2 15.8 %collective-permute-start.2 = (f32[136,128]{1,0:T(8,128)S(1)}, f32[136,128]{1,0:T(8,128)S(1)}, u32[]{:S(2)}, u32[]{:S(2)}) collective-permute-start(f32[136,128]{1,0:T(8,128)S(1)} %get-tuple-element.17), channel_id=1, source_target_pairs={{0,1},{1,2},{2,3},{4,5},{5,6},{6,7},{8,9},{9,10},{10,11},{12,13},{... | collective-permute-start | bytes 208904 | tf_op jit(solution)/shard_map/ppermute | solution.py:22
  16.7 14.2 %collective-permute-start.3 = (f32[4,32,128]{2,1,0:T(8,128)}, f32[4,32,128]{2,1,0:T(8,128)S(1)}, u32[]{:S(2)}, u32[]{:S(2)}) collective-permute-start(f32[4,32,128]{2,1,0:T(8,128)} %get-tuple-element.12), channel_id=1, source_target_pairs={{1,0},{2,1},{3,2},{5,4},{6,5},{7,6},{9,8},{10,9},{11,10},{13,12},{... | collective-permute-start | bytes 196616 | tf_op jit(solution)/shard_map/ppermute | solution.py:22
  20.0 10.9 %collective-permute-start.4 = (f32[4,32]{1,0:T(4,128)S(1)}, f32[4,32]{1,0:T(4,128)S(1)}, u32[]{:S(2)}, u32[]{:S(2)}) collective-permute-start(f32[4,32]{1,0:T(4,128)S(1)} %slice_reduce_fusion.1), channel_id=1, source_target_pairs={{1,4},{2,5},{3,6},{5,8},{6,9},{7,10},{9,12},{10,13},{11,14},{17,20... | collective-permute-start | bytes 1544 | tf_op jit(solution)/shard_map/ppermute | solution.py:22
  24.0 6.9 %collective-permute-start.5 = (f32[4,32]{1,0:T(4,128)S(1)}, f32[4,32]{1,0:T(4,128)S(1)}, u32[]{:S(2)}, u32[]{:S(2)}) collective-permute-start(f32[4,32]{1,0:T(4,128)S(1)} %slice_reduce_fusion), channel_id=1, source_target_pairs={{4,1},{5,2},{6,3},{8,5},{9,6},{10,7},{12,9},{13,10},{14,11},{20,17... | collective-permute-start | bytes 1544 | tf_op jit(solution)/shard_map/ppermute | solution.py:22
  30.9 0.6 copy-start.4
  30.9 0.6 copy-start.5
  30.9 0.6 copy-start.1
  31.0 0.6 copy-start.2
  49.0 14.9 %collective-permute-start.9 = (f32[32,32,128]{2,0,1:T(8,128)S(1)}, f32[32,32,128]{2,0,1:T(8,128)S(1)}, u32[]{:S(2)}, u32[]{:S(2)}) collective-permute-start(f32[32,32,128]{2,0,1:T(8,128)S(1)} %fusion.10), channel_id=1, source_target_pairs={{0,16},{16,0},{1,17},{17,1},{2,18},{18,2},{3,19},{19,3},{4,20},{20... | collective-permute-start | bytes 1572872 | tf_op jit(solution)/shard_map/ppermute | solution.py:209
  51.6 23.6 %collective-permute-start.8 = (f32[32,32,128]{2,0,1:T(8,128)S(1)}, f32[32,32,128]{2,0,1:T(8,128)S(1)}, u32[]{:S(2)}, u32[]{:S(2)}) collective-permute-start(f32[32,32,128]{2,0,1:T(8,128)S(1)} %fusion.13), channel_id=1, source_target_pairs={{0,16},{16,0},{1,17},{17,1},{2,18},{18,2},{3,19},{19,3},{4,20},{20... | collective-permute-start | bytes 1572872 | tf_op jit(solution)/shard_map/ppermute | solution.py:209
  53.1 33.2 %collective-permute-start.7 = (f32[32,32,128]{2,0,1:T(8,128)S(1)}, f32[32,32,128]{2,0,1:T(8,128)S(1)}, u32[]{:S(2)}, u32[]{:S(2)}) collective-permute-start(f32[32,32,128]{2,0,1:T(8,128)S(1)} %fusion.16), channel_id=1, source_target_pairs={{0,16},{16,0},{1,17},{17,1},{2,18},{18,2},{3,19},{19,3},{4,20},{20... | collective-permute-start | bytes 1572872 | tf_op jit(solution)/shard_map/ppermute | solution.py:209
  55.7 39.9 %collective-permute-start.6 = (f32[32,32,128]{2,0,1:T(8,128)S(1)}, f32[32,32,128]{2,0,1:T(8,128)S(1)}, u32[]{:S(2)}, u32[]{:S(2)}) collective-permute-start(f32[32,32,128]{2,0,1:T(8,128)S(1)} %fusion.19), channel_id=1, source_target_pairs={{0,16},{16,0},{1,17},{17,1},{2,18},{18,2},{3,19},{19,3},{4,20},{20... | collective-permute-start | bytes 1572872 | tf_op jit(solution)/shard_map/ppermute | solution.py:209
  100.7 4.2 %collective-permute-start.12 = (f32[32,5,128]{2,1,0:T(8,128)S(1)}, f32[32,5,128]{2,1,0:T(8,128)S(1)}, u32[]{:S(2)}, u32[]{:S(2)}) collective-permute-start(f32[32,5,128]{2,1,0:T(8,128)S(1)} %pad_maximum_fusion.1), channel_id=1, source_target_pairs={{0,12},{1,13},{2,14},{3,15},{16,28},{17,29},{18,30},{19,31}} | collective-permute-start | bytes 245768 | tf_op jit(solution)/shard_map/ppermute | solution.py:225
  101.6 9.1 %collective-permute-start.10 = (f32[32,5,128]{2,1,0:T(8,128)S(1)}, f32[32,5,128]{2,1,0:T(8,128)S(1)}, u32[]{:S(2)}, u32[]{:S(2)}) collective-permute-start(f32[32,5,128]{2,1,0:T(8,128)S(1)} %pad_maximum_fusion.1), channel_id=1, source_target_pairs={{0,4},{4,8},{8,12},{1,5},{5,9},{9,13},{2,6},{6,10},{10,14},{3,7},{... | collective-permute-start | bytes 245768 | tf_op jit(solution)/shard_map/ppermute | solution.py:225
  103.6 7.2 %collective-permute-start.11 = (f32[32,5,128]{2,1,0:T(8,128)S(1)}, f32[32,5,128]{2,1,0:T(8,128)S(1)}, u32[]{:S(2)}, u32[]{:S(2)}) collective-permute-start(f32[32,5,128]{2,1,0:T(8,128)S(1)} %pad_maximum_fusion.1), channel_id=1, source_target_pairs={{0,8},{4,12},{1,9},{5,13},{2,10},{6,14},{3,11},{7,15},{16,24},{20,... | collective-permute-start | bytes 245768 | tf_op jit(solution)/shard_map/ppermute | solution.py:225

commit v4 on v3

v4 whole, which is shorter than its diff:
```python
import functools
import math

import jax
import jax.numpy as jnp
from jax import lax
from jax.experimental import pallas as pl
from jax.experimental.pallas import tpu as pltpu
from jax.sharding import PartitionSpec as P

axial_coupling = 0.5
SAMPLE_BLOCK = 8


def shifted(block, axes, sizes, delta):
    route = []
    for i in range(sizes[0]):
        for j in range(sizes[1]):
            si, sj = i - delta[0], j - delta[1]
            if 0 <= si < sizes[0] and 0 <= sj < sizes[1]:
                route.append((si * sizes[1] + sj, i * sizes[1] + j))
    return lax.ppermute(block, axes, route)


def fourier_rows(row_ids, sample_ids, sample_count):
    half_count = sample_count // 2
    harmonic = jnp.where(row_ids <= half_count, row_ids, row_ids - half_count)
    phase_index = harmonic[:, None] * sample_ids[None, :] % sample_count
    angle_value = phase_index.astype(jnp.float32) * (2.0 * math.pi / sample_count)
    dft_table = jnp.where(
        (row_ids <= half_count)[:, None], jnp.cos(angle_value), jnp.sin(angle_value)
    )
    return dft_table * math.sqrt(2.0 / sample_count)


def edges_kernel(a_ref, x31_ref, x0_ref, c127_ref, c0_ref):
    n_s, planes, nx, ny = a_ref.shape
    iy = lax.broadcasted_iota(jnp.int32, (nx, ny), 1)

    def body(s, carry):
        acc127, acc0 = carry
        for p in range(planes):
            t = s * planes + p
            a = a_ref[s, p]
            x31_ref[p, pl.ds(s, 1), :] = a[nx - 1:nx, :]
            x0_ref[p, pl.ds(s, 1), :] = a[0:1, :]
            acc127 = jnp.where(iy == t, pltpu.roll(a, lax.rem(t + 1, ny), 1), acc127)
            acc0 = jnp.where(iy == t, pltpu.roll(a, t, 1), acc0)
        return acc127, acc0

    zero = jnp.zeros((nx, ny), jnp.float32)
    acc127, acc0 = lax.fori_loop(0, n_s, body, (zero, zero))
    c127_ref[...] = acc127
    c0_ref[...] = acc0


def edges(a):
    n_s, planes, nx, ny = a.shape
    vmem = pl.BlockSpec(memory_space=pltpu.VMEM)
    row = jax.ShapeDtypeStruct((planes, n_s, ny), jnp.float32)
    col = jax.ShapeDtypeStruct((nx, ny), jnp.float32)
    return pl.pallas_call(
        edges_kernel,
        in_specs=[vmem],
        out_specs=[vmem] * 4,
        out_shape=[row, row, col, col],
        name="halo_edges",
    )(a)


def residual_kernel(kinds, a_ref, src_ref, xlo_ref, xhi_ref, ylo_ref, yhi_ref, own0_ref, c2_ref, bt_ref,
                    c1_ref, base_ref, sat_ref, reg_ref, reg_xlo_ref, reg_ycol_ref, out_ref):
    blk = pl.program_id(0)
    n_s, planes, nx, ny = a_ref.shape
    ix = lax.broadcasted_iota(jnp.int32, (nx, ny), 0)
    iy = lax.broadcasted_iota(jnp.int32, (nx, ny), 1)
    iy_row = lax.broadcasted_iota(jnp.int32, (1, ny), 1)
    reg = reg_ref[...]
    reg_xlo = reg_xlo_ref[...]
    reg_ycol = reg_ycol_ref[...]

    def lookup(kind, pick):
        out = jnp.broadcast_to(pick(0), kind.shape).astype(jnp.float32)
        for k in range(1, kinds):
            out = jnp.where(kind == k, pick(k), out)
        return out

    sat = lookup(reg, lambda k: sat_ref[k])
    sat_xlo = lookup(reg_xlo, lambda k: sat_ref[k])
    c_lo = ylo_ref[...]
    lo_xp = jnp.where(ix == nx - 1, c2_ref[...], pltpu.roll(c_lo, nx - 1, 0))
    sx_c = lo_xp - c_lo
    sy_c = own0_ref[...] - c_lo
    kind_c = jnp.broadcast_to(reg_ycol, (nx, ny))
    base_c = lookup(kind_c, lambda k: bt_ref[k:k + 1, :])
    sat_c = lookup(kind_c, lambda k: sat_ref[k])
    fy_cols = base_c * (1.0 + sat_c * (sx_c * sx_c + sy_c * sy_c)) * sy_c
    c_hi = yhi_ref[...]

    def body(s, carry):
        s_glob = blk * n_s + s
        base = lookup(reg, lambda k: base_ref[s_glob, k])
        base_xlo = lookup(reg_xlo, lambda k: base_ref[s_glob, k])
        tiles = [a_ref[s, p] for p in range(planes)]
        for p in range(planes):
            t = s_glob * planes + p
            a = tiles[p]
            row_hi = xhi_ref[p, pl.ds(s, 1), :]
            row_lo = xlo_ref[p, pl.ds(s, 1), :]
            c1 = c1_ref[0, t]
            col_hi = pltpu.roll(c_hi, lax.rem(ny - 1 - t + ny, ny), 1)
            a_xp = jnp.where(ix == nx - 1, row_hi, pltpu.roll(a, nx - 1, 0))
            a_yp = jnp.where(iy == ny - 1, col_hi, pltpu.roll(a, ny - 1, 1))
            sx = a_xp - a
            sy = a_yp - a
            rel = base * (1.0 + sat * (sx * sx + sy * sy))
            fx = rel * sx
            fy = rel * sy
            lo_yp = jnp.where(iy_row == ny - 1, c1, pltpu.roll(row_lo, ny - 1, 1))
            sx_l = a[0:1, :] - row_lo
            sy_l = lo_yp - row_lo
            fx_l = base_xlo * (1.0 + sat_xlo * (sx_l * sx_l + sy_l * sy_l)) * sx_l
            fy_c = pltpu.roll(fy_cols, lax.rem(ny - t, ny), 1)
            fx_down = jnp.where(ix == 0, fx_l, pltpu.roll(fx, 1, 0))
            fy_left = jnp.where(iy == 0, fy_c, pltpu.roll(fy, 1, 1))
            curl = fx_down - fx + fy_left - fy
            axial = 2.0 * a
            if p > 0:
                axial = axial - tiles[p - 1]
            if p < planes - 1:
                axial = axial - tiles[p + 1]
            out_ref[p, s] = curl + axial_coupling * axial - src_ref[s, p]
        return carry

    lax.fori_loop(0, n_s, body, 0)


def residual(a, src, xlo, xhi, ylo, yhi, own0, c2, bt, c1, base_rows, saturation, reg, reg_xlo, reg_ycol):
    n_s, planes, nx, ny = a.shape
    kinds = base_rows.shape[1]
    sb = min(SAMPLE_BLOCK, n_s)
    tile = pl.BlockSpec((sb, planes, nx, ny), lambda i: (i, 0, 0, 0))
    edge = pl.BlockSpec((planes, sb, ny), lambda i: (0, i, 0))
    vmem_whole = pl.BlockSpec(memory_space=pltpu.VMEM)
    smem_whole = pl.BlockSpec(memory_space=pltpu.SMEM)
    return pl.pallas_call(
        functools.partial(residual_kernel, kinds),
        grid=(n_s // sb,),
        in_specs=[tile, tile, edge, edge] + [vmem_whole] * 5 + [smem_whole] * 3 + [vmem_whole] * 3,
        out_specs=pl.BlockSpec((planes, sb, nx, ny), lambda i: (0, i, 0, 0)),
        out_shape=jax.ShapeDtypeStruct((planes, n_s, nx, ny), jnp.float32),
        name="residual",
    )(a, src, xlo, xhi, ylo, yhi, own0, c2, bt, c1, base_rows, saturation, reg, reg_xlo, reg_ycol)


def local(potential, source, region, level_index, reluctivity, saturation, inverse, transmit):
    samples_dev, planes, cells_x, cells_y = potential.shape
    n_tm = lax.axis_size("tm")
    n_gx = lax.axis_size("gx")
    n_gy = lax.axis_size("gy")
    me_tm = lax.axis_index("tm")
    me_gx = lax.axis_index("gx")
    sample_count = samples_dev * n_tm
    q_dev = samples_dev
    grid = ("gx", "gy")
    sizes = (n_gx, n_gy)
    rows = planes * samples_dev

    gain_here = transmit[:, 0] * inverse[:, cells_x - 1, 0]
    own_info = jnp.concatenate([inverse[:, cells_x - 1, :], gain_here[:, None]], axis=1)
    infos = [own_info]
    for d in range(1, n_tm):
        infos.append(lax.ppermute(own_info, "tm", [(i, (i - d) % n_tm) for i in range(n_tm)]))
    info_all = jnp.concatenate(infos, axis=0)
    gain_all = info_all[:, cells_x]
    gains_prev = []
    for d in range(n_gx - 1, 0, -1):
        gains_prev.append(lax.ppermute(gain_all, "gx", [(i, i + d) for i in range(n_gx - d)]))

    e_x31, e_x0, e_c127, e_c0 = edges(potential)
    regf = region.astype(jnp.float32)
    pad = jnp.zeros((7, cells_y), jnp.float32)
    msg_xlo = jnp.concatenate([e_x31.reshape(rows, cells_y), regf[cells_x - 1][None], pad], axis=0)
    got_xlo = shifted(msg_xlo, grid, sizes, (1, 0))
    xhi = shifted(e_x0, grid, sizes, (-1, 0))
    ylo = shifted(e_c127, grid, sizes, (0, 1))
    yhi = shifted(e_c0, grid, sizes, (0, -1))
    reg_ycol = shifted(region[:, cells_y - 1:cells_y], grid, sizes, (0, 1))
    c1 = shifted(e_c0[cells_x - 1:cells_x], grid, sizes, (1, -1))
    c2 = shifted(e_c127[0:1], grid, sizes, (-1, 1))

    xlo = got_xlo[:rows].reshape(planes, samples_dev, cells_y)
    reg_xlo = got_xlo[rows:rows + 1].astype(jnp.int32)

    onehot = (level_index[:, None] == lax.iota(jnp.int32, reluctivity.shape[0])[None, :]).astype(jnp.float32)
    base_rows = jnp.sum(onehot[:, :, None] * reluctivity[None], axis=1)
    tile_sample = jnp.minimum(lax.iota(jnp.int32, cells_y) // planes, samples_dev - 1)
    bt = base_rows[tile_sample].T

    resid = residual(potential, source, xlo, xhi, ylo, yhi, e_c0, c2, bt, c1, base_rows, saturation,
                     region, reg_xlo, reg_ycol)

    sample_ids = me_tm * samples_dev + lax.iota(jnp.int32, samples_dev)
    tabs = [
        fourier_rows(((me_tm + d) % n_tm) * q_dev + lax.iota(jnp.int32, q_dev), sample_ids, sample_count)
        for d in range(n_tm)
    ]
    row_last = info_all[:, :cells_x].reshape(n_tm, q_dev, cells_x)
    out_planes = []
    for p in range(planes):
        plane = resid[p]
        parts = [jnp.einsum("qs,sxy->qxy", tabs[d], plane, precision=lax.Precision.HIGHEST) for d in range(n_tm)]
        got_parts = [
            lax.ppermute(parts[d], "tm", [(i, (i + d) % n_tm) for i in range(n_tm)]) for d in range(1, n_tm)
        ]
        tails = jnp.concatenate(
            [jnp.einsum("qb,qby->qy", row_last[d], parts[d], precision=lax.Precision.HIGHEST) for d in range(n_tm)],
            axis=0,
        )
        carried = jnp.zeros_like(tails)
        for idx, d in enumerate(range(n_gx - 1, 0, -1)):
            got = lax.ppermute(tails, "gx", [(i, i + d) for i in range(n_gx - d)])
            stepped = got + gains_prev[idx][:, None] * carried
            carried = jnp.where(me_gx >= d, stepped, carried)
        carried = carried.reshape(n_tm, q_dev, cells_y)
        got_carried = [
            lax.ppermute(carried[d], "tm", [(i, (i + d) % n_tm) for i in range(n_tm)]) for d in range(1, n_tm)
        ]
        spectrum = parts[0]
        for got in got_parts:
            spectrum = spectrum + got
        carried_own = carried[0]
        for got in got_carried:
            carried_own = carried_own + got
        solved = jnp.einsum("qab,qby->qay", inverse, spectrum, precision=lax.Precision.HIGHEST)
        injected = transmit[:, 0][:, None] * carried_own
        out_planes.append(solved + injected[:, None, :] * inverse[:, :, 0][:, :, None])
    return jnp.stack(out_planes, axis=1)


def solution(mesh):
    in_specs = (
        P("tm", None, "gx", "gy"),
        P("tm", None, "gx", "gy"),
        P("gx", "gy"),
        P("tm"),
        P(),
        P(),
        P("tm", "gx", None),
        P("tm", "gx"),
    )
    out_specs = P("tm", None, "gx", "gy")
    return jax.shard_map(local, mesh=mesh, in_specs=in_specs, out_specs=out_specs, check_vma=False)
```

time: 114 us -> 144 us (1.26)
  the two profiles are of different devices: /device:TPU:12 before, /device:TPU:0 now
where the time goes in v4:
time: 144 us; the launch traced here: 143 us
  starting transfers between devices  52.7 us (37%)
  waiting for transfers between devices  37.3 us (26%)
  matrix products  18.3 us (13%)
  Pallas kernels  14 us (10%)
  local copies, waits for them, and re-layouts  10.8 us (8%)
  other arithmetic  9.02 us (6%)
    ppermute x4, waiting for transfers between devices, local(): lax.ppermute(carried[d], 'tm', [(i, (i + d) % n_tm) for i in range(n_tm)])  32.9 us
    ppermute x12, starting transfers between devices, local(): got = lax.ppermute(tails, 'gx', [(i, i + d) for i in range(n_gx - d)])  15.9 us
    ppermute x3, starting transfers between devices, local(): lax.ppermute(gain_all, 'gx', [(i, i + d) for i in range(n_gx - d)])  14.4 us
    ppermute x7, starting transfers between devices, shifted(): return lax.ppermute(block, axes, route)  12.1 us
    pallas_call x1, Pallas kernels, residual(): pl.pallas_call(functools.partial(residual_kernel, kinds), grid=(n_s // sb...  8.54 us
    dot_general x8, matrix products, local(): jnp.einsum('qs,sxy->qxy', tabs[d], plane, precision=lax.Precision.HIGHEST)  7.95 us
    dot_general x8, matrix products, local(): jnp.einsum('qb,qby->qy', row_last[d], parts[d], precision=lax.Precision.H...  6.62 us
    pallas_call x1, Pallas kernels, edges(): pl.pallas_call(edges_kernel, in_specs=[vmem], out_specs=[vmem] * 4, out_s...  5.48 us
  transfers between devices with their start and end apart: 31, of which 3 were waited for; matrix products, arithmetic and copies ran while one was open for 22% of the time, Pallas kernels for 10%

profile of v4, /device:TPU:0, one launch (start us, length us, event | category | flops | bytes accessed | tf_op | source)
XLA Modules:
  0.0 142.9 jit_solution(1592026783593101368)
XLA Ops:
  0.0 1.3 slice_reduce_fusion
  3.0 2.9 %collective-permute-start.8 = (f32[32,33]{1,0:T(8,128)S(1)}, f32[32,33]{1,0:T(8,128)S(1)}, u32[]{:S(2)}, u32[]{:S(2)}) collective-permute-start(f32[32,33]{1,0:T(8,128)S(1)} %pad_maximum_fusion.7), channel_id=1, source_target_pairs={{0,16},{16,0},{1,17},{17,1},{2,18},{18,2},{3,19},{19,3},{4,20},{20... | collective-permute-start | bytes 12680 | tf_op jit(solution)/shard_map/ppermute | solution.py:173
  6.7 3.5 %collective-permute-start.6 = (s32[32,1]{1,0:T(8,128)S(1)}, s32[32,1]{1,0:T(8,128)S(1)}, u32[]{:S(2)}, u32[]{:S(2)}) collective-permute-start(s32[32,1]{1,0:T(8,128)S(1)} %slice.99), channel_id=1, source_target_pairs={{0,1},{1,2},{2,3},{4,5},{5,6},{6,7},{8,9},{9,10},{10,11},{12,13},{... | collective-permute-start | bytes 392 | tf_op jit(solution)/shard_map/ppermute | solution.py:22
  10.2 5.5 %halo_edges.1 = (f32[4,32,128]{2,1,0:T(8,128)}, f32[4,32,128]{2,1,0:T(8,128)}, f32[32,128]{1,0:T(8,128)}, f32[32,128]{1,0:T(8,128)}) custom-call(f32[32,4,32,128]{3,2,1,0:T(8,128)} %a_ref.3), custom_call_target="tpu_custom_call" | custom-call | tf_op jit(solution)/shard_map/halo_edges/pallas_call | solution.py:62
  15.7 3.5 %collective-permute-start.2 = (f32[32,128]{1,0:T(8,128)}, f32[32,128]{1,0:T(8,128)S(1)}, u32[]{:S(2)}, u32[]{:S(2)}) collective-permute-start(f32[32,128]{1,0:T(8,128)} %get-tuple-element.11), channel_id=1, source_target_pairs={{0,1},{1,2},{2,3},{4,5},{5,6},{6,7},{8,9},{9,10},{10,11},{12,13},{... | collective-permute-start | bytes 49160 | tf_op jit(solution)/shard_map/ppermute | solution.py:22
  19.2 1.3 collective-permute-start.3
  22.2 1.3 collective-permute-start
  28.0 1.3 collective-permute-start.1
  30.5 11.1 %collective-permute-start.14 = (f32[64]{0:T(128)S(1)}, f32[64]{0:T(128)S(1)}, u32[]{:S(2)}, u32[]{:S(2)}) collective-permute-start(f32[64]{0:T(128)S(1)} %fusion.44), channel_id=1, source_target_pairs={{0,12},{1,13},{2,14},{3,15},{16,28},{17,29},{18,30},{19,31}} | collective-permute-start | bytes 776 | tf_op jit(solution)/shard_map/ppermute | solution.py:178
  41.6 1.3 collective-permute-start.12
  42.9 2.0 %collective-permute-start.10 = (f32[64]{0:T(128)S(1)}, f32[64]{0:T(128)S(1)}, u32[]{:S(2)}, u32[]{:S(2)}) collective-permute-start(f32[64]{0:T(128)S(1)} %fusion.44), channel_id=1, source_target_pairs={{0,4},{4,8},{8,12},{1,5},{5,9},{9,13},{2,6},{6,10},{10,14},{3,7},{... | collective-permute-start | bytes 776 | tf_op jit(solution)/shard_map/ppermute | solution.py:178
  45.6 8.5 %residual.1 = f32[4,32,32,128]{3,2,1,0:T(8,128)} custom-call(f32[32,4,32,128]{3,2,1,0:T(8,128)} %a_ref.3, f32[32,4,32,128]{3,2,1,0:T(8,128)} %src_ref.1, f32[4,32,128]{2,1,0:T(8,128)} %bitcast.117, f32[4,32,128]{2,1,0:T(8,128)} %copy-done.5, f32[32,128]{1,0:T(8,128)} %copy-done.9, f32[32,128]{1,0:T(8,128)} %copy-done.10, ...), custom_call_target="tpu_custom_call" | custom-call | tf_op jit(solution)/shard_map/residual/pallas_call | solution.py:146
  54.1 1.8 %slice_bitcast_fusion.3 = (f32[32,32,128]{2,1,0:T(8,128)S(1)}, f32[32,32,128]{2,1,0:T(8,128)S(1)}, f32[32,32,128]{2,1,0:T(8,128)S(1)}, f32[32,32,128]{2,1,0:T(8,128)S(1)}) fusion(f32[4,32,32,128]{3,2,1,0:T(8,128)} %residual.1), kind=kLoop, calls=%fused_computation.17 | loop fusion | bytes 4194304 | tf_op jit(solution)/shard_map/squeeze | solution.py:211
  59.6 1.3 collective-permute-start.13
  60.9 1.5 %collective-permute-start.11 = (f32[64,128]{1,0:T(8,128)S(1)}, f32[64,128]{1,0:T(8,128)S(1)}, u32[]{:S(2)}, u32[]{:S(2)}) collective-permute-start(f32[64,128]{1,0:T(8,128)S(1)} %pad_maximum_fusion.3), channel_id=1, source_target_pairs={{0,8},{4,12},{1,9},{5,13},{2,10},{6,14},{3,11},{7,15},{16,24},{20,... | collective-permute-start | bytes 98312 | tf_op jit(solution)/shard_map/ppermute | solution.py:222
  74.1 1.3 collective-permute-start.9
  75.4 1.3 collective-permute-start.29
  76.8 1.3 collective-permute-start.28
  78.1 1.3 collective-permute-start.27
  79.4 1.3 collective-permute-start.24
  80.7 1.3 collective-permute-start.23
  82.0 1.3 collective-permute-start.22
  83.3 1.3 collective-permute-start.19
  84.7 1.3 collective-permute-start.18
  86.0 1.5 %collective-permute-start.17 = (f32[64,128]{1,0:T(8,128)S(1)}, f32[64,128]{1,0:T(8,128)S(1)}, u32[]{:S(2)}, u32[]{:S(2)}) collective-permute-start(f32[64,128]{1,0:T(8,128)S(1)} %pad_maximum_fusion.4), channel_id=1, source_target_pairs={{0,4},{4,8},{8,12},{1,5},{5,9},{9,13},{2,6},{6,10},{10,14},{3,7},{... | collective-permute-start | bytes 98312 | tf_op jit(solution)/shard_map/ppermute | solution.py:222
  88.1 1.5 %collective-permute-start.21 = (f32[32,32,128]{2,0,1:T(8,128)}, f32[32,32,128]{2,0,1:T(8,128)}, u32[]{:S(2)}, u32[]{:S(2)}) collective-permute-start(f32[32,32,128]{2,0,1:T(8,128)} %copy-done.3), channel_id=1, source_target_pairs={{0,16},{16,0},{1,17},{17,1},{2,18},{18,2},{3,19},{19,3},{4,20},{20... | collective-permute-start | bytes 1572872 | tf_op jit(solution)/shard_map/ppermute | solution.py:214
  91.1 1.5 %collective-permute-start.30 = (f32[32,128]{1,0:T(8,128)S(1)}, f32[32,128]{1,0:T(8,128)S(1)}, u32[]{:S(2)}, u32[]{:S(2)}) collective-permute-start(f32[32,128]{1,0:T(8,128)S(1)} %slice.134), channel_id=1, source_target_pairs={{0,16},{16,0},{1,17},{17,1},{2,18},{18,2},{3,19},{19,3},{4,20},{20... | collective-permute-start | bytes 49160 | tf_op jit(solution)/shard_map/ppermute | solution.py:227
  93.2 31.4 %collective-permute-done.30 = f32[32,128]{1,0:T(8,128)S(1)} collective-permute-done((f32[32,128]{1,0:T(8,128)S(1)}, f32[32,128]{1,0:T(8,128)S(1)}, u32[]{:S(2)}, u32[]{:S(2)}) %collective-permute-start.30) | collective-permute-done | bytes 16416 | tf_op jit(solution)/shard_map/ppermute | solution.py:227
  125.2 1.5 %collective-permute-start.15 = (f32[32,128]{1,0:T(8,128)S(1)}, f32[32,128]{1,0:T(8,128)S(1)}, u32[]{:S(2)}, u32[]{:S(2)}) collective-permute-start(f32[32,128]{1,0:T(8,128)S(1)} %slice.125), channel_id=1, source_target_pairs={{0,16},{16,0},{1,17},{17,1},{2,18},{18,2},{3,19},{19,3},{4,20},{20... | collective-permute-start | bytes 49160 | tf_op jit(solution)/shard_map/ppermute | solution.py:227
  126.9 1.5 %collective-permute-done.20 = f32[32,128]{1,0:T(8,128)S(1)} collective-permute-done((f32[32,128]{1,0:T(8,128)S(1)}, f32[32,128]{1,0:T(8,128)S(1)}, u32[]{:S(2)}, u32[]{:S(2)}) %collective-permute-start.20) | collective-permute-done | bytes 16416 | tf_op jit(solution)/shard_map/ppermute | solution.py:227
  135.8 4.3 %collective-permute-done.7 = f32[32,32,128]{2,0,1:T(8,128)S(1)} collective-permute-done((f32[32,32,128]{2,0,1:T(8,128)S(1)}, f32[32,32,128]{2,0,1:T(8,128)S(1)}, u32[]{:S(2)}, u32[]{:S(2)}) %collective-permute-start.7) | collective-permute-done | bytes 524320 | tf_op jit(solution)/shard_map/ppermute | solution.py:214
  141.3 1.5 %copy.60 = f32[32,4,32,128]{3,2,1,0:T(8,128)} copy(f32[32,4,32,128]{3,2,0,1:T(8,128)S(1)} %pad_maximum_fusion) | data formatting | bytes 4194304 | tf_op jit(solution)/shard_map/stack | solution.py:238
  (132 shorter events, 37.7 us)
Async XLA Ops:
  0.0 23.6 %copy-start.11 = (f32[16,8]{0,1:T(8,128)S(1)}, f32[16,8]{0,1:T(8,128)}, u32[]{:S(2)}) copy-start(f32[16,8]{0,1:T(8,128)} %param.12) | copy-start | bytes 1540
  3.0 23.5 %collective-permute-start.8 = (f32[32,33]{1,0:T(8,128)S(1)}, f32[32,33]{1,0:T(8,128)S(1)}, u32[]{:S(2)}, u32[]{:S(2)}) collective-permute-start(f32[32,33]{1,0:T(8,128)S(1)} %pad_maximum_fusion.7), channel_id=1, source_target_pairs={{0,16},{16,0},{1,17},{17,1},{2,18},{18,2},{3,19},{19,3},{4,20},{20... | collective-permute-start | bytes 12680 | tf_op jit(solution)/shard_map/ppermute | solution.py:173
  6.7 20.6 %collective-permute-start.6 = (s32[32,1]{1,0:T(8,128)S(1)}, s32[32,1]{1,0:T(8,128)S(1)}, u32[]{:S(2)}, u32[]{:S(2)}) collective-permute-start(s32[32,1]{1,0:T(8,128)S(1)} %slice.99), channel_id=1, source_target_pairs={{0,1},{1,2},{2,3},{4,5},{5,6},{6,7},{8,9},{9,10},{10,11},{12,13},{... | collective-permute-start | bytes 392 | tf_op jit(solution)/shard_map/ppermute | solution.py:22
  15.7 27.2 %collective-permute-start.2 = (f32[32,128]{1,0:T(8,128)}, f32[32,128]{1,0:T(8,128)S(1)}, u32[]{:S(2)}, u32[]{:S(2)}) collective-permute-start(f32[32,128]{1,0:T(8,128)} %get-tuple-element.11), channel_id=1, source_target_pairs={{0,1},{1,2},{2,3},{4,5},{5,6},{6,7},{8,9},{9,10},{10,11},{12,13},{... | collective-permute-start | bytes 49160 | tf_op jit(solution)/shard_map/ppermute | solution.py:22
  19.2 25.8 %collective-permute-start.3 = (f32[32,128]{1,0:T(8,128)}, f32[32,128]{1,0:T(8,128)S(1)}, u32[]{:S(2)}, u32[]{:S(2)}) collective-permute-start(f32[32,128]{1,0:T(8,128)} %get-tuple-element.12.own0_ref), channel_id=1, source_target_pairs={{1,0},{2,1},{3,2},{5,4},{6,5},{7,6},{9,8},{10,9},{11,10},{13,12},{... | collective-permute-start | bytes 49160 | tf_op jit(solution)/shard_map/ppermute | solution.py:22
  22.2 5.9 %collective-permute-start = (f32[136,128]{1,0:T(8,128)S(1)}, f32[136,128]{1,0:T(8,128)S(1)}, u32[]{:S(2)}, u32[]{:S(2)}) collective-permute-start(f32[136,128]{1,0:T(8,128)S(1)} %maximum_maximum_fusion), channel_id=1, source_target_pairs={{0,4},{1,5},{2,6},{3,7},{4,8},{5,9},{6,10},{7,11},{8,12},{9,13},{1... | collective-permute-start | bytes 208904 | tf_op jit(solution)/shard_map/ppermute | solution.py:22
  26.5 4.0 %collective-permute-start.5 = (f32[1,128]{1,0:T(1,128)S(1)}, f32[1,128]{1,0:T(1,128)S(1)}, u32[]{:S(2)}, u32[]{:S(2)}) collective-permute-start(f32[1,128]{1,0:T(1,128)S(1)} %slice.97), channel_id=1, source_target_pairs={{1,4},{2,5},{3,6},{5,8},{6,9},{7,10},{9,12},{10,13},{11,14},{17,20... | collective-permute-start | bytes 1544 | tf_op jit(solution)/shard_map/ppermute | solution.py:22
  27.4 14.2 %collective-permute-start.4 = (f32[1,128]{1,0:T(1,128)S(1)}, f32[1,128]{1,0:T(1,128)S(1)}, u32[]{:S(2)}, u32[]{:S(2)}) collective-permute-start(f32[1,128]{1,0:T(1,128)S(1)} %slice.96), channel_id=1, source_target_pairs={{4,1},{5,2},{6,3},{8,5},{9,6},{10,7},{12,9},{13,10},{14,11},{20,17... | collective-permute-start | bytes 1544 | tf_op jit(solution)/shard_map/ppermute | solution.py:22
  28.0 16.9 %collective-permute-start.1 = (f32[4,32,128]{2,1,0:T(8,128)}, f32[4,32,128]{2,1,0:T(8,128)S(1)}, u32[]{:S(2)}, u32[]{:S(2)}) collective-permute-start(f32[4,32,128]{2,1,0:T(8,128)} %get-tuple-element.10), channel_id=1, source_target_pairs={{4,0},{5,1},{6,2},{7,3},{8,4},{9,5},{10,6},{11,7},{12,8},{13,9},{1... | collective-permute-start | bytes 196616 | tf_op jit(solution)/shard_map/ppermute | solution.py:22
  30.5 43.6 %collective-permute-start.14 = (f32[64]{0:T(128)S(1)}, f32[64]{0:T(128)S(1)}, u32[]{:S(2)}, u32[]{:S(2)}) collective-permute-start(f32[64]{0:T(128)S(1)} %fusion.44), channel_id=1, source_target_pairs={{0,12},{1,13},{2,14},{3,15},{16,28},{17,29},{18,30},{19,31}} | collective-permute-start | bytes 776 | tf_op jit(solution)/shard_map/ppermute | solution.py:178
  41.6 33.8 %collective-permute-start.12 = (f32[64]{0:T(128)S(1)}, f32[64]{0:T(128)S(1)}, u32[]{:S(2)}, u32[]{:S(2)}) collective-permute-start(f32[64]{0:T(128)S(1)} %fusion.44), channel_id=1, source_target_pairs={{0,8},{4,12},{1,9},{5,13},{2,10},{6,14},{3,11},{7,15},{16,24},{20,... | collective-permute-start | bytes 776 | tf_op jit(solution)/shard_map/ppermute | solution.py:178
  42.9 33.8 %collective-permute-start.10 = (f32[64]{0:T(128)S(1)}, f32[64]{0:T(128)S(1)}, u32[]{:S(2)}, u32[]{:S(2)}) collective-permute-start(f32[64]{0:T(128)S(1)} %fusion.44), channel_id=1, source_target_pairs={{0,4},{4,8},{8,12},{1,5},{5,9},{9,13},{2,6},{6,10},{10,14},{3,7},{... | collective-permute-start | bytes 776 | tf_op jit(solution)/shard_map/ppermute | solution.py:178
  59.6 18.5 %collective-permute-start.13 = (f32[64,128]{1,0:T(8,128)S(1)}, f32[64,128]{1,0:T(8,128)S(1)}, u32[]{:S(2)}, u32[]{:S(2)}) collective-permute-start(f32[64,128]{1,0:T(8,128)S(1)} %pad_maximum_fusion.3), channel_id=1, source_target_pairs={{0,12},{1,13},{2,14},{3,15},{16,28},{17,29},{18,30},{19,31}} | collective-permute-start | bytes 98312 | tf_op jit(solution)/shard_map/ppermute | solution.py:222
  60.9 18.5 %collective-permute-start.11 = (f32[64,128]{1,0:T(8,128)S(1)}, f32[64,128]{1,0:T(8,128)S(1)}, u32[]{:S(2)}, u32[]{:S(2)}) collective-permute-start(f32[64,128]{1,0:T(8,128)S(1)} %pad_maximum_fusion.3), channel_id=1, source_target_pairs={{0,8},{4,12},{1,9},{5,13},{2,10},{6,14},{3,11},{7,15},{16,24},{20,... | collective-permute-start | bytes 98312 | tf_op jit(solution)/shard_map/ppermute | solution.py:222
  74.1 6.6 %collective-permute-start.9 = (f32[64,128]{1,0:T(8,128)S(1)}, f32[64,128]{1,0:T(8,128)S(1)}, u32[]{:S(2)}, u32[]{:S(2)}) collective-permute-start(f32[64,128]{1,0:T(8,128)S(1)} %pad_maximum_fusion.3), channel_id=1, source_target_pairs={{0,4},{4,8},{8,12},{1,5},{5,9},{9,13},{2,6},{6,10},{10,14},{3,7},{... | collective-permute-start | bytes 98312 | tf_op jit(solution)/shard_map/ppermute | solution.py:222
  75.4 6.6 %collective-permute-start.29 = (f32[64,128]{1,0:T(8,128)}, f32[64,128]{1,0:T(8,128)S(1)}, u32[]{:S(2)}, u32[]{:S(2)}) collective-permute-start(f32[64,128]{1,0:T(8,128)} %pad_maximum_fusion.6), channel_id=1, source_target_pairs={{0,12},{1,13},{2,14},{3,15},{16,28},{17,29},{18,30},{19,31}} | collective-permute-start | bytes 98312 | tf_op jit(solution)/shard_map/ppermute | solution.py:222
  76.8 6.6 %collective-permute-start.28 = (f32[64,128]{1,0:T(8,128)}, f32[64,128]{1,0:T(8,128)S(1)}, u32[]{:S(2)}, u32[]{:S(2)}) collective-permute-start(f32[64,128]{1,0:T(8,128)} %pad_maximum_fusion.6), channel_id=1, source_target_pairs={{0,8},{4,12},{1,9},{5,13},{2,10},{6,14},{3,11},{7,15},{16,24},{20,... | collective-permute-start | bytes 98312 | tf_op jit(solution)/shard_map/ppermute | solution.py:222
  78.1 6.6 %collective-permute-start.27 = (f32[64,128]{1,0:T(8,128)}, f32[64,128]{1,0:T(8,128)S(1)}, u32[]{:S(2)}, u32[]{:S(2)}) collective-permute-start(f32[64,128]{1,0:T(8,128)} %pad_maximum_fusion.6), channel_id=1, source_target_pairs={{0,4},{4,8},{8,12},{1,5},{5,9},{9,13},{2,6},{6,10},{10,14},{3,7},{... | collective-permute-start | bytes 98312 | tf_op jit(solution)/shard_map/ppermute | solution.py:222
  79.4 6.6 %collective-permute-start.24 = (f32[64,128]{1,0:T(8,128)S(1)}, f32[64,128]{1,0:T(8,128)S(1)}, u32[]{:S(2)}, u32[]{:S(2)}) collective-permute-start(f32[64,128]{1,0:T(8,128)S(1)} %pad_maximum_fusion.5), channel_id=1, source_target_pairs={{0,12},{1,13},{2,14},{3,15},{16,28},{17,29},{18,30},{19,31}} | collective-permute-start | bytes 98312 | tf_op jit(solution)/shard_map/ppermute | solution.py:222
  80.7 6.8 %collective-permute-start.23 = (f32[64,128]{1,0:T(8,128)S(1)}, f32[64,128]{1,0:T(8,128)S(1)}, u32[]{:S(2)}, u32[]{:S(2)}) collective-permute-start(f32[64,128]{1,0:T(8,128)S(1)} %pad_maximum_fusion.5), channel_id=1, source_target_pairs={{0,8},{4,12},{1,9},{5,13},{2,10},{6,14},{3,11},{7,15},{16,24},{20,... | collective-permute-start | bytes 98312 | tf_op jit(solution)/shard_map/ppermute | solution.py:222
  82.0 6.1 %collective-permute-start.22 = (f32[64,128]{1,0:T(8,128)S(1)}, f32[64,128]{1,0:T(8,128)S(1)}, u32[]{:S(2)}, u32[]{:S(2)}) collective-permute-start(f32[64,128]{1,0:T(8,128)S(1)} %pad_maximum_fusion.5), channel_id=1, source_target_pairs={{0,4},{4,8},{8,12},{1,5},{5,9},{9,13},{2,6},{6,10},{10,14},{3,7},{... | collective-permute-start | bytes 98312 | tf_op jit(solution)/shard_map/ppermute | solution.py:222
  83.3 6.3 %collective-permute-start.19 = (f32[64,128]{1,0:T(8,128)S(1)}, f32[64,128]{1,0:T(8,128)S(1)}, u32[]{:S(2)}, u32[]{:S(2)}) collective-permute-start(f32[64,128]{1,0:T(8,128)S(1)} %pad_maximum_fusion.4), channel_id=1, source_target_pairs={{0,12},{1,13},{2,14},{3,15},{16,28},{17,29},{18,30},{19,31}} | collective-permute-start | bytes 98312 | tf_op jit(solution)/shard_map/ppermute | solution.py:222
  84.7 5.5 %collective-permute-start.18 = (f32[64,128]{1,0:T(8,128)S(1)}, f32[64,128]{1,0:T(8,128)S(1)}, u32[]{:S(2)}, u32[]{:S(2)}) collective-permute-start(f32[64,128]{1,0:T(8,128)S(1)} %pad_maximum_fusion.4), channel_id=1, source_target_pairs={{0,8},{4,12},{1,9},{5,13},{2,10},{6,14},{3,11},{7,15},{16,24},{20,... | collective-permute-start | bytes 98312 | tf_op jit(solution)/shard_map/ppermute | solution.py:222
  86.0 4.2 %collective-permute-start.17 = (f32[64,128]{1,0:T(8,128)S(1)}, f32[64,128]{1,0:T(8,128)S(1)}, u32[]{:S(2)}, u32[]{:S(2)}) collective-permute-start(f32[64,128]{1,0:T(8,128)S(1)} %pad_maximum_fusion.4), channel_id=1, source_target_pairs={{0,4},{4,8},{8,12},{1,5},{5,9},{9,13},{2,6},{6,10},{10,14},{3,7},{... | collective-permute-start | bytes 98312 | tf_op jit(solution)/shard_map/ppermute | solution.py:222
  87.5 42.1 %collective-permute-start.16 = (f32[32,32,128]{2,0,1:T(8,128)}, f32[32,32,128]{2,0,1:T(8,128)}, u32[]{:S(2)}, u32[]{:S(2)}) collective-permute-start(f32[32,32,128]{2,0,1:T(8,128)} %copy-done.4), channel_id=1, source_target_pairs={{0,16},{16,0},{1,17},{17,1},{2,18},{18,2},{3,19},{19,3},{4,20},{20... | collective-permute-start | bytes 1572872 | tf_op jit(solution)/shard_map/ppermute | solution.py:214
  88.1 42.6 %collective-permute-start.21 = (f32[32,32,128]{2,0,1:T(8,128)}, f32[32,32,128]{2,0,1:T(8,128)}, u32[]{:S(2)}, u32[]{:S(2)}) collective-permute-start(f32[32,32,128]{2,0,1:T(8,128)} %copy-done.3), channel_id=1, source_target_pairs={{0,16},{16,0},{1,17},{17,1},{2,18},{18,2},{3,19},{19,3},{4,20},{20... | collective-permute-start | bytes 1572872 | tf_op jit(solution)/shard_map/ppermute | solution.py:214
  89.6 42.3 %collective-permute-start.26 = (f32[32,32,128]{2,0,1:T(8,128)}, f32[32,32,128]{2,0,1:T(8,128)}, u32[]{:S(2)}, u32[]{:S(2)}) collective-permute-start(f32[32,32,128]{2,0,1:T(8,128)} %copy-done.2), channel_id=1, source_target_pairs={{0,16},{16,0},{1,17},{17,1},{2,18},{18,2},{3,19},{19,3},{4,20},{20... | collective-permute-start | bytes 1572872 | tf_op jit(solution)/shard_map/ppermute | solution.py:214
  91.1 33.5 %collective-permute-start.30 = (f32[32,128]{1,0:T(8,128)S(1)}, f32[32,128]{1,0:T(8,128)S(1)}, u32[]{:S(2)}, u32[]{:S(2)}) collective-permute-start(f32[32,128]{1,0:T(8,128)S(1)} %slice.134), channel_id=1, source_target_pairs={{0,16},{16,0},{1,17},{17,1},{2,18},{18,2},{3,19},{19,3},{4,20},{20... | collective-permute-start | bytes 49160 | tf_op jit(solution)/shard_map/ppermute | solution.py:227
  92.6 32.5 %collective-permute-start.25 = (f32[32,128]{1,0:T(8,128)S(1)}, f32[32,128]{1,0:T(8,128)S(1)}, u32[]{:S(2)}, u32[]{:S(2)}) collective-permute-start(f32[32,128]{1,0:T(8,128)S(1)} %slice.131), channel_id=1, source_target_pairs={{0,16},{16,0},{1,17},{17,1},{2,18},{18,2},{3,19},{19,3},{4,20},{20... | collective-permute-start | bytes 49160 | tf_op jit(solution)/shard_map/ppermute | solution.py:227
  124.6 3.7 %collective-permute-start.20 = (f32[32,128]{1,0:T(8,128)S(1)}, f32[32,128]{1,0:T(8,128)S(1)}, u32[]{:S(2)}, u32[]{:S(2)}) collective-permute-start(f32[32,128]{1,0:T(8,128)S(1)} %slice.128), channel_id=1, source_target_pairs={{0,16},{16,0},{1,17},{17,1},{2,18},{18,2},{3,19},{19,3},{4,20},{20... | collective-permute-start | bytes 49160 | tf_op jit(solution)/shard_map/ppermute | solution.py:227
  125.2 3.7 %collective-permute-start.15 = (f32[32,128]{1,0:T(8,128)S(1)}, f32[32,128]{1,0:T(8,128)S(1)}, u32[]{:S(2)}, u32[]{:S(2)}) collective-permute-start(f32[32,128]{1,0:T(8,128)S(1)} %slice.125), channel_id=1, source_target_pairs={{0,16},{16,0},{1,17},{17,1},{2,18},{18,2},{3,19},{19,3},{4,20},{20... | collective-permute-start | bytes 49160 | tf_op jit(solution)/shard_map/ppermute | solution.py:227
  128.4 11.8 %collective-permute-start.7 = (f32[32,32,128]{2,0,1:T(8,128)S(1)}, f32[32,32,128]{2,0,1:T(8,128)S(1)}, u32[]{:S(2)}, u32[]{:S(2)}) collective-permute-start(f32[32,32,128]{2,0,1:T(8,128)S(1)} %fusion.40), channel_id=1, source_target_pairs={{0,16},{16,0},{1,17},{17,1},{2,18},{18,2},{3,19},{19,3},{4,20},{20... | collective-permute-start | bytes 1572872 | tf_op jit(solution)/shard_map/ppermute | solution.py:214
  (16 other events, 106.5 us)

commit v5 on v4

--- a/solution.py
+++ b/solution.py
@@ -173,9 +173,6 @@
         infos.append(lax.ppermute(own_info, "tm", [(i, (i - d) % n_tm) for i in range(n_tm)]))
     info_all = jnp.concatenate(infos, axis=0)
     gain_all = info_all[:, cells_x]
-    gains_prev = []
-    for d in range(n_gx - 1, 0, -1):
-        gains_prev.append(lax.ppermute(gain_all, "gx", [(i, i + d) for i in range(n_gx - d)]))
 
     e_x31, e_x0, e_c127, e_c0 = edges(potential)
     regf = region.astype(jnp.float32)
@@ -206,36 +203,33 @@
         for d in range(n_tm)
     ]
     row_last = info_all[:, :cells_x].reshape(n_tm, q_dev, cells_x)
-    out_planes = []
-    for p in range(planes):
-        plane = resid[p]
-        parts = [jnp.einsum("qs,sxy->qxy", tabs[d], plane, precision=lax.Precision.HIGHEST) for d in range(n_tm)]
-        got_parts = [
-            lax.ppermute(parts[d], "tm", [(i, (i + d) % n_tm) for i in range(n_tm)]) for d in range(1, n_tm)
-        ]
-        tails = jnp.concatenate(
-            [jnp.einsum("qb,qby->qy", row_last[d], parts[d], precision=lax.Precision.HIGHEST) for d in range(n_tm)],
-            axis=0,
-        )
-        carried = jnp.zeros_like(tails)
-        for idx, d in enumerate(range(n_gx - 1, 0, -1)):
-            got = lax.ppermute(tails, "gx", [(i, i + d) for i in range(n_gx - d)])
-            stepped = got + gains_prev[idx][:, None] * carried
-            carried = jnp.where(me_gx >= d, stepped, carried)
-        carried = carried.reshape(n_tm, q_dev, cells_y)
-        got_carried = [
-            lax.ppermute(carried[d], "tm", [(i, (i + d) % n_tm) for i in range(n_tm)]) for d in range(1, n_tm)
-        ]
-        spectrum = parts[0]
-        for got in got_parts:
-            spectrum = spectrum + got
-        carried_own = carried[0]
-        for got in got_carried:
-            carried_own = carried_own + got
-        solved = jnp.einsum("qab,qby->qay", inverse, spectrum, precision=lax.Precision.HIGHEST)
-        injected = transmit[:, 0][:, None] * carried_own
-        out_planes.append(solved + injected[:, None, :] * inverse[:, :, 0][:, :, None])
-    return jnp.stack(out_planes, axis=1)
+    parts = [jnp.einsum("qs,psxy->qpxy", tabs[d], resid, precision=lax.Precision.HIGHEST) for d in range(n_tm)]
+    got_parts = [
+        lax.ppermute(parts[d], "tm", [(i, (i + d) % n_tm) for i in range(n_tm)]) for d in range(1, n_tm)
+    ]
+    tails = jnp.concatenate(
+        [jnp.einsum("qb,qpby->qpy", row_last[d], parts[d], precision=lax.Precision.HIGHEST) for d in range(n_tm)],
+        axis=0,
+    )
+    msg_tail = jnp.concatenate([tails, jnp.broadcast_to(gain_all[:, None, None], (n_tm * q_dev, 1, cells_y))], axis=1)
+    carried = jnp.zeros_like(tails)
+    for d in range(n_gx - 1, 0, -1):
+        got = lax.ppermute(msg_tail, "gx", [(i, i + d) for i in range(n_gx - d)])
+        stepped = got[:, :planes] + got[:, planes:planes + 1] * carried
+        carried = jnp.where(me_gx >= d, stepped, carried)
+    carried = carried.reshape(n_tm, q_dev, planes, cells_y)
+    got_carried = [
+        lax.ppermute(carried[d], "tm", [(i, (i + d) % n_tm) for i in range(n_tm)]) for d in range(1, n_tm)
+    ]
+    spectrum = parts[0]
+    for got in got_parts:
+        spectrum = spectrum + got
+    carried_own = carried[0]
+    for got in got_carried:
+        carried_own = carried_own + got
+    solved = jnp.einsum("qab,qpby->qpay", inverse, spectrum, precision=lax.Precision.HIGHEST)
+    injected = transmit[:, 0][:, None, None] * carried_own
+    return solved + injected[:, :, None, :] * inverse[:, :, 0][:, None, :, None]
 
 
 def solution(mesh):

time: 144 us -> 107 us (0.74)
  the two profiles are of different devices: /device:TPU:0 before, /device:TPU:12 now
where the time goes in v5:
time: 107 us; the launch traced here: 105 us
  waiting for transfers between devices  28.8 us (27%)
  starting transfers between devices  27.8 us (26%)
  matrix products  21.7 us (20%)
  Pallas kernels  14 us (13%)
  other arithmetic  6.82 us (6%)
  local copies, waits for them, and re-layouts  5.89 us (6%)
    ppermute x7, starting transfers between devices, shifted(): return lax.ppermute(block, axes, route)  20 us
    ppermute x1, waiting for transfers between devices, local(): lax.ppermute(carried[d], 'tm', [(i, (i + d) % n_tm) for i in range(n_tm)])  19.9 us
    dot_general x2, matrix products, local(): jnp.einsum('qs,psxy->qpxy', tabs[d], resid, precision=lax.Precision.HIGHEST)  9.11 us
    ppermute x3, waiting for transfers between devices, local(): got = lax.ppermute(msg_tail, 'gx', [(i, i + d) for i in range(n_gx - d)])  8.9 us
    pallas_call x1, Pallas kernels, residual(): pl.pallas_call(functools.partial(residual_kernel, kinds), grid=(n_s // sb...  8.57 us
    dot_general x2, matrix products, local(): jnp.einsum('qb,qpby->qpy', row_last[d], parts[d], precision=lax.Precision...  7.55 us
    pallas_call x1, Pallas kernels, edges(): pl.pallas_call(edges_kernel, in_specs=[vmem], out_specs=[vmem] * 4, out_s...  5.48 us
    dot_general x1, matrix products, local(): jnp.einsum('qab,qpby->qpay', inverse, spectrum, precision=lax.Precision.H...  5.02 us
  transfers between devices with their start and end apart: 13, of which 3 were waited for; matrix products, arithmetic and copies ran while one was open for 25% of the time, Pallas kernels for 13%

profile of v5, /device:TPU:12, one launch (start us, length us, event | category | flops | bytes accessed | tf_op | source)
XLA Modules:
  0.0 105.4 jit_solution(4195522554328787845)
XLA Ops:
  0.0 0.8 slice.72
  0.9 3.5 %collective-permute-start.6 = (s32[32,1]{1,0:T(8,128)S(1)}, s32[32,1]{1,0:T(8,128)S(1)}, u32[]{:S(2)}, u32[]{:S(2)}) collective-permute-start(s32[32,1]{1,0:T(8,128)S(1)} %slice.72), channel_id=1, source_target_pairs={{0,1},{1,2},{2,3},{4,5},{5,6},{6,7},{8,9},{9,10},{10,11},{12,13},{... | collective-permute-start | bytes 392 | tf_op jit(solution)/shard_map/ppermute | solution.py:22
  4.3 5.5 %halo_edges.1 = (f32[4,32,128]{2,1,0:T(8,128)}, f32[4,32,128]{2,1,0:T(8,128)}, f32[32,128]{1,0:T(8,128)}, f32[32,128]{1,0:T(8,128)}) custom-call(f32[32,4,32,128]{3,2,1,0:T(8,128)} %a_ref.3), custom_call_target="tpu_custom_call" | custom-call | tf_op jit(solution)/shard_map/halo_edges/pallas_call | solution.py:62
  9.8 2.3 %collective-permute-start.3 = (f32[32,128]{1,0:T(8,128)}, f32[32,128]{1,0:T(8,128)S(1)}, u32[]{:S(2)}, u32[]{:S(2)}) collective-permute-start(f32[32,128]{1,0:T(8,128)} %get-tuple-element.12.own0_ref), channel_id=1, source_target_pairs={{1,0},{2,1},{3,2},{5,4},{6,5},{7,6},{9,8},{10,9},{11,10},{13,12},{... | collective-permute-start | bytes 49160 | tf_op jit(solution)/shard_map/ppermute | solution.py:22
  12.2 0.7 slice.70
  12.9 1.9 %collective-permute-start.5 = (f32[1,128]{1,0:T(1,128)S(1)}, f32[1,128]{1,0:T(1,128)S(1)}, u32[]{:S(2)}, u32[]{:S(2)}) collective-permute-start(f32[1,128]{1,0:T(1,128)S(1)} %slice.70), channel_id=1, source_target_pairs={{1,4},{2,5},{3,6},{5,8},{6,9},{7,10},{9,12},{10,13},{11,14},{17,20... | collective-permute-start | bytes 1544 | tf_op jit(solution)/shard_map/ppermute | solution.py:22
  14.8 3.5 %collective-permute-start.2 = (f32[32,128]{1,0:T(8,128)}, f32[32,128]{1,0:T(8,128)S(1)}, u32[]{:S(2)}, u32[]{:S(2)}) collective-permute-start(f32[32,128]{1,0:T(8,128)} %get-tuple-element.11), channel_id=1, source_target_pairs={{0,1},{1,2},{2,3},{4,5},{5,6},{6,7},{8,9},{9,10},{10,11},{12,13},{... | collective-permute-start | bytes 49160 | tf_op jit(solution)/shard_map/ppermute | solution.py:22
  18.3 0.7 slice_convert_fusion.1
  19.1 0.9 maximum_maximum_fusion
  20.0 1.9 %collective-permute-start = (f32[136,128]{1,0:T(8,128)S(1)}, f32[136,128]{1,0:T(8,128)S(1)}, u32[]{:S(2)}, u32[]{:S(2)}) collective-permute-start(f32[136,128]{1,0:T(8,128)S(1)} %maximum_maximum_fusion), channel_id=1, source_target_pairs={{0,4},{1,5},{2,6},{3,7},{4,8},{5,9},{6,10},{7,11},{8,12},{9,13},{1... | collective-permute-start | bytes 208904 | tf_op jit(solution)/shard_map/ppermute | solution.py:22
  22.3 0.7 slice.69
  24.1 0.7 copy.24
  24.8 4.2 %collective-permute-start.4 = (f32[1,128]{1,0:T(1,128)S(1)}, f32[1,128]{1,0:T(1,128)S(1)}, u32[]{:S(2)}, u32[]{:S(2)}) collective-permute-start(f32[1,128]{1,0:T(1,128)S(1)} %slice.69), channel_id=1, source_target_pairs={{4,1},{5,2},{6,3},{8,5},{9,6},{10,7},{12,9},{13,10},{14,11},{20,17... | collective-permute-start | bytes 1544 | tf_op jit(solution)/shard_map/ppermute | solution.py:22
  29.0 2.6 %collective-permute-start.1 = (f32[4,32,128]{2,1,0:T(8,128)}, f32[4,32,128]{2,1,0:T(8,128)S(1)}, u32[]{:S(2)}, u32[]{:S(2)}) collective-permute-start(f32[4,32,128]{2,1,0:T(8,128)} %get-tuple-element.10), channel_id=1, source_target_pairs={{4,0},{5,1},{6,2},{7,3},{8,4},{9,5},{10,6},{11,7},{12,8},{13,9},{1... | collective-permute-start | bytes 196616 | tf_op jit(solution)/shard_map/ppermute | solution.py:22
  32.8 1.5 %collective-permute-start.8 = (f32[32,33]{1,0:T(8,128)S(1)}, f32[32,33]{1,0:T(8,128)S(1)}, u32[]{:S(2)}, u32[]{:S(2)}) collective-permute-start(f32[32,33]{1,0:T(8,128)S(1)} %pad_maximum_fusion.3), channel_id=1, source_target_pairs={{0,16},{16,0},{1,17},{17,1},{2,18},{18,2},{3,19},{19,3},{4,20},{20... | collective-permute-start | bytes 12680 | tf_op jit(solution)/shard_map/ppermute | solution.py:173
  35.0 8.6 %residual.1 = f32[4,32,32,128]{3,2,1,0:T(8,128)} custom-call(f32[32,4,32,128]{3,2,1,0:T(8,128)} %a_ref.3, f32[32,4,32,128]{3,2,1,0:T(8,128)} %src_ref.1, f32[4,32,128]{2,1,0:T(8,128)} %bitcast.49, f32[4,32,128]{2,1,0:T(8,128)} %copy-done.3, f32[32,128]{1,0:T(8,128)} %copy-done.6, f32[32,128]{1,0:T(8,128)} %copy-done.5, ...), custom_call_target="tpu_custom_call" | custom-call | tf_op jit(solution)/shard_map/residual/pallas_call | solution.py:146
  43.5 6.0 %fusion.6 = f32[32,4,32,128]{3,0,2,1:T(8,128)} fusion(f32[4,32,32,128]{3,2,1,0:T(8,128)} %residual.1, s32[32]{0:T(128)S(1)} %get-tuple-element.13, s32[32]{0:T(128)S(1)} %get-tuple-element.14, pred[32]{0:T(512)(128)(4,1)S(1)} %fusion.64), kind=kOutput, calls=%fused_computation.8 | convolution fusion | flops 201342976 | bytes 4194592 | tf_op jit(solution)/shard_map/qs,psxy->qpxy/dot_general | solution.py:206
  49.5 1.0 collective-permute-start.7
  50.7 4.5 %fusion = f32[32,1,4,128]{3,1,2,0:T(1,128)S(1)} fusion(f32[32,32,1,1]{1,2,3,0:T(1,128)S(1)} %bitcast.57, f32[32,4,32,128]{3,0,2,1:T(8,128)} %fusion.6), kind=kOutput, calls=%fused_computation.2 | convolution fusion | flops 6291456 | bytes 2166784 | tf_op jit(solution)/shard_map/qb,qpby->qpy/dot_general | solution.py:211
  55.2 3.1 %fusion.8 = f32[32,4,32,128]{3,0,2,1:T(8,128)S(1)} fusion(f32[4,32,32,128]{3,2,1,0:T(8,128)S(1)} %copy-done.1, s32[32]{0:T(128)S(1)} %get-tuple-element.14, s32[32]{0:T(128)S(1)} %add_select_fusion.3, pred[32]{0:T(512)(128)(4,1)S(1)} %fusion.65), kind=kOutput, calls=%fused_computation.10 | convolution fusion | flops 201342976 | bytes 4194592 | tf_op jit(solution)/shard_map/qs,psxy->qpxy/dot_general | solution.py:206
  58.3 3.1 %fusion.2 = f32[32,1,4,128]{3,1,2,0:T(1,128)S(1)} fusion(f32[32,4,32,128]{3,0,2,1:T(8,128)S(1)} %fusion.8, f32[32,32,32]{2,1,0:T(8,128)S(1)} %copy-done.2), kind=kOutput, calls=%fused_computation.4 | convolution fusion | flops 6291456 | bytes 2179072 | tf_op jit(solution)/shard_map/qb,qpby->qpy/dot_general | solution.py:211
  61.6 1.3 %collective-permute-start.10 = (f32[64,5,128]{2,1,0:T(8,128)S(1)}, f32[64,5,128]{2,1,0:T(8,128)S(1)}, u32[]{:S(2)}, u32[]{:S(2)}) collective-permute-start(f32[64,5,128]{2,1,0:T(8,128)S(1)} %pad_maximum_fusion), channel_id=1, source_target_pairs={{0,8},{4,12},{1,9},{5,13},{2,10},{6,14},{3,11},{7,15},{16,24},{20,... | collective-permute-start | bytes 491528 | tf_op jit(solution)/shard_map/ppermute | solution.py:217
  62.9 1.9 %collective-permute-start.9 = (f32[64,5,128]{2,1,0:T(8,128)S(1)}, f32[64,5,128]{2,1,0:T(8,128)S(1)}, u32[]{:S(2)}, u32[]{:S(2)}) collective-permute-start(f32[64,5,128]{2,1,0:T(8,128)S(1)} %pad_maximum_fusion), channel_id=1, source_target_pairs={{0,4},{4,8},{8,12},{1,5},{5,9},{9,13},{2,6},{6,10},{10,14},{3,7},{... | collective-permute-start | bytes 491528 | tf_op jit(solution)/shard_map/ppermute | solution.py:217
  64.8 1.4 %collective-permute-start.11 = (f32[64,5,128]{2,1,0:T(8,128)S(1)}, f32[64,5,128]{2,1,0:T(8,128)}, u32[]{:S(2)}, u32[]{:S(2)}) collective-permute-start(f32[64,5,128]{2,1,0:T(8,128)S(1)} %pad_maximum_fusion), channel_id=1, source_target_pairs={{0,12},{1,13},{2,14},{3,15},{16,28},{17,29},{18,30},{19,31}} | collective-permute-start | bytes 491528 | tf_op jit(solution)/shard_map/ppermute | solution.py:217
  66.2 6.5 %collective-permute-done.10 = f32[64,5,128]{2,1,0:T(8,128)S(1)} collective-permute-done((f32[64,5,128]{2,1,0:T(8,128)S(1)}, f32[64,5,128]{2,1,0:T(8,128)S(1)}, u32[]{:S(2)}, u32[]{:S(2)}) %collective-permute-start.10) | collective-permute-done | bytes 163872 | tf_op jit(solution)/shard_map/ppermute | solution.py:217
  72.7 2.4 %collective-permute-done.9 = f32[64,5,128]{2,1,0:T(8,128)S(1)} collective-permute-done((f32[64,5,128]{2,1,0:T(8,128)S(1)}, f32[64,5,128]{2,1,0:T(8,128)S(1)}, u32[]{:S(2)}, u32[]{:S(2)}) %collective-permute-start.9) | collective-permute-done | bytes 163872 | tf_op jit(solution)/shard_map/ppermute | solution.py:217
  75.2 1.0 slice_multiply_fusion
  76.2 1.1 %fusion.17 = f32[64,4,128]{2,1,0:T(4,128)S(1)} fusion(f32[64,5,128]{2,1,0:T(8,128)S(1)} %collective-permute-done.9, f32[64,5,128]{2,1,0:T(8,128)S(1)} %collective-permute-done.10, f32[64,5,128]{2,1,0:T(8,128)} %collective-permute-done.11, f32[64,128]{1,0:T(8,128)S(1)} %bitcast.56, f32[64,128]{1,0:T(8,128)S(1)} %bitcast.54, f32[64,128]{1,0:T(8,128)S(1)} %bitcast.55, ...), kind=kLoop, calls=%fused_computation.19 | loop fusion | flops 262144 | bytes 622595 | tf_op jit(solution)/shard_map/jit(_where)/select_n | solution.py:219
  77.2 0.8 collective-permute-start.12
  78.3 19.9 %collective-permute-done.12 = f32[32,4,128]{2,1,0:T(4,128)S(1)} collective-permute-done((f32[32,4,128]{2,1,0:T(4,128)S(1)}, f32[32,4,128]{2,1,0:T(4,128)S(1)}, u32[]{:S(2)}, u32[]{:S(2)}) %collective-permute-start.12) | collective-permute-done | bytes 65568 | tf_op jit(solution)/shard_map/ppermute | solution.py:222
  98.3 2.1 %add.118 = f32[32,4,32,128]{3,0,2,1:T(8,128)S(1)} add(f32[32,4,32,128]{3,0,2,1:T(8,128)S(1)} %fusion.8, f32[32,4,32,128]{3,0,2,1:T(8,128)} %collective-permute-done.7) | non-fusion elementwise | flops 524288 | bytes 6291456 | tf_op jit(solution)/shard_map/add | solution.py:226
  100.4 5.0 %bitcast_add_fusion = f32[32,4,32,128]{3,2,1,0:T(8,128)} fusion(f32[32,32]{1,0:T(8,128)S(1)} %bitcast.58, f32[32,4,128]{2,1,0:T(4,128)S(1)} %fusion.18, f32[32,32,32]{2,1,0:T(8,128)S(1)} %copy-done.2, f32[32,4,32,128]{3,0,2,1:T(8,128)S(1)} %add.118), kind=kOutput, calls=%fused_computation.1 | convolution fusion | flops 202375168 | bytes 4395008 | tf_op jit(solution)/shard_map/qab,qpby->qpay/dot_general | solution.py:230
  (62 shorter events, 4.1 us)
Async XLA Ops:
  0.0 21.9 %copy-start.2 = (f32[32,32,32]{2,1,0:T(8,128)S(1)}, f32[32,32,32]{2,1,0:T(8,128)}, u32[]{:S(2)}) copy-start(f32[32,32,32]{2,1,0:T(8,128)} %param.14) | copy-start | bytes 393220
  0.0 23.0 %copy-start.9 = (s32[32]{0:T(128)S(1)}, s32[32]{0:T(128)}, u32[]{:S(2)}) copy-start(s32[32]{0:T(128)} %param.11) | copy-start | bytes 388
  0.0 23.0 %copy-start.7 = (f32[16,8]{0,1:T(8,128)S(1)}, f32[16,8]{0,1:T(8,128)}, u32[]{:S(2)}) copy-start(f32[16,8]{0,1:T(8,128)} %param.12) | copy-start | bytes 1540
  0.0 23.2 %copy-start.8 = (f32[32,1]{0,1:T(1,128)S(1)}, f32[32,1]{0,1:T(1,128)}, u32[]{:S(2)}) copy-start(f32[32,1]{0,1:T(1,128)} %param.15) | copy-start | bytes 388
  0.9 23.9 %collective-permute-start.6 = (s32[32,1]{1,0:T(8,128)S(1)}, s32[32,1]{1,0:T(8,128)S(1)}, u32[]{:S(2)}, u32[]{:S(2)}) collective-permute-start(s32[32,1]{1,0:T(8,128)S(1)} %slice.72), channel_id=1, source_target_pairs={{0,1},{1,2},{2,3},{4,5},{5,6},{6,7},{8,9},{9,10},{10,11},{12,13},{... | collective-permute-start | bytes 392 | tf_op jit(solution)/shard_map/ppermute | solution.py:22
  9.8 24.5 %collective-permute-start.3 = (f32[32,128]{1,0:T(8,128)}, f32[32,128]{1,0:T(8,128)S(1)}, u32[]{:S(2)}, u32[]{:S(2)}) collective-permute-start(f32[32,128]{1,0:T(8,128)} %get-tuple-element.12.own0_ref), channel_id=1, source_target_pairs={{1,0},{2,1},{3,2},{5,4},{6,5},{7,6},{9,8},{10,9},{11,10},{13,12},{... | collective-permute-start | bytes 49160 | tf_op jit(solution)/shard_map/ppermute | solution.py:22
  12.9 19.9 %collective-permute-start.5 = (f32[1,128]{1,0:T(1,128)S(1)}, f32[1,128]{1,0:T(1,128)S(1)}, u32[]{:S(2)}, u32[]{:S(2)}) collective-permute-start(f32[1,128]{1,0:T(1,128)S(1)} %slice.70), channel_id=1, source_target_pairs={{1,4},{2,5},{3,6},{5,8},{6,9},{7,10},{9,12},{10,13},{11,14},{17,20... | collective-permute-start | bytes 1544 | tf_op jit(solution)/shard_map/ppermute | solution.py:22
  14.8 19.5 %collective-permute-start.2 = (f32[32,128]{1,0:T(8,128)}, f32[32,128]{1,0:T(8,128)S(1)}, u32[]{:S(2)}, u32[]{:S(2)}) collective-permute-start(f32[32,128]{1,0:T(8,128)} %get-tuple-element.11), channel_id=1, source_target_pairs={{0,1},{1,2},{2,3},{4,5},{5,6},{6,7},{8,9},{9,10},{10,11},{12,13},{... | collective-permute-start | bytes 49160 | tf_op jit(solution)/shard_map/ppermute | solution.py:22
  20.0 9.0 %collective-permute-start = (f32[136,128]{1,0:T(8,128)S(1)}, f32[136,128]{1,0:T(8,128)S(1)}, u32[]{:S(2)}, u32[]{:S(2)}) collective-permute-start(f32[136,128]{1,0:T(8,128)S(1)} %maximum_maximum_fusion), channel_id=1, source_target_pairs={{0,4},{1,5},{2,6},{3,7},{4,8},{5,9},{6,10},{7,11},{8,12},{9,13},{1... | collective-permute-start | bytes 208904 | tf_op jit(solution)/shard_map/ppermute | solution.py:22
  23.3 11.1 %copy-start = (f32[32,8]{1,0:T(8,128)}, f32[32,8]{1,0:T(8,128)S(1)}, u32[]{:S(2)}) copy-start(f32[32,8]{1,0:T(8,128)S(1)} %copy.23.base_ref) | copy-start | bytes 3076
  24.7 9.6 %copy-start.4 = (s32[32,1]{1,0:T(8,128)}, s32[32,1]{1,0:T(8,128)S(1)}, u32[]{:S(2)}) copy-start(s32[32,1]{1,0:T(8,128)S(1)} %collective-permute-done.6.reg_ycol_ref) | copy-start | bytes 388
  24.8 9.5 %collective-permute-start.4 = (f32[1,128]{1,0:T(1,128)S(1)}, f32[1,128]{1,0:T(1,128)S(1)}, u32[]{:S(2)}, u32[]{:S(2)}) collective-permute-start(f32[1,128]{1,0:T(1,128)S(1)} %slice.69), channel_id=1, source_target_pairs={{4,1},{5,2},{6,3},{8,5},{9,6},{10,7},{12,9},{13,10},{14,11},{20,17... | collective-permute-start | bytes 1544 | tf_op jit(solution)/shard_map/ppermute | solution.py:22
  29.0 5.3 %collective-permute-start.1 = (f32[4,32,128]{2,1,0:T(8,128)}, f32[4,32,128]{2,1,0:T(8,128)S(1)}, u32[]{:S(2)}, u32[]{:S(2)}) collective-permute-start(f32[4,32,128]{2,1,0:T(8,128)} %get-tuple-element.10), channel_id=1, source_target_pairs={{4,0},{5,1},{6,2},{7,3},{8,4},{9,5},{10,6},{11,7},{12,8},{13,9},{1... | collective-permute-start | bytes 196616 | tf_op jit(solution)/shard_map/ppermute | solution.py:22
  32.8 1.6 %copy-start.10 = (f32[1,128]{1,0:T(1,128)}, f32[1,128]{1,0:T(1,128)S(1)}, u32[]{:S(2)}) copy-start(f32[1,128]{1,0:T(1,128)S(1)} %collective-permute-done.5.c1_ref) | copy-start | bytes 1540
  32.8 17.7 %collective-permute-start.8 = (f32[32,33]{1,0:T(8,128)S(1)}, f32[32,33]{1,0:T(8,128)S(1)}, u32[]{:S(2)}, u32[]{:S(2)}) collective-permute-start(f32[32,33]{1,0:T(8,128)S(1)} %pad_maximum_fusion.3), channel_id=1, source_target_pairs={{0,16},{16,0},{1,17},{17,1},{2,18},{18,2},{3,19},{19,3},{4,20},{20... | collective-permute-start | bytes 12680 | tf_op jit(solution)/shard_map/ppermute | solution.py:173
  34.3 0.5 copy-start.11
  34.3 0.6 copy-start.6
  34.3 0.6 copy-start.5
  34.3 0.6 copy-start.3
  49.5 5.6 %copy-start.1 = (f32[4,32,32,128]{3,2,1,0:T(8,128)S(1)}, f32[4,32,32,128]{3,2,1,0:T(8,128)}, u32[]{:S(2)}) copy-start(f32[4,32,32,128]{3,2,1,0:T(8,128)} %residual.1) | copy-start | bytes 6291460
  49.5 48.8 %collective-permute-start.7 = (f32[32,4,32,128]{3,0,2,1:T(8,128)}, f32[32,4,32,128]{3,0,2,1:T(8,128)}, u32[]{:S(2)}, u32[]{:S(2)}) collective-permute-start(f32[32,4,32,128]{3,0,2,1:T(8,128)} %fusion.6), channel_id=1, source_target_pairs={{0,16},{16,0},{1,17},{17,1},{2,18},{18,2},{3,19},{19,3},{4,20},{20... | collective-permute-start | bytes 6291464 | tf_op jit(solution)/shard_map/ppermute | solution.py:208
  61.6 11.1 %collective-permute-start.10 = (f32[64,5,128]{2,1,0:T(8,128)S(1)}, f32[64,5,128]{2,1,0:T(8,128)S(1)}, u32[]{:S(2)}, u32[]{:S(2)}) collective-permute-start(f32[64,5,128]{2,1,0:T(8,128)S(1)} %pad_maximum_fusion), channel_id=1, source_target_pairs={{0,8},{4,12},{1,9},{5,13},{2,10},{6,14},{3,11},{7,15},{16,24},{20,... | collective-permute-start | bytes 491528 | tf_op jit(solution)/shard_map/ppermute | solution.py:217
  62.9 12.2 %collective-permute-start.9 = (f32[64,5,128]{2,1,0:T(8,128)S(1)}, f32[64,5,128]{2,1,0:T(8,128)S(1)}, u32[]{:S(2)}, u32[]{:S(2)}) collective-permute-start(f32[64,5,128]{2,1,0:T(8,128)S(1)} %pad_maximum_fusion), channel_id=1, source_target_pairs={{0,4},{4,8},{8,12},{1,5},{5,9},{9,13},{2,6},{6,10},{10,14},{3,7},{... | collective-permute-start | bytes 491528 | tf_op jit(solution)/shard_map/ppermute | solution.py:217
  64.8 10.4 %collective-permute-start.11 = (f32[64,5,128]{2,1,0:T(8,128)S(1)}, f32[64,5,128]{2,1,0:T(8,128)}, u32[]{:S(2)}, u32[]{:S(2)}) collective-permute-start(f32[64,5,128]{2,1,0:T(8,128)S(1)} %pad_maximum_fusion), channel_id=1, source_target_pairs={{0,12},{1,13},{2,14},{3,15},{16,28},{17,29},{18,30},{19,31}} | collective-permute-start | bytes 491528 | tf_op jit(solution)/shard_map/ppermute | solution.py:217
  77.2 21.0 %collective-permute-start.12 = (f32[32,4,128]{2,1,0:T(4,128)S(1)}, f32[32,4,128]{2,1,0:T(4,128)S(1)}, u32[]{:S(2)}, u32[]{:S(2)}) collective-permute-start(f32[32,4,128]{2,1,0:T(4,128)S(1)} %slice.99), channel_id=1, source_target_pairs={{0,16},{16,0},{1,17},{17,1},{2,18},{18,2},{3,19},{19,3},{4,20},{20... | collective-permute-start | bytes 196616 | tf_op jit(solution)/shard_map/ppermute | solution.py:222

commit v6 on v5

--- a/solution.py
+++ b/solution.py
@@ -33,51 +33,80 @@
     return dft_table * math.sqrt(2.0 / sample_count)
 
 
-def edges_kernel(a_ref, x31_ref, x0_ref, c127_ref, c0_ref):
+def col_to_row(col, ix, iy):
+    full = jnp.broadcast_to(col, ix.shape)
+    return jnp.sum(jnp.where(ix == iy, full, 0.0), axis=0, keepdims=True)
+
+
+def row_to_col(row, ix, iy):
+    full = jnp.broadcast_to(row, ix.shape)
+    return jnp.sum(jnp.where(ix == iy, full, 0.0), axis=1, keepdims=True)
+
+
+def edges_kernel(a_ref, reg_ref, xlo_ref, xhi_ref, c127_ref, c0_ref, c1_ref, c2_ref):
     n_s, planes, nx, ny = a_ref.shape
+    rows = planes * n_s
+    ix = lax.broadcasted_iota(jnp.int32, (nx, ny), 0)
     iy = lax.broadcasted_iota(jnp.int32, (nx, ny), 1)
+    regf = reg_ref[...].astype(jnp.float32)
+    xlo_ref[pl.ds(rows, 8), :] = jnp.zeros((8, ny), jnp.float32)
+    xlo_ref[pl.ds(rows, 1), :] = regf[nx - 1:nx, :]
+    c127_ref[pl.ds(nx, 8), :] = jnp.zeros((8, ny), jnp.float32)
+    c127_ref[pl.ds(nx, 1), :] = col_to_row(regf[:, ny - 1:ny], ix, iy)
 
     def body(s, carry):
         acc127, acc0 = carry
         for p in range(planes):
             t = s * planes + p
             a = a_ref[s, p]
-            x31_ref[p, pl.ds(s, 1), :] = a[nx - 1:nx, :]
-            x0_ref[p, pl.ds(s, 1), :] = a[0:1, :]
+            xlo_ref[pl.ds(p * n_s + s, 1), :] = a[nx - 1:nx, :]
+            xhi_ref[pl.ds(p * n_s + s, 1), :] = a[0:1, :]
             acc127 = jnp.where(iy == t, pltpu.roll(a, lax.rem(t + 1, ny), 1), acc127)
             acc0 = jnp.where(iy == t, pltpu.roll(a, t, 1), acc0)
         return acc127, acc0
 
     zero = jnp.zeros((nx, ny), jnp.float32)
     acc127, acc0 = lax.fori_loop(0, n_s, body, (zero, zero))
-    c127_ref[...] = acc127
+    c127_ref[pl.ds(0, nx), :] = acc127
     c0_ref[...] = acc0
-
-
-def edges(a):
+    c1_ref[...] = acc0[nx - 1:nx, :]
+    c2_ref[...] = acc127[0:1, :]
+
+
+def edges(a, region):
     n_s, planes, nx, ny = a.shape
+    rows = planes * n_s
     vmem = pl.BlockSpec(memory_space=pltpu.VMEM)
-    row = jax.ShapeDtypeStruct((planes, n_s, ny), jnp.float32)
-    col = jax.ShapeDtypeStruct((nx, ny), jnp.float32)
+    f32 = jnp.float32
+    shapes = [
+        jax.ShapeDtypeStruct((rows + 8, ny), f32),
+        jax.ShapeDtypeStruct((rows, ny), f32),
+        jax.ShapeDtypeStruct((nx + 8, ny), f32),
+        jax.ShapeDtypeStruct((nx, ny), f32),
+        jax.ShapeDtypeStruct((1, ny), f32),
+        jax.ShapeDtypeStruct((1, ny), f32),
+    ]
     return pl.pallas_call(
         edges_kernel,
-        in_specs=[vmem],
-        out_specs=[vmem] * 4,
-        out_shape=[row, row, col, col],
+        in_specs=[vmem, vmem],
+        out_specs=[vmem] * 6,
+        out_shape=shapes,
         name="halo_edges",
-    )(a)
-
-
-def residual_kernel(kinds, a_ref, src_ref, xlo_ref, xhi_ref, ylo_ref, yhi_ref, own0_ref, c2_ref, bt_ref,
-                    c1_ref, base_ref, sat_ref, reg_ref, reg_xlo_ref, reg_ycol_ref, out_ref):
+    )(a, region)
+
+
+def residual_kernel(kinds, levels, a_ref, src_ref, xlo_ref, xhi_ref, ylo_ref, yhi_ref, own0_ref, c2_ref,
+                    c1_ref, level_ref, relu_ref, sat_ref, reg_ref, out_ref):
     blk = pl.program_id(0)
     n_s, planes, nx, ny = a_ref.shape
+    n_all = n_s * pl.num_programs(0)
+    rows = planes * n_all
     ix = lax.broadcasted_iota(jnp.int32, (nx, ny), 0)
     iy = lax.broadcasted_iota(jnp.int32, (nx, ny), 1)
     iy_row = lax.broadcasted_iota(jnp.int32, (1, ny), 1)
     reg = reg_ref[...]
-    reg_xlo = reg_xlo_ref[...]
-    reg_ycol = reg_ycol_ref[...]
+    reg_xlo = xlo_ref[pl.ds(rows, 1), :].astype(jnp.int32)
+    reg_ycol = row_to_col(ylo_ref[pl.ds(nx, 1), :], ix, iy).astype(jnp.int32)
 
     def lookup(kind, pick):
         out = jnp.broadcast_to(pick(0), kind.shape).astype(jnp.float32)
@@ -87,26 +116,37 @@
 
     sat = lookup(reg, lambda k: sat_ref[k])
     sat_xlo = lookup(reg_xlo, lambda k: sat_ref[k])
-    c_lo = ylo_ref[...]
+    lane_sample = iy_row // planes
+    lane_level = jnp.zeros((1, ny), jnp.int32)
+    for s in range(n_all):
+        lane_level = jnp.where(lane_sample == s, level_ref[s], lane_level)
+    bt = []
+    for k in range(kinds):
+        row = jnp.full((1, ny), relu_ref[0, k], jnp.float32)
+        for lv in range(1, levels):
+            row = jnp.where(lane_level == lv, relu_ref[lv, k], row)
+        bt.append(row)
+    c_lo = ylo_ref[pl.ds(0, nx), :]
     lo_xp = jnp.where(ix == nx - 1, c2_ref[...], pltpu.roll(c_lo, nx - 1, 0))
     sx_c = lo_xp - c_lo
     sy_c = own0_ref[...] - c_lo
     kind_c = jnp.broadcast_to(reg_ycol, (nx, ny))
-    base_c = lookup(kind_c, lambda k: bt_ref[k:k + 1, :])
+    base_c = lookup(kind_c, lambda k: bt[k])
     sat_c = lookup(kind_c, lambda k: sat_ref[k])
     fy_cols = base_c * (1.0 + sat_c * (sx_c * sx_c + sy_c * sy_c)) * sy_c
     c_hi = yhi_ref[...]
 
     def body(s, carry):
         s_glob = blk * n_s + s
-        base = lookup(reg, lambda k: base_ref[s_glob, k])
-        base_xlo = lookup(reg_xlo, lambda k: base_ref[s_glob, k])
+        lv = level_ref[s_glob]
+        base = lookup(reg, lambda k: relu_ref[lv, k])
+        base_xlo = lookup(reg_xlo, lambda k: relu_ref[lv, k])
         tiles = [a_ref[s, p] for p in range(planes)]
         for p in range(planes):
             t = s_glob * planes + p
             a = tiles[p]
-            row_hi = xhi_ref[p, pl.ds(s, 1), :]
-            row_lo = xlo_ref[p, pl.ds(s, 1), :]
+            row_hi = xhi_ref[pl.ds(p * n_all + s_glob, 1), :]
+            row_lo = xlo_ref[pl.ds(p * n_all + s_glob, 1), :]
             c1 = c1_ref[0, t]
             col_hi = pltpu.roll(c_hi, lax.rem(ny - 1 - t + ny, ny), 1)
             a_xp = jnp.where(ix == nx - 1, row_hi, pltpu.roll(a, nx - 1, 0))
@@ -135,22 +175,21 @@
     lax.fori_loop(0, n_s, body, 0)
 
 
-def residual(a, src, xlo, xhi, ylo, yhi, own0, c2, bt, c1, base_rows, saturation, reg, reg_xlo, reg_ycol):
+def residual(a, src, xlo, xhi, ylo, yhi, own0, c2, c1, level_index, reluctivity, saturation, reg):
     n_s, planes, nx, ny = a.shape
-    kinds = base_rows.shape[1]
+    levels, kinds = reluctivity.shape
     sb = min(SAMPLE_BLOCK, n_s)
     tile = pl.BlockSpec((sb, planes, nx, ny), lambda i: (i, 0, 0, 0))
-    edge = pl.BlockSpec((planes, sb, ny), lambda i: (0, i, 0))
     vmem_whole = pl.BlockSpec(memory_space=pltpu.VMEM)
     smem_whole = pl.BlockSpec(memory_space=pltpu.SMEM)
     return pl.pallas_call(
-        functools.partial(residual_kernel, kinds),
+        functools.partial(residual_kernel, kinds, levels),
         grid=(n_s // sb,),
-        in_specs=[tile, tile, edge, edge] + [vmem_whole] * 5 + [smem_whole] * 3 + [vmem_whole] * 3,
+        in_specs=[tile, tile] + [vmem_whole] * 6 + [smem_whole] * 4 + [vmem_whole],
         out_specs=pl.BlockSpec((planes, sb, nx, ny), lambda i: (0, i, 0, 0)),
         out_shape=jax.ShapeDtypeStruct((planes, n_s, nx, ny), jnp.float32),
         name="residual",
-    )(a, src, xlo, xhi, ylo, yhi, own0, c2, bt, c1, base_rows, saturation, reg, reg_xlo, reg_ycol)
+    )(a, src, xlo, xhi, ylo, yhi, own0, c2, c1, level_index, reluctivity, saturation, reg)
 
 
 def local(potential, source, region, level_index, reluctivity, saturation, inverse, transmit):
@@ -174,28 +213,15 @@
     info_all = jnp.concatenate(infos, axis=0)
     gain_all = info_all[:, cells_x]
 
-    e_x31, e_x0, e_c127, e_c0 = edges(potential)
-    regf = region.astype(jnp.float32)
-    pad = jnp.zeros((7, cells_y), jnp.float32)
-    msg_xlo = jnp.concatenate([e_x31.reshape(rows, cells_y), regf[cells_x - 1][None], pad], axis=0)
-    got_xlo = shifted(msg_xlo, grid, sizes, (1, 0))
-    xhi = shifted(e_x0, grid, sizes, (-1, 0))
-    ylo = shifted(e_c127, grid, sizes, (0, 1))
-    yhi = shifted(e_c0, grid, sizes, (0, -1))
-    reg_ycol = shifted(region[:, cells_y - 1:cells_y], grid, sizes, (0, 1))
-    c1 = shifted(e_c0[cells_x - 1:cells_x], grid, sizes, (1, -1))
-    c2 = shifted(e_c127[0:1], grid, sizes, (-1, 1))
-
-    xlo = got_xlo[:rows].reshape(planes, samples_dev, cells_y)
-    reg_xlo = got_xlo[rows:rows + 1].astype(jnp.int32)
-
-    onehot = (level_index[:, None] == lax.iota(jnp.int32, reluctivity.shape[0])[None, :]).astype(jnp.float32)
-    base_rows = jnp.sum(onehot[:, :, None] * reluctivity[None], axis=1)
-    tile_sample = jnp.minimum(lax.iota(jnp.int32, cells_y) // planes, samples_dev - 1)
-    bt = base_rows[tile_sample].T
-
-    resid = residual(potential, source, xlo, xhi, ylo, yhi, e_c0, c2, bt, c1, base_rows, saturation,
-                     region, reg_xlo, reg_ycol)
+    msg_xlo, msg_xhi, msg_c127, msg_c0, msg_c1, msg_c2 = edges(potential, region)
+    xlo = shifted(msg_xlo, grid, sizes, (1, 0))
+    xhi = shifted(msg_xhi, grid, sizes, (-1, 0))
+    ylo = shifted(msg_c127, grid, sizes, (0, 1))
+    yhi = shifted(msg_c0, grid, sizes, (0, -1))
+    c1 = shifted(msg_c1, grid, sizes, (1, -1))
+    c2 = shifted(msg_c2, grid, sizes, (-1, 1))
+    resid = residual(potential, source, xlo, xhi, ylo, yhi, msg_c0, c2, c1, level_index, reluctivity,
+                     saturation, region)
 
     sample_ids = me_tm * samples_dev + lax.iota(jnp.int32, samples_dev)
     tabs = [

time: 107 us -> 99.1 us (0.926)
  starting transfers between devices: 27.8 us -> 23.1 us
  local copies, waits for them, and re-layouts: 5.89 us -> 2.8 us
  other arithmetic: 6.82 us -> 4.55 us
  waiting for transfers between devices: 28.8 us -> 31 us
    ppermute x7 -> x6, starting transfers between devices: 20 us -> 14.9 us  [shifted(): return lax.ppermute(block, axes, route)]
    ppermute x7 -> x6, waiting for transfers between devices: 0.02 us -> 3.37 us  [shifted(): return lax.ppermute(block, axes, route)]
    slice x4 -> x0, local copies, waits for them, and re-layouts: 2.86 us -> none  [the longest x1 0.85 us: local(): reg_ycol = shifted(region[:, cells_y - 1:cells_y], grid, sizes, (0, 1))]
    ppermute x3, waiting for transfers between devices: 8.9 us -> 7.12 us  [local(): got = lax.ppermute(msg_tail, 'gx', [(i, i + d) for i in range(n_gx - d)])]
    gather x2 -> x0, local copies, waits for them, and re-layouts: 1.31 us -> none  [local(): bt = base_rows[tile_sample].T]
    convert_element_type x3 -> x0, other arithmetic: 1.24 us -> none  [the longest x1 0.69 us: local(): regf = region.astype(jnp.float32)]
    unnamed x26 -> x22, local copies, waits for them, and re-layouts: 0.94 us -> 2.17 us
  transfers between devices with their start and end apart: 13 -> 12, of which waited for: 3 -> 4; matrix products, arithmetic and copies ran while one was open for 25% -> 21% of each run, Pallas kernels for 13% -> 9%
where the time goes in v6:
time: 99.1 us; the launch traced here: 97.5 us
  waiting for transfers between devices  31 us (31%)
  starting transfers between devices  23.1 us (23%)
  matrix products  21.7 us (22%)
  Pallas kernels  14.1 us (14%)
  other arithmetic  4.55 us (5%)
  local copies, waits for them, and re-layouts  2.8 us (3%)
    ppermute x1, waiting for transfers between devices, local(): lax.ppermute(carried[d], 'tm', [(i, (i + d) % n_tm) for i in range(n_tm)])  20.5 us
    ppermute x6, starting transfers between devices, shifted(): return lax.ppermute(block, axes, route)  14.9 us
    dot_general x2, matrix products, local(): jnp.einsum('qs,psxy->qpxy', tabs[d], resid, precision=lax.Precision.HIGHEST)  9.1 us
    pallas_call x1, Pallas kernels, residual(): pl.pallas_call(functools.partial(residual_kernel, kinds, levels), grid=(n...  8.54 us
    dot_general x2, matrix products, local(): jnp.einsum('qb,qpby->qpy', row_last[d], parts[d], precision=lax.Precision...  7.55 us
    ppermute x3, waiting for transfers between devices, local(): got = lax.ppermute(msg_tail, 'gx', [(i, i + d) for i in range(n_gx - d)])  7.12 us
    pallas_call x1, Pallas kernels, edges(): pl.pallas_call(edges_kernel, in_specs=[vmem, vmem], out_specs=[vmem] * 6,...  5.6 us
    dot_general x1, matrix products, local(): jnp.einsum('qab,qpby->qpay', inverse, spectrum, precision=lax.Precision.H...  5.02 us
  transfers between devices with their start and end apart: 12, of which 4 were waited for; matrix products, arithmetic and copies ran while one was open for 21% of the time, Pallas kernels for 9%

profile of v6, /device:TPU:12, one launch (start us, length us, event | category | flops | bytes accessed | tf_op | source)
XLA Modules:
  0.0 97.5 jit_solution(11831457400966798344)
XLA Ops:
  0.0 5.6 %halo_edges.1 = (f32[136,128]{1,0:T(8,128)}, f32[128,128]{1,0:T(8,128)}, f32[40,128]{1,0:T(8,128)}, f32[32,128]{1,0:T(8,128)}, f32[1,128]{1,0:T(1,128)}, /*index=5*/f32[1,128]{1,0:T(1,128)}) custom-call(f32[32,4,32,128]{3,2,1,0:T(8,128)} %a_ref.3, s32[32,128]{1,0:T(8,128)} %reg_ref.3), custom_call_target="tpu_custom_call" | custom-call | tf_op jit(solution)/shard_map/halo_edges/pallas_call | solution.py:89
  5.6 2.9 %collective-permute-start.4 = (f32[1,128]{1,0:T(1,128)}, f32[1,128]{1,0:T(1,128)S(1)}, u32[]{:S(2)}, u32[]{:S(2)}) collective-permute-start(f32[1,128]{1,0:T(1,128)} %get-tuple-element.15), channel_id=1, source_target_pairs={{4,1},{5,2},{6,3},{8,5},{9,6},{10,7},{12,9},{13,10},{14,11},{20,17... | collective-permute-start | bytes 1544 | tf_op jit(solution)/shard_map/ppermute | solution.py:22
  8.5 2.4 %collective-permute-start.3 = (f32[32,128]{1,0:T(8,128)}, f32[32,128]{1,0:T(8,128)S(1)}, u32[]{:S(2)}, u32[]{:S(2)}) collective-permute-start(f32[32,128]{1,0:T(8,128)} %get-tuple-element.14.own0_ref), channel_id=1, source_target_pairs={{1,0},{2,1},{3,2},{5,4},{6,5},{7,6},{9,8},{10,9},{11,10},{13,12},{... | collective-permute-start | bytes 49160 | tf_op jit(solution)/shard_map/ppermute | solution.py:22
  10.8 3.5 %collective-permute-start.2 = (f32[40,128]{1,0:T(8,128)}, f32[40,128]{1,0:T(8,128)S(1)}, u32[]{:S(2)}, u32[]{:S(2)}) collective-permute-start(f32[40,128]{1,0:T(8,128)} %get-tuple-element.13), channel_id=1, source_target_pairs={{0,1},{1,2},{2,3},{4,5},{5,6},{6,7},{8,9},{9,10},{10,11},{12,13},{... | collective-permute-start | bytes 61448 | tf_op jit(solution)/shard_map/ppermute | solution.py:22
  14.3 2.2 %collective-permute-start.1 = (f32[128,128]{1,0:T(8,128)}, f32[128,128]{1,0:T(8,128)S(1)}, u32[]{:S(2)}, u32[]{:S(2)}) collective-permute-start(f32[128,128]{1,0:T(8,128)} %get-tuple-element.12), channel_id=1, source_target_pairs={{4,0},{5,1},{6,2},{7,3},{8,4},{9,5},{10,6},{11,7},{12,8},{13,9},{1... | collective-permute-start | bytes 196616 | tf_op jit(solution)/shard_map/ppermute | solution.py:22
  16.5 2.1 %collective-permute-start = (f32[136,128]{1,0:T(8,128)}, f32[136,128]{1,0:T(8,128)S(1)}, u32[]{:S(2)}, u32[]{:S(2)}) collective-permute-start(f32[136,128]{1,0:T(8,128)} %get-tuple-element.11), channel_id=1, source_target_pairs={{0,4},{1,5},{2,6},{3,7},{4,8},{5,9},{6,10},{7,11},{8,12},{9,13},{1... | collective-permute-start | bytes 208904 | tf_op jit(solution)/shard_map/ppermute | solution.py:22
  18.7 0.3 slice_reduce_fusion
  19.3 1.9 %collective-permute-start.5 = (f32[1,128]{1,0:T(1,128)}, f32[1,128]{1,0:T(1,128)S(1)}, u32[]{:S(2)}, u32[]{:S(2)}) collective-permute-start(f32[1,128]{1,0:T(1,128)} %get-tuple-element.16), channel_id=1, source_target_pairs={{1,4},{2,5},{3,6},{5,8},{6,9},{7,10},{9,12},{10,13},{11,14},{17,20... | collective-permute-start | bytes 1544 | tf_op jit(solution)/shard_map/ppermute | solution.py:22
  21.2 0.7 copy.14.relu_ref
  21.9 3.4 %collective-permute-done.5.c1_ref = f32[1,128]{1,0:T(1,128)S(1)} collective-permute-done((f32[1,128]{1,0:T(1,128)}, f32[1,128]{1,0:T(1,128)S(1)}, u32[]{:S(2)}, u32[]{:S(2)}) %collective-permute-start.5) | collective-permute-done | bytes 544 | tf_op jit(solution)/shard_map/ppermute | solution.py:22
  25.2 1.5 %collective-permute-start.7 = (f32[32,33]{1,0:T(8,128)S(1)}, f32[32,33]{1,0:T(8,128)S(1)}, u32[]{:S(2)}, u32[]{:S(2)}) collective-permute-start(f32[32,33]{1,0:T(8,128)S(1)} %pad_maximum_fusion.3), channel_id=1, source_target_pairs={{0,16},{16,0},{1,17},{17,1},{2,18},{18,2},{3,19},{19,3},{4,20},{20... | collective-permute-start | bytes 12680 | tf_op jit(solution)/shard_map/ppermute | solution.py:212
  26.8 0.5 copy-done.5
  27.4 0.6 copy-done.2
  28.0 8.5 %residual.1 = f32[4,32,32,128]{3,2,1,0:T(8,128)} custom-call(f32[32,4,32,128]{3,2,1,0:T(8,128)} %a_ref.3, f32[32,4,32,128]{3,2,1,0:T(8,128)} %src_ref.1, f32[136,128]{1,0:T(8,128)} %copy-done.2, f32[128,128]{1,0:T(8,128)} %copy-done.3, f32[40,128]{1,0:T(8,128)} %copy-done.4, f32[32,128]{1,0:T(8,128)} %copy-done.5, f32[32,128]{1,0:T(8,128)} %get-tuple-element.14.own0_ref, ...), custom_call_target="tpu_custom_call" | custom-call | tf_op jit(solution)/shard_map/residual/pallas_call | solution.py:185
  36.6 6.0 %fusion.6 = f32[32,4,32,128]{3,0,2,1:T(8,128)} fusion(f32[4,32,32,128]{3,2,1,0:T(8,128)} %residual.1, s32[32]{0:T(128)S(1)} %get-tuple-element.17, s32[32]{0:T(128)S(1)} %get-tuple-element.18, pred[32]{0:T(512)(128)(4,1)S(1)} %fusion.61), kind=kOutput, calls=%fused_computation.7 | convolution fusion | flops 201342976 | bytes 4194592 | tf_op jit(solution)/shard_map/qs,psxy->qpxy/dot_general | solution.py:232
  42.6 0.5 collective-permute-start.6
  43.1 0.2 fusion.19
  43.3 4.5 %fusion = f32[32,1,4,128]{3,1,2,0:T(1,128)S(1)} fusion(f32[32,32,1,1]{1,2,3,0:T(1,128)S(1)} %bitcast.51, f32[32,4,32,128]{3,0,2,1:T(8,128)} %fusion.6), kind=kOutput, calls=%fused_computation.1 | convolution fusion | flops 6291456 | bytes 2166784 | tf_op jit(solution)/shard_map/qb,qpby->qpy/dot_general | solution.py:237
  47.8 3.1 %fusion.8 = f32[32,4,32,128]{3,0,2,1:T(8,128)S(1)} fusion(f32[4,32,32,128]{3,2,1,0:T(8,128)S(1)} %copy-done, s32[32]{0:T(128)S(1)} %get-tuple-element.18, s32[32]{0:T(128)S(1)} %add_select_fusion.3, pred[32]{0:T(512)(128)(4,1)S(1)} %fusion.62), kind=kOutput, calls=%fused_computation.9 | convolution fusion | flops 201342976 | bytes 4194592 | tf_op jit(solution)/shard_map/qs,psxy->qpxy/dot_general | solution.py:232
  50.9 3.1 %fusion.2 = f32[32,1,4,128]{3,1,2,0:T(1,128)S(1)} fusion(f32[32,4,32,128]{3,0,2,1:T(8,128)S(1)} %fusion.8, f32[32,32,32]{2,1,0:T(8,128)S(1)} %copy-done.1), kind=kOutput, calls=%fused_computation.3 | convolution fusion | flops 6291456 | bytes 2179072 | tf_op jit(solution)/shard_map/qb,qpby->qpy/dot_general | solution.py:237
  54.2 1.3 %collective-permute-start.9 = (f32[64,5,128]{2,1,0:T(8,128)S(1)}, f32[64,5,128]{2,1,0:T(8,128)S(1)}, u32[]{:S(2)}, u32[]{:S(2)}) collective-permute-start(f32[64,5,128]{2,1,0:T(8,128)S(1)} %pad_maximum_fusion), channel_id=1, source_target_pairs={{0,8},{4,12},{1,9},{5,13},{2,10},{6,14},{3,11},{7,15},{16,24},{20,... | collective-permute-start | bytes 491528 | tf_op jit(solution)/shard_map/ppermute | solution.py:243
  55.5 1.9 %collective-permute-start.8 = (f32[64,5,128]{2,1,0:T(8,128)S(1)}, f32[64,5,128]{2,1,0:T(8,128)S(1)}, u32[]{:S(2)}, u32[]{:S(2)}) collective-permute-start(f32[64,5,128]{2,1,0:T(8,128)S(1)} %pad_maximum_fusion), channel_id=1, source_target_pairs={{0,4},{4,8},{8,12},{1,5},{5,9},{9,13},{2,6},{6,10},{10,14},{3,7},{... | collective-permute-start | bytes 491528 | tf_op jit(solution)/shard_map/ppermute | solution.py:243
  57.4 1.4 %collective-permute-start.10 = (f32[64,5,128]{2,1,0:T(8,128)S(1)}, f32[64,5,128]{2,1,0:T(8,128)}, u32[]{:S(2)}, u32[]{:S(2)}) collective-permute-start(f32[64,5,128]{2,1,0:T(8,128)S(1)} %pad_maximum_fusion), channel_id=1, source_target_pairs={{0,12},{1,13},{2,14},{3,15},{16,28},{17,29},{18,30},{19,31}} | collective-permute-start | bytes 491528 | tf_op jit(solution)/shard_map/ppermute | solution.py:243
  58.8 6.5 %collective-permute-done.9 = f32[64,5,128]{2,1,0:T(8,128)S(1)} collective-permute-done((f32[64,5,128]{2,1,0:T(8,128)S(1)}, f32[64,5,128]{2,1,0:T(8,128)S(1)}, u32[]{:S(2)}, u32[]{:S(2)}) %collective-permute-start.9) | collective-permute-done | bytes 163872 | tf_op jit(solution)/shard_map/ppermute | solution.py:243
  65.3 0.6 collective-permute-done.8
  66.0 1.0 %slice_multiply_fusion = f32[64,1,128]{2,1,0:T(1,128)S(1)} fusion(f32[64,5,128]{2,1,0:T(8,128)} %collective-permute-done.10), kind=kLoop, calls=%fused_computation.21 | loop fusion | flops 8192 | bytes 65536 | tf_op jit(solution)/shard_map/mul | solution.py:244
  67.0 1.1 %fusion.17 = f32[64,4,128]{2,1,0:T(4,128)S(1)} fusion(f32[64,5,128]{2,1,0:T(8,128)S(1)} %collective-permute-done.8, f32[64,5,128]{2,1,0:T(8,128)S(1)} %collective-permute-done.9, f32[64,5,128]{2,1,0:T(8,128)} %collective-permute-done.10, f32[64,128]{1,0:T(8,128)S(1)} %bitcast.50, f32[64,128]{1,0:T(8,128)S(1)} %bitcast.48, f32[64,128]{1,0:T(8,128)S(1)} %bitcast.49, ...), kind=kLoop, calls=%fused_computation.18 | loop fusion | flops 262144 | bytes 622595 | tf_op jit(solution)/shard_map/jit(_where)/select_n | solution.py:245
  68.1 1.6 %collective-permute-start.11 = (f32[32,4,128]{2,1,0:T(4,128)S(1)}, f32[32,4,128]{2,1,0:T(4,128)S(1)}, u32[]{:S(2)}, u32[]{:S(2)}) collective-permute-start(f32[32,4,128]{2,1,0:T(4,128)S(1)} %slice.70), channel_id=1, source_target_pairs={{0,16},{16,0},{1,17},{17,1},{2,18},{18,2},{3,19},{19,3},{4,20},{20... | collective-permute-start | bytes 196616 | tf_op jit(solution)/shard_map/ppermute | solution.py:248
  69.6 0.2 copy.29
  69.9 20.5 %collective-permute-done.11 = f32[32,4,128]{2,1,0:T(4,128)S(1)} collective-permute-done((f32[32,4,128]{2,1,0:T(4,128)S(1)}, f32[32,4,128]{2,1,0:T(4,128)S(1)}, u32[]{:S(2)}, u32[]{:S(2)}) %collective-permute-start.11) | collective-permute-done | bytes 65568 | tf_op jit(solution)/shard_map/ppermute | solution.py:248
  90.4 2.1 %add.95 = f32[32,4,32,128]{3,0,2,1:T(8,128)S(1)} add(f32[32,4,32,128]{3,0,2,1:T(8,128)S(1)} %fusion.8, f32[32,4,32,128]{3,0,2,1:T(8,128)} %collective-permute-done.6) | non-fusion elementwise | flops 524288 | bytes 6291456 | tf_op jit(solution)/shard_map/add | solution.py:252
  92.5 5.0 %bitcast_add_fusion = f32[32,4,32,128]{3,2,1,0:T(8,128)} fusion(f32[32,32]{1,0:T(8,128)S(1)} %bitcast.52, f32[32,4,128]{2,1,0:T(4,128)S(1)} %fusion.18, f32[32,32,32]{2,1,0:T(8,128)S(1)} %copy-done.1, f32[32,4,32,128]{3,0,2,1:T(8,128)S(1)} %add.95), kind=kOutput, calls=%fused_computation | convolution fusion | flops 202375168 | bytes 4395008 | tf_op jit(solution)/shard_map/qab,qpby->qpay/dot_general | solution.py:256
  (40 shorter events, 0.7 us)
Async XLA Ops:
  0.0 18.7 %copy-start.1 = (f32[32,32,32]{2,1,0:T(8,128)S(1)}, f32[32,32,32]{2,1,0:T(8,128)}, u32[]{:S(2)}) copy-start(f32[32,32,32]{2,1,0:T(8,128)} %param.14) | copy-start | bytes 393220
  0.0 19.1 %copy-start.7 = (f32[32,1]{0,1:T(1,128)S(1)}, f32[32,1]{0,1:T(1,128)}, u32[]{:S(2)}) copy-start(f32[32,1]{0,1:T(1,128)} %param.15) | copy-start | bytes 388
  0.0 21.2 %copy-start.6 = (f32[16,8]{0,1:T(8,128)S(1)}, f32[16,8]{0,1:T(8,128)}, u32[]{:S(2)}) copy-start(f32[16,8]{0,1:T(8,128)} %param.12) | copy-start | bytes 1540
  5.6 13.6 %collective-permute-start.4 = (f32[1,128]{1,0:T(1,128)}, f32[1,128]{1,0:T(1,128)S(1)}, u32[]{:S(2)}, u32[]{:S(2)}) collective-permute-start(f32[1,128]{1,0:T(1,128)} %get-tuple-element.15), channel_id=1, source_target_pairs={{4,1},{5,2},{6,3},{8,5},{9,6},{10,7},{12,9},{13,10},{14,11},{20,17... | collective-permute-start | bytes 1544 | tf_op jit(solution)/shard_map/ppermute | solution.py:22
  8.5 18.3 %collective-permute-start.3 = (f32[32,128]{1,0:T(8,128)}, f32[32,128]{1,0:T(8,128)S(1)}, u32[]{:S(2)}, u32[]{:S(2)}) collective-permute-start(f32[32,128]{1,0:T(8,128)} %get-tuple-element.14.own0_ref), channel_id=1, source_target_pairs={{1,0},{2,1},{3,2},{5,4},{6,5},{7,6},{9,8},{10,9},{11,10},{13,12},{... | collective-permute-start | bytes 49160 | tf_op jit(solution)/shard_map/ppermute | solution.py:22
  10.8 15.9 %collective-permute-start.2 = (f32[40,128]{1,0:T(8,128)}, f32[40,128]{1,0:T(8,128)S(1)}, u32[]{:S(2)}, u32[]{:S(2)}) collective-permute-start(f32[40,128]{1,0:T(8,128)} %get-tuple-element.13), channel_id=1, source_target_pairs={{0,1},{1,2},{2,3},{4,5},{5,6},{6,7},{8,9},{9,10},{10,11},{12,13},{... | collective-permute-start | bytes 61448 | tf_op jit(solution)/shard_map/ppermute | solution.py:22
  14.3 12.4 %collective-permute-start.1 = (f32[128,128]{1,0:T(8,128)}, f32[128,128]{1,0:T(8,128)S(1)}, u32[]{:S(2)}, u32[]{:S(2)}) collective-permute-start(f32[128,128]{1,0:T(8,128)} %get-tuple-element.12), channel_id=1, source_target_pairs={{4,0},{5,1},{6,2},{7,3},{8,4},{9,5},{10,6},{11,7},{12,8},{13,9},{1... | collective-permute-start | bytes 196616 | tf_op jit(solution)/shard_map/ppermute | solution.py:22
  16.5 10.2 %collective-permute-start = (f32[136,128]{1,0:T(8,128)}, f32[136,128]{1,0:T(8,128)S(1)}, u32[]{:S(2)}, u32[]{:S(2)}) collective-permute-start(f32[136,128]{1,0:T(8,128)} %get-tuple-element.11), channel_id=1, source_target_pairs={{0,4},{1,5},{2,6},{3,7},{4,8},{5,9},{6,10},{7,11},{8,12},{9,13},{1... | collective-permute-start | bytes 208904 | tf_op jit(solution)/shard_map/ppermute | solution.py:22
  19.3 7.5 %copy-start.8 = (f32[1,128]{1,0:T(1,128)}, f32[1,128]{1,0:T(1,128)S(1)}, u32[]{:S(2)}) copy-start(f32[1,128]{1,0:T(1,128)S(1)} %collective-permute-done.4.c2_ref) | copy-start | bytes 1540
  19.3 6.0 %collective-permute-start.5 = (f32[1,128]{1,0:T(1,128)}, f32[1,128]{1,0:T(1,128)S(1)}, u32[]{:S(2)}, u32[]{:S(2)}) collective-permute-start(f32[1,128]{1,0:T(1,128)} %get-tuple-element.16), channel_id=1, source_target_pairs={{1,4},{2,5},{3,6},{5,8},{6,9},{7,10},{9,12},{10,13},{11,14},{17,20... | collective-permute-start | bytes 1544 | tf_op jit(solution)/shard_map/ppermute | solution.py:22
  25.2 1.6 %copy-start.9 = (f32[1,128]{1,0:T(1,128)}, f32[1,128]{1,0:T(1,128)S(1)}, u32[]{:S(2)}) copy-start(f32[1,128]{1,0:T(1,128)S(1)} %collective-permute-done.5.c1_ref) | copy-start | bytes 1540
  25.2 17.9 %collective-permute-start.7 = (f32[32,33]{1,0:T(8,128)S(1)}, f32[32,33]{1,0:T(8,128)S(1)}, u32[]{:S(2)}, u32[]{:S(2)}) collective-permute-start(f32[32,33]{1,0:T(8,128)S(1)} %pad_maximum_fusion.3), channel_id=1, source_target_pairs={{0,16},{16,0},{1,17},{17,1},{2,18},{18,2},{3,19},{19,3},{4,20},{20... | collective-permute-start | bytes 12680 | tf_op jit(solution)/shard_map/ppermute | solution.py:212
  26.7 0.6 copy-start.5
  26.7 0.6 copy-start.4
  26.8 0.6 copy-start.3
  27.4 0.6 copy-start.2
  42.6 5.2 %copy-start = (f32[4,32,32,128]{3,2,1,0:T(8,128)S(1)}, f32[4,32,32,128]{3,2,1,0:T(8,128)}, u32[]{:S(2)}) copy-start(f32[4,32,32,128]{3,2,1,0:T(8,128)} %residual.1) | copy-start | bytes 6291460
  42.6 47.9 %collective-permute-start.6 = (f32[32,4,32,128]{3,0,2,1:T(8,128)}, f32[32,4,32,128]{3,0,2,1:T(8,128)}, u32[]{:S(2)}, u32[]{:S(2)}) collective-permute-start(f32[32,4,32,128]{3,0,2,1:T(8,128)} %fusion.6), channel_id=1, source_target_pairs={{0,16},{16,0},{1,17},{17,1},{2,18},{18,2},{3,19},{19,3},{4,20},{20... | collective-permute-start | bytes 6291464 | tf_op jit(solution)/shard_map/ppermute | solution.py:234
  54.2 11.1 %collective-permute-start.9 = (f32[64,5,128]{2,1,0:T(8,128)S(1)}, f32[64,5,128]{2,1,0:T(8,128)S(1)}, u32[]{:S(2)}, u32[]{:S(2)}) collective-permute-start(f32[64,5,128]{2,1,0:T(8,128)S(1)} %pad_maximum_fusion), channel_id=1, source_target_pairs={{0,8},{4,12},{1,9},{5,13},{2,10},{6,14},{3,11},{7,15},{16,24},{20,... | collective-permute-start | bytes 491528 | tf_op jit(solution)/shard_map/ppermute | solution.py:243
  55.5 10.5 %collective-permute-start.8 = (f32[64,5,128]{2,1,0:T(8,128)S(1)}, f32[64,5,128]{2,1,0:T(8,128)S(1)}, u32[]{:S(2)}, u32[]{:S(2)}) collective-permute-start(f32[64,5,128]{2,1,0:T(8,128)S(1)} %pad_maximum_fusion), channel_id=1, source_target_pairs={{0,4},{4,8},{8,12},{1,5},{5,9},{9,13},{2,6},{6,10},{10,14},{3,7},{... | collective-permute-start | bytes 491528 | tf_op jit(solution)/shard_map/ppermute | solution.py:243
  57.4 8.6 %collective-permute-start.10 = (f32[64,5,128]{2,1,0:T(8,128)S(1)}, f32[64,5,128]{2,1,0:T(8,128)}, u32[]{:S(2)}, u32[]{:S(2)}) collective-permute-start(f32[64,5,128]{2,1,0:T(8,128)S(1)} %pad_maximum_fusion), channel_id=1, source_target_pairs={{0,12},{1,13},{2,14},{3,15},{16,28},{17,29},{18,30},{19,31}} | collective-permute-start | bytes 491528 | tf_op jit(solution)/shard_map/ppermute | solution.py:243
  68.1 22.3 %collective-permute-start.11 = (f32[32,4,128]{2,1,0:T(4,128)S(1)}, f32[32,4,128]{2,1,0:T(4,128)S(1)}, u32[]{:S(2)}, u32[]{:S(2)}) collective-permute-start(f32[32,4,128]{2,1,0:T(4,128)S(1)} %slice.70), channel_id=1, source_target_pairs={{0,16},{16,0},{1,17},{17,1},{2,18},{18,2},{3,19},{19,3},{4,20},{20... | collective-permute-start | bytes 196616 | tf_op jit(solution)/shard_map/ppermute | solution.py:248

commit v7 on v6

--- a/solution.py
+++ b/solution.py
@@ -95,8 +95,12 @@
     )(a, region)
 
 
-def residual_kernel(kinds, levels, a_ref, src_ref, xlo_ref, xhi_ref, ylo_ref, yhi_ref, own0_ref, c2_ref,
-                    c1_ref, level_ref, relu_ref, sat_ref, reg_ref, out_ref):
+def residual_kernel(kinds, levels, halo, *refs):
+    if halo:
+        (a_ref, src_ref, xlo_ref, xhi_ref, ylo_ref, yhi_ref, own0_ref, c2_ref,
+         c1_ref, level_ref, relu_ref, sat_ref, reg_ref, out_ref) = refs
+    else:
+        a_ref, src_ref, level_ref, relu_ref, sat_ref, reg_ref, out_ref = refs
     blk = pl.program_id(0)
     n_s, planes, nx, ny = a_ref.shape
     n_all = n_s * pl.num_programs(0)
@@ -105,8 +109,10 @@
     iy = lax.broadcasted_iota(jnp.int32, (nx, ny), 1)
     iy_row = lax.broadcasted_iota(jnp.int32, (1, ny), 1)
     reg = reg_ref[...]
-    reg_xlo = xlo_ref[pl.ds(rows, 1), :].astype(jnp.int32)
-    reg_ycol = row_to_col(ylo_ref[pl.ds(nx, 1), :], ix, iy).astype(jnp.int32)
+    if halo:
+        reg_xlo = xlo_ref[pl.ds(rows, 1), :].astype(jnp.int32)
+    else:
+        reg_xlo = jnp.zeros((1, ny), jnp.int32)
 
     def lookup(kind, pick):
         out = jnp.broadcast_to(pick(0), kind.shape).astype(jnp.float32)
@@ -116,25 +122,29 @@
 
     sat = lookup(reg, lambda k: sat_ref[k])
     sat_xlo = lookup(reg_xlo, lambda k: sat_ref[k])
-    lane_sample = iy_row // planes
-    lane_level = jnp.zeros((1, ny), jnp.int32)
-    for s in range(n_all):
-        lane_level = jnp.where(lane_sample == s, level_ref[s], lane_level)
-    bt = []
-    for k in range(kinds):
-        row = jnp.full((1, ny), relu_ref[0, k], jnp.float32)
-        for lv in range(1, levels):
-            row = jnp.where(lane_level == lv, relu_ref[lv, k], row)
-        bt.append(row)
-    c_lo = ylo_ref[pl.ds(0, nx), :]
-    lo_xp = jnp.where(ix == nx - 1, c2_ref[...], pltpu.roll(c_lo, nx - 1, 0))
-    sx_c = lo_xp - c_lo
-    sy_c = own0_ref[...] - c_lo
-    kind_c = jnp.broadcast_to(reg_ycol, (nx, ny))
-    base_c = lookup(kind_c, lambda k: bt[k])
-    sat_c = lookup(kind_c, lambda k: sat_ref[k])
-    fy_cols = base_c * (1.0 + sat_c * (sx_c * sx_c + sy_c * sy_c)) * sy_c
-    c_hi = yhi_ref[...]
+    if halo:
+        reg_ycol = row_to_col(ylo_ref[pl.ds(nx, 1), :], ix, iy).astype(jnp.int32)
+        lane_sample = iy_row // planes
+        lane_level = jnp.zeros((1, ny), jnp.int32)
+        for s in range(n_all):
+            lane_level = jnp.where(lane_sample == s, level_ref[s], lane_level)
+        bt = []
+        for k in range(kinds):
+            row = jnp.full((1, ny), relu_ref[0, k], jnp.float32)
+            for lv in range(1, levels):
+                row = jnp.where(lane_level == lv, relu_ref[lv, k], row)
+            bt.append(row)
+        c_lo = ylo_ref[pl.ds(0, nx), :]
+        lo_xp = jnp.where(ix == nx - 1, c2_ref[...], pltpu.roll(c_lo, nx - 1, 0))
+        sx_c = lo_xp - c_lo
+        sy_c = own0_ref[...] - c_lo
+        kind_c = jnp.broadcast_to(reg_ycol, (nx, ny))
+        base_c = lookup(kind_c, lambda k: bt[k])
+        sat_c = lookup(kind_c, lambda k: sat_ref[k])
+        fy_cols = base_c * (1.0 + sat_c * (sx_c * sx_c + sy_c * sy_c)) * sy_c
+        c_hi = yhi_ref[...]
+    zero_row = jnp.zeros((1, ny), jnp.float32)
+    zero_tile = jnp.zeros((nx, ny), jnp.float32)
 
     def body(s, carry):
         s_glob = blk * n_s + s
@@ -145,10 +155,18 @@
         for p in range(planes):
             t = s_glob * planes + p
             a = tiles[p]
-            row_hi = xhi_ref[pl.ds(p * n_all + s_glob, 1), :]
-            row_lo = xlo_ref[pl.ds(p * n_all + s_glob, 1), :]
-            c1 = c1_ref[0, t]
-            col_hi = pltpu.roll(c_hi, lax.rem(ny - 1 - t + ny, ny), 1)
+            if halo:
+                row_hi = xhi_ref[pl.ds(p * n_all + s_glob, 1), :]
+                row_lo = xlo_ref[pl.ds(p * n_all + s_glob, 1), :]
+                c1 = c1_ref[0, t]
+                col_hi = pltpu.roll(c_hi, lax.rem(ny - 1 - t + ny, ny), 1)
+                fy_c = pltpu.roll(fy_cols, lax.rem(ny - t, ny), 1)
+            else:
+                row_hi = zero_row
+                row_lo = zero_row
+                c1 = 0.0
+                col_hi = zero_tile
+                fy_c = zero_tile
             a_xp = jnp.where(ix == nx - 1, row_hi, pltpu.roll(a, nx - 1, 0))
             a_yp = jnp.where(iy == ny - 1, col_hi, pltpu.roll(a, ny - 1, 1))
             sx = a_xp - a
@@ -160,7 +178,6 @@
             sx_l = a[0:1, :] - row_lo
             sy_l = lo_yp - row_lo
             fx_l = base_xlo * (1.0 + sat_xlo * (sx_l * sx_l + sy_l * sy_l)) * sx_l
-            fy_c = pltpu.roll(fy_cols, lax.rem(ny - t, ny), 1)
             fx_down = jnp.where(ix == 0, fx_l, pltpu.roll(fx, 1, 0))
             fy_left = jnp.where(iy == 0, fy_c, pltpu.roll(fy, 1, 1))
             curl = fx_down - fx + fy_left - fy
@@ -175,7 +192,7 @@
     lax.fori_loop(0, n_s, body, 0)
 
 
-def residual(a, src, xlo, xhi, ylo, yhi, own0, c2, c1, level_index, reluctivity, saturation, reg):
+def residual(a, src, halos, level_index, reluctivity, saturation, reg):
     n_s, planes, nx, ny = a.shape
     levels, kinds = reluctivity.shape
     sb = min(SAMPLE_BLOCK, n_s)
@@ -183,13 +200,13 @@
     vmem_whole = pl.BlockSpec(memory_space=pltpu.VMEM)
     smem_whole = pl.BlockSpec(memory_space=pltpu.SMEM)
     return pl.pallas_call(
-        functools.partial(residual_kernel, kinds, levels),
+        functools.partial(residual_kernel, kinds, levels, halos is not None),
         grid=(n_s // sb,),
-        in_specs=[tile, tile] + [vmem_whole] * 6 + [smem_whole] * 4 + [vmem_whole],
+        in_specs=[tile, tile] + ([vmem_whole] * 6 + [smem_whole] if halos else []) + [smem_whole] * 3 + [vmem_whole],
         out_specs=pl.BlockSpec((planes, sb, nx, ny), lambda i: (0, i, 0, 0)),
         out_shape=jax.ShapeDtypeStruct((planes, n_s, nx, ny), jnp.float32),
         name="residual",
-    )(a, src, xlo, xhi, ylo, yhi, own0, c2, c1, level_index, reluctivity, saturation, reg)
+    )(a, src, *(halos or ()), level_index, reluctivity, saturation, reg)
 
 
 def local(potential, source, region, level_index, reluctivity, saturation, inverse, transmit):
@@ -213,6 +230,17 @@
     info_all = jnp.concatenate(infos, axis=0)
     gain_all = info_all[:, cells_x]
 
+    sample_ids = me_tm * samples_dev + lax.iota(jnp.int32, samples_dev)
+    tabs = [
+        fourier_rows(((me_tm + d) % n_tm) * q_dev + lax.iota(jnp.int32, q_dev), sample_ids, sample_count)
+        for d in range(n_tm)
+    ]
+    resid0 = residual(potential, source, None, level_index, reluctivity, saturation, region)
+    parts = [jnp.einsum("qs,psxy->qpxy", tabs[d], resid0, precision=lax.Precision.HIGHEST) for d in range(n_tm)]
+    got_parts = [
+        lax.ppermute(parts[d], "tm", [(i, (i + d) % n_tm) for i in range(n_tm)]) for d in range(1, n_tm)
+    ]
+
     msg_xlo, msg_xhi, msg_c127, msg_c0, msg_c1, msg_c2 = edges(potential, region)
     xlo = shifted(msg_xlo, grid, sizes, (1, 0))
     xhi = shifted(msg_xhi, grid, sizes, (-1, 0))
@@ -220,21 +248,35 @@
     yhi = shifted(msg_c0, grid, sizes, (0, -1))
     c1 = shifted(msg_c1, grid, sizes, (1, -1))
     c2 = shifted(msg_c2, grid, sizes, (-1, 1))
-    resid = residual(potential, source, xlo, xhi, ylo, yhi, msg_c0, c2, c1, level_index, reluctivity,
-                     saturation, region)
-
-    sample_ids = me_tm * samples_dev + lax.iota(jnp.int32, samples_dev)
-    tabs = [
-        fourier_rows(((me_tm + d) % n_tm) * q_dev + lax.iota(jnp.int32, q_dev), sample_ids, sample_count)
-        for d in range(n_tm)
-    ]
+    resid1 = residual(potential, source, (xlo, xhi, ylo, yhi, msg_c0, c2, c1), level_index, reluctivity,
+                      saturation, region)
+    delta = resid1 - resid0
+    d_rows = jnp.stack([delta[:, :, 0], delta[:, :, cells_x - 1]], axis=2)
+    d_cols = jnp.stack([delta[:, :, 1:cells_x - 1, 0], delta[:, :, 1:cells_x - 1, cells_y - 1]], axis=3)
+    fix_rows = [jnp.einsum("qs,psry->qpry", tabs[d], d_rows, precision=lax.Precision.HIGHEST) for d in range(n_tm)]
+    fix_cols = [jnp.einsum("qs,psxc->qpxc", tabs[d], d_cols, precision=lax.Precision.HIGHEST) for d in range(n_tm)]
+    n_row = planes * 2 * cells_y
+    fix_msg = [jnp.concatenate([fix_rows[d].reshape(q_dev, -1), fix_cols[d].reshape(q_dev, -1)], axis=1)
+               for d in range(n_tm)]
+    got_fix = [
+        lax.ppermute(fix_msg[d], "tm", [(i, (i + d) % n_tm) for i in range(n_tm)]) for d in range(1, n_tm)
+    ]
+    xi = lax.broadcasted_iota(jnp.int32, (1, 1, cells_x, cells_y), 2)
+    yi = lax.broadcasted_iota(jnp.int32, (1, 1, cells_x, cells_y), 3)
+
+    def expand(msg):
+        r = msg[:, :n_row].reshape(q_dev, planes, 2, cells_y)
+        c = jnp.pad(msg[:, n_row:].reshape(q_dev, planes, cells_x - 2, 2), ((0, 0), (0, 0), (1, 1), (0, 0)))
+        out = jnp.where(yi == cells_y - 1, c[..., 1:2], 0.0)
+        out = jnp.where(yi == 0, c[..., 0:1], out)
+        out = jnp.where(xi == cells_x - 1, r[:, :, 1:2], out)
+        return jnp.where(xi == 0, r[:, :, 0:1], out)
+
+    true_parts = [parts[d] + expand(fix_msg[d]) for d in range(n_tm)]
     row_last = info_all[:, :cells_x].reshape(n_tm, q_dev, cells_x)
-    parts = [jnp.einsum("qs,psxy->qpxy", tabs[d], resid, precision=lax.Precision.HIGHEST) for d in range(n_tm)]
-    got_parts = [
-        lax.ppermute(parts[d], "tm", [(i, (i + d) % n_tm) for i in range(n_tm)]) for d in range(1, n_tm)
-    ]
     tails = jnp.concatenate(
-        [jnp.einsum("qb,qpby->qpy", row_last[d], parts[d], precision=lax.Precision.HIGHEST) for d in range(n_tm)],
+        [jnp.einsum("qb,qpby->qpy", row_last[d], true_parts[d], precision=lax.Precision.HIGHEST)
+         for d in range(n_tm)],
         axis=0,
     )
     msg_tail = jnp.concatenate([tails, jnp.broadcast_to(gain_all[:, None, None], (n_tm * q_dev, 1, cells_y))], axis=1)
@@ -247,9 +289,9 @@
     got_carried = [
         lax.ppermute(carried[d], "tm", [(i, (i + d) % n_tm) for i in range(n_tm)]) for d in range(1, n_tm)
     ]
-    spectrum = parts[0]
-    for got in got_parts:
-        spectrum = spectrum + got
+    spectrum = true_parts[0]
+    for got, fix in zip(got_parts, got_fix):
+        spectrum = spectrum + (got + expand(fix))
     carried_own = carried[0]
     for got in got_carried:
         carried_own = carried_own + got

time: 99.1 us -> 140 us (1.41)
  the two profiles are of different devices: /device:TPU:12 before, /device:TPU:0 now
where the time goes in v7:
time: 140 us
  starting transfers between devices  36.3 us (26%)
  waiting for transfers between devices  33.9 us (24%)
  matrix products  28.5 us (20%)
  Pallas kernels  21.7 us (16%)
  local copies, waits for them, and re-layouts  9.47 us (7%)
  other arithmetic  9.47 us (7%)
    ppermute x1, waiting for transfers between devices, local(): lax.ppermute(fix_msg[d], 'tm', [(i, (i + d) % n_tm) for i in range(n_tm)])  22.1 us
    ppermute x3, starting transfers between devices, local(): got = lax.ppermute(msg_tail, 'gx', [(i, i + d) for i in range(n_gx - d)])  19.7 us
    pallas_call x2, Pallas kernels, residual(): pl.pallas_call(functools.partial(residual_kernel, kinds, levels, halos is...  16.1 us
    dot_general x2, matrix products, local(): jnp.einsum('qs,psxy->qpxy', tabs[d], resid0, precision=lax.Precision.HIGH...  14.8 us
    ppermute x6, starting transfers between devices, shifted(): return lax.ppermute(block, axes, route)  11.4 us
    ppermute x3, waiting for transfers between devices, local(): got = lax.ppermute(msg_tail, 'gx', [(i, i + d) for i in range(n_gx - d)])  7.71 us
    dot_general x2, matrix products, local(): jnp.einsum('qb,qpby->qpy', row_last[d], true_parts[d], precision=lax.Prec...  5.83 us
    pallas_call x1, Pallas kernels, edges(): pl.pallas_call(edges_kernel, in_specs=[vmem, vmem], out_specs=[vmem] * 6,...  5.61 us
  transfers between devices with their start and end apart: 13, of which 5 were waited for; matrix products, arithmetic and copies ran while one was open for 17% of the time, Pallas kernels for 11%

profile of v7, /device:TPU:0, one launch (start us, length us, event | category | flops | bytes accessed | tf_op | source)
XLA Modules:
  0.0 139.9 jit_solution(8807476984848470397)
XLA Ops:
  0.0 5.6 %halo_edges.1 = (f32[136,128]{1,0:T(8,128)}, f32[128,128]{1,0:T(8,128)}, f32[40,128]{1,0:T(8,128)}, f32[32,128]{1,0:T(8,128)}, f32[1,128]{1,0:T(1,128)}, /*index=5*/f32[1,128]{1,0:T(1,128)}) custom-call(f32[32,4,32,128]{3,2,1,0:T(8,128)} %refs_0_.3, s32[32,128]{1,0:T(8,128)} %refs_12_.1), custom_call_target="tpu_custom_call" | custom-call | tf_op jit(solution)/shard_map/halo_edges/pallas_call | solution.py:89
  5.6 1.3 collective-permute-start.3
  6.9 2.4 %collective-permute-start = (f32[136,128]{1,0:T(8,128)}, f32[136,128]{1,0:T(8,128)S(1)}, u32[]{:S(2)}, u32[]{:S(2)}) collective-permute-start(f32[136,128]{1,0:T(8,128)} %get-tuple-element.11), channel_id=1, source_target_pairs={{0,4},{1,5},{2,6},{3,7},{4,8},{5,9},{6,10},{7,11},{8,12},{9,13},{1... | collective-permute-start | bytes 208904 | tf_op jit(solution)/shard_map/ppermute | solution.py:22
  9.3 1.3 collective-permute-start.1
  10.6 4.9 %collective-permute-start.2 = (f32[40,128]{1,0:T(8,128)}, f32[40,128]{1,0:T(8,128)S(1)}, u32[]{:S(2)}, u32[]{:S(2)}) collective-permute-start(f32[40,128]{1,0:T(8,128)} %get-tuple-element.13), channel_id=1, source_target_pairs={{0,1},{1,2},{2,3},{4,5},{5,6},{6,7},{8,9},{9,10},{10,11},{12,13},{... | collective-permute-start | bytes 61448 | tf_op jit(solution)/shard_map/ppermute | solution.py:22
  18.6 7.5 %residual.2 = f32[4,32,32,128]{3,2,1,0:T(8,128)} custom-call(f32[32,4,32,128]{3,2,1,0:T(8,128)} %refs_0_.3, f32[32,4,32,128]{3,2,1,0:T(8,128)} %refs_1_.3, s32[32]{0:T(128)} %refs_9_.1, f32[16,8]{1,0:T(8,128)} %copy.67.refs_3_.refs_10_, f32[8]{0:T(128)} %refs_11_.1, s32[32,128]{1,0:T(8,128)} %refs_12_.1), custom_call_target="tpu_custom_call" | custom-call | tf_op jit(solution)/shard_map/residual/pallas_call | solution.py:202
  26.2 6.0 %fusion.6 = f32[32,4,32,128]{3,0,2,1:T(8,128)} fusion(f32[4,32,32,128]{3,2,1,0:T(8,128)} %residual.2, s32[32]{0:T(128)S(1)} %get-tuple-element.36, s32[32]{0:T(128)S(1)} %get-tuple-element.37, pred[32]{0:T(512)(128)(4,1)S(1)} %fusion.45), kind=kOutput, calls=%fused_computation.11 | convolution fusion | flops 201342976 | bytes 4194592 | tf_op jit(solution)/shard_map/qs,psxy->qpxy/dot_general | solution.py:239
  32.8 1.6 %collective-permute-start.8 = (f32[32,33]{1,0:T(8,128)S(1)}, f32[32,33]{1,0:T(8,128)S(1)}, u32[]{:S(2)}, u32[]{:S(2)}) collective-permute-start(f32[32,33]{1,0:T(8,128)S(1)} %pad_maximum_fusion.6), channel_id=1, source_target_pairs={{0,16},{16,0},{1,17},{17,1},{2,18},{18,2},{3,19},{19,3},{4,20},{20... | collective-permute-start | bytes 12680 | tf_op jit(solution)/shard_map/ppermute | solution.py:229
  34.9 1.6 %collective-permute-done.8 = f32[32,33]{1,0:T(8,128)S(1)} collective-permute-done((f32[32,33]{1,0:T(8,128)S(1)}, f32[32,33]{1,0:T(8,128)S(1)}, u32[]{:S(2)}, u32[]{:S(2)}) %collective-permute-start.8) | collective-permute-done | bytes 4256 | tf_op jit(solution)/shard_map/ppermute | solution.py:229
  36.5 0.8 collective-permute-start.5
  38.1 1.6 %collective-permute-start.6 = (f32[32,4,32,128]{3,0,2,1:T(8,128)}, f32[32,4,32,128]{3,0,2,1:T(8,128)}, u32[]{:S(2)}, u32[]{:S(2)}) collective-permute-start(f32[32,4,32,128]{3,0,2,1:T(8,128)} %fusion.6), channel_id=1, source_target_pairs={{0,16},{16,0},{1,17},{17,1},{2,18},{18,2},{3,19},{19,3},{4,20},{20... | collective-permute-start | bytes 6291464 | tf_op jit(solution)/shard_map/ppermute | solution.py:241
  41.0 8.6 %residual.3 = f32[4,32,32,128]{3,2,1,0:T(8,128)} custom-call(f32[32,4,32,128]{3,2,1,0:T(8,128)} %refs_0_.3, f32[32,4,32,128]{3,2,1,0:T(8,128)} %refs_1_.3, f32[136,128]{1,0:T(8,128)} %copy-done.3, f32[128,128]{1,0:T(8,128)} %copy-done.4, f32[40,128]{1,0:T(8,128)} %copy-done.7, f32[32,128]{1,0:T(8,128)} %copy-done.9, f32[32,128]{1,0:T(8,128)} %get-tuple-element.14.refs_6_, ...), custom_call_target="tpu_custom_call" | custom-call | tf_op jit(solution)/shard_map/residual/pallas_call | solution.py:202
  49.6 2.1 %sub.10 = f32[4,32,32,128]{3,2,1,0:T(8,128)S(1)} subtract(f32[4,32,32,128]{3,2,1,0:T(8,128)} %residual.3, f32[4,32,32,128]{3,2,1,0:T(8,128)S(1)} %copy-done) | non-fusion elementwise | flops 524288 | bytes 6291456 | tf_op jit(solution)/shard_map/sub | solution.py:253
  51.6 0.8 fusion.79
  52.6 1.9 %pad_maximum_fusion = f32[4,32,30,2]{3,2,1,0:T(8,128)} fusion(f32[4,32,30,1]{3,2,1,0:T(8,128)S(1)} %get-tuple-element.20, f32[4,32,30,1]{3,2,1,0:T(8,128)S(1)} %get-tuple-element.19), kind=kLoop, calls=%fused_computation | loop fusion | flops 7680 | bytes 61440 | tf_op jit(solution)/shard_map/stack | solution.py:255
  54.5 2.5 %copy.71 = f32[4,32,30,2]{2,1,3,0:T(8,128)S(1)} copy(f32[4,32,30,2]{3,2,1,0:T(8,128)} %pad_maximum_fusion) | data formatting | bytes 61440 | tf_op jit(solution)/shard_map/stack | solution.py:255
  58.8 1.0 fusion.41
  62.3 1.0 fusion.22
  63.4 22.1 %collective-permute-done.7 = f32[32,1264]{1,0:T(8,128)S(1)} collective-permute-done((f32[32,1264]{1,0:T(8,128)S(1)}, f32[32,1264]{1,0:T(8,128)S(1)}, u32[]{:S(2)}, u32[]{:S(2)}) %collective-permute-start.7) | collective-permute-done | bytes 161824 | tf_op jit(solution)/shard_map/ppermute | solution.py:262
  86.0 8.8 %add_add_fusion = (f32[32,4,32,128]{3,0,2,1:T(8,128)}, f32[32,4,32,128]{3,0,2,1:T(8,128)S(1)}, f32[32,4,32,128]{3,0,2,1:T(8,128)S(1)}) fusion(f32[32,4,32,128]{3,0,2,1:T(8,128)} %collective-permute-done.6, f32[32,4,32]{0,2,1:T(8,128)S(1)} %bitcast.92, f32[32,4,32]{0,2,1:T(8,128)S(1)} %bitcast.91, f32[32,4,128]{2,0,1:T(8,128)S(1)} %copy.81, ...), kind=kOutput, calls=%fused_computation.9 | convolution fusion | flops 209731584 | bytes 13075040 | tf_op jit(solution)/shard_map/qs,psxy->qpxy/dot_general | solution.py:239
  94.8 2.9 %fusion.2 = f32[32,1,4,128]{3,1,2,0:T(1,128)S(1)} fusion(f32[32,4,32,128]{3,0,2,1:T(8,128)S(1)} %get-tuple-element.35, f32[32,32,32]{2,1,0:T(8,128)S(1)} %copy-done.1), kind=kOutput, calls=%fused_computation.4 | convolution fusion | flops 6291456 | bytes 2179072 | tf_op jit(solution)/shard_map/qb,qpby->qpy/dot_general | solution.py:278
  97.7 2.9 %fusion = f32[32,1,4,128]{3,1,2,0:T(1,128)S(1)} fusion(f32[32,32,1,1]{1,2,3,0:T(1,128)S(1)} %bitcast.89, f32[32,4,32,128]{3,0,2,1:T(8,128)S(1)} %get-tuple-element.34), kind=kOutput, calls=%fused_computation.2 | convolution fusion | flops 6291456 | bytes 2166784 | tf_op jit(solution)/shard_map/qb,qpby->qpy/dot_general | solution.py:278
  100.8 6.6 %collective-permute-start.9 = (f32[64,5,128]{2,1,0:T(8,128)S(1)}, f32[64,5,128]{2,1,0:T(8,128)S(1)}, u32[]{:S(2)}, u32[]{:S(2)}) collective-permute-start(f32[64,5,128]{2,1,0:T(8,128)S(1)} %pad_maximum_fusion.1), channel_id=1, source_target_pairs={{0,4},{4,8},{8,12},{1,5},{5,9},{9,13},{2,6},{6,10},{10,14},{3,7},{... | collective-permute-start | bytes 491528 | tf_op jit(solution)/shard_map/ppermute | solution.py:285
  107.4 11.1 %collective-permute-start.10 = (f32[64,5,128]{2,1,0:T(8,128)S(1)}, f32[64,5,128]{2,1,0:T(8,128)S(1)}, u32[]{:S(2)}, u32[]{:S(2)}) collective-permute-start(f32[64,5,128]{2,1,0:T(8,128)S(1)} %pad_maximum_fusion.1), channel_id=1, source_target_pairs={{0,8},{4,12},{1,9},{5,13},{2,10},{6,14},{3,11},{7,15},{16,24},{20,... | collective-permute-start | bytes 491528 | tf_op jit(solution)/shard_map/ppermute | solution.py:285
  118.6 2.0 %collective-permute-start.11 = (f32[64,5,128]{2,1,0:T(8,128)S(1)}, f32[64,5,128]{2,1,0:T(8,128)}, u32[]{:S(2)}, u32[]{:S(2)}) collective-permute-start(f32[64,5,128]{2,1,0:T(8,128)S(1)} %pad_maximum_fusion.1), channel_id=1, source_target_pairs={{0,12},{1,13},{2,14},{3,15},{16,28},{17,29},{18,30},{19,31}} | collective-permute-start | bytes 491528 | tf_op jit(solution)/shard_map/ppermute | solution.py:285
  120.6 4.7 %collective-permute-done.10 = f32[64,5,128]{2,1,0:T(8,128)S(1)} collective-permute-done((f32[64,5,128]{2,1,0:T(8,128)S(1)}, f32[64,5,128]{2,1,0:T(8,128)S(1)}, u32[]{:S(2)}, u32[]{:S(2)}) %collective-permute-start.10) | collective-permute-done | bytes 163872 | tf_op jit(solution)/shard_map/ppermute | solution.py:285
  125.3 3.0 %collective-permute-done.11 = f32[64,5,128]{2,1,0:T(8,128)} collective-permute-done((f32[64,5,128]{2,1,0:T(8,128)S(1)}, f32[64,5,128]{2,1,0:T(8,128)}, u32[]{:S(2)}, u32[]{:S(2)}) %collective-permute-start.11) | collective-permute-done | bytes 163872 | tf_op jit(solution)/shard_map/ppermute | solution.py:285
  128.3 1.0 slice_multiply_fusion
  129.3 1.1 fusion.19
  130.4 1.6 %collective-permute-start.12 = (f32[32,4,128]{2,1,0:T(4,128)S(1)}, f32[32,4,128]{2,1,0:T(4,128)S(1)}, u32[]{:S(2)}, u32[]{:S(2)}) collective-permute-start(f32[32,4,128]{2,1,0:T(4,128)S(1)} %slice.154), channel_id=1, source_target_pairs={{0,16},{16,0},{1,17},{17,1},{2,18},{18,2},{3,19},{19,3},{4,20},{20... | collective-permute-start | bytes 196616 | tf_op jit(solution)/shard_map/ppermute | solution.py:290
  132.2 2.5 %collective-permute-done.12 = f32[32,4,128]{2,1,0:T(4,128)S(1)} collective-permute-done((f32[32,4,128]{2,1,0:T(4,128)S(1)}, f32[32,4,128]{2,1,0:T(4,128)S(1)}, u32[]{:S(2)}, u32[]{:S(2)}) %collective-permute-start.12) | collective-permute-done | bytes 65568 | tf_op jit(solution)/shard_map/ppermute | solution.py:290
  134.9 5.0 %bitcast_add_fusion = f32[32,4,32,128]{3,2,1,0:T(8,128)} fusion(f32[32,32]{1,0:T(8,128)S(1)} %bitcast.90, f32[32,4,128]{2,1,0:T(4,128)S(1)} %fusion.28, f32[32,32,32]{2,1,0:T(8,128)S(1)} %copy-done.1, f32[32,4,32,128]{3,0,2,1:T(8,128)S(1)} %copy-done.2), kind=kOutput, calls=%fused_computation.1 | convolution fusion | flops 202375168 | bytes 4395008 | tf_op jit(solution)/shard_map/qab,qpby->qpay/dot_general | solution.py:298
  (89 shorter events, 11.5 us)
Async XLA Ops:
  0.0 17.4 %copy-start.1 = (f32[32,32,32]{2,1,0:T(8,128)S(1)}, f32[32,32,32]{2,1,0:T(8,128)}, u32[]{:S(2)}) copy-start(f32[32,32,32]{2,1,0:T(8,128)} %param.14) | copy-start | bytes 393220
  0.0 17.8 %copy-start.10 = (f32[16,8]{0,1:T(8,128)S(1)}, f32[16,8]{0,1:T(8,128)}, u32[]{:S(2)}) copy-start(f32[16,8]{0,1:T(8,128)} %param.12) | copy-start | bytes 1540
  0.0 18.5 %copy-start.12 = (f32[32,1]{0,1:T(1,128)S(1)}, f32[32,1]{0,1:T(1,128)}, u32[]{:S(2)}) copy-start(f32[32,1]{0,1:T(1,128)} %param.15) | copy-start | bytes 388
  5.6 34.1 %collective-permute-start.3 = (f32[32,128]{1,0:T(8,128)}, f32[32,128]{1,0:T(8,128)S(1)}, u32[]{:S(2)}, u32[]{:S(2)}) collective-permute-start(f32[32,128]{1,0:T(8,128)} %get-tuple-element.14.refs_6_), channel_id=1, source_target_pairs={{1,0},{2,1},{3,2},{5,4},{6,5},{7,6},{9,8},{10,9},{11,10},{13,12},{... | collective-permute-start | bytes 49160 | tf_op jit(solution)/shard_map/ppermute | solution.py:22
  6.9 32.9 %collective-permute-start = (f32[136,128]{1,0:T(8,128)}, f32[136,128]{1,0:T(8,128)S(1)}, u32[]{:S(2)}, u32[]{:S(2)}) collective-permute-start(f32[136,128]{1,0:T(8,128)} %get-tuple-element.11), channel_id=1, source_target_pairs={{0,4},{1,5},{2,6},{3,7},{4,8},{5,9},{6,10},{7,11},{8,12},{9,13},{1... | collective-permute-start | bytes 208904 | tf_op jit(solution)/shard_map/ppermute | solution.py:22
  9.3 30.5 %collective-permute-start.1 = (f32[128,128]{1,0:T(8,128)}, f32[128,128]{1,0:T(8,128)S(1)}, u32[]{:S(2)}, u32[]{:S(2)}) collective-permute-start(f32[128,128]{1,0:T(8,128)} %get-tuple-element.12), channel_id=1, source_target_pairs={{4,0},{5,1},{6,2},{7,3},{8,4},{9,5},{10,6},{11,7},{12,8},{13,9},{1... | collective-permute-start | bytes 196616 | tf_op jit(solution)/shard_map/ppermute | solution.py:22
  10.6 29.1 %collective-permute-start.2 = (f32[40,128]{1,0:T(8,128)}, f32[40,128]{1,0:T(8,128)S(1)}, u32[]{:S(2)}, u32[]{:S(2)}) collective-permute-start(f32[40,128]{1,0:T(8,128)} %get-tuple-element.13), channel_id=1, source_target_pairs={{0,1},{1,2},{2,3},{4,5},{5,6},{6,7},{8,9},{9,10},{10,11},{12,13},{... | collective-permute-start | bytes 61448 | tf_op jit(solution)/shard_map/ppermute | solution.py:22
  15.5 17.2 %collective-permute-start.4 = (f32[1,128]{1,0:T(1,128)}, f32[1,128]{1,0:T(1,128)S(1)}, u32[]{:S(2)}, u32[]{:S(2)}) collective-permute-start(f32[1,128]{1,0:T(1,128)} %get-tuple-element.15), channel_id=1, source_target_pairs={{4,1},{5,2},{6,3},{8,5},{9,6},{10,7},{12,9},{13,10},{14,11},{20,17... | collective-permute-start | bytes 1544 | tf_op jit(solution)/shard_map/ppermute | solution.py:22
  17.8 39.9 %copy-start.8 = (s32[32]{0:T(128)}, s32[32]{0:T(128)S(1)}, u32[]{:S(2)}) copy-start(s32[32]{0:T(128)S(1)} %get-tuple-element.37) | copy-start | bytes 388
  26.2 10.3 %copy-start.16 = (f32[1,128]{1,0:T(1,128)S(1)}, f32[1,128]{1,0:T(1,128)}, u32[]{:S(2)}) copy-start(f32[1,128]{1,0:T(1,128)} %get-tuple-element.16) | copy-start | bytes 1540
  32.7 7.0 %copy-start.14 = (f32[1,128]{1,0:T(1,128)}, f32[1,128]{1,0:T(1,128)S(1)}, u32[]{:S(2)}) copy-start(f32[1,128]{1,0:T(1,128)S(1)} %collective-permute-done.4.refs_7_) | copy-start | bytes 1540
  32.8 3.7 %collective-permute-start.8 = (f32[32,33]{1,0:T(8,128)S(1)}, f32[32,33]{1,0:T(8,128)S(1)}, u32[]{:S(2)}, u32[]{:S(2)}) collective-permute-start(f32[32,33]{1,0:T(8,128)S(1)} %pad_maximum_fusion.6), channel_id=1, source_target_pairs={{0,16},{16,0},{1,17},{17,1},{2,18},{18,2},{3,19},{19,3},{4,20},{20... | collective-permute-start | bytes 12680 | tf_op jit(solution)/shard_map/ppermute | solution.py:229
  36.5 1.6 %collective-permute-start.5 = (f32[1,128]{1,0:T(1,128)S(1)}, f32[1,128]{1,0:T(1,128)S(1)}, u32[]{:S(2)}, u32[]{:S(2)}) collective-permute-start(f32[1,128]{1,0:T(1,128)S(1)} %copy-done.16), channel_id=1, source_target_pairs={{1,4},{2,5},{3,6},{5,8},{6,9},{7,10},{9,12},{10,13},{11,14},{17,20... | collective-permute-start | bytes 1544 | tf_op jit(solution)/shard_map/ppermute | solution.py:22
  38.1 11.5 %copy-start = (f32[4,32,32,128]{3,2,1,0:T(8,128)S(1)}, f32[4,32,32,128]{3,2,1,0:T(8,128)}, u32[]{:S(2)}) copy-start(f32[4,32,32,128]{3,2,1,0:T(8,128)} %residual.2) | copy-start | bytes 6291460
  38.1 1.7 %copy-start.15 = (f32[1,128]{1,0:T(1,128)}, f32[1,128]{1,0:T(1,128)S(1)}, u32[]{:S(2)}) copy-start(f32[1,128]{1,0:T(1,128)S(1)} %collective-permute-done.5.refs_8_) | copy-start | bytes 1540
  38.1 47.9 %collective-permute-start.6 = (f32[32,4,32,128]{3,0,2,1:T(8,128)}, f32[32,4,32,128]{3,0,2,1:T(8,128)}, u32[]{:S(2)}, u32[]{:S(2)}) collective-permute-start(f32[32,4,32,128]{3,0,2,1:T(8,128)} %fusion.6), channel_id=1, source_target_pairs={{0,16},{16,0},{1,17},{17,1},{2,18},{18,2},{3,19},{19,3},{4,20},{20... | collective-permute-start | bytes 6291464 | tf_op jit(solution)/shard_map/ppermute | solution.py:241
  39.7 0.6 copy-start.9
  39.7 0.6 copy-start.7
  39.8 0.6 copy-start.4
  40.4 0.6 copy-start.3
  58.4 27.1 %collective-permute-start.7 = (f32[32,1264]{1,0:T(8,128)S(1)}, f32[32,1264]{1,0:T(8,128)S(1)}, u32[]{:S(2)}, u32[]{:S(2)}) collective-permute-start(f32[32,1264]{1,0:T(8,128)S(1)} %pad_maximum_fusion.2), channel_id=1, source_target_pairs={{0,16},{16,0},{1,17},{17,1},{2,18},{18,2},{3,19},{19,3},{4,20},{20... | collective-permute-start | bytes 485384 | tf_op jit(solution)/shard_map/ppermute | solution.py:262
  61.5 24.5 %copy-start.5 = (f32[32,4,32]{0,2,1:T(8,128)S(1)}, f32[32,4,32]{0,2,1:T(8,128)}, u32[]{:S(2)}) copy-start(f32[32,4,32]{0,2,1:T(8,128)} %copy.72) | copy-start | bytes 49156
  61.5 24.5 %copy-start.6 = (f32[32,4,32]{0,2,1:T(8,128)S(1)}, f32[32,4,32]{0,2,1:T(8,128)}, u32[]{:S(2)}) copy-start(f32[32,4,32]{0,2,1:T(8,128)} %copy.73) | copy-start | bytes 49156
  94.8 5.9 %copy-start.11 = (f32[64]{0:T(128)S(1)}, f32[64]{0:T(128)}, u32[]{:S(2)}) copy-start(f32[64]{0:T(128)} %fusion.29) | copy-start | bytes 772
  97.7 37.1 %copy-start.13 = (f32[32,1]{0,1:T(1,128)S(1)}, f32[32,1]{0,1:T(1,128)}, u32[]{:S(2)}) copy-start(f32[32,1]{0,1:T(1,128)} %param.15) | copy-start | bytes 388
  97.7 37.2 %copy-start.2 = (f32[32,4,32,128]{3,0,2,1:T(8,128)S(1)}, f32[32,4,32,128]{3,0,2,1:T(8,128)}, u32[]{:S(2)}) copy-start(f32[32,4,32,128]{3,0,2,1:T(8,128)} %get-tuple-element.33) | copy-start | bytes 6291460
  100.8 19.7 %collective-permute-start.9 = (f32[64,5,128]{2,1,0:T(8,128)S(1)}, f32[64,5,128]{2,1,0:T(8,128)S(1)}, u32[]{:S(2)}, u32[]{:S(2)}) collective-permute-start(f32[64,5,128]{2,1,0:T(8,128)S(1)} %pad_maximum_fusion.1), channel_id=1, source_target_pairs={{0,4},{4,8},{8,12},{1,5},{5,9},{9,13},{2,6},{6,10},{10,14},{3,7},{... | collective-permute-start | bytes 491528 | tf_op jit(solution)/shard_map/ppermute | solution.py:285
  107.4 17.9 %collective-permute-start.10 = (f32[64,5,128]{2,1,0:T(8,128)S(1)}, f32[64,5,128]{2,1,0:T(8,128)S(1)}, u32[]{:S(2)}, u32[]{:S(2)}) collective-permute-start(f32[64,5,128]{2,1,0:T(8,128)S(1)} %pad_maximum_fusion.1), channel_id=1, source_target_pairs={{0,8},{4,12},{1,9},{5,13},{2,10},{6,14},{3,11},{7,15},{16,24},{20,... | collective-permute-start | bytes 491528 | tf_op jit(solution)/shard_map/ppermute | solution.py:285
  118.6 9.8 %collective-permute-start.11 = (f32[64,5,128]{2,1,0:T(8,128)S(1)}, f32[64,5,128]{2,1,0:T(8,128)}, u32[]{:S(2)}, u32[]{:S(2)}) collective-permute-start(f32[64,5,128]{2,1,0:T(8,128)S(1)} %pad_maximum_fusion.1), channel_id=1, source_target_pairs={{0,12},{1,13},{2,14},{3,15},{16,28},{17,29},{18,30},{19,31}} | collective-permute-start | bytes 491528 | tf_op jit(solution)/shard_map/ppermute | solution.py:285
  130.4 4.3 %collective-permute-start.12 = (f32[32,4,128]{2,1,0:T(4,128)S(1)}, f32[32,4,128]{2,1,0:T(4,128)S(1)}, u32[]{:S(2)}, u32[]{:S(2)}) collective-permute-start(f32[32,4,128]{2,1,0:T(4,128)S(1)} %slice.154), channel_id=1, source_target_pairs={{0,16},{16,0},{1,17},{17,1},{2,18},{18,2},{3,19},{19,3},{4,20},{20... | collective-permute-start | bytes 196616 | tf_op jit(solution)/shard_map/ppermute | solution.py:290

commit v8 on v6

--- a/solution.py
+++ b/solution.py
@@ -54,19 +54,16 @@
     c127_ref[pl.ds(nx, 8), :] = jnp.zeros((8, ny), jnp.float32)
     c127_ref[pl.ds(nx, 1), :] = col_to_row(regf[:, ny - 1:ny], ix, iy)
 
-    def body(s, carry):
-        acc127, acc0 = carry
+    acc127 = jnp.zeros((nx, ny), jnp.float32)
+    acc0 = jnp.zeros((nx, ny), jnp.float32)
+    for s in range(n_s):
         for p in range(planes):
             t = s * planes + p
             a = a_ref[s, p]
             xlo_ref[pl.ds(p * n_s + s, 1), :] = a[nx - 1:nx, :]
             xhi_ref[pl.ds(p * n_s + s, 1), :] = a[0:1, :]
-            acc127 = jnp.where(iy == t, pltpu.roll(a, lax.rem(t + 1, ny), 1), acc127)
-            acc0 = jnp.where(iy == t, pltpu.roll(a, t, 1), acc0)
-        return acc127, acc0
-
-    zero = jnp.zeros((nx, ny), jnp.float32)
-    acc127, acc0 = lax.fori_loop(0, n_s, body, (zero, zero))
+            acc127 = jnp.where(iy == t, pltpu.roll(a, (t + 1) % ny, 1), acc127)
+            acc0 = jnp.where(iy == t, a if t == 0 else pltpu.roll(a, t, 1), acc0)
     c127_ref[pl.ds(0, nx), :] = acc127
     c0_ref[...] = acc0
     c1_ref[...] = acc0[nx - 1:nx, :]

time: 99.1 us -> 97 us (0.979)
  Pallas kernels: 14.1 us -> 12 us
    pallas_call x1, Pallas kernels: 5.6 us -> 3.43 us  [edges(): pl.pallas_call(edges_kernel, in_specs=[vmem, vmem], out_specs=[vmem] * 6,...]
  transfers between devices with their start and end apart: 12 -> 12, of which waited for: 4 -> 4; matrix products, arithmetic and copies ran while one was open for 21% -> 22% of each run, Pallas kernels for 9% -> 9%
where the time goes in v8:
time: 97 us; the launch traced here: 95.4 us
  waiting for transfers between devices  30.9 us (32%)
  starting transfers between devices  23.1 us (24%)
  matrix products  21.7 us (22%)
  Pallas kernels  12 us (12%)
  other arithmetic  4.55 us (5%)
  local copies, waits for them, and re-layouts  2.8 us (3%)
    ppermute x1, waiting for transfers between devices, local(): lax.ppermute(carried[d], 'tm', [(i, (i + d) % n_tm) for i in range(n_tm)])  20.5 us
    ppermute x6, starting transfers between devices, shifted(): return lax.ppermute(block, axes, route)  14.9 us
    dot_general x2, matrix products, local(): jnp.einsum('qs,psxy->qpxy', tabs[d], resid, precision=lax.Precision.HIGHEST)  9.11 us
    pallas_call x1, Pallas kernels, residual(): pl.pallas_call(functools.partial(residual_kernel, kinds, levels), grid=(n...  8.54 us
    dot_general x2, matrix products, local(): jnp.einsum('qb,qpby->qpy', row_last[d], parts[d], precision=lax.Precision...  7.55 us
    ppermute x3, waiting for transfers between devices, local(): got = lax.ppermute(msg_tail, 'gx', [(i, i + d) for i in range(n_gx - d)])  7.11 us
    dot_general x1, matrix products, local(): jnp.einsum('qab,qpby->qpay', inverse, spectrum, precision=lax.Precision.H...  5.02 us
    ppermute x3, starting transfers between devices, local(): got = lax.ppermute(msg_tail, 'gx', [(i, i + d) for i in range(n_gx - d)])  4.59 us
  transfers between devices with their start and end apart: 12, of which 4 were waited for; matrix products, arithmetic and copies ran while one was open for 22% of the time, Pallas kernels for 9%

profile of v8, /device:TPU:12, one launch (start us, length us, event | category | flops | bytes accessed | tf_op | source)
XLA Modules:
  0.0 95.4 jit_solution(2597086126310537111)
XLA Ops:
  0.0 3.4 %halo_edges.1 = (f32[136,128]{1,0:T(8,128)}, f32[128,128]{1,0:T(8,128)}, f32[40,128]{1,0:T(8,128)}, f32[32,128]{1,0:T(8,128)}, f32[1,128]{1,0:T(1,128)}, /*index=5*/f32[1,128]{1,0:T(1,128)}) custom-call(f32[32,4,32,128]{3,2,1,0:T(8,128)} %a_ref.3, s32[32,128]{1,0:T(8,128)} %reg_ref.3), custom_call_target="tpu_custom_call" | custom-call | tf_op jit(solution)/shard_map/halo_edges/pallas_call | solution.py:86
  3.4 2.9 %collective-permute-start.4 = (f32[1,128]{1,0:T(1,128)}, f32[1,128]{1,0:T(1,128)S(1)}, u32[]{:S(2)}, u32[]{:S(2)}) collective-permute-start(f32[1,128]{1,0:T(1,128)} %get-tuple-element.15), channel_id=1, source_target_pairs={{4,1},{5,2},{6,3},{8,5},{9,6},{10,7},{12,9},{13,10},{14,11},{20,17... | collective-permute-start | bytes 1544 | tf_op jit(solution)/shard_map/ppermute | solution.py:22
  6.3 2.4 %collective-permute-start.3 = (f32[32,128]{1,0:T(8,128)}, f32[32,128]{1,0:T(8,128)S(1)}, u32[]{:S(2)}, u32[]{:S(2)}) collective-permute-start(f32[32,128]{1,0:T(8,128)} %get-tuple-element.14.own0_ref), channel_id=1, source_target_pairs={{1,0},{2,1},{3,2},{5,4},{6,5},{7,6},{9,8},{10,9},{11,10},{13,12},{... | collective-permute-start | bytes 49160 | tf_op jit(solution)/shard_map/ppermute | solution.py:22
  8.7 3.5 %collective-permute-start.2 = (f32[40,128]{1,0:T(8,128)}, f32[40,128]{1,0:T(8,128)S(1)}, u32[]{:S(2)}, u32[]{:S(2)}) collective-permute-start(f32[40,128]{1,0:T(8,128)} %get-tuple-element.13), channel_id=1, source_target_pairs={{0,1},{1,2},{2,3},{4,5},{5,6},{6,7},{8,9},{9,10},{10,11},{12,13},{... | collective-permute-start | bytes 61448 | tf_op jit(solution)/shard_map/ppermute | solution.py:22
  12.2 2.2 %collective-permute-start.1 = (f32[128,128]{1,0:T(8,128)}, f32[128,128]{1,0:T(8,128)S(1)}, u32[]{:S(2)}, u32[]{:S(2)}) collective-permute-start(f32[128,128]{1,0:T(8,128)} %get-tuple-element.12), channel_id=1, source_target_pairs={{4,0},{5,1},{6,2},{7,3},{8,4},{9,5},{10,6},{11,7},{12,8},{13,9},{1... | collective-permute-start | bytes 196616 | tf_op jit(solution)/shard_map/ppermute | solution.py:22
  14.4 2.1 %collective-permute-start = (f32[136,128]{1,0:T(8,128)}, f32[136,128]{1,0:T(8,128)S(1)}, u32[]{:S(2)}, u32[]{:S(2)}) collective-permute-start(f32[136,128]{1,0:T(8,128)} %get-tuple-element.11), channel_id=1, source_target_pairs={{0,4},{1,5},{2,6},{3,7},{4,8},{5,9},{6,10},{7,11},{8,12},{9,13},{1... | collective-permute-start | bytes 208904 | tf_op jit(solution)/shard_map/ppermute | solution.py:22
  16.5 0.3 slice_reduce_fusion
  17.1 1.9 %collective-permute-start.5 = (f32[1,128]{1,0:T(1,128)}, f32[1,128]{1,0:T(1,128)S(1)}, u32[]{:S(2)}, u32[]{:S(2)}) collective-permute-start(f32[1,128]{1,0:T(1,128)} %get-tuple-element.16), channel_id=1, source_target_pairs={{1,4},{2,5},{3,6},{5,8},{6,9},{7,10},{9,12},{10,13},{11,14},{17,20... | collective-permute-start | bytes 1544 | tf_op jit(solution)/shard_map/ppermute | solution.py:22
  19.0 0.7 copy.14.relu_ref
  19.7 3.4 %collective-permute-done.5.c1_ref = f32[1,128]{1,0:T(1,128)S(1)} collective-permute-done((f32[1,128]{1,0:T(1,128)}, f32[1,128]{1,0:T(1,128)S(1)}, u32[]{:S(2)}, u32[]{:S(2)}) %collective-permute-start.5) | collective-permute-done | bytes 544 | tf_op jit(solution)/shard_map/ppermute | solution.py:22
  23.1 1.5 %collective-permute-start.7 = (f32[32,33]{1,0:T(8,128)S(1)}, f32[32,33]{1,0:T(8,128)S(1)}, u32[]{:S(2)}, u32[]{:S(2)}) collective-permute-start(f32[32,33]{1,0:T(8,128)S(1)} %pad_maximum_fusion.3), channel_id=1, source_target_pairs={{0,16},{16,0},{1,17},{17,1},{2,18},{18,2},{3,19},{19,3},{4,20},{20... | collective-permute-start | bytes 12680 | tf_op jit(solution)/shard_map/ppermute | solution.py:209
  24.6 0.5 copy-done.5
  25.2 0.6 copy-done.2
  25.9 8.5 %residual.1 = f32[4,32,32,128]{3,2,1,0:T(8,128)} custom-call(f32[32,4,32,128]{3,2,1,0:T(8,128)} %a_ref.3, f32[32,4,32,128]{3,2,1,0:T(8,128)} %src_ref.1, f32[136,128]{1,0:T(8,128)} %copy-done.2, f32[128,128]{1,0:T(8,128)} %copy-done.3, f32[40,128]{1,0:T(8,128)} %copy-done.4, f32[32,128]{1,0:T(8,128)} %copy-done.5, f32[32,128]{1,0:T(8,128)} %get-tuple-element.14.own0_ref, ...), custom_call_target="tpu_custom_call" | custom-call | tf_op jit(solution)/shard_map/residual/pallas_call | solution.py:182
  34.4 6.0 %fusion.6 = f32[32,4,32,128]{3,0,2,1:T(8,128)} fusion(f32[4,32,32,128]{3,2,1,0:T(8,128)} %residual.1, s32[32]{0:T(128)S(1)} %get-tuple-element.17, s32[32]{0:T(128)S(1)} %get-tuple-element.18, pred[32]{0:T(512)(128)(4,1)S(1)} %fusion.61), kind=kOutput, calls=%fused_computation.7 | convolution fusion | flops 201342976 | bytes 4194592 | tf_op jit(solution)/shard_map/qs,psxy->qpxy/dot_general | solution.py:229
  40.4 0.5 collective-permute-start.6
  41.0 0.2 fusion.19
  41.1 4.5 %fusion = f32[32,1,4,128]{3,1,2,0:T(1,128)S(1)} fusion(f32[32,32,1,1]{1,2,3,0:T(1,128)S(1)} %bitcast.51, f32[32,4,32,128]{3,0,2,1:T(8,128)} %fusion.6), kind=kOutput, calls=%fused_computation.1 | convolution fusion | flops 6291456 | bytes 2166784 | tf_op jit(solution)/shard_map/qb,qpby->qpy/dot_general | solution.py:234
  45.6 3.1 %fusion.8 = f32[32,4,32,128]{3,0,2,1:T(8,128)S(1)} fusion(f32[4,32,32,128]{3,2,1,0:T(8,128)S(1)} %copy-done, s32[32]{0:T(128)S(1)} %get-tuple-element.18, s32[32]{0:T(128)S(1)} %add_select_fusion.3, pred[32]{0:T(512)(128)(4,1)S(1)} %fusion.62), kind=kOutput, calls=%fused_computation.9 | convolution fusion | flops 201342976 | bytes 4194592 | tf_op jit(solution)/shard_map/qs,psxy->qpxy/dot_general | solution.py:229
  48.7 3.1 %fusion.2 = f32[32,1,4,128]{3,1,2,0:T(1,128)S(1)} fusion(f32[32,4,32,128]{3,0,2,1:T(8,128)S(1)} %fusion.8, f32[32,32,32]{2,1,0:T(8,128)S(1)} %copy-done.1), kind=kOutput, calls=%fused_computation.3 | convolution fusion | flops 6291456 | bytes 2179072 | tf_op jit(solution)/shard_map/qb,qpby->qpy/dot_general | solution.py:234
  52.0 1.3 %collective-permute-start.9 = (f32[64,5,128]{2,1,0:T(8,128)S(1)}, f32[64,5,128]{2,1,0:T(8,128)S(1)}, u32[]{:S(2)}, u32[]{:S(2)}) collective-permute-start(f32[64,5,128]{2,1,0:T(8,128)S(1)} %pad_maximum_fusion), channel_id=1, source_target_pairs={{0,8},{4,12},{1,9},{5,13},{2,10},{6,14},{3,11},{7,15},{16,24},{20,... | collective-permute-start | bytes 491528 | tf_op jit(solution)/shard_map/ppermute | solution.py:240
  53.3 1.9 %collective-permute-start.8 = (f32[64,5,128]{2,1,0:T(8,128)S(1)}, f32[64,5,128]{2,1,0:T(8,128)S(1)}, u32[]{:S(2)}, u32[]{:S(2)}) collective-permute-start(f32[64,5,128]{2,1,0:T(8,128)S(1)} %pad_maximum_fusion), channel_id=1, source_target_pairs={{0,4},{4,8},{8,12},{1,5},{5,9},{9,13},{2,6},{6,10},{10,14},{3,7},{... | collective-permute-start | bytes 491528 | tf_op jit(solution)/shard_map/ppermute | solution.py:240
  55.2 1.4 %collective-permute-start.10 = (f32[64,5,128]{2,1,0:T(8,128)S(1)}, f32[64,5,128]{2,1,0:T(8,128)}, u32[]{:S(2)}, u32[]{:S(2)}) collective-permute-start(f32[64,5,128]{2,1,0:T(8,128)S(1)} %pad_maximum_fusion), channel_id=1, source_target_pairs={{0,12},{1,13},{2,14},{3,15},{16,28},{17,29},{18,30},{19,31}} | collective-permute-start | bytes 491528 | tf_op jit(solution)/shard_map/ppermute | solution.py:240
  56.6 6.5 %collective-permute-done.9 = f32[64,5,128]{2,1,0:T(8,128)S(1)} collective-permute-done((f32[64,5,128]{2,1,0:T(8,128)S(1)}, f32[64,5,128]{2,1,0:T(8,128)S(1)}, u32[]{:S(2)}, u32[]{:S(2)}) %collective-permute-start.9) | collective-permute-done | bytes 163872 | tf_op jit(solution)/shard_map/ppermute | solution.py:240
  63.1 0.7 collective-permute-done.8
  63.8 1.0 %slice_multiply_fusion = f32[64,1,128]{2,1,0:T(1,128)S(1)} fusion(f32[64,5,128]{2,1,0:T(8,128)} %collective-permute-done.10), kind=kLoop, calls=%fused_computation.21 | loop fusion | flops 8192 | bytes 65536 | tf_op jit(solution)/shard_map/mul | solution.py:241
  64.8 1.1 %fusion.17 = f32[64,4,128]{2,1,0:T(4,128)S(1)} fusion(f32[64,5,128]{2,1,0:T(8,128)S(1)} %collective-permute-done.8, f32[64,5,128]{2,1,0:T(8,128)S(1)} %collective-permute-done.9, f32[64,5,128]{2,1,0:T(8,128)} %collective-permute-done.10, f32[64,128]{1,0:T(8,128)S(1)} %bitcast.50, f32[64,128]{1,0:T(8,128)S(1)} %bitcast.48, f32[64,128]{1,0:T(8,128)S(1)} %bitcast.49, ...), kind=kLoop, calls=%fused_computation.18 | loop fusion | flops 262144 | bytes 622595 | tf_op jit(solution)/shard_map/jit(_where)/select_n | solution.py:242
  65.9 1.6 %collective-permute-start.11 = (f32[32,4,128]{2,1,0:T(4,128)S(1)}, f32[32,4,128]{2,1,0:T(4,128)S(1)}, u32[]{:S(2)}, u32[]{:S(2)}) collective-permute-start(f32[32,4,128]{2,1,0:T(4,128)S(1)} %slice.70), channel_id=1, source_target_pairs={{0,16},{16,0},{1,17},{17,1},{2,18},{18,2},{3,19},{19,3},{4,20},{20... | collective-permute-start | bytes 196616 | tf_op jit(solution)/shard_map/ppermute | solution.py:245
  67.5 0.2 copy.29
  67.7 20.5 %collective-permute-done.11 = f32[32,4,128]{2,1,0:T(4,128)S(1)} collective-permute-done((f32[32,4,128]{2,1,0:T(4,128)S(1)}, f32[32,4,128]{2,1,0:T(4,128)S(1)}, u32[]{:S(2)}, u32[]{:S(2)}) %collective-permute-start.11) | collective-permute-done | bytes 65568 | tf_op jit(solution)/shard_map/ppermute | solution.py:245
  88.3 2.1 %add.95 = f32[32,4,32,128]{3,0,2,1:T(8,128)S(1)} add(f32[32,4,32,128]{3,0,2,1:T(8,128)S(1)} %fusion.8, f32[32,4,32,128]{3,0,2,1:T(8,128)} %collective-permute-done.6) | non-fusion elementwise | flops 524288 | bytes 6291456 | tf_op jit(solution)/shard_map/add | solution.py:249
  90.3 5.0 %bitcast_add_fusion = f32[32,4,32,128]{3,2,1,0:T(8,128)} fusion(f32[32,32]{1,0:T(8,128)S(1)} %bitcast.52, f32[32,4,128]{2,1,0:T(4,128)S(1)} %fusion.18, f32[32,32,32]{2,1,0:T(8,128)S(1)} %copy-done.1, f32[32,4,32,128]{3,0,2,1:T(8,128)S(1)} %add.95), kind=kOutput, calls=%fused_computation | convolution fusion | flops 202375168 | bytes 4395008 | tf_op jit(solution)/shard_map/qab,qpby->qpay/dot_general | solution.py:253
  (40 shorter events, 0.7 us)
Async XLA Ops:
  0.0 16.5 %copy-start.1 = (f32[32,32,32]{2,1,0:T(8,128)S(1)}, f32[32,32,32]{2,1,0:T(8,128)}, u32[]{:S(2)}) copy-start(f32[32,32,32]{2,1,0:T(8,128)} %param.14) | copy-start | bytes 393220
  0.0 16.9 %copy-start.7 = (f32[32,1]{0,1:T(1,128)S(1)}, f32[32,1]{0,1:T(1,128)}, u32[]{:S(2)}) copy-start(f32[32,1]{0,1:T(1,128)} %param.15) | copy-start | bytes 388
  0.0 19.0 %copy-start.6 = (f32[16,8]{0,1:T(8,128)S(1)}, f32[16,8]{0,1:T(8,128)}, u32[]{:S(2)}) copy-start(f32[16,8]{0,1:T(8,128)} %param.12) | copy-start | bytes 1540
  3.4 13.6 %collective-permute-start.4 = (f32[1,128]{1,0:T(1,128)}, f32[1,128]{1,0:T(1,128)S(1)}, u32[]{:S(2)}, u32[]{:S(2)}) collective-permute-start(f32[1,128]{1,0:T(1,128)} %get-tuple-element.15), channel_id=1, source_target_pairs={{4,1},{5,2},{6,3},{8,5},{9,6},{10,7},{12,9},{13,10},{14,11},{20,17... | collective-permute-start | bytes 1544 | tf_op jit(solution)/shard_map/ppermute | solution.py:22
  6.3 18.3 %collective-permute-start.3 = (f32[32,128]{1,0:T(8,128)}, f32[32,128]{1,0:T(8,128)S(1)}, u32[]{:S(2)}, u32[]{:S(2)}) collective-permute-start(f32[32,128]{1,0:T(8,128)} %get-tuple-element.14.own0_ref), channel_id=1, source_target_pairs={{1,0},{2,1},{3,2},{5,4},{6,5},{7,6},{9,8},{10,9},{11,10},{13,12},{... | collective-permute-start | bytes 49160 | tf_op jit(solution)/shard_map/ppermute | solution.py:22
  8.7 15.9 %collective-permute-start.2 = (f32[40,128]{1,0:T(8,128)}, f32[40,128]{1,0:T(8,128)S(1)}, u32[]{:S(2)}, u32[]{:S(2)}) collective-permute-start(f32[40,128]{1,0:T(8,128)} %get-tuple-element.13), channel_id=1, source_target_pairs={{0,1},{1,2},{2,3},{4,5},{5,6},{6,7},{8,9},{9,10},{10,11},{12,13},{... | collective-permute-start | bytes 61448 | tf_op jit(solution)/shard_map/ppermute | solution.py:22
  12.2 12.4 %collective-permute-start.1 = (f32[128,128]{1,0:T(8,128)}, f32[128,128]{1,0:T(8,128)S(1)}, u32[]{:S(2)}, u32[]{:S(2)}) collective-permute-start(f32[128,128]{1,0:T(8,128)} %get-tuple-element.12), channel_id=1, source_target_pairs={{4,0},{5,1},{6,2},{7,3},{8,4},{9,5},{10,6},{11,7},{12,8},{13,9},{1... | collective-permute-start | bytes 196616 | tf_op jit(solution)/shard_map/ppermute | solution.py:22
  14.4 10.2 %collective-permute-start = (f32[136,128]{1,0:T(8,128)}, f32[136,128]{1,0:T(8,128)S(1)}, u32[]{:S(2)}, u32[]{:S(2)}) collective-permute-start(f32[136,128]{1,0:T(8,128)} %get-tuple-element.11), channel_id=1, source_target_pairs={{0,4},{1,5},{2,6},{3,7},{4,8},{5,9},{6,10},{7,11},{8,12},{9,13},{1... | collective-permute-start | bytes 208904 | tf_op jit(solution)/shard_map/ppermute | solution.py:22
  17.1 7.5 %copy-start.8 = (f32[1,128]{1,0:T(1,128)}, f32[1,128]{1,0:T(1,128)S(1)}, u32[]{:S(2)}) copy-start(f32[1,128]{1,0:T(1,128)S(1)} %collective-permute-done.4.c2_ref) | copy-start | bytes 1540
  17.1 6.0 %collective-permute-start.5 = (f32[1,128]{1,0:T(1,128)}, f32[1,128]{1,0:T(1,128)S(1)}, u32[]{:S(2)}, u32[]{:S(2)}) collective-permute-start(f32[1,128]{1,0:T(1,128)} %get-tuple-element.16), channel_id=1, source_target_pairs={{1,4},{2,5},{3,6},{5,8},{6,9},{7,10},{9,12},{10,13},{11,14},{17,20... | collective-permute-start | bytes 1544 | tf_op jit(solution)/shard_map/ppermute | solution.py:22
  23.1 1.6 %copy-start.9 = (f32[1,128]{1,0:T(1,128)}, f32[1,128]{1,0:T(1,128)S(1)}, u32[]{:S(2)}) copy-start(f32[1,128]{1,0:T(1,128)S(1)} %collective-permute-done.5.c1_ref) | copy-start | bytes 1540
  23.1 17.9 %collective-permute-start.7 = (f32[32,33]{1,0:T(8,128)S(1)}, f32[32,33]{1,0:T(8,128)S(1)}, u32[]{:S(2)}, u32[]{:S(2)}) collective-permute-start(f32[32,33]{1,0:T(8,128)S(1)} %pad_maximum_fusion.3), channel_id=1, source_target_pairs={{0,16},{16,0},{1,17},{17,1},{2,18},{18,2},{3,19},{19,3},{4,20},{20... | collective-permute-start | bytes 12680 | tf_op jit(solution)/shard_map/ppermute | solution.py:209
  24.6 0.6 copy-start.5
  24.6 0.6 copy-start.4
  24.6 0.6 copy-start.3
  25.2 0.6 copy-start.2
  40.4 5.2 %copy-start = (f32[4,32,32,128]{3,2,1,0:T(8,128)S(1)}, f32[4,32,32,128]{3,2,1,0:T(8,128)}, u32[]{:S(2)}) copy-start(f32[4,32,32,128]{3,2,1,0:T(8,128)} %residual.1) | copy-start | bytes 6291460
  40.4 47.9 %collective-permute-start.6 = (f32[32,4,32,128]{3,0,2,1:T(8,128)}, f32[32,4,32,128]{3,0,2,1:T(8,128)}, u32[]{:S(2)}, u32[]{:S(2)}) collective-permute-start(f32[32,4,32,128]{3,0,2,1:T(8,128)} %fusion.6), channel_id=1, source_target_pairs={{0,16},{16,0},{1,17},{17,1},{2,18},{18,2},{3,19},{19,3},{4,20},{20... | collective-permute-start | bytes 6291464 | tf_op jit(solution)/shard_map/ppermute | solution.py:231
  52.0 11.1 %collective-permute-start.9 = (f32[64,5,128]{2,1,0:T(8,128)S(1)}, f32[64,5,128]{2,1,0:T(8,128)S(1)}, u32[]{:S(2)}, u32[]{:S(2)}) collective-permute-start(f32[64,5,128]{2,1,0:T(8,128)S(1)} %pad_maximum_fusion), channel_id=1, source_target_pairs={{0,8},{4,12},{1,9},{5,13},{2,10},{6,14},{3,11},{7,15},{16,24},{20,... | collective-permute-start | bytes 491528 | tf_op jit(solution)/shard_map/ppermute | solution.py:240
  53.3 10.5 %collective-permute-start.8 = (f32[64,5,128]{2,1,0:T(8,128)S(1)}, f32[64,5,128]{2,1,0:T(8,128)S(1)}, u32[]{:S(2)}, u32[]{:S(2)}) collective-permute-start(f32[64,5,128]{2,1,0:T(8,128)S(1)} %pad_maximum_fusion), channel_id=1, source_target_pairs={{0,4},{4,8},{8,12},{1,5},{5,9},{9,13},{2,6},{6,10},{10,14},{3,7},{... | collective-permute-start | bytes 491528 | tf_op jit(solution)/shard_map/ppermute | solution.py:240
  55.2 8.6 %collective-permute-start.10 = (f32[64,5,128]{2,1,0:T(8,128)S(1)}, f32[64,5,128]{2,1,0:T(8,128)}, u32[]{:S(2)}, u32[]{:S(2)}) collective-permute-start(f32[64,5,128]{2,1,0:T(8,128)S(1)} %pad_maximum_fusion), channel_id=1, source_target_pairs={{0,12},{1,13},{2,14},{3,15},{16,28},{17,29},{18,30},{19,31}} | collective-permute-start | bytes 491528 | tf_op jit(solution)/shard_map/ppermute | solution.py:240
  65.9 22.3 %collective-permute-start.11 = (f32[32,4,128]{2,1,0:T(4,128)S(1)}, f32[32,4,128]{2,1,0:T(4,128)S(1)}, u32[]{:S(2)}, u32[]{:S(2)}) collective-permute-start(f32[32,4,128]{2,1,0:T(4,128)S(1)} %slice.70), channel_id=1, source_target_pairs={{0,16},{16,0},{1,17},{17,1},{2,18},{18,2},{3,19},{19,3},{4,20},{20... | collective-permute-start | bytes 196616 | tf_op jit(solution)/shard_map/ppermute | solution.py:245

commit v9 on v8

--- a/solution.py
+++ b/solution.py
@@ -226,12 +226,12 @@
         for d in range(n_tm)
     ]
     row_last = info_all[:, :cells_x].reshape(n_tm, q_dev, cells_x)
-    parts = [jnp.einsum("qs,psxy->qpxy", tabs[d], resid, precision=lax.Precision.HIGHEST) for d in range(n_tm)]
+    parts = [jnp.einsum("qs,psxy->qpxy", tabs[d], resid, precision=lax.Precision.HIGH) for d in range(n_tm)]
     got_parts = [
         lax.ppermute(parts[d], "tm", [(i, (i + d) % n_tm) for i in range(n_tm)]) for d in range(1, n_tm)
     ]
     tails = jnp.concatenate(
-        [jnp.einsum("qb,qpby->qpy", row_last[d], parts[d], precision=lax.Precision.HIGHEST) for d in range(n_tm)],
+        [jnp.einsum("qb,qpby->qpy", row_last[d], parts[d], precision=lax.Precision.HIGH) for d in range(n_tm)],
         axis=0,
     )
     msg_tail = jnp.concatenate([tails, jnp.broadcast_to(gain_all[:, None, None], (n_tm * q_dev, 1, cells_y))], axis=1)
@@ -250,7 +250,7 @@
     carried_own = carried[0]
     for got in got_carried:
         carried_own = carried_own + got
-    solved = jnp.einsum("qab,qpby->qpay", inverse, spectrum, precision=lax.Precision.HIGHEST)
+    solved = jnp.einsum("qab,qpby->qpay", inverse, spectrum, precision=lax.Precision.HIGH)
     injected = transmit[:, 0][:, None, None] * carried_own
     return solved + injected[:, :, None, :] * inverse[:, :, 0][:, None, :, None]
 

time: 97 us -> 95.4 us (0.984)
  matrix products: 21.7 us -> 18.1 us
  waiting for transfers between devices: 30.9 us -> 32.9 us
    ppermute x1, waiting for transfers between devices: 20.5 us -> 22.4 us  [local(): lax.ppermute(carried[d], 'tm', [(i, (i + d) % n_tm) for i in range(n_tm)])]
    dot_general x2, matrix products: 9.11 us -> 7.4 us  [local(): jnp.einsum('qs,psxy->qpxy', tabs[d], resid, precision=lax.Precision.HIGH)]
    dot_general x2, matrix products: 7.55 us -> 6.47 us  [local(): jnp.einsum('qb,qpby->qpy', row_last[d], parts[d], precision=lax.Precision...]
  transfers between devices with their start and end apart: 12 -> 12, of which waited for: 4 -> 4; matrix products, arithmetic and copies ran while one was open for 22% -> 19% of each run, Pallas kernels for 9% -> 9%
where the time goes in v9:
time: 95.4 us; the launch traced here: 93.8 us
  waiting for transfers between devices  32.9 us (34%)
  starting transfers between devices  23.1 us (24%)
  matrix products  18.1 us (19%)
  Pallas kernels  12 us (13%)
  other arithmetic  4.55 us (5%)
  local copies, waits for them, and re-layouts  2.8 us (3%)
    ppermute x1, waiting for transfers between devices, local(): lax.ppermute(carried[d], 'tm', [(i, (i + d) % n_tm) for i in range(n_tm)])  22.4 us
    ppermute x6, starting transfers between devices, shifted(): return lax.ppermute(block, axes, route)  14.9 us
    pallas_call x1, Pallas kernels, residual(): pl.pallas_call(functools.partial(residual_kernel, kinds, levels), grid=(n...  8.54 us
    dot_general x2, matrix products, local(): jnp.einsum('qs,psxy->qpxy', tabs[d], resid, precision=lax.Precision.HIGH)  7.4 us
    ppermute x3, waiting for transfers between devices, local(): got = lax.ppermute(msg_tail, 'gx', [(i, i + d) for i in range(n_gx - d)])  7.11 us
    dot_general x2, matrix products, local(): jnp.einsum('qb,qpby->qpy', row_last[d], parts[d], precision=lax.Precision...  6.47 us
    ppermute x3, starting transfers between devices, local(): got = lax.ppermute(msg_tail, 'gx', [(i, i + d) for i in range(n_gx - d)])  4.59 us
    dot_general x1, matrix products, local(): jnp.einsum('qab,qpby->qpay', inverse, spectrum, precision=lax.Precision.H...  4.25 us
  transfers between devices with their start and end apart: 12, of which 4 were waited for; matrix products, arithmetic and copies ran while one was open for 19% of the time, Pallas kernels for 9%

profile of v9, /device:TPU:12, one launch (start us, length us, event | category | flops | bytes accessed | tf_op | source)
XLA Modules:
  0.0 93.8 jit_solution(15390909732079754818)
XLA Ops:
  0.0 3.4 %halo_edges.1 = (f32[136,128]{1,0:T(8,128)}, f32[128,128]{1,0:T(8,128)}, f32[40,128]{1,0:T(8,128)}, f32[32,128]{1,0:T(8,128)}, f32[1,128]{1,0:T(1,128)}, /*index=5*/f32[1,128]{1,0:T(1,128)}) custom-call(f32[32,4,32,128]{3,2,1,0:T(8,128)} %a_ref.3, s32[32,128]{1,0:T(8,128)} %reg_ref.3), custom_call_target="tpu_custom_call" | custom-call | tf_op jit(solution)/shard_map/halo_edges/pallas_call | solution.py:86
  3.4 2.9 %collective-permute-start.4 = (f32[1,128]{1,0:T(1,128)}, f32[1,128]{1,0:T(1,128)S(1)}, u32[]{:S(2)}, u32[]{:S(2)}) collective-permute-start(f32[1,128]{1,0:T(1,128)} %get-tuple-element.15), channel_id=1, source_target_pairs={{4,1},{5,2},{6,3},{8,5},{9,6},{10,7},{12,9},{13,10},{14,11},{20,17... | collective-permute-start | bytes 1544 | tf_op jit(solution)/shard_map/ppermute | solution.py:22
  6.3 2.4 %collective-permute-start.3 = (f32[32,128]{1,0:T(8,128)}, f32[32,128]{1,0:T(8,128)S(1)}, u32[]{:S(2)}, u32[]{:S(2)}) collective-permute-start(f32[32,128]{1,0:T(8,128)} %get-tuple-element.14.own0_ref), channel_id=1, source_target_pairs={{1,0},{2,1},{3,2},{5,4},{6,5},{7,6},{9,8},{10,9},{11,10},{13,12},{... | collective-permute-start | bytes 49160 | tf_op jit(solution)/shard_map/ppermute | solution.py:22
  8.7 3.5 %collective-permute-start.2 = (f32[40,128]{1,0:T(8,128)}, f32[40,128]{1,0:T(8,128)S(1)}, u32[]{:S(2)}, u32[]{:S(2)}) collective-permute-start(f32[40,128]{1,0:T(8,128)} %get-tuple-element.13), channel_id=1, source_target_pairs={{0,1},{1,2},{2,3},{4,5},{5,6},{6,7},{8,9},{9,10},{10,11},{12,13},{... | collective-permute-start | bytes 61448 | tf_op jit(solution)/shard_map/ppermute | solution.py:22
  12.2 2.2 %collective-permute-start.1 = (f32[128,128]{1,0:T(8,128)}, f32[128,128]{1,0:T(8,128)S(1)}, u32[]{:S(2)}, u32[]{:S(2)}) collective-permute-start(f32[128,128]{1,0:T(8,128)} %get-tuple-element.12), channel_id=1, source_target_pairs={{4,0},{5,1},{6,2},{7,3},{8,4},{9,5},{10,6},{11,7},{12,8},{13,9},{1... | collective-permute-start | bytes 196616 | tf_op jit(solution)/shard_map/ppermute | solution.py:22
  14.4 2.1 %collective-permute-start = (f32[136,128]{1,0:T(8,128)}, f32[136,128]{1,0:T(8,128)S(1)}, u32[]{:S(2)}, u32[]{:S(2)}) collective-permute-start(f32[136,128]{1,0:T(8,128)} %get-tuple-element.11), channel_id=1, source_target_pairs={{0,4},{1,5},{2,6},{3,7},{4,8},{5,9},{6,10},{7,11},{8,12},{9,13},{1... | collective-permute-start | bytes 208904 | tf_op jit(solution)/shard_map/ppermute | solution.py:22
  16.5 0.3 slice_reduce_fusion
  17.1 1.9 %collective-permute-start.5 = (f32[1,128]{1,0:T(1,128)}, f32[1,128]{1,0:T(1,128)S(1)}, u32[]{:S(2)}, u32[]{:S(2)}) collective-permute-start(f32[1,128]{1,0:T(1,128)} %get-tuple-element.16), channel_id=1, source_target_pairs={{1,4},{2,5},{3,6},{5,8},{6,9},{7,10},{9,12},{10,13},{11,14},{17,20... | collective-permute-start | bytes 1544 | tf_op jit(solution)/shard_map/ppermute | solution.py:22
  19.0 0.7 copy.14.relu_ref
  19.7 3.4 %collective-permute-done.5.c1_ref = f32[1,128]{1,0:T(1,128)S(1)} collective-permute-done((f32[1,128]{1,0:T(1,128)}, f32[1,128]{1,0:T(1,128)S(1)}, u32[]{:S(2)}, u32[]{:S(2)}) %collective-permute-start.5) | collective-permute-done | bytes 544 | tf_op jit(solution)/shard_map/ppermute | solution.py:22
  23.1 1.5 %collective-permute-start.7 = (f32[32,33]{1,0:T(8,128)S(1)}, f32[32,33]{1,0:T(8,128)S(1)}, u32[]{:S(2)}, u32[]{:S(2)}) collective-permute-start(f32[32,33]{1,0:T(8,128)S(1)} %pad_maximum_fusion.3), channel_id=1, source_target_pairs={{0,16},{16,0},{1,17},{17,1},{2,18},{18,2},{3,19},{19,3},{4,20},{20... | collective-permute-start | bytes 12680 | tf_op jit(solution)/shard_map/ppermute | solution.py:209
  24.6 0.5 copy-done.5
  25.2 0.6 copy-done.2
  25.9 8.5 %residual.1 = f32[4,32,32,128]{3,2,1,0:T(8,128)} custom-call(f32[32,4,32,128]{3,2,1,0:T(8,128)} %a_ref.3, f32[32,4,32,128]{3,2,1,0:T(8,128)} %src_ref.1, f32[136,128]{1,0:T(8,128)} %copy-done.2, f32[128,128]{1,0:T(8,128)} %copy-done.3, f32[40,128]{1,0:T(8,128)} %copy-done.4, f32[32,128]{1,0:T(8,128)} %copy-done.5, f32[32,128]{1,0:T(8,128)} %get-tuple-element.14.own0_ref, ...), custom_call_target="tpu_custom_call" | custom-call | tf_op jit(solution)/shard_map/residual/pallas_call | solution.py:182
  34.4 5.2 %fusion.6 = f32[32,4,32,128]{3,0,2,1:T(8,128)} fusion(f32[4,32,32,128]{3,2,1,0:T(8,128)} %residual.1, s32[32]{0:T(128)S(1)} %get-tuple-element.17, s32[32]{0:T(128)S(1)} %get-tuple-element.18, pred[32]{0:T(512)(128)(4,1)S(1)} %fusion.61), kind=kOutput, calls=%fused_computation.7 | convolution fusion | flops 100679680 | bytes 4194592 | tf_op jit(solution)/shard_map/qs,psxy->qpxy/dot_general | solution.py:229
  39.6 0.5 collective-permute-start.6
  40.1 0.2 fusion.19
  40.3 4.0 %fusion = f32[32,1,4,128]{3,1,2,0:T(1,128)S(1)} fusion(f32[32,32,1,1]{1,2,3,0:T(1,128)S(1)} %bitcast.51, f32[32,4,32,128]{3,0,2,1:T(8,128)} %fusion.6), kind=kOutput, calls=%fused_computation.1 | convolution fusion | flops 3145728 | bytes 2166784 | tf_op jit(solution)/shard_map/qb,qpby->qpy/dot_general | solution.py:234
  44.3 2.2 %fusion.8 = f32[32,4,32,128]{3,0,2,1:T(8,128)S(1)} fusion(f32[4,32,32,128]{3,2,1,0:T(8,128)S(1)} %copy-done, s32[32]{0:T(128)S(1)} %get-tuple-element.18, s32[32]{0:T(128)S(1)} %add_select_fusion.3, pred[32]{0:T(512)(128)(4,1)S(1)} %fusion.62), kind=kOutput, calls=%fused_computation.9 | convolution fusion | flops 100679680 | bytes 4194592 | tf_op jit(solution)/shard_map/qs,psxy->qpxy/dot_general | solution.py:229
  46.6 2.4 %fusion.2 = f32[32,1,4,128]{3,1,2,0:T(1,128)S(1)} fusion(f32[32,4,32,128]{3,0,2,1:T(8,128)S(1)} %fusion.8, f32[32,32,32]{2,1,0:T(8,128)S(1)} %copy-done.1), kind=kOutput, calls=%fused_computation.3 | convolution fusion | flops 3145728 | bytes 2179072 | tf_op jit(solution)/shard_map/qb,qpby->qpy/dot_general | solution.py:234
  49.2 1.3 %collective-permute-start.9 = (f32[64,5,128]{2,1,0:T(8,128)S(1)}, f32[64,5,128]{2,1,0:T(8,128)S(1)}, u32[]{:S(2)}, u32[]{:S(2)}) collective-permute-start(f32[64,5,128]{2,1,0:T(8,128)S(1)} %pad_maximum_fusion), channel_id=1, source_target_pairs={{0,8},{4,12},{1,9},{5,13},{2,10},{6,14},{3,11},{7,15},{16,24},{20,... | collective-permute-start | bytes 491528 | tf_op jit(solution)/shard_map/ppermute | solution.py:240
  50.5 1.9 %collective-permute-start.8 = (f32[64,5,128]{2,1,0:T(8,128)S(1)}, f32[64,5,128]{2,1,0:T(8,128)S(1)}, u32[]{:S(2)}, u32[]{:S(2)}) collective-permute-start(f32[64,5,128]{2,1,0:T(8,128)S(1)} %pad_maximum_fusion), channel_id=1, source_target_pairs={{0,4},{4,8},{8,12},{1,5},{5,9},{9,13},{2,6},{6,10},{10,14},{3,7},{... | collective-permute-start | bytes 491528 | tf_op jit(solution)/shard_map/ppermute | solution.py:240
  52.4 1.4 %collective-permute-start.10 = (f32[64,5,128]{2,1,0:T(8,128)S(1)}, f32[64,5,128]{2,1,0:T(8,128)}, u32[]{:S(2)}, u32[]{:S(2)}) collective-permute-start(f32[64,5,128]{2,1,0:T(8,128)S(1)} %pad_maximum_fusion), channel_id=1, source_target_pairs={{0,12},{1,13},{2,14},{3,15},{16,28},{17,29},{18,30},{19,31}} | collective-permute-start | bytes 491528 | tf_op jit(solution)/shard_map/ppermute | solution.py:240
  53.8 6.4 %collective-permute-done.9 = f32[64,5,128]{2,1,0:T(8,128)S(1)} collective-permute-done((f32[64,5,128]{2,1,0:T(8,128)S(1)}, f32[64,5,128]{2,1,0:T(8,128)S(1)}, u32[]{:S(2)}, u32[]{:S(2)}) %collective-permute-start.9) | collective-permute-done | bytes 163872 | tf_op jit(solution)/shard_map/ppermute | solution.py:240
  60.3 0.7 collective-permute-done.8
  61.0 1.0 %slice_multiply_fusion = f32[64,1,128]{2,1,0:T(1,128)S(1)} fusion(f32[64,5,128]{2,1,0:T(8,128)} %collective-permute-done.10), kind=kLoop, calls=%fused_computation.21 | loop fusion | flops 8192 | bytes 65536 | tf_op jit(solution)/shard_map/mul | solution.py:241
  62.0 1.1 %fusion.17 = f32[64,4,128]{2,1,0:T(4,128)S(1)} fusion(f32[64,5,128]{2,1,0:T(8,128)S(1)} %collective-permute-done.8, f32[64,5,128]{2,1,0:T(8,128)S(1)} %collective-permute-done.9, f32[64,5,128]{2,1,0:T(8,128)} %collective-permute-done.10, f32[64,128]{1,0:T(8,128)S(1)} %bitcast.50, f32[64,128]{1,0:T(8,128)S(1)} %bitcast.48, f32[64,128]{1,0:T(8,128)S(1)} %bitcast.49, ...), kind=kLoop, calls=%fused_computation.18 | loop fusion | flops 262144 | bytes 622595 | tf_op jit(solution)/shard_map/jit(_where)/select_n | solution.py:242
  63.1 1.6 %collective-permute-start.11 = (f32[32,4,128]{2,1,0:T(4,128)S(1)}, f32[32,4,128]{2,1,0:T(4,128)S(1)}, u32[]{:S(2)}, u32[]{:S(2)}) collective-permute-start(f32[32,4,128]{2,1,0:T(4,128)S(1)} %slice.70), channel_id=1, source_target_pairs={{0,16},{16,0},{1,17},{17,1},{2,18},{18,2},{3,19},{19,3},{4,20},{20... | collective-permute-start | bytes 196616 | tf_op jit(solution)/shard_map/ppermute | solution.py:245
  64.7 0.2 copy.29
  64.9 22.4 %collective-permute-done.11 = f32[32,4,128]{2,1,0:T(4,128)S(1)} collective-permute-done((f32[32,4,128]{2,1,0:T(4,128)S(1)}, f32[32,4,128]{2,1,0:T(4,128)S(1)}, u32[]{:S(2)}, u32[]{:S(2)}) %collective-permute-start.11) | collective-permute-done | bytes 65568 | tf_op jit(solution)/shard_map/ppermute | solution.py:245
  87.4 2.1 %add.95 = f32[32,4,32,128]{3,0,2,1:T(8,128)S(1)} add(f32[32,4,32,128]{3,0,2,1:T(8,128)S(1)} %fusion.8, f32[32,4,32,128]{3,0,2,1:T(8,128)} %collective-permute-done.6) | non-fusion elementwise | flops 524288 | bytes 6291456 | tf_op jit(solution)/shard_map/add | solution.py:249
  89.5 4.2 %bitcast_add_fusion = f32[32,4,32,128]{3,2,1,0:T(8,128)} fusion(f32[32,32]{1,0:T(8,128)S(1)} %bitcast.52, f32[32,4,128]{2,1,0:T(4,128)S(1)} %fusion.18, f32[32,32,32]{2,1,0:T(8,128)S(1)} %copy-done.1, f32[32,4,32,128]{3,0,2,1:T(8,128)S(1)} %add.95), kind=kOutput, calls=%fused_computation | convolution fusion | flops 101711872 | bytes 4395008 | tf_op jit(solution)/shard_map/qab,qpby->qpay/dot_general | solution.py:253
  (40 shorter events, 0.7 us)
Async XLA Ops:
  0.0 16.5 %copy-start.1 = (f32[32,32,32]{2,1,0:T(8,128)S(1)}, f32[32,32,32]{2,1,0:T(8,128)}, u32[]{:S(2)}) copy-start(f32[32,32,32]{2,1,0:T(8,128)} %param.14) | copy-start | bytes 393220
  0.0 16.9 %copy-start.7 = (f32[32,1]{0,1:T(1,128)S(1)}, f32[32,1]{0,1:T(1,128)}, u32[]{:S(2)}) copy-start(f32[32,1]{0,1:T(1,128)} %param.15) | copy-start | bytes 388
  0.0 19.0 %copy-start.6 = (f32[16,8]{0,1:T(8,128)S(1)}, f32[16,8]{0,1:T(8,128)}, u32[]{:S(2)}) copy-start(f32[16,8]{0,1:T(8,128)} %param.12) | copy-start | bytes 1540
  3.4 13.6 %collective-permute-start.4 = (f32[1,128]{1,0:T(1,128)}, f32[1,128]{1,0:T(1,128)S(1)}, u32[]{:S(2)}, u32[]{:S(2)}) collective-permute-start(f32[1,128]{1,0:T(1,128)} %get-tuple-element.15), channel_id=1, source_target_pairs={{4,1},{5,2},{6,3},{8,5},{9,6},{10,7},{12,9},{13,10},{14,11},{20,17... | collective-permute-start | bytes 1544 | tf_op jit(solution)/shard_map/ppermute | solution.py:22
  6.3 18.3 %collective-permute-start.3 = (f32[32,128]{1,0:T(8,128)}, f32[32,128]{1,0:T(8,128)S(1)}, u32[]{:S(2)}, u32[]{:S(2)}) collective-permute-start(f32[32,128]{1,0:T(8,128)} %get-tuple-element.14.own0_ref), channel_id=1, source_target_pairs={{1,0},{2,1},{3,2},{5,4},{6,5},{7,6},{9,8},{10,9},{11,10},{13,12},{... | collective-permute-start | bytes 49160 | tf_op jit(solution)/shard_map/ppermute | solution.py:22
  8.7 15.9 %collective-permute-start.2 = (f32[40,128]{1,0:T(8,128)}, f32[40,128]{1,0:T(8,128)S(1)}, u32[]{:S(2)}, u32[]{:S(2)}) collective-permute-start(f32[40,128]{1,0:T(8,128)} %get-tuple-element.13), channel_id=1, source_target_pairs={{0,1},{1,2},{2,3},{4,5},{5,6},{6,7},{8,9},{9,10},{10,11},{12,13},{... | collective-permute-start | bytes 61448 | tf_op jit(solution)/shard_map/ppermute | solution.py:22
  12.2 12.4 %collective-permute-start.1 = (f32[128,128]{1,0:T(8,128)}, f32[128,128]{1,0:T(8,128)S(1)}, u32[]{:S(2)}, u32[]{:S(2)}) collective-permute-start(f32[128,128]{1,0:T(8,128)} %get-tuple-element.12), channel_id=1, source_target_pairs={{4,0},{5,1},{6,2},{7,3},{8,4},{9,5},{10,6},{11,7},{12,8},{13,9},{1... | collective-permute-start | bytes 196616 | tf_op jit(solution)/shard_map/ppermute | solution.py:22
  14.4 10.2 %collective-permute-start = (f32[136,128]{1,0:T(8,128)}, f32[136,128]{1,0:T(8,128)S(1)}, u32[]{:S(2)}, u32[]{:S(2)}) collective-permute-start(f32[136,128]{1,0:T(8,128)} %get-tuple-element.11), channel_id=1, source_target_pairs={{0,4},{1,5},{2,6},{3,7},{4,8},{5,9},{6,10},{7,11},{8,12},{9,13},{1... | collective-permute-start | bytes 208904 | tf_op jit(solution)/shard_map/ppermute | solution.py:22
  17.1 7.5 %copy-start.8 = (f32[1,128]{1,0:T(1,128)}, f32[1,128]{1,0:T(1,128)S(1)}, u32[]{:S(2)}) copy-start(f32[1,128]{1,0:T(1,128)S(1)} %collective-permute-done.4.c2_ref) | copy-start | bytes 1540
  17.1 6.0 %collective-permute-start.5 = (f32[1,128]{1,0:T(1,128)}, f32[1,128]{1,0:T(1,128)S(1)}, u32[]{:S(2)}, u32[]{:S(2)}) collective-permute-start(f32[1,128]{1,0:T(1,128)} %get-tuple-element.16), channel_id=1, source_target_pairs={{1,4},{2,5},{3,6},{5,8},{6,9},{7,10},{9,12},{10,13},{11,14},{17,20... | collective-permute-start | bytes 1544 | tf_op jit(solution)/shard_map/ppermute | solution.py:22
  23.1 1.6 %copy-start.9 = (f32[1,128]{1,0:T(1,128)}, f32[1,128]{1,0:T(1,128)S(1)}, u32[]{:S(2)}) copy-start(f32[1,128]{1,0:T(1,128)S(1)} %collective-permute-done.5.c1_ref) | copy-start | bytes 1540
  23.1 17.0 %collective-permute-start.7 = (f32[32,33]{1,0:T(8,128)S(1)}, f32[32,33]{1,0:T(8,128)S(1)}, u32[]{:S(2)}, u32[]{:S(2)}) collective-permute-start(f32[32,33]{1,0:T(8,128)S(1)} %pad_maximum_fusion.3), channel_id=1, source_target_pairs={{0,16},{16,0},{1,17},{17,1},{2,18},{18,2},{3,19},{19,3},{4,20},{20... | collective-permute-start | bytes 12680 | tf_op jit(solution)/shard_map/ppermute | solution.py:209
  24.6 0.6 copy-start.5
  24.6 0.6 copy-start.4
  24.6 0.6 copy-start.3
  25.2 0.6 copy-start.2
  39.6 4.8 %copy-start = (f32[4,32,32,128]{3,2,1,0:T(8,128)S(1)}, f32[4,32,32,128]{3,2,1,0:T(8,128)}, u32[]{:S(2)}) copy-start(f32[4,32,32,128]{3,2,1,0:T(8,128)} %residual.1) | copy-start | bytes 6291460
  39.6 47.9 %collective-permute-start.6 = (f32[32,4,32,128]{3,0,2,1:T(8,128)}, f32[32,4,32,128]{3,0,2,1:T(8,128)}, u32[]{:S(2)}, u32[]{:S(2)}) collective-permute-start(f32[32,4,32,128]{3,0,2,1:T(8,128)} %fusion.6), channel_id=1, source_target_pairs={{0,16},{16,0},{1,17},{17,1},{2,18},{18,2},{3,19},{19,3},{4,20},{20... | collective-permute-start | bytes 6291464 | tf_op jit(solution)/shard_map/ppermute | solution.py:231
  49.2 11.0 %collective-permute-start.9 = (f32[64,5,128]{2,1,0:T(8,128)S(1)}, f32[64,5,128]{2,1,0:T(8,128)S(1)}, u32[]{:S(2)}, u32[]{:S(2)}) collective-permute-start(f32[64,5,128]{2,1,0:T(8,128)S(1)} %pad_maximum_fusion), channel_id=1, source_target_pairs={{0,8},{4,12},{1,9},{5,13},{2,10},{6,14},{3,11},{7,15},{16,24},{20,... | collective-permute-start | bytes 491528 | tf_op jit(solution)/shard_map/ppermute | solution.py:240
  50.5 10.5 %collective-permute-start.8 = (f32[64,5,128]{2,1,0:T(8,128)S(1)}, f32[64,5,128]{2,1,0:T(8,128)S(1)}, u32[]{:S(2)}, u32[]{:S(2)}) collective-permute-start(f32[64,5,128]{2,1,0:T(8,128)S(1)} %pad_maximum_fusion), channel_id=1, source_target_pairs={{0,4},{4,8},{8,12},{1,5},{5,9},{9,13},{2,6},{6,10},{10,14},{3,7},{... | collective-permute-start | bytes 491528 | tf_op jit(solution)/shard_map/ppermute | solution.py:240
  52.4 8.6 %collective-permute-start.10 = (f32[64,5,128]{2,1,0:T(8,128)S(1)}, f32[64,5,128]{2,1,0:T(8,128)}, u32[]{:S(2)}, u32[]{:S(2)}) collective-permute-start(f32[64,5,128]{2,1,0:T(8,128)S(1)} %pad_maximum_fusion), channel_id=1, source_target_pairs={{0,12},{1,13},{2,14},{3,15},{16,28},{17,29},{18,30},{19,31}} | collective-permute-start | bytes 491528 | tf_op jit(solution)/shard_map/ppermute | solution.py:240
  63.1 24.2 %collective-permute-start.11 = (f32[32,4,128]{2,1,0:T(4,128)S(1)}, f32[32,4,128]{2,1,0:T(4,128)S(1)}, u32[]{:S(2)}, u32[]{:S(2)}) collective-permute-start(f32[32,4,128]{2,1,0:T(4,128)S(1)} %slice.70), channel_id=1, source_target_pairs={{0,16},{16,0},{1,17},{17,1},{2,18},{18,2},{3,19},{19,3},{4,20},{20... | collective-permute-start | bytes 196616 | tf_op jit(solution)/shard_map/ppermute | solution.py:245

commit v10 on v9

--- a/solution.py
+++ b/solution.py
@@ -189,6 +189,32 @@
     )(a, src, xlo, xhi, ylo, yhi, own0, c2, c1, level_index, reluctivity, saturation, reg)
 
 
+def post_kernel(own_ref, recv_ref, inv_ref, inj_ref, out_ref):
+    n_q, planes = own_ref.shape[:2]
+    for q in range(n_q):
+        m = inv_ref[q]
+        col0 = m[:, 0:1]
+        for p in range(planes):
+            spectrum = own_ref[q, p] + recv_ref[q, p]
+            solved = jnp.dot(m, spectrum, precision=lax.Precision.HIGHEST, preferred_element_type=jnp.float32)
+            out_ref[q, p] = solved + inj_ref[q, pl.ds(p, 1), :] * col0
+
+
+def post(own, recv, inverse, inj):
+    n_q, planes, nx, ny = own.shape
+    qb = 4 if n_q % 4 == 0 else 1
+    tile = pl.BlockSpec((qb, planes, nx, ny), lambda i: (i, 0, 0, 0))
+    return pl.pallas_call(
+        post_kernel,
+        grid=(n_q // qb,),
+        in_specs=[tile, tile, pl.BlockSpec((qb, nx, nx), lambda i: (i, 0, 0)),
+                  pl.BlockSpec((qb, planes, ny), lambda i: (i, 0, 0))],
+        out_specs=tile,
+        out_shape=jax.ShapeDtypeStruct(own.shape, jnp.float32),
+        name="block_solve",
+    )(own, recv, inverse, inj)
+
+
 def local(potential, source, region, level_index, reluctivity, saturation, inverse, transmit):
     samples_dev, planes, cells_x, cells_y = potential.shape
     n_tm = lax.axis_size("tm")
@@ -244,15 +270,14 @@
     got_carried = [
         lax.ppermute(carried[d], "tm", [(i, (i + d) % n_tm) for i in range(n_tm)]) for d in range(1, n_tm)
     ]
-    spectrum = parts[0]
-    for got in got_parts:
-        spectrum = spectrum + got
+    recv = got_parts[0]
+    for got in got_parts[1:]:
+        recv = recv + got
     carried_own = carried[0]
     for got in got_carried:
         carried_own = carried_own + got
-    solved = jnp.einsum("qab,qpby->qpay", inverse, spectrum, precision=lax.Precision.HIGH)
     injected = transmit[:, 0][:, None, None] * carried_own
-    return solved + injected[:, :, None, :] * inverse[:, :, 0][:, None, :, None]
+    return post(parts[0], recv, inverse, injected)
 
 
 def solution(mesh):

time: 95.4 us -> 101 us (1.059); the launches traced: 93.8 us -> 101 us
  Pallas kernels: 12 us -> 19.5 us
  local copies, waits for them, and re-layouts: 2.8 us -> 9.44 us
  matrix products: 18.1 us -> 11.9 us
  other arithmetic: 4.55 us -> 1.21 us
  starting transfers between devices: 23.1 us -> 24.4 us
  waiting for transfers between devices: 32.9 us -> 34 us
    pallas_call x0 -> x1, Pallas kernels: none -> 7.58 us  [post(): pl.pallas_call(post_kernel, grid=(n_q // qb,), in_specs=[tile, tile, pl.B...]
    dot_general x0 -> x2, local copies, waits for them, and re-layouts: none -> 5.1 us  [local(): jnp.einsum('qs,psxy->qpxy', tabs[d], resid, precision=lax.Precision.HIGH)]
    dot_general x1 -> x0, matrix products: 4.25 us -> none  [local(): jnp.einsum('qab,qpby->qpay', inverse, spectrum, precision=lax.Precision.H...]
    add x1 -> x0, other arithmetic: 2.07 us -> none  [local(): spectrum = spectrum + got]
    ppermute x3, waiting for transfers between devices: 7.11 us -> 9.11 us  [local(): got = lax.ppermute(msg_tail, 'gx', [(i, i + d) for i in range(n_gx - d)])]
    ppermute x6, starting transfers between devices: 14.9 us -> 16.9 us  [shifted(): return lax.ppermute(block, axes, route)]
    dot_general x2, matrix products: 7.4 us -> 6.06 us  [local(): jnp.einsum('qs,psxy->qpxy', tabs[d], resid, precision=lax.Precision.HIGH)]
    ppermute x6, waiting for transfers between devices: 3.37 us -> 2.29 us  [shifted(): return lax.ppermute(block, axes, route)]
  transfers between devices with their start and end apart: 12 -> 12, of which waited for: 4 -> 4; matrix products, arithmetic and copies ran while one was open for 19% -> 21% of each run, Pallas kernels for 9% -> 8%
where the time goes in v10:
time: 101 us
  waiting for transfers between devices  34 us (34%)
  starting transfers between devices  24.4 us (24%)
  Pallas kernels  19.5 us (19%)
  matrix products  11.9 us (12%)
  local copies, waits for them, and re-layouts  9.44 us (9%)
  other arithmetic  1.21 us (1%)
    ppermute x1, waiting for transfers between devices, local(): lax.ppermute(carried[d], 'tm', [(i, (i + d) % n_tm) for i in range(n_tm)])  22.6 us
    ppermute x6, starting transfers between devices, shifted(): return lax.ppermute(block, axes, route)  16.9 us
    ppermute x3, waiting for transfers between devices, local(): got = lax.ppermute(msg_tail, 'gx', [(i, i + d) for i in range(n_gx - d)])  9.11 us
    pallas_call x1, Pallas kernels, residual(): pl.pallas_call(functools.partial(residual_kernel, kinds, levels), grid=(n...  8.54 us
    pallas_call x1, Pallas kernels, post(): pl.pallas_call(post_kernel, grid=(n_q // qb,), in_specs=[tile, tile, pl.B...  7.58 us
    dot_general x2, matrix products, local(): jnp.einsum('qs,psxy->qpxy', tabs[d], resid, precision=lax.Precision.HIGH)  6.06 us
    dot_general x2, matrix products, local(): jnp.einsum('qb,qpby->qpy', row_last[d], parts[d], precision=lax.Precision...  5.82 us
    dot_general x2, local copies, waits for them, and re-layouts, local(): jnp.einsum('qs,psxy->qpxy', tabs[d], resid, precision=lax.Precision.HIGH)  5.1 us
  transfers between devices with their start and end apart: 12, of which 4 were waited for; matrix products, arithmetic and copies ran while one was open for 21% of the time, Pallas kernels for 8%

profile of v10, /device:TPU:12, one launch (start us, length us, event | category | flops | bytes accessed | tf_op | source)
XLA Modules:
  0.0 100.8 jit_solution(3790859558702197749)
XLA Ops:
  0.0 3.4 %halo_edges.1 = (f32[136,128]{1,0:T(8,128)}, f32[128,128]{1,0:T(8,128)}, f32[40,128]{1,0:T(8,128)}, f32[32,128]{1,0:T(8,128)}, f32[1,128]{1,0:T(1,128)}, /*index=5*/f32[1,128]{1,0:T(1,128)}) custom-call(f32[32,4,32,128]{3,2,1,0:T(8,128)} %a_ref.3, s32[32,128]{1,0:T(8,128)} %reg_ref.3), custom_call_target="tpu_custom_call" | custom-call | tf_op jit(solution)/shard_map/halo_edges/pallas_call | solution.py:86
  3.4 2.3 %collective-permute-start.3 = (f32[32,128]{1,0:T(8,128)}, f32[32,128]{1,0:T(8,128)S(1)}, u32[]{:S(2)}, u32[]{:S(2)}) collective-permute-start(f32[32,128]{1,0:T(8,128)} %get-tuple-element.14.own0_ref), channel_id=1, source_target_pairs={{1,0},{2,1},{3,2},{5,4},{6,5},{7,6},{9,8},{10,9},{11,10},{13,12},{... | collective-permute-start | bytes 49160 | tf_op jit(solution)/shard_map/ppermute | solution.py:22
  5.8 1.9 %collective-permute-start = (f32[136,128]{1,0:T(8,128)}, f32[136,128]{1,0:T(8,128)S(1)}, u32[]{:S(2)}, u32[]{:S(2)}) collective-permute-start(f32[136,128]{1,0:T(8,128)} %get-tuple-element.11), channel_id=1, source_target_pairs={{0,4},{1,5},{2,6},{3,7},{4,8},{5,9},{6,10},{7,11},{8,12},{9,13},{1... | collective-permute-start | bytes 208904 | tf_op jit(solution)/shard_map/ppermute | solution.py:22
  7.7 3.6 %collective-permute-start.1 = (f32[128,128]{1,0:T(8,128)}, f32[128,128]{1,0:T(8,128)S(1)}, u32[]{:S(2)}, u32[]{:S(2)}) collective-permute-start(f32[128,128]{1,0:T(8,128)} %get-tuple-element.12), channel_id=1, source_target_pairs={{4,0},{5,1},{6,2},{7,3},{8,4},{9,5},{10,6},{11,7},{12,8},{13,9},{1... | collective-permute-start | bytes 196616 | tf_op jit(solution)/shard_map/ppermute | solution.py:22
  11.3 3.5 %collective-permute-start.2 = (f32[40,128]{1,0:T(8,128)}, f32[40,128]{1,0:T(8,128)S(1)}, u32[]{:S(2)}, u32[]{:S(2)}) collective-permute-start(f32[40,128]{1,0:T(8,128)} %get-tuple-element.13), channel_id=1, source_target_pairs={{0,1},{1,2},{2,3},{4,5},{5,6},{6,7},{8,9},{9,10},{10,11},{12,13},{... | collective-permute-start | bytes 61448 | tf_op jit(solution)/shard_map/ppermute | solution.py:22
  14.8 2.6 %collective-permute-start.4 = (f32[1,128]{1,0:T(1,128)}, f32[1,128]{1,0:T(1,128)S(1)}, u32[]{:S(2)}, u32[]{:S(2)}) collective-permute-start(f32[1,128]{1,0:T(1,128)} %get-tuple-element.15), channel_id=1, source_target_pairs={{4,1},{5,2},{6,3},{8,5},{9,6},{10,7},{12,9},{13,10},{14,11},{20,17... | collective-permute-start | bytes 1544 | tf_op jit(solution)/shard_map/ppermute | solution.py:22
  17.5 1.2 %slice_reduce_fusion = f32[32]{0:T(128)S(1)} fusion(f32[32,32,32]{2,1,0:T(8,128)} %inv_ref.1), kind=kLoop, calls=%fused_computation.38 | loop fusion | bytes 256 | tf_op jit(solution)/shard_map/slice | solution.py:231
  18.7 0.9 slice.46
  19.9 2.9 %collective-permute-start.5 = (f32[1,128]{1,0:T(1,128)}, f32[1,128]{1,0:T(1,128)S(1)}, u32[]{:S(2)}, u32[]{:S(2)}) collective-permute-start(f32[1,128]{1,0:T(1,128)} %get-tuple-element.16), channel_id=1, source_target_pairs={{1,4},{2,5},{3,6},{5,8},{6,9},{7,10},{9,12},{10,13},{11,14},{17,20... | collective-permute-start | bytes 1544 | tf_op jit(solution)/shard_map/ppermute | solution.py:22
  22.8 0.7 copy.15.relu_ref
  23.5 2.2 %collective-permute-done.5.c1_ref = f32[1,128]{1,0:T(1,128)S(1)} collective-permute-done((f32[1,128]{1,0:T(1,128)}, f32[1,128]{1,0:T(1,128)S(1)}, u32[]{:S(2)}, u32[]{:S(2)}) %collective-permute-start.5) | collective-permute-done | bytes 544 | tf_op jit(solution)/shard_map/ppermute | solution.py:22
  25.7 1.5 %collective-permute-start.7 = (f32[32,33]{1,0:T(8,128)S(1)}, f32[32,33]{1,0:T(8,128)S(1)}, u32[]{:S(2)}, u32[]{:S(2)}) collective-permute-start(f32[32,33]{1,0:T(8,128)S(1)} %pad_maximum_fusion.3), channel_id=1, source_target_pairs={{0,16},{16,0},{1,17},{17,1},{2,18},{18,2},{3,19},{19,3},{4,20},{20... | collective-permute-start | bytes 12680 | tf_op jit(solution)/shard_map/ppermute | solution.py:235
  27.3 0.5 copy-done.4
  27.9 0.6 copy-done.1
  28.5 8.5 %residual.1 = f32[4,32,32,128]{3,2,1,0:T(8,128)} custom-call(f32[32,4,32,128]{3,2,1,0:T(8,128)} %a_ref.3, f32[32,4,32,128]{3,2,1,0:T(8,128)} %src_ref.1, f32[136,128]{1,0:T(8,128)} %copy-done.1, f32[128,128]{1,0:T(8,128)} %copy-done.2, f32[40,128]{1,0:T(8,128)} %copy-done.3, f32[32,128]{1,0:T(8,128)} %copy-done.4, f32[32,128]{1,0:T(8,128)} %get-tuple-element.14.own0_ref, ...), custom_call_target="tpu_custom_call" | custom-call | tf_op jit(solution)/shard_map/residual/pallas_call | solution.py:182
  37.0 3.8 %fusion = f32[32,4,32,128]{3,0,2,1:T(8,128)S(1)} fusion(f32[4,32,32,128]{3,2,1,0:T(8,128)} %residual.1, s32[32]{0:T(128)S(1)} %get-tuple-element.17, s32[32]{0:T(128)S(1)} %get-tuple-element.18, pred[32]{0:T(512)(128)(4,1)S(1)} %fusion.51), kind=kOutput, calls=%fused_computation | convolution fusion | flops 100679680 | bytes 4194592 | tf_op jit(solution)/shard_map/qs,psxy->qpxy/dot_general | solution.py:255
  40.9 2.5 %copy.18 = f32[32,4,32,128]{3,2,1,0:T(8,128)} copy(f32[32,4,32,128]{3,0,2,1:T(8,128)S(1)} %fusion) | data formatting | bytes 4194304 | tf_op jit(solution)/shard_map/qs,psxy->qpxy/dot_general | solution.py:255
  43.4 0.5 collective-permute-start.6
  44.0 0.2 fusion.8
  44.1 2.5 %fusion.65 = f32[32,1,4,128]{3,1,2,0:T(1,128)S(1)} fusion(f32[32,32,1,1]{1,2,3,0:T(1,128)S(1)} %bitcast.39, f32[32,4,32,128]{3,0,2,1:T(8,128)S(1)} %fusion), kind=kOutput, calls=%fused_computation.89 | convolution fusion | flops 3145728 | bytes 2166784 | tf_op jit(solution)/shard_map/qb,qpby->qpy/dot_general | solution.py:260
  46.6 2.2 %fusion.2 = f32[32,4,32,128]{3,0,2,1:T(8,128)S(1)} fusion(f32[4,32,32,128]{3,2,1,0:T(8,128)S(1)} %copy-done, s32[32]{0:T(128)S(1)} %get-tuple-element.18, s32[32]{0:T(128)S(1)} %add_select_fusion.3, pred[32]{0:T(512)(128)(4,1)S(1)} %fusion.52), kind=kOutput, calls=%fused_computation.2 | convolution fusion | flops 100679680 | bytes 4194592 | tf_op jit(solution)/shard_map/qs,psxy->qpxy/dot_general | solution.py:255
  48.9 3.3 %fusion.15 = f32[32,1,4,128]{3,1,2,0:T(1,128)S(1)} fusion(f32[32,32,32]{2,1,0:T(8,128)} %inv_ref.1, f32[32,4,32,128]{3,0,2,1:T(8,128)S(1)} %fusion.2), kind=kOutput, calls=%fused_computation.34 | convolution fusion | flops 3145728 | bytes 2179072 | tf_op jit(solution)/shard_map/qb,qpby->qpy/dot_general | solution.py:260
  52.4 1.9 %collective-permute-start.8 = (f32[64,5,128]{2,1,0:T(8,128)S(1)}, f32[64,5,128]{2,1,0:T(8,128)S(1)}, u32[]{:S(2)}, u32[]{:S(2)}) collective-permute-start(f32[64,5,128]{2,1,0:T(8,128)S(1)} %pad_maximum_fusion), channel_id=1, source_target_pairs={{0,4},{4,8},{8,12},{1,5},{5,9},{9,13},{2,6},{6,10},{10,14},{3,7},{... | collective-permute-start | bytes 491528 | tf_op jit(solution)/shard_map/ppermute | solution.py:266
  54.4 1.3 %collective-permute-start.9 = (f32[64,5,128]{2,1,0:T(8,128)S(1)}, f32[64,5,128]{2,1,0:T(8,128)S(1)}, u32[]{:S(2)}, u32[]{:S(2)}) collective-permute-start(f32[64,5,128]{2,1,0:T(8,128)S(1)} %pad_maximum_fusion), channel_id=1, source_target_pairs={{0,8},{4,12},{1,9},{5,13},{2,10},{6,14},{3,11},{7,15},{16,24},{20,... | collective-permute-start | bytes 491528 | tf_op jit(solution)/shard_map/ppermute | solution.py:266
  55.7 0.7 collective-permute-start.10
  56.4 4.0 %collective-permute-done.8 = f32[64,5,128]{2,1,0:T(8,128)S(1)} collective-permute-done((f32[64,5,128]{2,1,0:T(8,128)S(1)}, f32[64,5,128]{2,1,0:T(8,128)S(1)}, u32[]{:S(2)}, u32[]{:S(2)}) %collective-permute-start.8) | collective-permute-done | bytes 163872 | tf_op jit(solution)/shard_map/ppermute | solution.py:266
  60.4 5.1 %collective-permute-done.9 = f32[64,5,128]{2,1,0:T(8,128)S(1)} collective-permute-done((f32[64,5,128]{2,1,0:T(8,128)S(1)}, f32[64,5,128]{2,1,0:T(8,128)S(1)}, u32[]{:S(2)}, u32[]{:S(2)}) %collective-permute-start.9) | collective-permute-done | bytes 163872 | tf_op jit(solution)/shard_map/ppermute | solution.py:266
  65.7 1.5 %collective-permute-start.11 = (f32[32,4,128]{2,1,0:T(4,128)S(1)}, f32[32,4,128]{2,1,0:T(4,128)S(1)}, u32[]{:S(2)}, u32[]{:S(2)}) collective-permute-start(f32[32,4,128]{2,1,0:T(4,128)S(1)} %slice.66), channel_id=1, source_target_pairs={{0,16},{16,0},{1,17},{17,1},{2,18},{18,2},{3,19},{19,3},{4,20},{20... | collective-permute-start | bytes 196616 | tf_op jit(solution)/shard_map/ppermute | solution.py:271
  67.3 2.6 %copy.20.own_ref = f32[32,4,32,128]{3,2,1,0:T(8,128)} copy(f32[32,4,32,128]{3,0,2,1:T(8,128)S(1)} %fusion.2) | data formatting | bytes 4194304 | tf_op jit(solution)/shard_map/qs,psxy->qpxy/dot_general | solution.py:255
  69.8 22.6 %collective-permute-done.11 = f32[32,4,128]{2,1,0:T(4,128)S(1)} collective-permute-done((f32[32,4,128]{2,1,0:T(4,128)S(1)}, f32[32,4,128]{2,1,0:T(4,128)S(1)}, u32[]{:S(2)}, u32[]{:S(2)}) %collective-permute-start.11) | collective-permute-done | bytes 65568 | tf_op jit(solution)/shard_map/ppermute | solution.py:271
  92.5 0.7 fusion.7.inj_ref
  93.2 7.6 %block_solve.1 = f32[32,4,32,128]{3,2,1,0:T(8,128)} custom-call(f32[32,4,32,128]{3,2,1,0:T(8,128)} %copy.20.own_ref, f32[32,4,32,128]{3,2,1,0:T(8,128)} %collective-permute-done.6.recv_ref, f32[32,32,32]{2,1,0:T(8,128)} %inv_ref.1, f32[32,4,128]{2,1,0:T(4,128)} %fusion.7.inj_ref), custom_call_target="tpu_custom_call" | custom-call | tf_op jit(solution)/shard_map/block_solve/pallas_call | solution.py:207
  (38 shorter events, 0.7 us)
Async XLA Ops:
  0.0 19.7 %copy-start.6 = (f32[32,1]{0,1:T(1,128)S(1)}, f32[32,1]{0,1:T(1,128)}, u32[]{:S(2)}) copy-start(f32[32,1]{0,1:T(1,128)} %param.15) | copy-start | bytes 388
  0.0 22.8 %copy-start.5 = (f32[16,8]{0,1:T(8,128)S(1)}, f32[16,8]{0,1:T(8,128)}, u32[]{:S(2)}) copy-start(f32[16,8]{0,1:T(8,128)} %param.12) | copy-start | bytes 1540
  3.4 23.8 %collective-permute-start.3 = (f32[32,128]{1,0:T(8,128)}, f32[32,128]{1,0:T(8,128)S(1)}, u32[]{:S(2)}, u32[]{:S(2)}) collective-permute-start(f32[32,128]{1,0:T(8,128)} %get-tuple-element.14.own0_ref), channel_id=1, source_target_pairs={{1,0},{2,1},{3,2},{5,4},{6,5},{7,6},{9,8},{10,9},{11,10},{13,12},{... | collective-permute-start | bytes 49160 | tf_op jit(solution)/shard_map/ppermute | solution.py:22
  5.8 21.5 %collective-permute-start = (f32[136,128]{1,0:T(8,128)}, f32[136,128]{1,0:T(8,128)S(1)}, u32[]{:S(2)}, u32[]{:S(2)}) collective-permute-start(f32[136,128]{1,0:T(8,128)} %get-tuple-element.11), channel_id=1, source_target_pairs={{0,4},{1,5},{2,6},{3,7},{4,8},{5,9},{6,10},{7,11},{8,12},{9,13},{1... | collective-permute-start | bytes 208904 | tf_op jit(solution)/shard_map/ppermute | solution.py:22
  7.7 19.5 %collective-permute-start.1 = (f32[128,128]{1,0:T(8,128)}, f32[128,128]{1,0:T(8,128)S(1)}, u32[]{:S(2)}, u32[]{:S(2)}) collective-permute-start(f32[128,128]{1,0:T(8,128)} %get-tuple-element.12), channel_id=1, source_target_pairs={{4,0},{5,1},{6,2},{7,3},{8,4},{9,5},{10,6},{11,7},{12,8},{13,9},{1... | collective-permute-start | bytes 196616 | tf_op jit(solution)/shard_map/ppermute | solution.py:22
  11.3 15.9 %collective-permute-start.2 = (f32[40,128]{1,0:T(8,128)}, f32[40,128]{1,0:T(8,128)S(1)}, u32[]{:S(2)}, u32[]{:S(2)}) collective-permute-start(f32[40,128]{1,0:T(8,128)} %get-tuple-element.13), channel_id=1, source_target_pairs={{0,1},{1,2},{2,3},{4,5},{5,6},{6,7},{8,9},{9,10},{10,11},{12,13},{... | collective-permute-start | bytes 61448 | tf_op jit(solution)/shard_map/ppermute | solution.py:22
  14.8 5.1 %collective-permute-start.4 = (f32[1,128]{1,0:T(1,128)}, f32[1,128]{1,0:T(1,128)S(1)}, u32[]{:S(2)}, u32[]{:S(2)}) collective-permute-start(f32[1,128]{1,0:T(1,128)} %get-tuple-element.15), channel_id=1, source_target_pairs={{4,1},{5,2},{6,3},{8,5},{9,6},{10,7},{12,9},{13,10},{14,11},{20,17... | collective-permute-start | bytes 1544 | tf_op jit(solution)/shard_map/ppermute | solution.py:22
  19.9 7.4 %copy-start.7 = (f32[1,128]{1,0:T(1,128)}, f32[1,128]{1,0:T(1,128)S(1)}, u32[]{:S(2)}) copy-start(f32[1,128]{1,0:T(1,128)S(1)} %collective-permute-done.4.c2_ref) | copy-start | bytes 1540
  19.9 5.8 %collective-permute-start.5 = (f32[1,128]{1,0:T(1,128)}, f32[1,128]{1,0:T(1,128)S(1)}, u32[]{:S(2)}, u32[]{:S(2)}) collective-permute-start(f32[1,128]{1,0:T(1,128)} %get-tuple-element.16), channel_id=1, source_target_pairs={{1,4},{2,5},{3,6},{5,8},{6,9},{7,10},{9,12},{10,13},{11,14},{17,20... | collective-permute-start | bytes 1544 | tf_op jit(solution)/shard_map/ppermute | solution.py:22
  25.7 1.6 %copy-start.8 = (f32[1,128]{1,0:T(1,128)}, f32[1,128]{1,0:T(1,128)S(1)}, u32[]{:S(2)}) copy-start(f32[1,128]{1,0:T(1,128)S(1)} %collective-permute-done.5.c1_ref) | copy-start | bytes 1540
  25.7 18.3 %collective-permute-start.7 = (f32[32,33]{1,0:T(8,128)S(1)}, f32[32,33]{1,0:T(8,128)S(1)}, u32[]{:S(2)}, u32[]{:S(2)}) collective-permute-start(f32[32,33]{1,0:T(8,128)S(1)} %pad_maximum_fusion.3), channel_id=1, source_target_pairs={{0,16},{16,0},{1,17},{17,1},{2,18},{18,2},{3,19},{19,3},{4,20},{20... | collective-permute-start | bytes 12680 | tf_op jit(solution)/shard_map/ppermute | solution.py:235
  27.2 0.6 copy-start.4
  27.2 0.6 copy-start.3
  27.2 0.6 copy-start.2
  27.9 0.6 copy-start.1
  43.4 3.2 %copy-start = (f32[4,32,32,128]{3,2,1,0:T(8,128)S(1)}, f32[4,32,32,128]{3,2,1,0:T(8,128)}, u32[]{:S(2)}) copy-start(f32[4,32,32,128]{3,2,1,0:T(8,128)} %residual.1) | copy-start | bytes 6291460
  43.4 49.8 %collective-permute-start.6 = (f32[32,4,32,128]{3,2,1,0:T(8,128)}, f32[32,4,32,128]{3,2,1,0:T(8,128)}, u32[]{:S(2)}, u32[]{:S(2)}) collective-permute-start(f32[32,4,32,128]{3,2,1,0:T(8,128)} %copy.18), channel_id=1, source_target_pairs={{0,16},{16,0},{1,17},{17,1},{2,18},{18,2},{3,19},{19,3},{4,20},{20... | collective-permute-start | bytes 6291464 | tf_op jit(solution)/shard_map/ppermute | solution.py:257
  52.4 7.9 %collective-permute-start.8 = (f32[64,5,128]{2,1,0:T(8,128)S(1)}, f32[64,5,128]{2,1,0:T(8,128)S(1)}, u32[]{:S(2)}, u32[]{:S(2)}) collective-permute-start(f32[64,5,128]{2,1,0:T(8,128)S(1)} %pad_maximum_fusion), channel_id=1, source_target_pairs={{0,4},{4,8},{8,12},{1,5},{5,9},{9,13},{2,6},{6,10},{10,14},{3,7},{... | collective-permute-start | bytes 491528 | tf_op jit(solution)/shard_map/ppermute | solution.py:266
  54.4 11.1 %collective-permute-start.9 = (f32[64,5,128]{2,1,0:T(8,128)S(1)}, f32[64,5,128]{2,1,0:T(8,128)S(1)}, u32[]{:S(2)}, u32[]{:S(2)}) collective-permute-start(f32[64,5,128]{2,1,0:T(8,128)S(1)} %pad_maximum_fusion), channel_id=1, source_target_pairs={{0,8},{4,12},{1,9},{5,13},{2,10},{6,14},{3,11},{7,15},{16,24},{20,... | collective-permute-start | bytes 491528 | tf_op jit(solution)/shard_map/ppermute | solution.py:266
  55.7 9.9 %collective-permute-start.10 = (f32[64,5,128]{2,1,0:T(8,128)S(1)}, f32[64,5,128]{2,1,0:T(8,128)S(1)}, u32[]{:S(2)}, u32[]{:S(2)}) collective-permute-start(f32[64,5,128]{2,1,0:T(8,128)S(1)} %pad_maximum_fusion), channel_id=1, source_target_pairs={{0,12},{1,13},{2,14},{3,15},{16,28},{17,29},{18,30},{19,31}} | collective-permute-start | bytes 491528 | tf_op jit(solution)/shard_map/ppermute | solution.py:266
  65.7 26.7 %collective-permute-start.11 = (f32[32,4,128]{2,1,0:T(4,128)S(1)}, f32[32,4,128]{2,1,0:T(4,128)S(1)}, u32[]{:S(2)}, u32[]{:S(2)}) collective-permute-start(f32[32,4,128]{2,1,0:T(4,128)S(1)} %slice.66), channel_id=1, source_target_pairs={{0,16},{16,0},{1,17},{17,1},{2,18},{18,2},{3,19},{19,3},{4,20},{20... | collective-permute-start | bytes 196616 | tf_op jit(solution)/shard_map/ppermute | solution.py:271

commit v11 on v9

--- a/solution.py
+++ b/solution.py
@@ -43,7 +43,7 @@
     return jnp.sum(jnp.where(ix == iy, full, 0.0), axis=1, keepdims=True)
 
 
-def edges_kernel(a_ref, reg_ref, xlo_ref, xhi_ref, c127_ref, c0_ref, c1_ref, c2_ref):
+def edges_kernel(a_ref, reg_ref, xlo_ref, xhi_ref, c127_ref, c0_ref):
     n_s, planes, nx, ny = a_ref.shape
     rows = planes * n_s
     ix = lax.broadcasted_iota(jnp.int32, (nx, ny), 0)
@@ -51,6 +51,7 @@
     regf = reg_ref[...].astype(jnp.float32)
     xlo_ref[pl.ds(rows, 8), :] = jnp.zeros((8, ny), jnp.float32)
     xlo_ref[pl.ds(rows, 1), :] = regf[nx - 1:nx, :]
+    xhi_ref[pl.ds(rows, 8), :] = jnp.zeros((8, ny), jnp.float32)
     c127_ref[pl.ds(nx, 8), :] = jnp.zeros((8, ny), jnp.float32)
     c127_ref[pl.ds(nx, 1), :] = col_to_row(regf[:, ny - 1:ny], ix, iy)
 
@@ -66,8 +67,6 @@
             acc0 = jnp.where(iy == t, a if t == 0 else pltpu.roll(a, t, 1), acc0)
     c127_ref[pl.ds(0, nx), :] = acc127
     c0_ref[...] = acc0
-    c1_ref[...] = acc0[nx - 1:nx, :]
-    c2_ref[...] = acc127[0:1, :]
 
 
 def edges(a, region):
@@ -77,23 +76,21 @@
     f32 = jnp.float32
     shapes = [
         jax.ShapeDtypeStruct((rows + 8, ny), f32),
-        jax.ShapeDtypeStruct((rows, ny), f32),
+        jax.ShapeDtypeStruct((rows + 8, ny), f32),
         jax.ShapeDtypeStruct((nx + 8, ny), f32),
         jax.ShapeDtypeStruct((nx, ny), f32),
-        jax.ShapeDtypeStruct((1, ny), f32),
-        jax.ShapeDtypeStruct((1, ny), f32),
     ]
     return pl.pallas_call(
         edges_kernel,
         in_specs=[vmem, vmem],
-        out_specs=[vmem] * 6,
+        out_specs=[vmem] * 4,
         out_shape=shapes,
         name="halo_edges",
     )(a, region)
 
 
-def residual_kernel(kinds, levels, a_ref, src_ref, xlo_ref, xhi_ref, ylo_ref, yhi_ref, own0_ref, c2_ref,
-                    c1_ref, level_ref, relu_ref, sat_ref, reg_ref, out_ref):
+def residual_kernel(kinds, levels, a_ref, src_ref, xlo_ref, xhi_ref, ylo_ref, yhi_ref, own0_ref,
+                    level_ref, relu_ref, sat_ref, reg_ref, out_ref):
     blk = pl.program_id(0)
     n_s, planes, nx, ny = a_ref.shape
     n_all = n_s * pl.num_programs(0)
@@ -124,7 +121,8 @@
             row = jnp.where(lane_level == lv, relu_ref[lv, k], row)
         bt.append(row)
     c_lo = ylo_ref[pl.ds(0, nx), :]
-    lo_xp = jnp.where(ix == nx - 1, c2_ref[...], pltpu.roll(c_lo, nx - 1, 0))
+    lo_xp = jnp.where(ix == nx - 1, xhi_ref[pl.ds(rows, 1), :], pltpu.roll(c_lo, nx - 1, 0))
+    c1_row = xlo_ref[pl.ds(rows + 1, 1), :]
     sx_c = lo_xp - c_lo
     sy_c = own0_ref[...] - c_lo
     kind_c = jnp.broadcast_to(reg_ycol, (nx, ny))
@@ -144,7 +142,7 @@
             a = tiles[p]
             row_hi = xhi_ref[pl.ds(p * n_all + s_glob, 1), :]
             row_lo = xlo_ref[pl.ds(p * n_all + s_glob, 1), :]
-            c1 = c1_ref[0, t]
+            c1 = pltpu.roll(c1_row, lax.rem(ny - 1 - t + ny, ny), 1)
             col_hi = pltpu.roll(c_hi, lax.rem(ny - 1 - t + ny, ny), 1)
             a_xp = jnp.where(ix == nx - 1, row_hi, pltpu.roll(a, nx - 1, 0))
             a_yp = jnp.where(iy == ny - 1, col_hi, pltpu.roll(a, ny - 1, 1))
@@ -172,7 +170,7 @@
     lax.fori_loop(0, n_s, body, 0)
 
 
-def residual(a, src, xlo, xhi, ylo, yhi, own0, c2, c1, level_index, reluctivity, saturation, reg):
+def residual(a, src, xlo, xhi, ylo, yhi, own0, level_index, reluctivity, saturation, reg):
     n_s, planes, nx, ny = a.shape
     levels, kinds = reluctivity.shape
     sb = min(SAMPLE_BLOCK, n_s)
@@ -182,11 +180,11 @@
     return pl.pallas_call(
         functools.partial(residual_kernel, kinds, levels),
         grid=(n_s // sb,),
-        in_specs=[tile, tile] + [vmem_whole] * 6 + [smem_whole] * 4 + [vmem_whole],
+        in_specs=[tile, tile] + [vmem_whole] * 5 + [smem_whole] * 3 + [vmem_whole],
         out_specs=pl.BlockSpec((planes, sb, nx, ny), lambda i: (0, i, 0, 0)),
         out_shape=jax.ShapeDtypeStruct((planes, n_s, nx, ny), jnp.float32),
         name="residual",
-    )(a, src, xlo, xhi, ylo, yhi, own0, c2, c1, level_index, reluctivity, saturation, reg)
+    )(a, src, xlo, xhi, ylo, yhi, own0, level_index, reluctivity, saturation, reg)
 
 
 def local(potential, source, region, level_index, reluctivity, saturation, inverse, transmit):
@@ -210,14 +208,14 @@
     info_all = jnp.concatenate(infos, axis=0)
     gain_all = info_all[:, cells_x]
 
-    msg_xlo, msg_xhi, msg_c127, msg_c0, msg_c1, msg_c2 = edges(potential, region)
+    msg_xlo, msg_xhi, msg_c127, msg_c0 = edges(potential, region)
+    ylo = shifted(msg_c127, grid, sizes, (0, 1))
+    yhi = shifted(msg_c0, grid, sizes, (0, -1))
+    msg_xlo = lax.dynamic_update_slice_in_dim(msg_xlo, yhi[cells_x - 1:cells_x], rows + 1, 0)
+    msg_xhi = lax.dynamic_update_slice_in_dim(msg_xhi, ylo[0:1], rows, 0)
     xlo = shifted(msg_xlo, grid, sizes, (1, 0))
     xhi = shifted(msg_xhi, grid, sizes, (-1, 0))
-    ylo = shifted(msg_c127, grid, sizes, (0, 1))
-    yhi = shifted(msg_c0, grid, sizes, (0, -1))
-    c1 = shifted(msg_c1, grid, sizes, (1, -1))
-    c2 = shifted(msg_c2, grid, sizes, (-1, 1))
-    resid = residual(potential, source, xlo, xhi, ylo, yhi, msg_c0, c2, c1, level_index, reluctivity,
+    resid = residual(potential, source, xlo, xhi, ylo, yhi, msg_c0, level_index, reluctivity,
                      saturation, region)
 
     sample_ids = me_tm * samples_dev + lax.iota(jnp.int32, samples_dev)

time: 95.4 us -> 95.7 us (level)
  the two profiles are of different devices: /device:TPU:12 before, /device:TPU:1 now
where the time goes in v11:
time: 95.7 us; the launch traced here: 95.1 us
  waiting for transfers between devices  33.1 us (35%)
  starting transfers between devices  19.7 us (21%)
  matrix products  18.3 us (19%)
  Pallas kernels  11.9 us (12%)
  local copies, waits for them, and re-layouts  6.59 us (7%)
  other arithmetic  5.23 us (5%)
    ppermute x1, waiting for transfers between devices, local(): lax.ppermute(carried[d], 'tm', [(i, (i + d) % n_tm) for i in range(n_tm)])  22.5 us
    ppermute x4, starting transfers between devices, shifted(): return lax.ppermute(block, axes, route)  11.7 us
    pallas_call x1, Pallas kernels, residual(): pl.pallas_call(functools.partial(residual_kernel, kinds, levels), grid=(n...  8.52 us
    dot_general x2, matrix products, local(): jnp.einsum('qs,psxy->qpxy', tabs[d], resid, precision=lax.Precision.HIGH)  7.4 us
    ppermute x3, waiting for transfers between devices, local(): got = lax.ppermute(msg_tail, 'gx', [(i, i + d) for i in range(n_gx - d)])  6.76 us
    dot_general x2, matrix products, local(): jnp.einsum('qb,qpby->qpy', row_last[d], parts[d], precision=lax.Precision...  6.63 us
    ppermute x3, starting transfers between devices, local(): got = lax.ppermute(msg_tail, 'gx', [(i, i + d) for i in range(n_gx - d)])  4.77 us
    dot_general x1, matrix products, local(): jnp.einsum('qab,qpby->qpay', inverse, spectrum, precision=lax.Precision.H...  4.26 us
  transfers between devices with their start and end apart: 10, of which 4 were waited for; matrix products, arithmetic and copies ran while one was open for 21% of the time, Pallas kernels for 13%

profile of v11, /device:TPU:1, one launch (start us, length us, event | category | flops | bytes accessed | tf_op | source)
XLA Modules:
  0.0 95.1 jit_solution(2520159145946510332)
XLA Ops:
  0.0 1.2 %slice_reduce_fusion = f32[32]{0:T(128)S(1)} fusion(f32[32,32,32]{2,1,0:T(8,128)} %param.14), kind=kLoop, calls=%fused_computation.45 | loop fusion | bytes 256 | tf_op jit(solution)/shard_map/slice | solution.py:203
  1.2 0.9 slice.57
  2.2 0.7 bitcast_multiply_fusion
  3.0 2.0 %collective-permute-start.5 = (f32[32,33]{1,0:T(8,128)S(1)}, f32[32,33]{1,0:T(8,128)S(1)}, u32[]{:S(2)}, u32[]{:S(2)}) collective-permute-start(f32[32,33]{1,0:T(8,128)S(1)} %pad_maximum_fusion.3), channel_id=1, source_target_pairs={{0,16},{16,0},{1,17},{17,1},{2,18},{18,2},{3,19},{19,3},{4,20},{20... | collective-permute-start | bytes 12680 | tf_op jit(solution)/shard_map/ppermute | solution.py:207
  5.0 3.4 %halo_edges.1 = (f32[136,128]{1,0:T(8,128)}, f32[136,128]{1,0:T(8,128)}, f32[40,128]{1,0:T(8,128)}, f32[32,128]{1,0:T(8,128)}) custom-call(f32[32,4,32,128]{3,2,1,0:T(8,128)} %a_ref.3, s32[32,128]{1,0:T(8,128)} %reg_ref.3), custom_call_target="tpu_custom_call" | custom-call | tf_op jit(solution)/shard_map/halo_edges/pallas_call | solution.py:83
  8.4 1.3 %collective-permute-start = (f32[32,128]{1,0:T(8,128)}, f32[32,128]{1,0:T(8,128)S(1)}, u32[]{:S(2)}, u32[]{:S(2)}) collective-permute-start(f32[32,128]{1,0:T(8,128)} %get-tuple-element.10.own0_ref), channel_id=1, source_target_pairs={{1,0},{2,1},{3,2},{5,4},{6,5},{7,6},{9,8},{10,9},{11,10},{13,12},{... | collective-permute-start | bytes 49160 | tf_op jit(solution)/shard_map/ppermute | solution.py:22
  9.7 4.0 %collective-permute-start.2 = (f32[40,128]{1,0:T(8,128)}, f32[40,128]{1,0:T(8,128)S(1)}, u32[]{:S(2)}, u32[]{:S(2)}) collective-permute-start(f32[40,128]{1,0:T(8,128)} %get-tuple-element.12), channel_id=1, source_target_pairs={{0,1},{1,2},{2,3},{4,5},{5,6},{6,7},{8,9},{9,10},{10,11},{12,13},{... | collective-permute-start | bytes 61448 | tf_op jit(solution)/shard_map/ppermute | solution.py:22
  13.7 0.7 copy.14.relu_ref
  14.4 1.3 %dynamic_update_slice.6 = f32[136,128]{1,0:T(8,128)} dynamic-update-slice(f32[136,128]{1,0:T(8,128)} %get-tuple-element.9, f32[1,128]{1,0:T(1,128)S(1)} %slice.70, s32[]{:T(128)} %constant.61.clone.1, s32[]{:T(128)} %constant.52.clone.1) | dynamic-update-slice | bytes 1028 | tf_op jit(solution)/shard_map/dynamic_update_slice | solution.py:214
  15.7 4.5 %collective-permute-start.1 = (f32[136,128]{1,0:T(8,128)}, f32[136,128]{1,0:T(8,128)S(1)}, u32[]{:S(2)}, u32[]{:S(2)}) collective-permute-start(f32[136,128]{1,0:T(8,128)} %dynamic_update_slice.6), channel_id=1, source_target_pairs={{0,4},{1,5},{2,6},{3,7},{4,8},{5,9},{6,10},{7,11},{8,12},{9,13},{1... | collective-permute-start | bytes 208904 | tf_op jit(solution)/shard_map/ppermute | solution.py:22
  20.3 1.3 %dynamic_update_slice.7 = f32[136,128]{1,0:T(8,128)} dynamic-update-slice(f32[136,128]{1,0:T(8,128)} %get-tuple-element.11, f32[1,128]{1,0:T(1,128)S(1)} %slice.71, s32[]{:T(128)} %constant.62.clone.1, s32[]{:T(128)} %constant.52.clone.1) | dynamic-update-slice | bytes 1028 | tf_op jit(solution)/shard_map/dynamic_update_slice | solution.py:215
  21.6 1.9 %collective-permute-start.3 = (f32[136,128]{1,0:T(8,128)}, f32[136,128]{1,0:T(8,128)S(1)}, u32[]{:S(2)}, u32[]{:S(2)}) collective-permute-start(f32[136,128]{1,0:T(8,128)} %dynamic_update_slice.7), channel_id=1, source_target_pairs={{4,0},{5,1},{6,2},{7,3},{8,4},{9,5},{10,6},{11,7},{12,8},{13,9},{1... | collective-permute-start | bytes 208904 | tf_op jit(solution)/shard_map/ppermute | solution.py:22
  23.5 3.9 %collective-permute-done.3.xhi_ref = f32[136,128]{1,0:T(8,128)S(1)} collective-permute-done((f32[136,128]{1,0:T(8,128)}, f32[136,128]{1,0:T(8,128)S(1)}, u32[]{:S(2)}, u32[]{:S(2)}) %collective-permute-start.3) | collective-permute-done | bytes 69664 | tf_op jit(solution)/shard_map/ppermute | solution.py:22
  27.4 0.6 copy-done.3
  28.0 8.5 %residual.1 = f32[4,32,32,128]{3,2,1,0:T(8,128)} custom-call(f32[32,4,32,128]{3,2,1,0:T(8,128)} %a_ref.3, f32[32,4,32,128]{3,2,1,0:T(8,128)} %src_ref.1, f32[136,128]{1,0:T(8,128)} %copy-done.2, f32[136,128]{1,0:T(8,128)} %copy-done.3, f32[40,128]{1,0:T(8,128)} %copy-done.4, f32[32,128]{1,0:T(8,128)} %copy-done.5, f32[32,128]{1,0:T(8,128)} %get-tuple-element.10.own0_ref, ...), custom_call_target="tpu_custom_call" | custom-call | tf_op jit(solution)/shard_map/residual/pallas_call | solution.py:180
  36.6 5.2 %fusion.6 = f32[32,4,32,128]{3,0,2,1:T(8,128)} fusion(f32[4,32,32,128]{3,2,1,0:T(8,128)} %residual.1, s32[32]{0:T(128)S(1)} %get-tuple-element.13, s32[32]{0:T(128)S(1)} %get-tuple-element.14, pred[32]{0:T(512)(128)(4,1)S(1)} %fusion.61), kind=kOutput, calls=%fused_computation.7 | convolution fusion | flops 100679680 | bytes 4194592 | tf_op jit(solution)/shard_map/qs,psxy->qpxy/dot_general | solution.py:227
  41.7 0.3 collective-permute-start.4
  42.2 4.2 %fusion = f32[32,1,4,128]{3,1,2,0:T(1,128)S(1)} fusion(f32[32,32,1,1]{1,2,3,0:T(1,128)S(1)} %bitcast.51, f32[32,4,32,128]{3,0,2,1:T(8,128)} %fusion.6), kind=kOutput, calls=%fused_computation.1 | convolution fusion | flops 3145728 | bytes 2166784 | tf_op jit(solution)/shard_map/qb,qpby->qpy/dot_general | solution.py:232
  46.4 2.2 %fusion.8 = f32[32,4,32,128]{3,0,2,1:T(8,128)S(1)} fusion(f32[4,32,32,128]{3,2,1,0:T(8,128)S(1)} %copy-done, s32[32]{0:T(128)S(1)} %get-tuple-element.14, s32[32]{0:T(128)S(1)} %add_select_fusion.3, pred[32]{0:T(512)(128)(4,1)S(1)} %fusion.62), kind=kOutput, calls=%fused_computation.9 | convolution fusion | flops 100679680 | bytes 4194592 | tf_op jit(solution)/shard_map/qs,psxy->qpxy/dot_general | solution.py:227
  48.7 2.4 %fusion.2 = f32[32,1,4,128]{3,1,2,0:T(1,128)S(1)} fusion(f32[32,4,32,128]{3,0,2,1:T(8,128)S(1)} %fusion.8, f32[32,32,32]{2,1,0:T(8,128)S(1)} %copy-done.1), kind=kOutput, calls=%fused_computation.3 | convolution fusion | flops 3145728 | bytes 2179072 | tf_op jit(solution)/shard_map/qb,qpby->qpy/dot_general | solution.py:232
  51.3 1.3 %collective-permute-start.7 = (f32[64,5,128]{2,1,0:T(8,128)S(1)}, f32[64,5,128]{2,1,0:T(8,128)S(1)}, u32[]{:S(2)}, u32[]{:S(2)}) collective-permute-start(f32[64,5,128]{2,1,0:T(8,128)S(1)} %pad_maximum_fusion), channel_id=1, source_target_pairs={{0,8},{4,12},{1,9},{5,13},{2,10},{6,14},{3,11},{7,15},{16,24},{20,... | collective-permute-start | bytes 491528 | tf_op jit(solution)/shard_map/ppermute | solution.py:238
  52.6 2.1 %collective-permute-start.6 = (f32[64,5,128]{2,1,0:T(8,128)S(1)}, f32[64,5,128]{2,1,0:T(8,128)S(1)}, u32[]{:S(2)}, u32[]{:S(2)}) collective-permute-start(f32[64,5,128]{2,1,0:T(8,128)S(1)} %pad_maximum_fusion), channel_id=1, source_target_pairs={{0,4},{4,8},{8,12},{1,5},{5,9},{9,13},{2,6},{6,10},{10,14},{3,7},{... | collective-permute-start | bytes 491528 | tf_op jit(solution)/shard_map/ppermute | solution.py:238
  54.7 1.4 %collective-permute-start.8 = (f32[64,5,128]{2,1,0:T(8,128)S(1)}, f32[64,5,128]{2,1,0:T(8,128)}, u32[]{:S(2)}, u32[]{:S(2)}) collective-permute-start(f32[64,5,128]{2,1,0:T(8,128)S(1)} %pad_maximum_fusion), channel_id=1, source_target_pairs={{0,12},{1,13},{2,14},{3,15},{16,28},{17,29},{18,30},{19,31}} | collective-permute-start | bytes 491528 | tf_op jit(solution)/shard_map/ppermute | solution.py:238
  56.1 1.2 %collective-permute-done.7 = f32[64,5,128]{2,1,0:T(8,128)S(1)} collective-permute-done((f32[64,5,128]{2,1,0:T(8,128)S(1)}, f32[64,5,128]{2,1,0:T(8,128)S(1)}, u32[]{:S(2)}, u32[]{:S(2)}) %collective-permute-start.7) | collective-permute-done | bytes 163872 | tf_op jit(solution)/shard_map/ppermute | solution.py:238
  57.3 5.6 %collective-permute-done.6 = f32[64,5,128]{2,1,0:T(8,128)S(1)} collective-permute-done((f32[64,5,128]{2,1,0:T(8,128)S(1)}, f32[64,5,128]{2,1,0:T(8,128)S(1)}, u32[]{:S(2)}, u32[]{:S(2)}) %collective-permute-start.6) | collective-permute-done | bytes 163872 | tf_op jit(solution)/shard_map/ppermute | solution.py:238
  62.9 1.0 %slice_multiply_fusion = f32[64,1,128]{2,1,0:T(1,128)S(1)} fusion(f32[64,5,128]{2,1,0:T(8,128)} %collective-permute-done.8), kind=kLoop, calls=%fused_computation.21 | loop fusion | flops 8192 | bytes 65536 | tf_op jit(solution)/shard_map/mul | solution.py:239
  63.9 1.1 %fusion.17 = f32[64,4,128]{2,1,0:T(4,128)S(1)} fusion(f32[64,5,128]{2,1,0:T(8,128)S(1)} %collective-permute-done.6, f32[64,5,128]{2,1,0:T(8,128)S(1)} %collective-permute-done.7, f32[64,5,128]{2,1,0:T(8,128)} %collective-permute-done.8, f32[64,128]{1,0:T(8,128)S(1)} %bitcast.50, f32[64,128]{1,0:T(8,128)S(1)} %bitcast.48, f32[64,128]{1,0:T(8,128)S(1)} %bitcast.49, ...), kind=kLoop, calls=%fused_computation.18 | loop fusion | flops 262144 | bytes 622595 | tf_op jit(solution)/shard_map/jit(_where)/select_n | solution.py:240
  65.0 0.9 collective-permute-start.9
  66.0 0.2 copy.29
  66.2 22.5 %collective-permute-done.9 = f32[32,4,128]{2,1,0:T(4,128)S(1)} collective-permute-done((f32[32,4,128]{2,1,0:T(4,128)S(1)}, f32[32,4,128]{2,1,0:T(4,128)S(1)}, u32[]{:S(2)}, u32[]{:S(2)}) %collective-permute-start.9) | collective-permute-done | bytes 65568 | tf_op jit(solution)/shard_map/ppermute | solution.py:243
  88.8 2.1 %add.95 = f32[32,4,32,128]{3,0,2,1:T(8,128)S(1)} add(f32[32,4,32,128]{3,0,2,1:T(8,128)S(1)} %fusion.8, f32[32,4,32,128]{3,0,2,1:T(8,128)} %collective-permute-done.4) | non-fusion elementwise | flops 524288 | bytes 6291456 | tf_op jit(solution)/shard_map/add | solution.py:247
  90.9 4.3 %bitcast_add_fusion = f32[32,4,32,128]{3,2,1,0:T(8,128)} fusion(f32[32,32]{1,0:T(8,128)S(1)} %bitcast.52, f32[32,4,128]{2,1,0:T(4,128)S(1)} %fusion.18, f32[32,32,32]{2,1,0:T(8,128)S(1)} %copy-done.1, f32[32,4,32,128]{3,0,2,1:T(8,128)S(1)} %add.95), kind=kOutput, calls=%fused_computation | convolution fusion | flops 101711872 | bytes 4395008 | tf_op jit(solution)/shard_map/qab,qpby->qpay/dot_general | solution.py:251
  (36 shorter events, 0.8 us)
Async XLA Ops:
  0.0 13.7 %copy-start.6 = (f32[16,8]{0,1:T(8,128)S(1)}, f32[16,8]{0,1:T(8,128)}, u32[]{:S(2)}) copy-start(f32[16,8]{0,1:T(8,128)} %param.12) | copy-start | bytes 1540
  3.0 39.0 %collective-permute-start.5 = (f32[32,33]{1,0:T(8,128)S(1)}, f32[32,33]{1,0:T(8,128)S(1)}, u32[]{:S(2)}, u32[]{:S(2)}) collective-permute-start(f32[32,33]{1,0:T(8,128)S(1)} %pad_maximum_fusion.3), channel_id=1, source_target_pairs={{0,16},{16,0},{1,17},{17,1},{2,18},{18,2},{3,19},{19,3},{4,20},{20... | collective-permute-start | bytes 12680 | tf_op jit(solution)/shard_map/ppermute | solution.py:207
  8.4 6.0 %collective-permute-start = (f32[32,128]{1,0:T(8,128)}, f32[32,128]{1,0:T(8,128)S(1)}, u32[]{:S(2)}, u32[]{:S(2)}) collective-permute-start(f32[32,128]{1,0:T(8,128)} %get-tuple-element.10.own0_ref), channel_id=1, source_target_pairs={{1,0},{2,1},{3,2},{5,4},{6,5},{7,6},{9,8},{10,9},{11,10},{13,12},{... | collective-permute-start | bytes 49160 | tf_op jit(solution)/shard_map/ppermute | solution.py:22
  9.7 10.6 %collective-permute-start.2 = (f32[40,128]{1,0:T(8,128)}, f32[40,128]{1,0:T(8,128)S(1)}, u32[]{:S(2)}, u32[]{:S(2)}) collective-permute-start(f32[40,128]{1,0:T(8,128)} %get-tuple-element.12), channel_id=1, source_target_pairs={{0,1},{1,2},{2,3},{4,5},{5,6},{6,7},{8,9},{9,10},{10,11},{12,13},{... | collective-permute-start | bytes 61448 | tf_op jit(solution)/shard_map/ppermute | solution.py:22
  14.4 13.0 %copy-start.5 = (f32[32,128]{1,0:T(8,128)}, f32[32,128]{1,0:T(8,128)S(1)}, u32[]{:S(2)}) copy-start(f32[32,128]{1,0:T(8,128)S(1)} %collective-permute-done.yhi_ref) | copy-start | bytes 49156
  15.7 7.8 %collective-permute-start.1 = (f32[136,128]{1,0:T(8,128)}, f32[136,128]{1,0:T(8,128)S(1)}, u32[]{:S(2)}, u32[]{:S(2)}) collective-permute-start(f32[136,128]{1,0:T(8,128)} %dynamic_update_slice.6), channel_id=1, source_target_pairs={{0,4},{1,5},{2,6},{3,7},{4,8},{5,9},{6,10},{7,11},{8,12},{9,13},{1... | collective-permute-start | bytes 208904 | tf_op jit(solution)/shard_map/ppermute | solution.py:22
  20.3 7.1 %copy-start.4 = (f32[40,128]{1,0:T(8,128)}, f32[40,128]{1,0:T(8,128)S(1)}, u32[]{:S(2)}) copy-start(f32[40,128]{1,0:T(8,128)S(1)} %collective-permute-done.2.ylo_ref) | copy-start | bytes 61444
  21.6 5.8 %collective-permute-start.3 = (f32[136,128]{1,0:T(8,128)}, f32[136,128]{1,0:T(8,128)S(1)}, u32[]{:S(2)}, u32[]{:S(2)}) collective-permute-start(f32[136,128]{1,0:T(8,128)} %dynamic_update_slice.7), channel_id=1, source_target_pairs={{4,0},{5,1},{6,2},{7,3},{8,4},{9,5},{10,6},{11,7},{12,8},{13,9},{1... | collective-permute-start | bytes 208904 | tf_op jit(solution)/shard_map/ppermute | solution.py:22
  23.5 3.9 %copy-start.2 = (f32[136,128]{1,0:T(8,128)}, f32[136,128]{1,0:T(8,128)S(1)}, u32[]{:S(2)}) copy-start(f32[136,128]{1,0:T(8,128)S(1)} %collective-permute-done.1.xlo_ref) | copy-start | bytes 208900
  27.4 0.6 copy-start.3
  41.7 4.7 %copy-start = (f32[4,32,32,128]{3,2,1,0:T(8,128)S(1)}, f32[4,32,32,128]{3,2,1,0:T(8,128)}, u32[]{:S(2)}) copy-start(f32[4,32,32,128]{3,2,1,0:T(8,128)} %residual.1) | copy-start | bytes 6291460
  41.7 47.1 %collective-permute-start.4 = (f32[32,4,32,128]{3,0,2,1:T(8,128)}, f32[32,4,32,128]{3,0,2,1:T(8,128)}, u32[]{:S(2)}, u32[]{:S(2)}) collective-permute-start(f32[32,4,32,128]{3,0,2,1:T(8,128)} %fusion.6), channel_id=1, source_target_pairs={{0,16},{16,0},{1,17},{17,1},{2,18},{18,2},{3,19},{19,3},{4,20},{20... | collective-permute-start | bytes 6291464 | tf_op jit(solution)/shard_map/ppermute | solution.py:229
  46.4 2.3 %copy-start.1 = (f32[32,32,32]{2,1,0:T(8,128)S(1)}, f32[32,32,32]{2,1,0:T(8,128)}, u32[]{:S(2)}) copy-start(f32[32,32,32]{2,1,0:T(8,128)} %param.14) | copy-start | bytes 393220
  48.6 40.0 %copy-start.7 = (f32[32,1]{0,1:T(1,128)S(1)}, f32[32,1]{0,1:T(1,128)}, u32[]{:S(2)}) copy-start(f32[32,1]{0,1:T(1,128)} %param.15) | copy-start | bytes 388
  51.3 6.0 %collective-permute-start.7 = (f32[64,5,128]{2,1,0:T(8,128)S(1)}, f32[64,5,128]{2,1,0:T(8,128)S(1)}, u32[]{:S(2)}, u32[]{:S(2)}) collective-permute-start(f32[64,5,128]{2,1,0:T(8,128)S(1)} %pad_maximum_fusion), channel_id=1, source_target_pairs={{0,8},{4,12},{1,9},{5,13},{2,10},{6,14},{3,11},{7,15},{16,24},{20,... | collective-permute-start | bytes 491528 | tf_op jit(solution)/shard_map/ppermute | solution.py:238
  52.6 10.3 %collective-permute-start.6 = (f32[64,5,128]{2,1,0:T(8,128)S(1)}, f32[64,5,128]{2,1,0:T(8,128)S(1)}, u32[]{:S(2)}, u32[]{:S(2)}) collective-permute-start(f32[64,5,128]{2,1,0:T(8,128)S(1)} %pad_maximum_fusion), channel_id=1, source_target_pairs={{0,4},{4,8},{8,12},{1,5},{5,9},{9,13},{2,6},{6,10},{10,14},{3,7},{... | collective-permute-start | bytes 491528 | tf_op jit(solution)/shard_map/ppermute | solution.py:238
  54.7 8.2 %collective-permute-start.8 = (f32[64,5,128]{2,1,0:T(8,128)S(1)}, f32[64,5,128]{2,1,0:T(8,128)}, u32[]{:S(2)}, u32[]{:S(2)}) collective-permute-start(f32[64,5,128]{2,1,0:T(8,128)S(1)} %pad_maximum_fusion), channel_id=1, source_target_pairs={{0,12},{1,13},{2,14},{3,15},{16,28},{17,29},{18,30},{19,31}} | collective-permute-start | bytes 491528 | tf_op jit(solution)/shard_map/ppermute | solution.py:238
  65.0 23.7 %collective-permute-start.9 = (f32[32,4,128]{2,1,0:T(4,128)S(1)}, f32[32,4,128]{2,1,0:T(4,128)S(1)}, u32[]{:S(2)}, u32[]{:S(2)}) collective-permute-start(f32[32,4,128]{2,1,0:T(4,128)S(1)} %slice.80), channel_id=1, source_target_pairs={{0,16},{16,0},{1,17},{17,1},{2,18},{18,2},{3,19},{19,3},{4,20},{20... | collective-permute-start | bytes 196616 | tf_op jit(solution)/shard_map/ppermute | solution.py:243

commit v12 on v9

--- a/solution.py
+++ b/solution.py
@@ -169,7 +169,7 @@
             out_ref[p, s] = curl + axial_coupling * axial - src_ref[s, p]
         return carry
 
-    lax.fori_loop(0, n_s, body, 0)
+    lax.fori_loop(0, n_s, body, 0, unroll=2)
 
 
 def residual(a, src, xlo, xhi, ylo, yhi, own0, c2, c1, level_index, reluctivity, saturation, reg):

time: 95.4 us -> 94.1 us (0.986)
  Pallas kernels: 12 us -> 10.6 us
    pallas_call x1, Pallas kernels: 8.54 us -> 7.17 us  [residual(): pl.pallas_call(functools.partial(residual_kernel, kinds, levels), grid=(n...]
  transfers between devices with their start and end apart: 12 -> 12, of which waited for: 4 -> 4; matrix products, arithmetic and copies ran while one was open for 19% -> 19% of each run, Pallas kernels for 9% -> 8%
where the time goes in v12:
time: 94.1 us; the launch traced here: 92.4 us
  waiting for transfers between devices  32.7 us (35%)
  starting transfers between devices  23.3 us (25%)
  matrix products  18.1 us (19%)
  Pallas kernels  10.6 us (11%)
  other arithmetic  4.55 us (5%)
  local copies, waits for them, and re-layouts  2.8 us (3%)
    ppermute x1, waiting for transfers between devices, local(): lax.ppermute(carried[d], 'tm', [(i, (i + d) % n_tm) for i in range(n_tm)])  22.4 us
    ppermute x6, starting transfers between devices, shifted(): return lax.ppermute(block, axes, route)  14.9 us
    dot_general x2, matrix products, local(): jnp.einsum('qs,psxy->qpxy', tabs[d], resid, precision=lax.Precision.HIGH)  7.4 us
    pallas_call x1, Pallas kernels, residual(): pl.pallas_call(functools.partial(residual_kernel, kinds, levels), grid=(n...  7.17 us
    ppermute x3, waiting for transfers between devices, local(): got = lax.ppermute(msg_tail, 'gx', [(i, i + d) for i in range(n_gx - d)])  6.93 us
    dot_general x2, matrix products, local(): jnp.einsum('qb,qpby->qpy', row_last[d], parts[d], precision=lax.Precision...  6.47 us
    ppermute x3, starting transfers between devices, local(): got = lax.ppermute(msg_tail, 'gx', [(i, i + d) for i in range(n_gx - d)])  4.77 us
    dot_general x1, matrix products, local(): jnp.einsum('qab,qpby->qpay', inverse, spectrum, precision=lax.Precision.H...  4.25 us
  transfers between devices with their start and end apart: 12, of which 4 were waited for; matrix products, arithmetic and copies ran while one was open for 19% of the time, Pallas kernels for 8%

profile of v12, /device:TPU:12, one launch (start us, length us, event | category | flops | bytes accessed | tf_op | source)
XLA Modules:
  0.0 92.4 jit_solution(1119125490047033529)
XLA Ops:
  0.0 3.4 %halo_edges.1 = (f32[136,128]{1,0:T(8,128)}, f32[128,128]{1,0:T(8,128)}, f32[40,128]{1,0:T(8,128)}, f32[32,128]{1,0:T(8,128)}, f32[1,128]{1,0:T(1,128)}, /*index=5*/f32[1,128]{1,0:T(1,128)}) custom-call(f32[32,4,32,128]{3,2,1,0:T(8,128)} %a_ref.3, s32[32,128]{1,0:T(8,128)} %reg_ref.3), custom_call_target="tpu_custom_call" | custom-call | tf_op jit(solution)/shard_map/halo_edges/pallas_call | solution.py:86
  3.4 2.9 %collective-permute-start.4 = (f32[1,128]{1,0:T(1,128)}, f32[1,128]{1,0:T(1,128)S(1)}, u32[]{:S(2)}, u32[]{:S(2)}) collective-permute-start(f32[1,128]{1,0:T(1,128)} %get-tuple-element.15), channel_id=1, source_target_pairs={{4,1},{5,2},{6,3},{8,5},{9,6},{10,7},{12,9},{13,10},{14,11},{20,17... | collective-permute-start | bytes 1544 | tf_op jit(solution)/shard_map/ppermute | solution.py:22
  6.3 2.4 %collective-permute-start.3 = (f32[32,128]{1,0:T(8,128)}, f32[32,128]{1,0:T(8,128)S(1)}, u32[]{:S(2)}, u32[]{:S(2)}) collective-permute-start(f32[32,128]{1,0:T(8,128)} %get-tuple-element.14.own0_ref), channel_id=1, source_target_pairs={{1,0},{2,1},{3,2},{5,4},{6,5},{7,6},{9,8},{10,9},{11,10},{13,12},{... | collective-permute-start | bytes 49160 | tf_op jit(solution)/shard_map/ppermute | solution.py:22
  8.7 3.5 %collective-permute-start.2 = (f32[40,128]{1,0:T(8,128)}, f32[40,128]{1,0:T(8,128)S(1)}, u32[]{:S(2)}, u32[]{:S(2)}) collective-permute-start(f32[40,128]{1,0:T(8,128)} %get-tuple-element.13), channel_id=1, source_target_pairs={{0,1},{1,2},{2,3},{4,5},{5,6},{6,7},{8,9},{9,10},{10,11},{12,13},{... | collective-permute-start | bytes 61448 | tf_op jit(solution)/shard_map/ppermute | solution.py:22
  12.2 2.2 %collective-permute-start.1 = (f32[128,128]{1,0:T(8,128)}, f32[128,128]{1,0:T(8,128)S(1)}, u32[]{:S(2)}, u32[]{:S(2)}) collective-permute-start(f32[128,128]{1,0:T(8,128)} %get-tuple-element.12), channel_id=1, source_target_pairs={{4,0},{5,1},{6,2},{7,3},{8,4},{9,5},{10,6},{11,7},{12,8},{13,9},{1... | collective-permute-start | bytes 196616 | tf_op jit(solution)/shard_map/ppermute | solution.py:22
  14.4 2.1 %collective-permute-start = (f32[136,128]{1,0:T(8,128)}, f32[136,128]{1,0:T(8,128)S(1)}, u32[]{:S(2)}, u32[]{:S(2)}) collective-permute-start(f32[136,128]{1,0:T(8,128)} %get-tuple-element.11), channel_id=1, source_target_pairs={{0,4},{1,5},{2,6},{3,7},{4,8},{5,9},{6,10},{7,11},{8,12},{9,13},{1... | collective-permute-start | bytes 208904 | tf_op jit(solution)/shard_map/ppermute | solution.py:22
  16.5 0.3 slice_reduce_fusion
  17.1 1.9 %collective-permute-start.5 = (f32[1,128]{1,0:T(1,128)}, f32[1,128]{1,0:T(1,128)S(1)}, u32[]{:S(2)}, u32[]{:S(2)}) collective-permute-start(f32[1,128]{1,0:T(1,128)} %get-tuple-element.16), channel_id=1, source_target_pairs={{1,4},{2,5},{3,6},{5,8},{6,9},{7,10},{9,12},{10,13},{11,14},{17,20... | collective-permute-start | bytes 1544 | tf_op jit(solution)/shard_map/ppermute | solution.py:22
  19.0 0.7 copy.14.relu_ref
  19.7 3.4 %collective-permute-done.5.c1_ref = f32[1,128]{1,0:T(1,128)S(1)} collective-permute-done((f32[1,128]{1,0:T(1,128)}, f32[1,128]{1,0:T(1,128)S(1)}, u32[]{:S(2)}, u32[]{:S(2)}) %collective-permute-start.5) | collective-permute-done | bytes 544 | tf_op jit(solution)/shard_map/ppermute | solution.py:22
  23.1 1.5 %collective-permute-start.7 = (f32[32,33]{1,0:T(8,128)S(1)}, f32[32,33]{1,0:T(8,128)S(1)}, u32[]{:S(2)}, u32[]{:S(2)}) collective-permute-start(f32[32,33]{1,0:T(8,128)S(1)} %pad_maximum_fusion.3), channel_id=1, source_target_pairs={{0,16},{16,0},{1,17},{17,1},{2,18},{18,2},{3,19},{19,3},{4,20},{20... | collective-permute-start | bytes 12680 | tf_op jit(solution)/shard_map/ppermute | solution.py:209
  24.6 0.5 copy-done.5
  25.2 0.6 copy-done.2
  25.9 7.2 %residual.1 = f32[4,32,32,128]{3,2,1,0:T(8,128)} custom-call(f32[32,4,32,128]{3,2,1,0:T(8,128)} %a_ref.3, f32[32,4,32,128]{3,2,1,0:T(8,128)} %src_ref.1, f32[136,128]{1,0:T(8,128)} %copy-done.2, f32[128,128]{1,0:T(8,128)} %copy-done.3, f32[40,128]{1,0:T(8,128)} %copy-done.4, f32[32,128]{1,0:T(8,128)} %copy-done.5, f32[32,128]{1,0:T(8,128)} %get-tuple-element.14.own0_ref, ...), custom_call_target="tpu_custom_call" | custom-call | tf_op jit(solution)/shard_map/residual/pallas_call | solution.py:182
  33.0 5.2 %fusion.6 = f32[32,4,32,128]{3,0,2,1:T(8,128)} fusion(f32[4,32,32,128]{3,2,1,0:T(8,128)} %residual.1, s32[32]{0:T(128)S(1)} %get-tuple-element.17, s32[32]{0:T(128)S(1)} %get-tuple-element.18, pred[32]{0:T(512)(128)(4,1)S(1)} %fusion.61), kind=kOutput, calls=%fused_computation.7 | convolution fusion | flops 100679680 | bytes 4194592 | tf_op jit(solution)/shard_map/qs,psxy->qpxy/dot_general | solution.py:229
  38.2 0.5 collective-permute-start.6
  38.8 0.2 fusion.19
  38.9 4.0 %fusion = f32[32,1,4,128]{3,1,2,0:T(1,128)S(1)} fusion(f32[32,32,1,1]{1,2,3,0:T(1,128)S(1)} %bitcast.51, f32[32,4,32,128]{3,0,2,1:T(8,128)} %fusion.6), kind=kOutput, calls=%fused_computation.1 | convolution fusion | flops 3145728 | bytes 2166784 | tf_op jit(solution)/shard_map/qb,qpby->qpy/dot_general | solution.py:234
  43.0 2.2 %fusion.8 = f32[32,4,32,128]{3,0,2,1:T(8,128)S(1)} fusion(f32[4,32,32,128]{3,2,1,0:T(8,128)S(1)} %copy-done, s32[32]{0:T(128)S(1)} %get-tuple-element.18, s32[32]{0:T(128)S(1)} %add_select_fusion.3, pred[32]{0:T(512)(128)(4,1)S(1)} %fusion.62), kind=kOutput, calls=%fused_computation.9 | convolution fusion | flops 100679680 | bytes 4194592 | tf_op jit(solution)/shard_map/qs,psxy->qpxy/dot_general | solution.py:229
  45.2 2.4 %fusion.2 = f32[32,1,4,128]{3,1,2,0:T(1,128)S(1)} fusion(f32[32,4,32,128]{3,0,2,1:T(8,128)S(1)} %fusion.8, f32[32,32,32]{2,1,0:T(8,128)S(1)} %copy-done.1), kind=kOutput, calls=%fused_computation.3 | convolution fusion | flops 3145728 | bytes 2179072 | tf_op jit(solution)/shard_map/qb,qpby->qpy/dot_general | solution.py:234
  47.9 1.3 %collective-permute-start.9 = (f32[64,5,128]{2,1,0:T(8,128)S(1)}, f32[64,5,128]{2,1,0:T(8,128)S(1)}, u32[]{:S(2)}, u32[]{:S(2)}) collective-permute-start(f32[64,5,128]{2,1,0:T(8,128)S(1)} %pad_maximum_fusion), channel_id=1, source_target_pairs={{0,8},{4,12},{1,9},{5,13},{2,10},{6,14},{3,11},{7,15},{16,24},{20,... | collective-permute-start | bytes 491528 | tf_op jit(solution)/shard_map/ppermute | solution.py:240
  49.2 1.9 %collective-permute-start.8 = (f32[64,5,128]{2,1,0:T(8,128)S(1)}, f32[64,5,128]{2,1,0:T(8,128)S(1)}, u32[]{:S(2)}, u32[]{:S(2)}) collective-permute-start(f32[64,5,128]{2,1,0:T(8,128)S(1)} %pad_maximum_fusion), channel_id=1, source_target_pairs={{0,4},{4,8},{8,12},{1,5},{5,9},{9,13},{2,6},{6,10},{10,14},{3,7},{... | collective-permute-start | bytes 491528 | tf_op jit(solution)/shard_map/ppermute | solution.py:240
  51.1 1.6 %collective-permute-start.10 = (f32[64,5,128]{2,1,0:T(8,128)S(1)}, f32[64,5,128]{2,1,0:T(8,128)}, u32[]{:S(2)}, u32[]{:S(2)}) collective-permute-start(f32[64,5,128]{2,1,0:T(8,128)S(1)} %pad_maximum_fusion), channel_id=1, source_target_pairs={{0,12},{1,13},{2,14},{3,15},{16,28},{17,29},{18,30},{19,31}} | collective-permute-start | bytes 491528 | tf_op jit(solution)/shard_map/ppermute | solution.py:240
  52.6 6.3 %collective-permute-done.9 = f32[64,5,128]{2,1,0:T(8,128)S(1)} collective-permute-done((f32[64,5,128]{2,1,0:T(8,128)S(1)}, f32[64,5,128]{2,1,0:T(8,128)S(1)}, u32[]{:S(2)}, u32[]{:S(2)}) %collective-permute-start.9) | collective-permute-done | bytes 163872 | tf_op jit(solution)/shard_map/ppermute | solution.py:240
  58.9 0.7 collective-permute-done.8
  59.7 1.0 %slice_multiply_fusion = f32[64,1,128]{2,1,0:T(1,128)S(1)} fusion(f32[64,5,128]{2,1,0:T(8,128)} %collective-permute-done.10), kind=kLoop, calls=%fused_computation.21 | loop fusion | flops 8192 | bytes 65536 | tf_op jit(solution)/shard_map/mul | solution.py:241
  60.7 1.1 %fusion.17 = f32[64,4,128]{2,1,0:T(4,128)S(1)} fusion(f32[64,5,128]{2,1,0:T(8,128)S(1)} %collective-permute-done.8, f32[64,5,128]{2,1,0:T(8,128)S(1)} %collective-permute-done.9, f32[64,5,128]{2,1,0:T(8,128)} %collective-permute-done.10, f32[64,128]{1,0:T(8,128)S(1)} %bitcast.50, f32[64,128]{1,0:T(8,128)S(1)} %bitcast.48, f32[64,128]{1,0:T(8,128)S(1)} %bitcast.49, ...), kind=kLoop, calls=%fused_computation.18 | loop fusion | flops 262144 | bytes 622595 | tf_op jit(solution)/shard_map/jit(_where)/select_n | solution.py:242
  61.7 1.6 %collective-permute-start.11 = (f32[32,4,128]{2,1,0:T(4,128)S(1)}, f32[32,4,128]{2,1,0:T(4,128)S(1)}, u32[]{:S(2)}, u32[]{:S(2)}) collective-permute-start(f32[32,4,128]{2,1,0:T(4,128)S(1)} %slice.70), channel_id=1, source_target_pairs={{0,16},{16,0},{1,17},{17,1},{2,18},{18,2},{3,19},{19,3},{4,20},{20... | collective-permute-start | bytes 196616 | tf_op jit(solution)/shard_map/ppermute | solution.py:245
  63.3 0.2 copy.29
  63.6 22.4 %collective-permute-done.11 = f32[32,4,128]{2,1,0:T(4,128)S(1)} collective-permute-done((f32[32,4,128]{2,1,0:T(4,128)S(1)}, f32[32,4,128]{2,1,0:T(4,128)S(1)}, u32[]{:S(2)}, u32[]{:S(2)}) %collective-permute-start.11) | collective-permute-done | bytes 65568 | tf_op jit(solution)/shard_map/ppermute | solution.py:245
  86.1 2.1 %add.95 = f32[32,4,32,128]{3,0,2,1:T(8,128)S(1)} add(f32[32,4,32,128]{3,0,2,1:T(8,128)S(1)} %fusion.8, f32[32,4,32,128]{3,0,2,1:T(8,128)} %collective-permute-done.6) | non-fusion elementwise | flops 524288 | bytes 6291456 | tf_op jit(solution)/shard_map/add | solution.py:249
  88.2 4.2 %bitcast_add_fusion = f32[32,4,32,128]{3,2,1,0:T(8,128)} fusion(f32[32,32]{1,0:T(8,128)S(1)} %bitcast.52, f32[32,4,128]{2,1,0:T(4,128)S(1)} %fusion.18, f32[32,32,32]{2,1,0:T(8,128)S(1)} %copy-done.1, f32[32,4,32,128]{3,0,2,1:T(8,128)S(1)} %add.95), kind=kOutput, calls=%fused_computation | convolution fusion | flops 101711872 | bytes 4395008 | tf_op jit(solution)/shard_map/qab,qpby->qpay/dot_general | solution.py:253
  (40 shorter events, 0.7 us)
Async XLA Ops:
  0.0 16.5 %copy-start.1 = (f32[32,32,32]{2,1,0:T(8,128)S(1)}, f32[32,32,32]{2,1,0:T(8,128)}, u32[]{:S(2)}) copy-start(f32[32,32,32]{2,1,0:T(8,128)} %param.14) | copy-start | bytes 393220
  0.0 16.9 %copy-start.7 = (f32[32,1]{0,1:T(1,128)S(1)}, f32[32,1]{0,1:T(1,128)}, u32[]{:S(2)}) copy-start(f32[32,1]{0,1:T(1,128)} %param.15) | copy-start | bytes 388
  0.0 19.0 %copy-start.6 = (f32[16,8]{0,1:T(8,128)S(1)}, f32[16,8]{0,1:T(8,128)}, u32[]{:S(2)}) copy-start(f32[16,8]{0,1:T(8,128)} %param.12) | copy-start | bytes 1540
  3.4 13.6 %collective-permute-start.4 = (f32[1,128]{1,0:T(1,128)}, f32[1,128]{1,0:T(1,128)S(1)}, u32[]{:S(2)}, u32[]{:S(2)}) collective-permute-start(f32[1,128]{1,0:T(1,128)} %get-tuple-element.15), channel_id=1, source_target_pairs={{4,1},{5,2},{6,3},{8,5},{9,6},{10,7},{12,9},{13,10},{14,11},{20,17... | collective-permute-start | bytes 1544 | tf_op jit(solution)/shard_map/ppermute | solution.py:22
  6.3 18.3 %collective-permute-start.3 = (f32[32,128]{1,0:T(8,128)}, f32[32,128]{1,0:T(8,128)S(1)}, u32[]{:S(2)}, u32[]{:S(2)}) collective-permute-start(f32[32,128]{1,0:T(8,128)} %get-tuple-element.14.own0_ref), channel_id=1, source_target_pairs={{1,0},{2,1},{3,2},{5,4},{6,5},{7,6},{9,8},{10,9},{11,10},{13,12},{... | collective-permute-start | bytes 49160 | tf_op jit(solution)/shard_map/ppermute | solution.py:22
  8.7 15.9 %collective-permute-start.2 = (f32[40,128]{1,0:T(8,128)}, f32[40,128]{1,0:T(8,128)S(1)}, u32[]{:S(2)}, u32[]{:S(2)}) collective-permute-start(f32[40,128]{1,0:T(8,128)} %get-tuple-element.13), channel_id=1, source_target_pairs={{0,1},{1,2},{2,3},{4,5},{5,6},{6,7},{8,9},{9,10},{10,11},{12,13},{... | collective-permute-start | bytes 61448 | tf_op jit(solution)/shard_map/ppermute | solution.py:22
  12.2 12.4 %collective-permute-start.1 = (f32[128,128]{1,0:T(8,128)}, f32[128,128]{1,0:T(8,128)S(1)}, u32[]{:S(2)}, u32[]{:S(2)}) collective-permute-start(f32[128,128]{1,0:T(8,128)} %get-tuple-element.12), channel_id=1, source_target_pairs={{4,0},{5,1},{6,2},{7,3},{8,4},{9,5},{10,6},{11,7},{12,8},{13,9},{1... | collective-permute-start | bytes 196616 | tf_op jit(solution)/shard_map/ppermute | solution.py:22
  14.4 10.2 %collective-permute-start = (f32[136,128]{1,0:T(8,128)}, f32[136,128]{1,0:T(8,128)S(1)}, u32[]{:S(2)}, u32[]{:S(2)}) collective-permute-start(f32[136,128]{1,0:T(8,128)} %get-tuple-element.11), channel_id=1, source_target_pairs={{0,4},{1,5},{2,6},{3,7},{4,8},{5,9},{6,10},{7,11},{8,12},{9,13},{1... | collective-permute-start | bytes 208904 | tf_op jit(solution)/shard_map/ppermute | solution.py:22
  17.1 7.5 %copy-start.8 = (f32[1,128]{1,0:T(1,128)}, f32[1,128]{1,0:T(1,128)S(1)}, u32[]{:S(2)}) copy-start(f32[1,128]{1,0:T(1,128)S(1)} %collective-permute-done.4.c2_ref) | copy-start | bytes 1540
  17.1 6.0 %collective-permute-start.5 = (f32[1,128]{1,0:T(1,128)}, f32[1,128]{1,0:T(1,128)S(1)}, u32[]{:S(2)}, u32[]{:S(2)}) collective-permute-start(f32[1,128]{1,0:T(1,128)} %get-tuple-element.16), channel_id=1, source_target_pairs={{1,4},{2,5},{3,6},{5,8},{6,9},{7,10},{9,12},{10,13},{11,14},{17,20... | collective-permute-start | bytes 1544 | tf_op jit(solution)/shard_map/ppermute | solution.py:22
  23.1 1.6 %copy-start.9 = (f32[1,128]{1,0:T(1,128)}, f32[1,128]{1,0:T(1,128)S(1)}, u32[]{:S(2)}) copy-start(f32[1,128]{1,0:T(1,128)S(1)} %collective-permute-done.5.c1_ref) | copy-start | bytes 1540
  23.1 15.7 %collective-permute-start.7 = (f32[32,33]{1,0:T(8,128)S(1)}, f32[32,33]{1,0:T(8,128)S(1)}, u32[]{:S(2)}, u32[]{:S(2)}) collective-permute-start(f32[32,33]{1,0:T(8,128)S(1)} %pad_maximum_fusion.3), channel_id=1, source_target_pairs={{0,16},{16,0},{1,17},{17,1},{2,18},{18,2},{3,19},{19,3},{4,20},{20... | collective-permute-start | bytes 12680 | tf_op jit(solution)/shard_map/ppermute | solution.py:209
  24.6 0.6 copy-start.5
  24.6 0.6 copy-start.4
  24.6 0.6 copy-start.3
  25.2 0.6 copy-start.2
  38.2 4.8 %copy-start = (f32[4,32,32,128]{3,2,1,0:T(8,128)S(1)}, f32[4,32,32,128]{3,2,1,0:T(8,128)}, u32[]{:S(2)}) copy-start(f32[4,32,32,128]{3,2,1,0:T(8,128)} %residual.1) | copy-start | bytes 6291460
  38.2 47.9 %collective-permute-start.6 = (f32[32,4,32,128]{3,0,2,1:T(8,128)}, f32[32,4,32,128]{3,0,2,1:T(8,128)}, u32[]{:S(2)}, u32[]{:S(2)}) collective-permute-start(f32[32,4,32,128]{3,0,2,1:T(8,128)} %fusion.6), channel_id=1, source_target_pairs={{0,16},{16,0},{1,17},{17,1},{2,18},{18,2},{3,19},{19,3},{4,20},{20... | collective-permute-start | bytes 6291464 | tf_op jit(solution)/shard_map/ppermute | solution.py:231
  47.9 11.0 %collective-permute-start.9 = (f32[64,5,128]{2,1,0:T(8,128)S(1)}, f32[64,5,128]{2,1,0:T(8,128)S(1)}, u32[]{:S(2)}, u32[]{:S(2)}) collective-permute-start(f32[64,5,128]{2,1,0:T(8,128)S(1)} %pad_maximum_fusion), channel_id=1, source_target_pairs={{0,8},{4,12},{1,9},{5,13},{2,10},{6,14},{3,11},{7,15},{16,24},{20,... | collective-permute-start | bytes 491528 | tf_op jit(solution)/shard_map/ppermute | solution.py:240
  49.2 10.5 %collective-permute-start.8 = (f32[64,5,128]{2,1,0:T(8,128)S(1)}, f32[64,5,128]{2,1,0:T(8,128)S(1)}, u32[]{:S(2)}, u32[]{:S(2)}) collective-permute-start(f32[64,5,128]{2,1,0:T(8,128)S(1)} %pad_maximum_fusion), channel_id=1, source_target_pairs={{0,4},{4,8},{8,12},{1,5},{5,9},{9,13},{2,6},{6,10},{10,14},{3,7},{... | collective-permute-start | bytes 491528 | tf_op jit(solution)/shard_map/ppermute | solution.py:240
  51.1 8.6 %collective-permute-start.10 = (f32[64,5,128]{2,1,0:T(8,128)S(1)}, f32[64,5,128]{2,1,0:T(8,128)}, u32[]{:S(2)}, u32[]{:S(2)}) collective-permute-start(f32[64,5,128]{2,1,0:T(8,128)S(1)} %pad_maximum_fusion), channel_id=1, source_target_pairs={{0,12},{1,13},{2,14},{3,15},{16,28},{17,29},{18,30},{19,31}} | collective-permute-start | bytes 491528 | tf_op jit(solution)/shard_map/ppermute | solution.py:240
  61.7 24.2 %collective-permute-start.11 = (f32[32,4,128]{2,1,0:T(4,128)S(1)}, f32[32,4,128]{2,1,0:T(4,128)S(1)}, u32[]{:S(2)}, u32[]{:S(2)}) collective-permute-start(f32[32,4,128]{2,1,0:T(4,128)S(1)} %slice.70), channel_id=1, source_target_pairs={{0,16},{16,0},{1,17},{17,1},{2,18},{18,2},{3,19},{19,3},{4,20},{20... | collective-permute-start | bytes 196616 | tf_op jit(solution)/shard_map/ppermute | solution.py:245
